TPU v7x, 128 devices: a whole 4x4x4 slice. The times are simulated.
128 devices in a mesh: src: 16 (over y_lo, z, core), tgt: 8 (over y_hi, x).
Axes of the slice: x: 4, y: 4 (y_hi: 2, y_lo: 2; y = y_hi * 2 + y_lo), z: 4, core: 2. Of those that a mesh axis runs over, the one named last changes fastest.
Arguments:
- src_emb: bfloat16 [16384, 768], P(('src', 'tgt')), may hold values from -0.05119037 to 0.05119037
- right_sentence_vectors: bfloat16 [8192, 768], P(('tgt', 'src')), may hold values from -0.05119037 to 0.05119037
- src_mass: float32 [16384], P('src'), may hold values from 0.25 to 4
- tgt_mass: float32 [8192], P('tgt'), may hold values from 0.5 to 8
Outputs:
- grad_src: float32 [16384, 768], P(('src', 'tgt'))
- grad_tgt: float32 [8192, 768], P(('tgt', 'src'))
All inputs are finite; a program needn't handle non-finite values.
Results may differ from a plain program's by a relative error of at most 0.00045.
Values may be sent and summed in bfloat16 or wider, within the bound.
No kernel may reach another device: no remote copies, remote signals or barrier semaphores. Data moves between devices by JAX's collectives and lax.ppermute only.
A program may use at most 64 MiB of HBM per device.

v0:
```python
import jax
import jax.numpy as jnp
from jax import lax
from jax.sharding import PartitionSpec as P

ITERS = 4


regularizer_epsilon = 0.05
highest = lax.Precision.HIGHEST

GATHER_BITS = {"tgt": ((1, 2, 0), (1, 0, 2)), "src": ((2, 1, 3, 0), (2, 3, 1, 0))}
SCATTER_BITS = {"tgt": ((0, 2, 1), (2, 0, 1)), "src": ((0, 3, 1, 2), (0, 1, 3, 2))}


def partner(axis, n, bit):
    return [(i, i ^ (1 << bit)) for i in range(n)]


def axis_size(axis):
    return lax.axis_size(axis)


def tree_sum(x, axis):
    n = axis_size(axis)
    spread = jnp.broadcast_to(x[None], (n,) + x.shape)
    return lax.all_to_all(spread, axis, 0, 0, tiled=False).sum(0)


def tree_gather(x, axis, order):
    n = axis_size(axis)
    me = lax.axis_index(axis)
    for bit in order:
        other = lax.ppermute(x, axis, partner(axis, n, bit))
        up = ((me >> bit) & 1) == 1
        x = jnp.where(up, jnp.stack([other, x]), jnp.stack([x, other]))
    held = list(reversed(order))
    perm = [held.index(b) for b in reversed(range(len(order)))]
    x = jnp.transpose(x, perm + list(range(len(order), x.ndim)))
    return x.reshape((n * x.shape[len(order)],) + x.shape[len(order) + 1:])


def tree_scatter(x, axis, order):
    n = axis_size(axis)
    me = lax.axis_index(axis)
    k = len(order)
    rows = x.shape[0] // n
    x = x.reshape((2,) * k + (rows,) + x.shape[1:])
    held = list(reversed(range(k)))
    for bit in order:
        a = held.index(bit)
        lo = lax.index_in_dim(x, 0, a, keepdims=False)
        hi = lax.index_in_dim(x, 1, a, keepdims=False)
        up = ((me >> bit) & 1) == 1
        keep = jnp.where(up, hi, lo)
        send = jnp.where(up, lo, hi)
        x = keep + lax.ppermute(send, axis, partner(axis, n, bit))
        held.pop(a)
    return x


def split_gather(x, axis):
    orders = GATHER_BITS[axis]
    w = x.shape[1] // len(orders)
    return jnp.concatenate(
        [tree_gather(x[:, i * w:(i + 1) * w], axis, o) for i, o in enumerate(orders)], 1
    )


def split_scatter(x, axis):
    orders = SCATTER_BITS[axis]
    w = x.shape[1] // len(orders)
    return jnp.concatenate(
        [tree_scatter(x[:, i * w:(i + 1) * w], axis, o) for i, o in enumerate(orders)], 1
    )


def row_total(part):
    return tree_sum(part, "tgt")


def col_total(part):
    return tree_sum(part, "src")


def times_vector(kernel, vector):
    return jnp.sum(kernel.astype(jnp.float32) * vector[None, :], axis=1)


def vector_times(vector, kernel):
    return jnp.sum(vector[:, None] * kernel.astype(jnp.float32), axis=0)


def per_device(src_emb, right_sentence_vectors, src_mass, tgt_mass):
    src_rows = split_gather(src_emb, "tgt")
    target_rows = split_gather(right_sentence_vectors, "src")

    kernel_grid = (
        lax.dot_general(
            src_rows, target_rows, (((1,), (1,)), ((), ())), preferred_element_type=jnp.float32
        )
        / regularizer_epsilon
    )
    kernel = lax.optimization_barrier(jnp.exp(kernel_grid).astype(jnp.bfloat16))
    weighted = kernel * kernel_grid

    vector = jnp.ones(tgt_mass.shape, jnp.float32)
    old_saved, row_saved, src_saved, col_saved, tgt_saved = ([], [], [], [], [])
    tgt_adj = None
    for iteration in range(ITERS):
        old_saved.append(vector)
        row_sum = row_total(times_vector(kernel, vector))
        src_scale = src_mass / row_sum
        if iteration == ITERS - 1:
            both = col_total(
                jnp.stack([vector_times(src_scale, kernel), vector_times(src_scale, weighted)])
            )
            col_sum, tgt_adj = both[0], both[1]
        else:
            col_sum = col_total(vector_times(src_scale, kernel))
        vector = tgt_mass / col_sum
        row_saved.append(row_sum)
        src_saved.append(src_scale)
        col_saved.append(col_sum)
        tgt_saved.append(vector)
    last_src = src_saved[-1]
    last_tgt = tgt_saved[-1]
    row_bars = [None] * ITERS
    col_bars = [None] * ITERS
    for iteration in reversed(range(ITERS)):
        col_bar = -tgt_adj * tgt_saved[iteration] / col_saved[iteration]
        part = times_vector(kernel, col_bar)
        if iteration == ITERS - 1:
            part = part + times_vector(weighted, last_tgt)
        back = row_total(part)
        row_bar = -back * src_saved[iteration] / row_saved[iteration]
        if iteration > 0:
            tgt_adj = col_total(vector_times(row_bar, kernel))
        row_bars[iteration] = row_bar
        col_bars[iteration] = col_bar
    left = jnp.stack(row_bars + src_saved, axis=1)
    right = jnp.stack(old_saved + col_bars, axis=1)
    lowrank = lax.dot_general(
        left, right, (((1,), (1,)), ((), ())), precision=highest, preferred_element_type=jnp.float32
    )
    cross_term_grid = (
        kernel * (last_src[:, None] * last_tgt[None, :] * (1.0 + kernel_grid) + lowrank)
    ).astype(jnp.bfloat16)
    left_share_piece = (
        jnp.dot(cross_term_grid, target_rows, preferred_element_type=jnp.float32)
        / regularizer_epsilon
    )
    right_share_piece = (
        lax.dot_general(
            cross_term_grid, src_rows, (((0,), (0,)), ((), ())), preferred_element_type=jnp.float32
        )
        / regularizer_epsilon
    )
    grad_src = split_scatter(left_share_piece, "tgt")
    grad_tgt = split_scatter(right_share_piece, "src")
    return (grad_src, grad_tgt)


def solution(mesh):
    placed = (P(("src", "tgt"), None), P(("tgt", "src"), None), P("src"), P("tgt"))
    return jax.shard_map(
        per_device,
        mesh=mesh,
        in_specs=placed,
        out_specs=(P(("src", "tgt"), None), P(("tgt", "src"), None)),
        check_vma=False,
    )
```

profile of v0, /device:TPU:0, one launch (start us, length us, event | category | flops | bytes accessed | tf_op | source)
XLA Modules:
  0.0 269.6 jit_solution(2940202652006284062)
XLA Ops:
  1.5 4.0 %collective-permute-start.10 = (bf16[64,384]{1,0:T(8,128)(2,1)S(1)}, bf16[64,384]{1,0:T(8,128)(2,1)S(1)}, u32[]{:S(2)}, u32[]{:S(2)}) collective-permute-start(bf16[64,384]{1,0:T(8,128)(2,1)S(1)} %get-tuple-element.31), channel_id=1, source_target_pairs={{0,32},{8,40},{16,48},{24,56},{32,0},{40,8},{48,16},{56,24},{64,96... | collective-permute-start | bytes 147464 | tf_op jit(solution)/shard_map/ppermute | solution.py:34
  6.6 3.1 %collective-permute-start.3 = (bf16[128,384]{1,0:T(8,128)(2,1)S(1)}, bf16[128,384]{1,0:T(8,128)(2,1)S(1)}, u32[]{:S(2)}, u32[]{:S(2)}) collective-permute-start(bf16[128,384]{1,0:T(8,128)(2,1)S(1)} %get-tuple-element.23), channel_id=1, source_target_pairs={{0,2},{1,3},{2,0},{3,1},{4,6},{5,7},{6,4},{7,5},{8,10},{9,11},{10,... | collective-permute-start | bytes 294920 | tf_op jit(solution)/shard_map/ppermute | solution.py:34
  15.9 3.3 %collective-permute-start.1 = (bf16[2,128,384]{2,1,0:T(8,128)(2,1)S(1)}, bf16[2,128,384]{2,1,0:T(8,128)(2,1)S(1)}, u32[]{:S(2)}, u32[]{:S(2)}) collective-permute-start(bf16[2,128,384]{2,1,0:T(8,128)(2,1)S(1)} %maximum_select_fusion.12), channel_id=1, source_target_pairs={{0,4},{1,5},{2,6},{3,7},{4,0},{5,1},{6,2},{7,3},{8,12},{9,13},{10,... | collective-permute-start | bytes 589832 | tf_op jit(solution)/shard_map/ppermute | solution.py:34
  22.6 2.5 collective-permute-done.4
  26.4 3.2 %collective-permute-done.8 = bf16[2,2,64,384]{3,2,0,1:T(8,128)(2,1)S(1)} collective-permute-done((bf16[2,2,64,384]{3,2,0,1:T(8,128)(2,1)S(1)}, bf16[2,2,64,384]{3,2,0,1:T(8,128)(2,1)S(1)}, u32[]{:S(2)}, u32[]{:S(2)}) %collective-permute-start.8) | collective-permute-done | bytes 196640 | tf_op jit(solution)/shard_map/ppermute | solution.py:34
  30.5 5.8 %collective-permute-done.5 = bf16[2,2,128,384]{3,2,1,0:T(8,128)(2,1)S(1)} collective-permute-done((bf16[2,2,128,384]{3,2,1,0:T(8,128)(2,1)S(1)}, bf16[2,2,128,384]{3,2,1,0:T(8,128)(2,1)S(1)}, u32[]{:S(2)}, u32[]{:S(2)}) %collective-permute-start.5) | collective-permute-done | bytes 393248 | tf_op jit(solution)/shard_map/ppermute | solution.py:34
  37.5 3.8 %exponential_convert_fusion = (bf16[1024,1024]{1,0:T(8,128)(2,1)S(1)}, f32[1024,1024]{1,0:T(8,128)}) fusion(bf16[1024,384]{1,0:T(8,128)(2,1)S(1)} %bitcast.201, bf16[1024,384]{1,0:T(8,128)(2,1)S(1)} %bitcast.203, bf16[1024,384]{1,0:T(8,128)(2,1)S(1)} %bitcast.205, bf16[1024,384]{1,0:T(8,128)(2,1)S(1)} %bitcast.207), kind=kOutput, calls=%fused_computation.34 | convolution fusion | flops 1619001344 | bytes 9437184 | tf_op jit(solution)/shard_map/dot_general | solution.py:99
  41.6 12.7 %all_to_all.89 = f32[8,1,1024]{2,1,0:T(1,128)S(1)} all-to-all(f32[8,1,1024]{2,1,0:T(1,128)S(1)} %broadcast_in_dim.44), channel_id=1, replica_groups=mesh['src'=16,'tgt'=8] {'tgt'}, dimensions={0} | all-to-all | bytes 65536 | tf_op jit(solution)/shard_map/all_to_all | solution.py:27
  54.9 10.8 %all_to_all.90 = f32[16,1,1024]{2,1,0:T(1,128)S(1)} all-to-all(f32[16,1,1024]{2,1,0:T(1,128)S(1)} %broadcast_in_dim.45), channel_id=1, replica_groups=mesh['src'=16,'tgt'=8] {'src'}, dimensions={0} | all-to-all | bytes 131072 | tf_op jit(solution)/shard_map/all_to_all | solution.py:27
  66.2 10.7 %all_to_all.91 = f32[8,1,1024]{2,1,0:T(1,128)S(1)} all-to-all(f32[8,1,1024]{2,1,0:T(1,128)S(1)} %broadcast_in_dim.46), channel_id=1, replica_groups=mesh['src'=16,'tgt'=8] {'tgt'}, dimensions={0} | all-to-all | bytes 65536 | tf_op jit(solution)/shard_map/all_to_all | solution.py:27
  77.5 8.7 %all_to_all.92 = f32[16,1,1024]{2,1,0:T(1,128)S(1)} all-to-all(f32[16,1,1024]{2,1,0:T(1,128)S(1)} %broadcast_in_dim.47), channel_id=1, replica_groups=mesh['src'=16,'tgt'=8] {'src'}, dimensions={0} | all-to-all | bytes 131072 | tf_op jit(solution)/shard_map/all_to_all | solution.py:27
  86.8 10.1 %all_to_all.93 = f32[8,1,1024]{2,1,0:T(1,128)S(1)} all-to-all(f32[8,1,1024]{2,1,0:T(1,128)S(1)} %broadcast_in_dim.48), channel_id=1, replica_groups=mesh['src'=16,'tgt'=8] {'tgt'}, dimensions={0} | all-to-all | bytes 65536 | tf_op jit(solution)/shard_map/all_to_all | solution.py:27
  97.5 8.7 %all_to_all.94 = f32[16,1,1024]{2,1,0:T(1,128)S(1)} all-to-all(f32[16,1,1024]{2,1,0:T(1,128)S(1)} %broadcast_in_dim.49), channel_id=1, replica_groups=mesh['src'=16,'tgt'=8] {'src'}, dimensions={0} | all-to-all | bytes 131072 | tf_op jit(solution)/shard_map/all_to_all | solution.py:27
  106.8 10.5 %all_to_all.95 = f32[8,1,1024]{2,1,0:T(1,128)S(1)} all-to-all(f32[8,1,1024]{2,1,0:T(1,128)S(1)} %broadcast_in_dim.50), channel_id=1, replica_groups=mesh['src'=16,'tgt'=8] {'tgt'}, dimensions={0} | all-to-all | bytes 65536 | tf_op jit(solution)/shard_map/all_to_all | solution.py:27
  117.4 3.2 %fusion.6 = (f32[1024]{0:T(1024)S(1)}, f32[1024]{0:T(1024)S(1)}) fusion(bf16[1024,1024]{1,0:T(8,128)(2,1)S(1)} %get-tuple-element.35, f32[1024]{0:T(1024)S(1)} %div.68, f32[1024,1024]{1,0:T(8,128)} %get-tuple-element.36), kind=kLoop, calls=%fused_computation.23 | loop fusion | flops 7337984 | bytes 6303744 | tf_op jit(solution)/shard_map/reduce_sum | solution.py:91
  120.7 9.3 %all_to_all.96 = f32[16,2,1024]{2,1,0:T(2,128)S(1)} all-to-all(f32[16,2,1024]{2,1,0:T(2,128)S(1)} %broadcast_in_dim.51), channel_id=1, replica_groups=mesh['src'=16,'tgt'=8] {'src'}, dimensions={0} | all-to-all | bytes 262144 | tf_op jit(solution)/shard_map/all_to_all | solution.py:27
  130.1 3.5 %multiply_reduce_fusion = (f32[1024]{0:T(1024)S(1)}, f32[1024]{0:T(1024)S(1)}) fusion(f32[1024,1024]{1,0:T(8,128)} %get-tuple-element.36, bf16[1024,1024]{1,0:T(8,128)(2,1)S(1)} %get-tuple-element.35, f32[1024]{0:T(1024)S(1)} %get-tuple-element.7, f32[1024]{0:T(1024)S(1)} %get-tuple-element.6), kind=kLoop, calls=%fused_computation.32 | loop fusion | flops 7337984 | bytes 6307840 | tf_op jit(solution)/shard_map/reduce_sum | solution.py:87
  133.6 10.1 %all_to_all.97 = f32[8,1,1024]{2,1,0:T(1,128)S(1)} all-to-all(f32[8,1,1024]{2,1,0:T(1,128)S(1)} %broadcast_in_dim.52), channel_id=1, replica_groups=mesh['src'=16,'tgt'=8] {'tgt'}, dimensions={0} | all-to-all | bytes 65536 | tf_op jit(solution)/shard_map/all_to_all | solution.py:27
  144.3 8.7 %all_to_all.98 = f32[16,1,1024]{2,1,0:T(1,128)S(1)} all-to-all(f32[16,1,1024]{2,1,0:T(1,128)S(1)} %broadcast_in_dim.53), channel_id=1, replica_groups=mesh['src'=16,'tgt'=8] {'src'}, dimensions={0} | all-to-all | bytes 131072 | tf_op jit(solution)/shard_map/all_to_all | solution.py:27
  153.6 10.3 %all_to_all.99 = f32[8,1,1024]{2,1,0:T(1,128)S(1)} all-to-all(f32[8,1,1024]{2,1,0:T(1,128)S(1)} %broadcast_in_dim.54), channel_id=1, replica_groups=mesh['src'=16,'tgt'=8] {'tgt'}, dimensions={0} | all-to-all | bytes 65536 | tf_op jit(solution)/shard_map/all_to_all | solution.py:27
  164.5 8.7 %all_to_all.100 = f32[16,1,1024]{2,1,0:T(1,128)S(1)} all-to-all(f32[16,1,1024]{2,1,0:T(1,128)S(1)} %broadcast_in_dim.55), channel_id=1, replica_groups=mesh['src'=16,'tgt'=8] {'src'}, dimensions={0} | all-to-all | bytes 131072 | tf_op jit(solution)/shard_map/all_to_all | solution.py:27
  173.8 10.4 %all_to_all.101 = f32[8,1,1024]{2,1,0:T(1,128)S(1)} all-to-all(f32[8,1,1024]{2,1,0:T(1,128)S(1)} %broadcast_in_dim.56), channel_id=1, replica_groups=mesh['src'=16,'tgt'=8] {'tgt'}, dimensions={0} | all-to-all | bytes 65536 | tf_op jit(solution)/shard_map/all_to_all | solution.py:27
  184.8 8.7 %all_to_all.102 = f32[16,1,1024]{2,1,0:T(1,128)S(1)} all-to-all(f32[16,1,1024]{2,1,0:T(1,128)S(1)} %broadcast_in_dim.57), channel_id=1, replica_groups=mesh['src'=16,'tgt'=8] {'src'}, dimensions={0} | all-to-all | bytes 131072 | tf_op jit(solution)/shard_map/all_to_all | solution.py:27
  194.7 3.6 %all-to-all-start.14 = ((f32[8,1,1024]{2,1,0:T(1,128)}), f32[8,1,1024]{2,1,0:T(1,128)S(1)}, u32[]{:S(2)}, u32[]{:S(2)}) async-start(f32[8,1,1024]{2,1,0:T(1,128)} %broadcast_in_dim.58), calls=%async_computation.14 | async-start | bytes 65536 | tf_op jit(solution)/shard_map/all_to_all | solution.py:27
  198.3 7.4 %all-to-all-done.14 = f32[8,1,1024]{2,1,0:T(1,128)S(1)} async-done(((f32[8,1,1024]{2,1,0:T(1,128)}), f32[8,1,1024]{2,1,0:T(1,128)S(1)}, u32[]{:S(2)}, u32[]{:S(2)}) %all-to-all-start.14) | async-done | bytes 32800 | tf_op jit(solution)/shard_map/all_to_all | solution.py:27
  205.9 6.2 %fusion.14 = bf16[1024,1024]{1,0:T(8,128)(2,1)S(1)} fusion(bf16[1024,1024]{1,0:T(8,128)(2,1)S(1)} %get-tuple-element.35, f32[1024,1024]{1,0:T(8,128)} %get-tuple-element.36, f32[1024,8]{0,1:T(8,128)S(1)} %stack.392, f32[1024,8]{0,1:T(8,128)S(1)} %stack.400, f32[1024]{0:T(1024)S(1)} %get-tuple-element.7, f32[1024]{0:T(1024)S(1)} %div.68), kind=kOutput, calls=%fused_computation.31 | convolution fusion | flops 109051904 | bytes 8462336 | tf_op jit(solution)/shard_map/dot_general | solution.py:143
  220.9 16.2 %collective-permute-done.14 = f32[2,2,128,384]{3,2,1,0:T(8,128)S(1)} collective-permute-done((f32[2,2,128,384]{3,2,1,0:T(8,128)S(1)}, f32[2,2,128,384]{3,2,1,0:T(8,128)S(1)}, u32[]{:S(2)}, u32[]{:S(2)}) %collective-permute-start.14) | collective-permute-done | bytes 786464 | tf_op jit(solution)/shard_map/ppermute | solution.py:57
  238.0 2.6 collective-permute-done.17
  242.9 3.7 %collective-permute-done.21 = f32[2,2,64,384]{3,2,1,0:T(8,128)S(1)} collective-permute-done((f32[2,2,64,384]{3,2,1,0:T(8,128)S(1)}, f32[2,2,64,384]{3,2,1,0:T(8,128)S(1)}, u32[]{:S(2)}, u32[]{:S(2)}) %collective-permute-start.21) | collective-permute-done | bytes 393248 | tf_op jit(solution)/shard_map/ppermute | solution.py:57
  247.3 10.1 %collective-permute-done.15 = f32[2,128,384]{2,1,0:T(8,128)S(1)} collective-permute-done((f32[2,128,384]{2,1,0:T(8,128)S(1)}, f32[2,128,384]{2,1,0:T(8,128)S(1)}, u32[]{:S(2)}, u32[]{:S(2)}) %collective-permute-start.15) | collective-permute-done | bytes 393248 | tf_op jit(solution)/shard_map/ppermute | solution.py:57
  257.5 2.1 collective-permute-start.16
  262.7 2.4 collective-permute-start.23
  (196 shorter events, 42.9 us)
Async XLA Ops:
  1.5 8.7 %collective-permute-start.10 = (bf16[64,384]{1,0:T(8,128)(2,1)S(1)}, bf16[64,384]{1,0:T(8,128)(2,1)S(1)}, u32[]{:S(2)}, u32[]{:S(2)}) collective-permute-start(bf16[64,384]{1,0:T(8,128)(2,1)S(1)} %get-tuple-element.31), channel_id=1, source_target_pairs={{0,32},{8,40},{16,48},{24,56},{32,0},{40,8},{48,16},{56,24},{64,96... | collective-permute-start | bytes 147464 | tf_op jit(solution)/shard_map/ppermute | solution.py:34
  5.5 5.6 %collective-permute-start.6 = (bf16[64,384]{1,0:T(8,128)(2,1)S(1)}, bf16[64,384]{1,0:T(8,128)(2,1)S(1)}, u32[]{:S(2)}, u32[]{:S(2)}) collective-permute-start(bf16[64,384]{1,0:T(8,128)(2,1)S(1)} %get-tuple-element.32), channel_id=1, source_target_pairs={{0,32},{8,40},{16,48},{24,56},{32,0},{40,8},{48,16},{56,24},{64,96... | collective-permute-start | bytes 147464 | tf_op jit(solution)/shard_map/ppermute | solution.py:34
  6.6 12.6 %collective-permute-start.3 = (bf16[128,384]{1,0:T(8,128)(2,1)S(1)}, bf16[128,384]{1,0:T(8,128)(2,1)S(1)}, u32[]{:S(2)}, u32[]{:S(2)}) collective-permute-start(bf16[128,384]{1,0:T(8,128)(2,1)S(1)} %get-tuple-element.23), channel_id=1, source_target_pairs={{0,2},{1,3},{2,0},{3,1},{4,6},{5,7},{6,4},{7,5},{8,10},{9,11},{10,... | collective-permute-start | bytes 294920 | tf_op jit(solution)/shard_map/ppermute | solution.py:34
  9.7 6.1 %collective-permute-start = (bf16[128,384]{1,0:T(8,128)(2,1)S(1)}, bf16[128,384]{1,0:T(8,128)(2,1)S(1)}, u32[]{:S(2)}, u32[]{:S(2)}) collective-permute-start(bf16[128,384]{1,0:T(8,128)(2,1)S(1)} %get-tuple-element.24), channel_id=1, source_target_pairs={{0,2},{1,3},{2,0},{3,1},{4,6},{5,7},{6,4},{7,5},{8,10},{9,11},{10,... | collective-permute-start | bytes 294920 | tf_op jit(solution)/shard_map/ppermute | solution.py:34
  11.1 10.5 %collective-permute-start.7 = (bf16[2,64,384]{2,1,0:T(8,128)(2,1)S(1)}, bf16[2,64,384]{2,1,0:T(8,128)(2,1)S(1)}, u32[]{:S(2)}, u32[]{:S(2)}) collective-permute-start(bf16[2,64,384]{2,1,0:T(8,128)(2,1)S(1)} %maximum_select_fusion.19), channel_id=1, source_target_pairs={{0,16},{8,24},{16,0},{24,8},{32,48},{40,56},{48,32},{56,40},{64,80... | collective-permute-start | bytes 294920 | tf_op jit(solution)/shard_map/ppermute | solution.py:34
  12.3 7.8 %collective-permute-start.11 = (bf16[2,64,384]{2,1,0:T(8,128)(2,1)S(1)}, bf16[2,64,384]{2,1,0:T(8,128)(2,1)S(1)}, u32[]{:S(2)}, u32[]{:S(2)}) collective-permute-start(bf16[2,64,384]{2,1,0:T(8,128)(2,1)S(1)} %maximum_select_fusion.20), channel_id=1, source_target_pairs={{0,64},{8,72},{16,80},{24,88},{32,96},{40,104},{48,112},{56,120},{... | collective-permute-start | bytes 294920 | tf_op jit(solution)/shard_map/ppermute | solution.py:34
  15.9 9.6 %collective-permute-start.1 = (bf16[2,128,384]{2,1,0:T(8,128)(2,1)S(1)}, bf16[2,128,384]{2,1,0:T(8,128)(2,1)S(1)}, u32[]{:S(2)}, u32[]{:S(2)}) collective-permute-start(bf16[2,128,384]{2,1,0:T(8,128)(2,1)S(1)} %maximum_select_fusion.12), channel_id=1, source_target_pairs={{0,4},{1,5},{2,6},{3,7},{4,0},{5,1},{6,2},{7,3},{8,12},{9,13},{10,... | collective-permute-start | bytes 589832 | tf_op jit(solution)/shard_map/ppermute | solution.py:34
  19.3 5.8 %collective-permute-start.4 = (bf16[2,128,384]{2,1,0:T(8,128)(2,1)S(1)}, bf16[2,128,384]{2,1,0:T(8,128)(2,1)S(1)}, u32[]{:S(2)}, u32[]{:S(2)}) collective-permute-start(bf16[2,128,384]{2,1,0:T(8,128)(2,1)S(1)} %maximum_select_fusion.14), channel_id=1, source_target_pairs={{0,1},{1,0},{2,3},{3,2},{4,5},{5,4},{6,7},{7,6},{8,9},{9,8},{10,11... | collective-permute-start | bytes 589832 | tf_op jit(solution)/shard_map/ppermute | solution.py:34
  20.1 9.7 %collective-permute-start.12 = (bf16[2,2,64,384]{3,2,1,0:T(8,128)(2,1)S(1)}, bf16[2,2,64,384]{3,2,1,0:T(8,128)(2,1)S(1)}, u32[]{:S(2)}, u32[]{:S(2)}) collective-permute-start(bf16[2,2,64,384]{3,2,1,0:T(8,128)(2,1)S(1)} %maximum_select_fusion.17), channel_id=1, source_target_pairs={{0,16},{8,24},{16,0},{24,8},{32,48},{40,56},{48,32},{56,40},{64,80... | collective-permute-start | bytes 589832 | tf_op jit(solution)/shard_map/ppermute | solution.py:34
  21.7 7.9 %collective-permute-start.8 = (bf16[2,2,64,384]{3,2,0,1:T(8,128)(2,1)S(1)}, bf16[2,2,64,384]{3,2,0,1:T(8,128)(2,1)S(1)}, u32[]{:S(2)}, u32[]{:S(2)}) collective-permute-start(bf16[2,2,64,384]{3,2,0,1:T(8,128)(2,1)S(1)} %maximum_select_fusion.16), channel_id=1, source_target_pairs={{0,64},{8,72},{16,80},{24,88},{32,96},{40,104},{48,112},{56,120},{... | collective-permute-start | bytes 589832 | tf_op jit(solution)/shard_map/ppermute | solution.py:34
  25.1 11.2 %collective-permute-start.5 = (bf16[2,2,128,384]{3,2,1,0:T(8,128)(2,1)S(1)}, bf16[2,2,128,384]{3,2,1,0:T(8,128)(2,1)S(1)}, u32[]{:S(2)}, u32[]{:S(2)}) collective-permute-start(bf16[2,2,128,384]{3,2,1,0:T(8,128)(2,1)S(1)} %maximum_select_fusion.6), channel_id=1, source_target_pairs={{0,4},{1,5},{2,6},{3,7},{4,0},{5,1},{6,2},{7,3},{8,12},{9,13},{10,... | collective-permute-start | bytes 1179656 | tf_op jit(solution)/shard_map/ppermute | solution.py:34
  25.6 11.0 %collective-permute-start.2 = (bf16[2,2,128,384]{3,2,1,0:T(8,128)(2,1)S(1)}, bf16[2,2,128,384]{3,2,1,0:T(8,128)(2,1)S(1)}, u32[]{:S(2)}, u32[]{:S(2)}) collective-permute-start(bf16[2,2,128,384]{3,2,1,0:T(8,128)(2,1)S(1)} %maximum_select_fusion.4), channel_id=1, source_target_pairs={{0,1},{1,0},{2,3},{3,2},{4,5},{5,4},{6,7},{7,6},{8,9},{9,8},{10,11... | collective-permute-start | bytes 1179656 | tf_op jit(solution)/shard_map/ppermute | solution.py:34
  29.6 7.3 %collective-permute-start.9 = (bf16[2,2,2,64,384]{4,3,1,2,0:T(8,128)(2,1)S(1)}, bf16[2,2,2,64,384]{4,3,1,2,0:T(8,128)(2,1)S(1)}, u32[]{:S(2)}, u32[]{:S(2)}) collective-permute-start(bf16[2,2,2,64,384]{4,3,1,2,0:T(8,128)(2,1)S(1)} %maximum_select_fusion.8), channel_id=1, source_target_pairs={{0,8},{8,0},{16,24},{24,16},{32,40},{40,32},{48,56},{56,48},{64,72... | collective-permute-start | bytes 1179656 | tf_op jit(solution)/shard_map/ppermute | solution.py:34
  29.8 6.9 %collective-permute-start.13 = (bf16[2,2,2,64,384]{4,3,2,1,0:T(8,128)(2,1)S(1)}, bf16[2,2,2,64,384]{4,3,2,1,0:T(8,128)(2,1)S(1)}, u32[]{:S(2)}, u32[]{:S(2)}) collective-permute-start(bf16[2,2,2,64,384]{4,3,2,1,0:T(8,128)(2,1)S(1)} %maximum_select_fusion.10), channel_id=1, source_target_pairs={{0,8},{8,0},{16,24},{24,16},{32,40},{40,32},{48,56},{56,48},{64,72... | collective-permute-start | bytes 1179656 | tf_op jit(solution)/shard_map/ppermute | solution.py:34
  37.5 16.9 %copy-start.6 = (f32[1024]{0:T(1024)S(1)}, f32[1024]{0:T(1024)}, u32[]{:S(2)}) copy-start(f32[1024]{0:T(1024)} %param.6) | copy-start | bytes 12292
  41.3 24.4 %copy-start.7 = (f32[1024]{0:T(1024)S(1)}, f32[1024]{0:T(1024)}, u32[]{:S(2)}) copy-start(f32[1024]{0:T(1024)} %param.7) | copy-start | bytes 12292
  194.7 11.0 %all-to-all-start.14 = ((f32[8,1,1024]{2,1,0:T(1,128)}), f32[8,1,1024]{2,1,0:T(1,128)S(1)}, u32[]{:S(2)}, u32[]{:S(2)}) async-start(f32[8,1,1024]{2,1,0:T(1,128)} %broadcast_in_dim.58), calls=%async_computation.14 | async-start | bytes 65536 | tf_op jit(solution)/shard_map/all_to_all | solution.py:27
  205.8 6.3 %copy-start.3 = (bf16[2,2,2,128,384]{4,3,2,1,0:T(8,128)(2,1)S(1)}, bf16[2,2,2,128,384]{4,3,2,1,0:T(8,128)(2,1)}, u32[]{:S(2)}) copy-start(bf16[2,2,2,128,384]{4,3,2,1,0:T(8,128)(2,1)} %copy-done.2) | copy-start | bytes 2359300
  214.7 4.5 %collective-permute-start.24 = (f32[2,2,2,64,384]{4,3,1,0,2:T(8,128)S(1)}, f32[2,2,2,64,384]{4,3,1,0,2:T(8,128)S(1)}, u32[]{:S(2)}, u32[]{:S(2)}) collective-permute-start(f32[2,2,2,64,384]{4,3,1,0,2:T(8,128)S(1)} %select_bitcast_fusion), channel_id=1, source_target_pairs={{0,8},{8,0},{16,24},{24,16},{32,40},{40,32},{48,56},{56,48},{64,72... | collective-permute-start | bytes 2359304 | tf_op jit(solution)/shard_map/ppermute | solution.py:57
  214.9 5.1 %collective-permute-start.20 = (f32[2,2,2,64,384]{4,3,1,0,2:T(8,128)S(1)}, f32[2,2,2,64,384]{4,3,1,0,2:T(8,128)S(1)}, u32[]{:S(2)}, u32[]{:S(2)}) collective-permute-start(f32[2,2,2,64,384]{4,3,1,0,2:T(8,128)S(1)} %select_bitcast_fusion.1), channel_id=1, source_target_pairs={{0,8},{8,0},{16,24},{24,16},{32,40},{40,32},{48,56},{56,48},{64,72... | collective-permute-start | bytes 2359304 | tf_op jit(solution)/shard_map/ppermute | solution.py:57
  217.9 19.3 %collective-permute-start.14 = (f32[2,2,128,384]{3,2,1,0:T(8,128)S(1)}, f32[2,2,128,384]{3,2,1,0:T(8,128)S(1)}, u32[]{:S(2)}, u32[]{:S(2)}) collective-permute-start(f32[2,2,128,384]{3,2,1,0:T(8,128)S(1)} %select_bitcast_fusion.2), channel_id=1, source_target_pairs={{0,1},{1,0},{2,3},{3,2},{4,5},{5,4},{6,7},{7,6},{8,9},{9,8},{10,11... | collective-permute-start | bytes 2359304 | tf_op jit(solution)/shard_map/ppermute | solution.py:57
  218.6 22.0 %collective-permute-start.17 = (f32[2,2,128,384]{3,2,0,1:T(8,128)S(1)}, f32[2,2,128,384]{3,2,0,1:T(8,128)S(1)}, u32[]{:S(2)}, u32[]{:S(2)}) collective-permute-start(f32[2,2,128,384]{3,2,0,1:T(8,128)S(1)} %copy.97), channel_id=1, source_target_pairs={{0,4},{1,5},{2,6},{3,7},{4,0},{5,1},{6,2},{7,3},{8,12},{9,13},{10,... | collective-permute-start | bytes 2359304 | tf_op jit(solution)/shard_map/ppermute | solution.py:57
  219.3 22.9 %collective-permute-start.25 = (f32[2,2,64,384]{3,2,1,0:T(8,128)S(1)}, f32[2,2,64,384]{3,2,1,0:T(8,128)S(1)}, u32[]{:S(2)}, u32[]{:S(2)}) collective-permute-start(f32[2,2,64,384]{3,2,1,0:T(8,128)S(1)} %select_bitcast_fusion.3), channel_id=1, source_target_pairs={{0,16},{8,24},{16,0},{24,8},{32,48},{40,56},{48,32},{56,40},{64,80... | collective-permute-start | bytes 1179656 | tf_op jit(solution)/shard_map/ppermute | solution.py:57
  220.2 26.3 %collective-permute-start.21 = (f32[2,2,64,384]{3,2,1,0:T(8,128)S(1)}, f32[2,2,64,384]{3,2,1,0:T(8,128)S(1)}, u32[]{:S(2)}, u32[]{:S(2)}) collective-permute-start(f32[2,2,64,384]{3,2,1,0:T(8,128)S(1)} %fusion.18), channel_id=1, source_target_pairs={{0,64},{8,72},{16,80},{24,88},{32,96},{40,104},{48,112},{56,120},{... | collective-permute-start | bytes 1179656 | tf_op jit(solution)/shard_map/ppermute | solution.py:57
  237.4 20.1 %collective-permute-start.15 = (f32[2,128,384]{2,1,0:T(8,128)S(1)}, f32[2,128,384]{2,1,0:T(8,128)S(1)}, u32[]{:S(2)}, u32[]{:S(2)}) collective-permute-start(f32[2,128,384]{2,1,0:T(8,128)S(1)} %select_bitcast_fusion.6), channel_id=1, source_target_pairs={{0,4},{1,5},{2,6},{3,7},{4,0},{5,1},{6,2},{7,3},{8,12},{9,13},{10,... | collective-permute-start | bytes 1179656 | tf_op jit(solution)/shard_map/ppermute | solution.py:57
  240.8 18.9 %collective-permute-start.18 = (f32[2,128,384]{2,1,0:T(8,128)S(1)}, f32[2,128,384]{2,1,0:T(8,128)S(1)}, u32[]{:S(2)}, u32[]{:S(2)}) collective-permute-start(f32[2,128,384]{2,1,0:T(8,128)S(1)} %select_bitcast_fusion.5), channel_id=1, source_target_pairs={{0,1},{1,0},{2,3},{3,2},{4,5},{5,4},{6,7},{7,6},{8,9},{9,8},{10,11... | collective-permute-start | bytes 1179656 | tf_op jit(solution)/shard_map/ppermute | solution.py:57
  242.3 19.0 %collective-permute-start.26 = (f32[2,64,384]{2,1,0:T(8,128)S(1)}, f32[2,64,384]{2,1,0:T(8,128)S(1)}, u32[]{:S(2)}, u32[]{:S(2)}) collective-permute-start(f32[2,64,384]{2,1,0:T(8,128)S(1)} %select_bitcast_fusion.7), channel_id=1, source_target_pairs={{0,64},{8,72},{16,80},{24,88},{32,96},{40,104},{48,112},{56,120},{... | collective-permute-start | bytes 589832 | tf_op jit(solution)/shard_map/ppermute | solution.py:57
  246.7 16.0 %collective-permute-start.22 = (f32[2,64,384]{2,1,0:T(8,128)S(1)}, f32[2,64,384]{2,1,0:T(8,128)S(1)}, u32[]{:S(2)}, u32[]{:S(2)}) collective-permute-start(f32[2,64,384]{2,1,0:T(8,128)S(1)} %select_bitcast_fusion.8), channel_id=1, source_target_pairs={{0,16},{8,24},{16,0},{24,8},{32,48},{40,56},{48,32},{56,40},{64,80... | collective-permute-start | bytes 589832 | tf_op jit(solution)/shard_map/ppermute | solution.py:57
  257.5 7.6 %collective-permute-start.16 = (f32[128,384]{1,0:T(8,128)S(1)}, f32[128,384]{1,0:T(8,128)S(1)}, u32[]{:S(2)}, u32[]{:S(2)}) collective-permute-start(f32[128,384]{1,0:T(8,128)S(1)} %select_bitcast_fusion.10), channel_id=1, source_target_pairs={{0,2},{1,3},{2,0},{3,1},{4,6},{5,7},{6,4},{7,5},{8,10},{9,11},{10,... | collective-permute-start | bytes 589832 | tf_op jit(solution)/shard_map/ppermute | solution.py:57
  259.7 7.4 %collective-permute-start.19 = (f32[128,384]{1,0:T(8,128)S(1)}, f32[128,384]{1,0:T(8,128)S(1)}, u32[]{:S(2)}, u32[]{:S(2)}) collective-permute-start(f32[128,384]{1,0:T(8,128)S(1)} %select_bitcast_fusion.9), channel_id=1, source_target_pairs={{0,2},{1,3},{2,0},{3,1},{4,6},{5,7},{6,4},{7,5},{8,10},{9,11},{10,... | collective-permute-start | bytes 589832 | tf_op jit(solution)/shard_map/ppermute | solution.py:57
  261.4 6.6 %collective-permute-start.27 = (f32[64,384]{1,0:T(8,128)S(1)}, f32[64,384]{1,0:T(8,128)S(1)}, u32[]{:S(2)}, u32[]{:S(2)}) collective-permute-start(f32[64,384]{1,0:T(8,128)S(1)} %select_bitcast_fusion.11), channel_id=1, source_target_pairs={{0,32},{8,40},{16,48},{24,56},{32,0},{40,8},{48,16},{56,24},{64,96... | collective-permute-start | bytes 294920 | tf_op jit(solution)/shard_map/ppermute | solution.py:57
  262.7 6.2 %collective-permute-start.23 = (f32[64,384]{1,0:T(8,128)S(1)}, f32[64,384]{1,0:T(8,128)S(1)}, u32[]{:S(2)}, u32[]{:S(2)}) collective-permute-start(f32[64,384]{1,0:T(8,128)S(1)} %select_bitcast_fusion.12), channel_id=1, source_target_pairs={{0,32},{8,40},{16,48},{24,56},{32,0},{40,8},{48,16},{56,24},{64,96... | collective-permute-start | bytes 294920 | tf_op jit(solution)/shard_map/ppermute | solution.py:57
  (5 other events, 17.0 us)
where the time goes:
time: 271 us; the launch traced here: 270 us
  blocking collectives  139 us (51%)
  waiting for transfers between devices  57.1 us (21%)
  starting transfers between devices  36 us (13%)
  other arithmetic  18.2 us (7%)
  matrix products  13.7 us (5%)
  local copies, waits for them, and re-layouts  4.48 us (2%)
    all_to_all x14, blocking collectives, tree_sum(): return lax.all_to_all(spread, axis, 0, 0, tiled=False).sum(0)  139 us
    ppermute x14, waiting for transfers between devices, tree_scatter(): x = keep + lax.ppermute(send, axis, partner(axis, n, bit))  35.6 us
    ppermute x14, starting transfers between devices, tree_gather(): other = lax.ppermute(x, axis, partner(axis, n, bit))  18.5 us
    ppermute x14, waiting for transfers between devices, tree_gather(): other = lax.ppermute(x, axis, partner(axis, n, bit))  14.2 us
    ppermute x14, starting transfers between devices, tree_scatter(): x = keep + lax.ppermute(send, axis, partner(axis, n, bit))  14 us
    all_to_all x1, waiting for transfers between devices, tree_sum(): return lax.all_to_all(spread, axis, 0, 0, tiled=False).sum(0)  7.4 us
    reduce_sum x8, other arithmetic, times_vector(): return jnp.sum(kernel.astype(jnp.float32) * vector[None, :], axis=1)  6.72 us
    dot_general x1, matrix products, per_device(): lax.dot_general(left, right, (((1,), (1,)), ((), ())), precision=highest,...  6.23 us
  transfers between devices with their start and end apart: 29, of which 12 were waited for; matrix products, arithmetic and copies ran while one was open for 3% of the time, Pallas kernels for 0%

commit v1 on v0

--- a/solution.py
+++ b/solution.py
@@ -140,9 +140,9 @@
         col_bars[iteration] = col_bar
     left = jnp.stack(row_bars + src_saved, axis=1)
     right = jnp.stack(old_saved + col_bars, axis=1)
-    lowrank = lax.dot_general(
-        left, right, (((1,), (1,)), ((), ())), precision=highest, preferred_element_type=jnp.float32
-    )
+    lowrank = left[:, 0, None] * right[None, :, 0]
+    for k in range(1, left.shape[1]):
+        lowrank = lowrank + left[:, k, None] * right[None, :, k]
     cross_term_grid = (
         kernel * (last_src[:, None] * last_tgt[None, :] * (1.0 + kernel_grid) + lowrank)
     ).astype(jnp.bfloat16)

time: 271 us -> 268 us (0.989)
  blocking collectives: 139 us -> 149 us
  waiting for transfers between devices: 57.1 us -> 50 us
  matrix products: 13.7 us -> 7.51 us
  other arithmetic: 18.2 us -> 23.6 us
  starting transfers between devices: 36 us -> 32.3 us
    all_to_all x14 -> x15, blocking collectives: 139 us -> 149 us  [tree_sum(): return lax.all_to_all(spread, axis, 0, 0, tiled=False).sum(0)]
    all_to_all x1 -> x0, waiting for transfers between devices: 7.4 us -> none  [tree_sum(): return lax.all_to_all(spread, axis, 0, 0, tiled=False).sum(0)]
    dot_general x1 -> x0, matrix products: 6.23 us -> none  [per_device(): lax.dot_general(left, right, (((1,), (1,)), ((), ())), precision=highest,...]
    convert_element_type x0 -> x1, other arithmetic: none -> 5.42 us  [per_device(): cross_term_grid = (kernel * (last_src[:, None] * last_tgt[None, :] * (1.0...]
    all_to_all x1 -> x0, starting transfers between devices: 3.56 us -> none  [tree_sum(): return lax.all_to_all(spread, axis, 0, 0, tiled=False).sum(0)]
  transfers between devices with their start and end apart: 29 -> 28, of which waited for: 12 -> 12; matrix products, arithmetic and copies ran while one was open for 3% -> 3% of each run, Pallas kernels for 0% -> 0%
where the time goes in v1:
time: 268 us; the launch traced here: 267 us
  blocking collectives  149 us (56%)
  waiting for transfers between devices  50 us (19%)
  starting transfers between devices  32.3 us (12%)
  other arithmetic  23.6 us (9%)
  matrix products  7.51 us (3%)
  local copies, waits for them, and re-layouts  3.09 us (1%)
    all_to_all x15, blocking collectives, tree_sum(): return lax.all_to_all(spread, axis, 0, 0, tiled=False).sum(0)  149 us
    ppermute x14, waiting for transfers between devices, tree_scatter(): x = keep + lax.ppermute(send, axis, partner(axis, n, bit))  35.8 us
    ppermute x14, starting transfers between devices, tree_gather(): other = lax.ppermute(x, axis, partner(axis, n, bit))  18.5 us
    ppermute x14, waiting for transfers between devices, tree_gather(): other = lax.ppermute(x, axis, partner(axis, n, bit))  14.2 us
    ppermute x14, starting transfers between devices, tree_scatter(): x = keep + lax.ppermute(send, axis, partner(axis, n, bit))  13.9 us
    reduce_sum x8, other arithmetic, times_vector(): return jnp.sum(kernel.astype(jnp.float32) * vector[None, :], axis=1)  6.73 us
    reduce_sum x7, other arithmetic, vector_times(): return jnp.sum(vector[:, None] * kernel.astype(jnp.float32), axis=0)  6.08 us
    convert_element_type x1, other arithmetic, per_device(): cross_term_grid = (kernel * (last_src[:, None] * last_tgt[None, :] * (1.0...  5.42 us
  transfers between devices with their start and end apart: 28, of which 12 were waited for; matrix products, arithmetic and copies ran while one was open for 3% of the time, Pallas kernels for 0%

profile of v1, /device:TPU:0, one launch (start us, length us, event | category | flops | bytes accessed | tf_op | source)
XLA Modules:
  0.0 266.9 jit_solution(13271964297371193191)
XLA Ops:
  1.5 4.0 %collective-permute-start.10 = (bf16[64,384]{1,0:T(8,128)(2,1)S(1)}, bf16[64,384]{1,0:T(8,128)(2,1)S(1)}, u32[]{:S(2)}, u32[]{:S(2)}) collective-permute-start(bf16[64,384]{1,0:T(8,128)(2,1)S(1)} %get-tuple-element.31), channel_id=1, source_target_pairs={{0,32},{8,40},{16,48},{24,56},{32,0},{40,8},{48,16},{56,24},{64,96... | collective-permute-start | bytes 147464 | tf_op jit(solution)/shard_map/ppermute | solution.py:34
  6.6 3.1 %collective-permute-start.3 = (bf16[128,384]{1,0:T(8,128)(2,1)S(1)}, bf16[128,384]{1,0:T(8,128)(2,1)S(1)}, u32[]{:S(2)}, u32[]{:S(2)}) collective-permute-start(bf16[128,384]{1,0:T(8,128)(2,1)S(1)} %get-tuple-element.23), channel_id=1, source_target_pairs={{0,2},{1,3},{2,0},{3,1},{4,6},{5,7},{6,4},{7,5},{8,10},{9,11},{10,... | collective-permute-start | bytes 294920 | tf_op jit(solution)/shard_map/ppermute | solution.py:34
  15.9 3.3 %collective-permute-start.1 = (bf16[2,128,384]{2,1,0:T(8,128)(2,1)S(1)}, bf16[2,128,384]{2,1,0:T(8,128)(2,1)S(1)}, u32[]{:S(2)}, u32[]{:S(2)}) collective-permute-start(bf16[2,128,384]{2,1,0:T(8,128)(2,1)S(1)} %maximum_select_fusion.12), channel_id=1, source_target_pairs={{0,4},{1,5},{2,6},{3,7},{4,0},{5,1},{6,2},{7,3},{8,12},{9,13},{10,... | collective-permute-start | bytes 589832 | tf_op jit(solution)/shard_map/ppermute | solution.py:34
  22.6 2.5 collective-permute-done.4
  26.4 3.2 %collective-permute-done.8 = bf16[2,2,64,384]{3,2,0,1:T(8,128)(2,1)S(1)} collective-permute-done((bf16[2,2,64,384]{3,2,0,1:T(8,128)(2,1)S(1)}, bf16[2,2,64,384]{3,2,0,1:T(8,128)(2,1)S(1)}, u32[]{:S(2)}, u32[]{:S(2)}) %collective-permute-start.8) | collective-permute-done | bytes 196640 | tf_op jit(solution)/shard_map/ppermute | solution.py:34
  30.5 5.8 %collective-permute-done.5 = bf16[2,2,128,384]{3,2,1,0:T(8,128)(2,1)S(1)} collective-permute-done((bf16[2,2,128,384]{3,2,1,0:T(8,128)(2,1)S(1)}, bf16[2,2,128,384]{3,2,1,0:T(8,128)(2,1)S(1)}, u32[]{:S(2)}, u32[]{:S(2)}) %collective-permute-start.5) | collective-permute-done | bytes 393248 | tf_op jit(solution)/shard_map/ppermute | solution.py:34
  37.1 3.8 %exponential_convert_fusion = (bf16[1024,1024]{1,0:T(8,128)(2,1)S(1)}, f32[1024,1024]{1,0:T(8,128)}) fusion(bf16[1024,384]{1,0:T(8,128)(2,1)S(1)} %bitcast.184, bf16[1024,384]{1,0:T(8,128)(2,1)S(1)} %bitcast.186, bf16[1024,384]{1,0:T(8,128)(2,1)S(1)} %bitcast.188, bf16[1024,384]{1,0:T(8,128)(2,1)S(1)} %bitcast.190), kind=kOutput, calls=%fused_computation.34 | convolution fusion | flops 1619001344 | bytes 9437184 | tf_op jit(solution)/shard_map/dot_general | solution.py:99
  41.3 12.7 %all_to_all.89 = f32[8,1,1024]{2,1,0:T(1,128)S(1)} all-to-all(f32[8,1,1024]{2,1,0:T(1,128)S(1)} %broadcast_in_dim.30), channel_id=1, replica_groups=mesh['src'=16,'tgt'=8] {'tgt'}, dimensions={0} | all-to-all | bytes 65536 | tf_op jit(solution)/shard_map/all_to_all | solution.py:27
  54.5 10.8 %all_to_all.90 = f32[16,1,1024]{2,1,0:T(1,128)S(1)} all-to-all(f32[16,1,1024]{2,1,0:T(1,128)S(1)} %broadcast_in_dim.31), channel_id=1, replica_groups=mesh['src'=16,'tgt'=8] {'src'}, dimensions={0} | all-to-all | bytes 131072 | tf_op jit(solution)/shard_map/all_to_all | solution.py:27
  65.9 10.7 %all_to_all.91 = f32[8,1,1024]{2,1,0:T(1,128)S(1)} all-to-all(f32[8,1,1024]{2,1,0:T(1,128)S(1)} %broadcast_in_dim.32), channel_id=1, replica_groups=mesh['src'=16,'tgt'=8] {'tgt'}, dimensions={0} | all-to-all | bytes 65536 | tf_op jit(solution)/shard_map/all_to_all | solution.py:27
  77.2 8.7 %all_to_all.92 = f32[16,1,1024]{2,1,0:T(1,128)S(1)} all-to-all(f32[16,1,1024]{2,1,0:T(1,128)S(1)} %broadcast_in_dim.33), channel_id=1, replica_groups=mesh['src'=16,'tgt'=8] {'src'}, dimensions={0} | all-to-all | bytes 131072 | tf_op jit(solution)/shard_map/all_to_all | solution.py:27
  86.5 10.1 %all_to_all.93 = f32[8,1,1024]{2,1,0:T(1,128)S(1)} all-to-all(f32[8,1,1024]{2,1,0:T(1,128)S(1)} %broadcast_in_dim.34), channel_id=1, replica_groups=mesh['src'=16,'tgt'=8] {'tgt'}, dimensions={0} | all-to-all | bytes 65536 | tf_op jit(solution)/shard_map/all_to_all | solution.py:27
  97.2 8.7 %all_to_all.94 = f32[16,1,1024]{2,1,0:T(1,128)S(1)} all-to-all(f32[16,1,1024]{2,1,0:T(1,128)S(1)} %broadcast_in_dim.35), channel_id=1, replica_groups=mesh['src'=16,'tgt'=8] {'src'}, dimensions={0} | all-to-all | bytes 131072 | tf_op jit(solution)/shard_map/all_to_all | solution.py:27
  106.5 10.5 %all_to_all.95 = f32[8,1,1024]{2,1,0:T(1,128)S(1)} all-to-all(f32[8,1,1024]{2,1,0:T(1,128)S(1)} %broadcast_in_dim.36), channel_id=1, replica_groups=mesh['src'=16,'tgt'=8] {'tgt'}, dimensions={0} | all-to-all | bytes 65536 | tf_op jit(solution)/shard_map/all_to_all | solution.py:27
  117.1 3.2 %fusion.6 = (f32[1024]{0:T(1024)S(1)}, f32[1024]{0:T(1024)S(1)}) fusion(bf16[1024,1024]{1,0:T(8,128)(2,1)S(1)} %get-tuple-element.35, f32[1024]{0:T(1024)S(1)} %div.68, f32[1024,1024]{1,0:T(8,128)} %get-tuple-element.36), kind=kLoop, calls=%fused_computation.23 | loop fusion | flops 7337984 | bytes 6303744 | tf_op jit(solution)/shard_map/reduce_sum | solution.py:91
  120.3 9.3 %all_to_all.96 = f32[16,2,1024]{2,1,0:T(2,128)S(1)} all-to-all(f32[16,2,1024]{2,1,0:T(2,128)S(1)} %broadcast_in_dim.37), channel_id=1, replica_groups=mesh['src'=16,'tgt'=8] {'src'}, dimensions={0} | all-to-all | bytes 262144 | tf_op jit(solution)/shard_map/all_to_all | solution.py:27
  129.7 3.5 %multiply_reduce_fusion = (f32[1024]{0:T(1024)S(1)}, f32[1024]{0:T(1024)S(1)}) fusion(f32[1024,1024]{1,0:T(8,128)} %get-tuple-element.36, bf16[1024,1024]{1,0:T(8,128)(2,1)S(1)} %get-tuple-element.35, f32[1024]{0:T(1024)S(1)} %get-tuple-element.7, f32[1024]{0:T(1024)S(1)} %get-tuple-element.6), kind=kLoop, calls=%fused_computation.32 | loop fusion | flops 7337984 | bytes 6307840 | tf_op jit(solution)/shard_map/reduce_sum | solution.py:87
  133.3 10.1 %all_to_all.97 = f32[8,1,1024]{2,1,0:T(1,128)S(1)} all-to-all(f32[8,1,1024]{2,1,0:T(1,128)S(1)} %broadcast_in_dim.38), channel_id=1, replica_groups=mesh['src'=16,'tgt'=8] {'tgt'}, dimensions={0} | all-to-all | bytes 65536 | tf_op jit(solution)/shard_map/all_to_all | solution.py:27
  144.0 8.7 %all_to_all.98 = f32[16,1,1024]{2,1,0:T(1,128)S(1)} all-to-all(f32[16,1,1024]{2,1,0:T(1,128)S(1)} %broadcast_in_dim.39), channel_id=1, replica_groups=mesh['src'=16,'tgt'=8] {'src'}, dimensions={0} | all-to-all | bytes 131072 | tf_op jit(solution)/shard_map/all_to_all | solution.py:27
  153.3 10.3 %all_to_all.99 = f32[8,1,1024]{2,1,0:T(1,128)S(1)} all-to-all(f32[8,1,1024]{2,1,0:T(1,128)S(1)} %broadcast_in_dim.40), channel_id=1, replica_groups=mesh['src'=16,'tgt'=8] {'tgt'}, dimensions={0} | all-to-all | bytes 65536 | tf_op jit(solution)/shard_map/all_to_all | solution.py:27
  164.2 8.7 %all_to_all.100 = f32[16,1,1024]{2,1,0:T(1,128)S(1)} all-to-all(f32[16,1,1024]{2,1,0:T(1,128)S(1)} %broadcast_in_dim.41), channel_id=1, replica_groups=mesh['src'=16,'tgt'=8] {'src'}, dimensions={0} | all-to-all | bytes 131072 | tf_op jit(solution)/shard_map/all_to_all | solution.py:27
  173.5 10.4 %all_to_all.101 = f32[8,1,1024]{2,1,0:T(1,128)S(1)} all-to-all(f32[8,1,1024]{2,1,0:T(1,128)S(1)} %broadcast_in_dim.42), channel_id=1, replica_groups=mesh['src'=16,'tgt'=8] {'tgt'}, dimensions={0} | all-to-all | bytes 65536 | tf_op jit(solution)/shard_map/all_to_all | solution.py:27
  184.4 8.7 %all_to_all.102 = f32[16,1,1024]{2,1,0:T(1,128)S(1)} all-to-all(f32[16,1,1024]{2,1,0:T(1,128)S(1)} %broadcast_in_dim.43), channel_id=1, replica_groups=mesh['src'=16,'tgt'=8] {'src'}, dimensions={0} | all-to-all | bytes 131072 | tf_op jit(solution)/shard_map/all_to_all | solution.py:27
  193.7 10.3 %all_to_all.103 = f32[8,1,1024]{2,1,0:T(1,128)S(1)} all-to-all(f32[8,1,1024]{2,1,0:T(1,128)S(1)} %broadcast_in_dim.44), channel_id=1, replica_groups=mesh['src'=16,'tgt'=8] {'tgt'}, dimensions={0} | all-to-all | bytes 65536 | tf_op jit(solution)/shard_map/all_to_all | solution.py:27
  204.1 5.4 %fusion.14 = bf16[1024,1024]{1,0:T(8,128)(2,1)S(1)} fusion(bf16[1024,1024]{1,0:T(8,128)(2,1)S(1)} %get-tuple-element.35, f32[1024,1024]{1,0:T(8,128)} %get-tuple-element.36, f32[1024]{0:T(1024)S(1)} %multiply_divide_fusion, f32[1024]{0:T(1024)S(1)} %multiply_divide_fusion.1, f32[1024]{0:T(1024)S(1)} %multiply_divide_fusion.2, ...), kind=kLoop, calls=%fused_computation.31 | loop fusion | flops 23068672 | bytes 8454144 | tf_op jit(solution)/shard_map/convert_element_type | solution.py:148
  218.1 16.7 %collective-permute-done.14 = f32[2,2,128,384]{3,2,1,0:T(8,128)S(1)} collective-permute-done((f32[2,2,128,384]{3,2,1,0:T(8,128)S(1)}, f32[2,2,128,384]{3,2,1,0:T(8,128)S(1)}, u32[]{:S(2)}, u32[]{:S(2)}) %collective-permute-start.14) | collective-permute-done | bytes 786464 | tf_op jit(solution)/shard_map/ppermute | solution.py:57
  235.6 2.3 collective-permute-done.17
  240.1 3.7 %collective-permute-done.21 = f32[2,2,64,384]{3,2,1,0:T(8,128)S(1)} collective-permute-done((f32[2,2,64,384]{3,2,1,0:T(8,128)S(1)}, f32[2,2,64,384]{3,2,1,0:T(8,128)S(1)}, u32[]{:S(2)}, u32[]{:S(2)}) %collective-permute-start.21) | collective-permute-done | bytes 393248 | tf_op jit(solution)/shard_map/ppermute | solution.py:57
  244.5 10.3 %collective-permute-done.15 = f32[2,128,384]{2,1,0:T(8,128)S(1)} collective-permute-done((f32[2,128,384]{2,1,0:T(8,128)S(1)}, f32[2,128,384]{2,1,0:T(8,128)S(1)}, u32[]{:S(2)}, u32[]{:S(2)}) %collective-permute-start.15) | collective-permute-done | bytes 393248 | tf_op jit(solution)/shard_map/ppermute | solution.py:57
  254.9 2.1 collective-permute-start.16
  260.0 2.4 collective-permute-start.23
  263.0 2.1 collective-permute-done.19
  (192 shorter events, 39.3 us)
Async XLA Ops:
  1.5 8.7 %collective-permute-start.10 = (bf16[64,384]{1,0:T(8,128)(2,1)S(1)}, bf16[64,384]{1,0:T(8,128)(2,1)S(1)}, u32[]{:S(2)}, u32[]{:S(2)}) collective-permute-start(bf16[64,384]{1,0:T(8,128)(2,1)S(1)} %get-tuple-element.31), channel_id=1, source_target_pairs={{0,32},{8,40},{16,48},{24,56},{32,0},{40,8},{48,16},{56,24},{64,96... | collective-permute-start | bytes 147464 | tf_op jit(solution)/shard_map/ppermute | solution.py:34
  5.5 5.6 %collective-permute-start.6 = (bf16[64,384]{1,0:T(8,128)(2,1)S(1)}, bf16[64,384]{1,0:T(8,128)(2,1)S(1)}, u32[]{:S(2)}, u32[]{:S(2)}) collective-permute-start(bf16[64,384]{1,0:T(8,128)(2,1)S(1)} %get-tuple-element.32), channel_id=1, source_target_pairs={{0,32},{8,40},{16,48},{24,56},{32,0},{40,8},{48,16},{56,24},{64,96... | collective-permute-start | bytes 147464 | tf_op jit(solution)/shard_map/ppermute | solution.py:34
  6.6 12.6 %collective-permute-start.3 = (bf16[128,384]{1,0:T(8,128)(2,1)S(1)}, bf16[128,384]{1,0:T(8,128)(2,1)S(1)}, u32[]{:S(2)}, u32[]{:S(2)}) collective-permute-start(bf16[128,384]{1,0:T(8,128)(2,1)S(1)} %get-tuple-element.23), channel_id=1, source_target_pairs={{0,2},{1,3},{2,0},{3,1},{4,6},{5,7},{6,4},{7,5},{8,10},{9,11},{10,... | collective-permute-start | bytes 294920 | tf_op jit(solution)/shard_map/ppermute | solution.py:34
  9.7 6.1 %collective-permute-start = (bf16[128,384]{1,0:T(8,128)(2,1)S(1)}, bf16[128,384]{1,0:T(8,128)(2,1)S(1)}, u32[]{:S(2)}, u32[]{:S(2)}) collective-permute-start(bf16[128,384]{1,0:T(8,128)(2,1)S(1)} %get-tuple-element.24), channel_id=1, source_target_pairs={{0,2},{1,3},{2,0},{3,1},{4,6},{5,7},{6,4},{7,5},{8,10},{9,11},{10,... | collective-permute-start | bytes 294920 | tf_op jit(solution)/shard_map/ppermute | solution.py:34
  11.1 10.5 %collective-permute-start.7 = (bf16[2,64,384]{2,1,0:T(8,128)(2,1)S(1)}, bf16[2,64,384]{2,1,0:T(8,128)(2,1)S(1)}, u32[]{:S(2)}, u32[]{:S(2)}) collective-permute-start(bf16[2,64,384]{2,1,0:T(8,128)(2,1)S(1)} %maximum_select_fusion.19), channel_id=1, source_target_pairs={{0,16},{8,24},{16,0},{24,8},{32,48},{40,56},{48,32},{56,40},{64,80... | collective-permute-start | bytes 294920 | tf_op jit(solution)/shard_map/ppermute | solution.py:34
  12.3 7.8 %collective-permute-start.11 = (bf16[2,64,384]{2,1,0:T(8,128)(2,1)S(1)}, bf16[2,64,384]{2,1,0:T(8,128)(2,1)S(1)}, u32[]{:S(2)}, u32[]{:S(2)}) collective-permute-start(bf16[2,64,384]{2,1,0:T(8,128)(2,1)S(1)} %maximum_select_fusion.20), channel_id=1, source_target_pairs={{0,64},{8,72},{16,80},{24,88},{32,96},{40,104},{48,112},{56,120},{... | collective-permute-start | bytes 294920 | tf_op jit(solution)/shard_map/ppermute | solution.py:34
  15.9 9.6 %collective-permute-start.1 = (bf16[2,128,384]{2,1,0:T(8,128)(2,1)S(1)}, bf16[2,128,384]{2,1,0:T(8,128)(2,1)S(1)}, u32[]{:S(2)}, u32[]{:S(2)}) collective-permute-start(bf16[2,128,384]{2,1,0:T(8,128)(2,1)S(1)} %maximum_select_fusion.12), channel_id=1, source_target_pairs={{0,4},{1,5},{2,6},{3,7},{4,0},{5,1},{6,2},{7,3},{8,12},{9,13},{10,... | collective-permute-start | bytes 589832 | tf_op jit(solution)/shard_map/ppermute | solution.py:34
  19.3 5.8 %collective-permute-start.4 = (bf16[2,128,384]{2,1,0:T(8,128)(2,1)S(1)}, bf16[2,128,384]{2,1,0:T(8,128)(2,1)S(1)}, u32[]{:S(2)}, u32[]{:S(2)}) collective-permute-start(bf16[2,128,384]{2,1,0:T(8,128)(2,1)S(1)} %maximum_select_fusion.14), channel_id=1, source_target_pairs={{0,1},{1,0},{2,3},{3,2},{4,5},{5,4},{6,7},{7,6},{8,9},{9,8},{10,11... | collective-permute-start | bytes 589832 | tf_op jit(solution)/shard_map/ppermute | solution.py:34
  20.1 9.7 %collective-permute-start.12 = (bf16[2,2,64,384]{3,2,1,0:T(8,128)(2,1)S(1)}, bf16[2,2,64,384]{3,2,1,0:T(8,128)(2,1)S(1)}, u32[]{:S(2)}, u32[]{:S(2)}) collective-permute-start(bf16[2,2,64,384]{3,2,1,0:T(8,128)(2,1)S(1)} %maximum_select_fusion.17), channel_id=1, source_target_pairs={{0,16},{8,24},{16,0},{24,8},{32,48},{40,56},{48,32},{56,40},{64,80... | collective-permute-start | bytes 589832 | tf_op jit(solution)/shard_map/ppermute | solution.py:34
  21.7 7.9 %collective-permute-start.8 = (bf16[2,2,64,384]{3,2,0,1:T(8,128)(2,1)S(1)}, bf16[2,2,64,384]{3,2,0,1:T(8,128)(2,1)S(1)}, u32[]{:S(2)}, u32[]{:S(2)}) collective-permute-start(bf16[2,2,64,384]{3,2,0,1:T(8,128)(2,1)S(1)} %maximum_select_fusion.16), channel_id=1, source_target_pairs={{0,64},{8,72},{16,80},{24,88},{32,96},{40,104},{48,112},{56,120},{... | collective-permute-start | bytes 589832 | tf_op jit(solution)/shard_map/ppermute | solution.py:34
  25.1 11.2 %collective-permute-start.5 = (bf16[2,2,128,384]{3,2,1,0:T(8,128)(2,1)S(1)}, bf16[2,2,128,384]{3,2,1,0:T(8,128)(2,1)S(1)}, u32[]{:S(2)}, u32[]{:S(2)}) collective-permute-start(bf16[2,2,128,384]{3,2,1,0:T(8,128)(2,1)S(1)} %maximum_select_fusion.6), channel_id=1, source_target_pairs={{0,4},{1,5},{2,6},{3,7},{4,0},{5,1},{6,2},{7,3},{8,12},{9,13},{10,... | collective-permute-start | bytes 1179656 | tf_op jit(solution)/shard_map/ppermute | solution.py:34
  25.6 11.0 %collective-permute-start.2 = (bf16[2,2,128,384]{3,2,1,0:T(8,128)(2,1)S(1)}, bf16[2,2,128,384]{3,2,1,0:T(8,128)(2,1)S(1)}, u32[]{:S(2)}, u32[]{:S(2)}) collective-permute-start(bf16[2,2,128,384]{3,2,1,0:T(8,128)(2,1)S(1)} %maximum_select_fusion.4), channel_id=1, source_target_pairs={{0,1},{1,0},{2,3},{3,2},{4,5},{5,4},{6,7},{7,6},{8,9},{9,8},{10,11... | collective-permute-start | bytes 1179656 | tf_op jit(solution)/shard_map/ppermute | solution.py:34
  29.6 7.3 %collective-permute-start.9 = (bf16[2,2,2,64,384]{4,3,1,2,0:T(8,128)(2,1)S(1)}, bf16[2,2,2,64,384]{4,3,1,2,0:T(8,128)(2,1)S(1)}, u32[]{:S(2)}, u32[]{:S(2)}) collective-permute-start(bf16[2,2,2,64,384]{4,3,1,2,0:T(8,128)(2,1)S(1)} %maximum_select_fusion.8), channel_id=1, source_target_pairs={{0,8},{8,0},{16,24},{24,16},{32,40},{40,32},{48,56},{56,48},{64,72... | collective-permute-start | bytes 1179656 | tf_op jit(solution)/shard_map/ppermute | solution.py:34
  29.8 6.9 %collective-permute-start.13 = (bf16[2,2,2,64,384]{4,3,2,1,0:T(8,128)(2,1)S(1)}, bf16[2,2,2,64,384]{4,3,2,1,0:T(8,128)(2,1)S(1)}, u32[]{:S(2)}, u32[]{:S(2)}) collective-permute-start(bf16[2,2,2,64,384]{4,3,2,1,0:T(8,128)(2,1)S(1)} %maximum_select_fusion.10), channel_id=1, source_target_pairs={{0,8},{8,0},{16,24},{24,16},{32,40},{40,32},{48,56},{56,48},{64,72... | collective-permute-start | bytes 1179656 | tf_op jit(solution)/shard_map/ppermute | solution.py:34
  37.1 16.9 %copy-start.6 = (f32[1024]{0:T(1024)S(1)}, f32[1024]{0:T(1024)}, u32[]{:S(2)}) copy-start(f32[1024]{0:T(1024)} %param.6) | copy-start | bytes 12292
  40.9 24.4 %copy-start.7 = (f32[1024]{0:T(1024)S(1)}, f32[1024]{0:T(1024)}, u32[]{:S(2)}) copy-start(f32[1024]{0:T(1024)} %param.7) | copy-start | bytes 12292
  204.1 5.4 %copy-start.3 = (bf16[2,2,2,128,384]{4,3,2,1,0:T(8,128)(2,1)S(1)}, bf16[2,2,2,128,384]{4,3,2,1,0:T(8,128)(2,1)}, u32[]{:S(2)}) copy-start(bf16[2,2,2,128,384]{4,3,2,1,0:T(8,128)(2,1)} %copy-done.2) | copy-start | bytes 2359300
  204.1 5.4 %copy-start.5 = (bf16[2,2,2,128,384]{4,3,0,2,1:T(8,128)(2,1)S(1)}, bf16[2,2,2,128,384]{4,3,0,2,1:T(8,128)(2,1)}, u32[]{:S(2)}) copy-start(bf16[2,2,2,128,384]{4,3,0,2,1:T(8,128)(2,1)} %copy-done.4) | copy-start | bytes 2359300
  212.1 4.5 %collective-permute-start.24 = (f32[2,2,2,64,384]{4,3,1,0,2:T(8,128)S(1)}, f32[2,2,2,64,384]{4,3,1,0,2:T(8,128)S(1)}, u32[]{:S(2)}, u32[]{:S(2)}) collective-permute-start(f32[2,2,2,64,384]{4,3,1,0,2:T(8,128)S(1)} %select_bitcast_fusion), channel_id=1, source_target_pairs={{0,8},{8,0},{16,24},{24,16},{32,40},{40,32},{48,56},{56,48},{64,72... | collective-permute-start | bytes 2359304 | tf_op jit(solution)/shard_map/ppermute | solution.py:57
  212.5 4.8 %collective-permute-start.20 = (f32[2,2,2,64,384]{4,3,1,0,2:T(8,128)S(1)}, f32[2,2,2,64,384]{4,3,1,0,2:T(8,128)S(1)}, u32[]{:S(2)}, u32[]{:S(2)}) collective-permute-start(f32[2,2,2,64,384]{4,3,1,0,2:T(8,128)S(1)} %select_bitcast_fusion.1), channel_id=1, source_target_pairs={{0,8},{8,0},{16,24},{24,16},{32,40},{40,32},{48,56},{56,48},{64,72... | collective-permute-start | bytes 2359304 | tf_op jit(solution)/shard_map/ppermute | solution.py:57
  215.2 19.5 %collective-permute-start.14 = (f32[2,2,128,384]{3,2,1,0:T(8,128)S(1)}, f32[2,2,128,384]{3,2,1,0:T(8,128)S(1)}, u32[]{:S(2)}, u32[]{:S(2)}) collective-permute-start(f32[2,2,128,384]{3,2,1,0:T(8,128)S(1)} %select_bitcast_fusion.2), channel_id=1, source_target_pairs={{0,1},{1,0},{2,3},{3,2},{4,5},{5,4},{6,7},{7,6},{8,9},{9,8},{10,11... | collective-permute-start | bytes 2359304 | tf_op jit(solution)/shard_map/ppermute | solution.py:57
  216.0 21.9 %collective-permute-start.17 = (f32[2,2,128,384]{3,2,0,1:T(8,128)S(1)}, f32[2,2,128,384]{3,2,0,1:T(8,128)S(1)}, u32[]{:S(2)}, u32[]{:S(2)}) collective-permute-start(f32[2,2,128,384]{3,2,0,1:T(8,128)S(1)} %copy.97), channel_id=1, source_target_pairs={{0,4},{1,5},{2,6},{3,7},{4,0},{5,1},{6,2},{7,3},{8,12},{9,13},{10,... | collective-permute-start | bytes 2359304 | tf_op jit(solution)/shard_map/ppermute | solution.py:57
  216.7 22.8 %collective-permute-start.25 = (f32[2,2,64,384]{3,2,1,0:T(8,128)S(1)}, f32[2,2,64,384]{3,2,1,0:T(8,128)S(1)}, u32[]{:S(2)}, u32[]{:S(2)}) collective-permute-start(f32[2,2,64,384]{3,2,1,0:T(8,128)S(1)} %select_bitcast_fusion.3), channel_id=1, source_target_pairs={{0,16},{8,24},{16,0},{24,8},{32,48},{40,56},{48,32},{56,40},{64,80... | collective-permute-start | bytes 1179656 | tf_op jit(solution)/shard_map/ppermute | solution.py:57
  217.6 26.2 %collective-permute-start.21 = (f32[2,2,64,384]{3,2,1,0:T(8,128)S(1)}, f32[2,2,64,384]{3,2,1,0:T(8,128)S(1)}, u32[]{:S(2)}, u32[]{:S(2)}) collective-permute-start(f32[2,2,64,384]{3,2,1,0:T(8,128)S(1)} %fusion.18), channel_id=1, source_target_pairs={{0,64},{8,72},{16,80},{24,88},{32,96},{40,104},{48,112},{56,120},{... | collective-permute-start | bytes 1179656 | tf_op jit(solution)/shard_map/ppermute | solution.py:57
  235.0 19.8 %collective-permute-start.15 = (f32[2,128,384]{2,1,0:T(8,128)S(1)}, f32[2,128,384]{2,1,0:T(8,128)S(1)}, u32[]{:S(2)}, u32[]{:S(2)}) collective-permute-start(f32[2,128,384]{2,1,0:T(8,128)S(1)} %select_bitcast_fusion.6), channel_id=1, source_target_pairs={{0,4},{1,5},{2,6},{3,7},{4,0},{5,1},{6,2},{7,3},{8,12},{9,13},{10,... | collective-permute-start | bytes 1179656 | tf_op jit(solution)/shard_map/ppermute | solution.py:57
  238.1 18.9 %collective-permute-start.18 = (f32[2,128,384]{2,1,0:T(8,128)S(1)}, f32[2,128,384]{2,1,0:T(8,128)S(1)}, u32[]{:S(2)}, u32[]{:S(2)}) collective-permute-start(f32[2,128,384]{2,1,0:T(8,128)S(1)} %select_bitcast_fusion.5), channel_id=1, source_target_pairs={{0,1},{1,0},{2,3},{3,2},{4,5},{5,4},{6,7},{7,6},{8,9},{9,8},{10,11... | collective-permute-start | bytes 1179656 | tf_op jit(solution)/shard_map/ppermute | solution.py:57
  239.6 19.0 %collective-permute-start.26 = (f32[2,64,384]{2,1,0:T(8,128)S(1)}, f32[2,64,384]{2,1,0:T(8,128)S(1)}, u32[]{:S(2)}, u32[]{:S(2)}) collective-permute-start(f32[2,64,384]{2,1,0:T(8,128)S(1)} %select_bitcast_fusion.7), channel_id=1, source_target_pairs={{0,64},{8,72},{16,80},{24,88},{32,96},{40,104},{48,112},{56,120},{... | collective-permute-start | bytes 589832 | tf_op jit(solution)/shard_map/ppermute | solution.py:57
  243.8 16.1 %collective-permute-start.22 = (f32[2,64,384]{2,1,0:T(8,128)S(1)}, f32[2,64,384]{2,1,0:T(8,128)S(1)}, u32[]{:S(2)}, u32[]{:S(2)}) collective-permute-start(f32[2,64,384]{2,1,0:T(8,128)S(1)} %select_bitcast_fusion.8), channel_id=1, source_target_pairs={{0,16},{8,24},{16,0},{24,8},{32,48},{40,56},{48,32},{56,40},{64,80... | collective-permute-start | bytes 589832 | tf_op jit(solution)/shard_map/ppermute | solution.py:57
  254.9 8.1 %collective-permute-start.16 = (f32[128,384]{1,0:T(8,128)S(1)}, f32[128,384]{1,0:T(8,128)S(1)}, u32[]{:S(2)}, u32[]{:S(2)}) collective-permute-start(f32[128,384]{1,0:T(8,128)S(1)} %select_bitcast_fusion.10), channel_id=1, source_target_pairs={{0,2},{1,3},{2,0},{3,1},{4,6},{5,7},{6,4},{7,5},{8,10},{9,11},{10,... | collective-permute-start | bytes 589832 | tf_op jit(solution)/shard_map/ppermute | solution.py:57
  257.0 8.0 %collective-permute-start.19 = (f32[128,384]{1,0:T(8,128)S(1)}, f32[128,384]{1,0:T(8,128)S(1)}, u32[]{:S(2)}, u32[]{:S(2)}) collective-permute-start(f32[128,384]{1,0:T(8,128)S(1)} %select_bitcast_fusion.9), channel_id=1, source_target_pairs={{0,2},{1,3},{2,0},{3,1},{4,6},{5,7},{6,4},{7,5},{8,10},{9,11},{10,... | collective-permute-start | bytes 589832 | tf_op jit(solution)/shard_map/ppermute | solution.py:57
  258.7 7.2 %collective-permute-start.27 = (f32[64,384]{1,0:T(8,128)S(1)}, f32[64,384]{1,0:T(8,128)S(1)}, u32[]{:S(2)}, u32[]{:S(2)}) collective-permute-start(f32[64,384]{1,0:T(8,128)S(1)} %select_bitcast_fusion.11), channel_id=1, source_target_pairs={{0,32},{8,40},{16,48},{24,56},{32,0},{40,8},{48,16},{56,24},{64,96... | collective-permute-start | bytes 294920 | tf_op jit(solution)/shard_map/ppermute | solution.py:57
  260.0 6.2 %collective-permute-start.23 = (f32[64,384]{1,0:T(8,128)S(1)}, f32[64,384]{1,0:T(8,128)S(1)}, u32[]{:S(2)}, u32[]{:S(2)}) collective-permute-start(f32[64,384]{1,0:T(8,128)S(1)} %select_bitcast_fusion.12), channel_id=1, source_target_pairs={{0,32},{8,40},{16,48},{24,56},{32,0},{40,8},{48,16},{56,24},{64,96... | collective-permute-start | bytes 294920 | tf_op jit(solution)/shard_map/ppermute | solution.py:57
  (4 other events, 13.6 us)

commit v2 on v0

--- a/solution.py
+++ b/solution.py
@@ -75,6 +75,18 @@
     )
 
 
+def to_bf16_grid(x):
+    return lax.reduce_precision(x, exponent_bits=8, mantissa_bits=7)
+
+
+def split3(x):
+    high = to_bf16_grid(x)
+    rest = x - high
+    mid = to_bf16_grid(rest)
+    low = rest - mid
+    return [p.astype(jnp.bfloat16) for p in (high, mid, low)]
+
+
 def row_total(part):
     return tree_sum(part, "tgt")
 
@@ -140,8 +152,11 @@
         col_bars[iteration] = col_bar
     left = jnp.stack(row_bars + src_saved, axis=1)
     right = jnp.stack(old_saved + col_bars, axis=1)
+    left_pieces, right_pieces = split3(left), split3(right)
+    left_all = jnp.concatenate([a for a in left_pieces for b in right_pieces], axis=1)
+    right_all = jnp.concatenate([b for a in left_pieces for b in right_pieces], axis=1)
     lowrank = lax.dot_general(
-        left, right, (((1,), (1,)), ((), ())), precision=highest, preferred_element_type=jnp.float32
+        left_all, right_all, (((1,), (1,)), ((), ())), preferred_element_type=jnp.float32
     )
     cross_term_grid = (
         kernel * (last_src[:, None] * last_tgt[None, :] * (1.0 + kernel_grid) + lowrank)

time: 271 us -> 268 us (0.989)
  no operation moved by 1% of the time
where the time goes in v2:
time: 268 us; the launch traced here: 267 us
  blocking collectives  139 us (52%)
  waiting for transfers between devices  57 us (21%)
  starting transfers between devices  36 us (13%)
  other arithmetic  18.4 us (7%)
  matrix products  11 us (4%)
  local copies, waits for them, and re-layouts  4.48 us (2%)
    all_to_all x14, blocking collectives, tree_sum(): return lax.all_to_all(spread, axis, 0, 0, tiled=False).sum(0)  139 us
    ppermute x14, waiting for transfers between devices, tree_scatter(): x = keep + lax.ppermute(send, axis, partner(axis, n, bit))  35.5 us
    ppermute x14, starting transfers between devices, tree_gather(): other = lax.ppermute(x, axis, partner(axis, n, bit))  18.5 us
    ppermute x14, waiting for transfers between devices, tree_gather(): other = lax.ppermute(x, axis, partner(axis, n, bit))  14.2 us
    ppermute x14, starting transfers between devices, tree_scatter(): x = keep + lax.ppermute(send, axis, partner(axis, n, bit))  13.9 us
    all_to_all x1, waiting for transfers between devices, tree_sum(): return lax.all_to_all(spread, axis, 0, 0, tiled=False).sum(0)  7.28 us
    reduce_sum x8, other arithmetic, times_vector(): return jnp.sum(kernel.astype(jnp.float32) * vector[None, :], axis=1)  6.72 us
    reduce_sum x7, other arithmetic, vector_times(): return jnp.sum(vector[:, None] * kernel.astype(jnp.float32), axis=0)  6.08 us
  transfers between devices with their start and end apart: 29, of which 12 were waited for; matrix products, arithmetic and copies ran while one was open for 3% of the time, Pallas kernels for 0%

profile of v2, /device:TPU:0, one launch (start us, length us, event | category | flops | bytes accessed | tf_op | source)
XLA Modules:
  0.0 267.1 jit_solution(1121651713126970832)
XLA Ops:
  1.5 4.0 %collective-permute-start.10 = (bf16[64,384]{1,0:T(8,128)(2,1)S(1)}, bf16[64,384]{1,0:T(8,128)(2,1)S(1)}, u32[]{:S(2)}, u32[]{:S(2)}) collective-permute-start(bf16[64,384]{1,0:T(8,128)(2,1)S(1)} %get-tuple-element.31), channel_id=1, source_target_pairs={{0,32},{8,40},{16,48},{24,56},{32,0},{40,8},{48,16},{56,24},{64,96... | collective-permute-start | bytes 147464 | tf_op jit(solution)/shard_map/ppermute | solution.py:34
  6.6 3.1 %collective-permute-start.3 = (bf16[128,384]{1,0:T(8,128)(2,1)S(1)}, bf16[128,384]{1,0:T(8,128)(2,1)S(1)}, u32[]{:S(2)}, u32[]{:S(2)}) collective-permute-start(bf16[128,384]{1,0:T(8,128)(2,1)S(1)} %get-tuple-element.23), channel_id=1, source_target_pairs={{0,2},{1,3},{2,0},{3,1},{4,6},{5,7},{6,4},{7,5},{8,10},{9,11},{10,... | collective-permute-start | bytes 294920 | tf_op jit(solution)/shard_map/ppermute | solution.py:34
  15.9 3.3 %collective-permute-start.1 = (bf16[2,128,384]{2,1,0:T(8,128)(2,1)S(1)}, bf16[2,128,384]{2,1,0:T(8,128)(2,1)S(1)}, u32[]{:S(2)}, u32[]{:S(2)}) collective-permute-start(bf16[2,128,384]{2,1,0:T(8,128)(2,1)S(1)} %maximum_select_fusion.12), channel_id=1, source_target_pairs={{0,4},{1,5},{2,6},{3,7},{4,0},{5,1},{6,2},{7,3},{8,12},{9,13},{10,... | collective-permute-start | bytes 589832 | tf_op jit(solution)/shard_map/ppermute | solution.py:34
  22.6 2.5 collective-permute-done.4
  26.4 3.2 %collective-permute-done.8 = bf16[2,2,64,384]{3,2,0,1:T(8,128)(2,1)S(1)} collective-permute-done((bf16[2,2,64,384]{3,2,0,1:T(8,128)(2,1)S(1)}, bf16[2,2,64,384]{3,2,0,1:T(8,128)(2,1)S(1)}, u32[]{:S(2)}, u32[]{:S(2)}) %collective-permute-start.8) | collective-permute-done | bytes 196640 | tf_op jit(solution)/shard_map/ppermute | solution.py:34
  30.5 5.8 %collective-permute-done.5 = bf16[2,2,128,384]{3,2,1,0:T(8,128)(2,1)S(1)} collective-permute-done((bf16[2,2,128,384]{3,2,1,0:T(8,128)(2,1)S(1)}, bf16[2,2,128,384]{3,2,1,0:T(8,128)(2,1)S(1)}, u32[]{:S(2)}, u32[]{:S(2)}) %collective-permute-start.5) | collective-permute-done | bytes 393248 | tf_op jit(solution)/shard_map/ppermute | solution.py:34
  37.5 3.8 %exponential_convert_fusion = (bf16[1024,1024]{1,0:T(8,128)(2,1)S(1)}, f32[1024,1024]{1,0:T(8,128)}) fusion(bf16[1024,384]{1,0:T(8,128)(2,1)S(1)} %bitcast.201, bf16[1024,384]{1,0:T(8,128)(2,1)S(1)} %bitcast.203, bf16[1024,384]{1,0:T(8,128)(2,1)S(1)} %bitcast.205, bf16[1024,384]{1,0:T(8,128)(2,1)S(1)} %bitcast.207), kind=kOutput, calls=%fused_computation.34 | convolution fusion | flops 1619001344 | bytes 9437184 | tf_op jit(solution)/shard_map/dot_general | solution.py:111
  41.6 12.7 %all_to_all.89 = f32[8,1,1024]{2,1,0:T(1,128)S(1)} all-to-all(f32[8,1,1024]{2,1,0:T(1,128)S(1)} %broadcast_in_dim.44), channel_id=1, replica_groups=mesh['src'=16,'tgt'=8] {'tgt'}, dimensions={0} | all-to-all | bytes 65536 | tf_op jit(solution)/shard_map/all_to_all | solution.py:27
  54.9 10.8 %all_to_all.90 = f32[16,1,1024]{2,1,0:T(1,128)S(1)} all-to-all(f32[16,1,1024]{2,1,0:T(1,128)S(1)} %broadcast_in_dim.45), channel_id=1, replica_groups=mesh['src'=16,'tgt'=8] {'src'}, dimensions={0} | all-to-all | bytes 131072 | tf_op jit(solution)/shard_map/all_to_all | solution.py:27
  66.2 10.7 %all_to_all.91 = f32[8,1,1024]{2,1,0:T(1,128)S(1)} all-to-all(f32[8,1,1024]{2,1,0:T(1,128)S(1)} %broadcast_in_dim.46), channel_id=1, replica_groups=mesh['src'=16,'tgt'=8] {'tgt'}, dimensions={0} | all-to-all | bytes 65536 | tf_op jit(solution)/shard_map/all_to_all | solution.py:27
  77.5 8.7 %all_to_all.92 = f32[16,1,1024]{2,1,0:T(1,128)S(1)} all-to-all(f32[16,1,1024]{2,1,0:T(1,128)S(1)} %broadcast_in_dim.47), channel_id=1, replica_groups=mesh['src'=16,'tgt'=8] {'src'}, dimensions={0} | all-to-all | bytes 131072 | tf_op jit(solution)/shard_map/all_to_all | solution.py:27
  86.8 10.1 %all_to_all.93 = f32[8,1,1024]{2,1,0:T(1,128)S(1)} all-to-all(f32[8,1,1024]{2,1,0:T(1,128)S(1)} %broadcast_in_dim.48), channel_id=1, replica_groups=mesh['src'=16,'tgt'=8] {'tgt'}, dimensions={0} | all-to-all | bytes 65536 | tf_op jit(solution)/shard_map/all_to_all | solution.py:27
  97.5 8.7 %all_to_all.94 = f32[16,1,1024]{2,1,0:T(1,128)S(1)} all-to-all(f32[16,1,1024]{2,1,0:T(1,128)S(1)} %broadcast_in_dim.49), channel_id=1, replica_groups=mesh['src'=16,'tgt'=8] {'src'}, dimensions={0} | all-to-all | bytes 131072 | tf_op jit(solution)/shard_map/all_to_all | solution.py:27
  106.8 10.5 %all_to_all.95 = f32[8,1,1024]{2,1,0:T(1,128)S(1)} all-to-all(f32[8,1,1024]{2,1,0:T(1,128)S(1)} %broadcast_in_dim.50), channel_id=1, replica_groups=mesh['src'=16,'tgt'=8] {'tgt'}, dimensions={0} | all-to-all | bytes 65536 | tf_op jit(solution)/shard_map/all_to_all | solution.py:27
  117.4 3.2 %fusion.6 = (f32[1024]{0:T(1024)S(1)}, f32[1024]{0:T(1024)S(1)}) fusion(bf16[1024,1024]{1,0:T(8,128)(2,1)S(1)} %get-tuple-element.35, f32[1024]{0:T(1024)S(1)} %div.68, f32[1024,1024]{1,0:T(8,128)} %get-tuple-element.36), kind=kLoop, calls=%fused_computation.23 | loop fusion | flops 7337984 | bytes 6303744 | tf_op jit(solution)/shard_map/reduce_sum | solution.py:103
  120.7 9.3 %all_to_all.96 = f32[16,2,1024]{2,1,0:T(2,128)S(1)} all-to-all(f32[16,2,1024]{2,1,0:T(2,128)S(1)} %broadcast_in_dim.51), channel_id=1, replica_groups=mesh['src'=16,'tgt'=8] {'src'}, dimensions={0} | all-to-all | bytes 262144 | tf_op jit(solution)/shard_map/all_to_all | solution.py:27
  130.1 3.5 %multiply_reduce_fusion = (f32[1024]{0:T(1024)S(1)}, f32[1024]{0:T(1024)S(1)}) fusion(f32[1024,1024]{1,0:T(8,128)} %get-tuple-element.36, bf16[1024,1024]{1,0:T(8,128)(2,1)S(1)} %get-tuple-element.35, f32[1024]{0:T(1024)S(1)} %get-tuple-element.7, f32[1024]{0:T(1024)S(1)} %get-tuple-element.6), kind=kLoop, calls=%fused_computation.32 | loop fusion | flops 7337984 | bytes 6307840 | tf_op jit(solution)/shard_map/reduce_sum | solution.py:99
  133.6 10.1 %all_to_all.97 = f32[8,1,1024]{2,1,0:T(1,128)S(1)} all-to-all(f32[8,1,1024]{2,1,0:T(1,128)S(1)} %broadcast_in_dim.52), channel_id=1, replica_groups=mesh['src'=16,'tgt'=8] {'tgt'}, dimensions={0} | all-to-all | bytes 65536 | tf_op jit(solution)/shard_map/all_to_all | solution.py:27
  144.3 8.7 %all_to_all.98 = f32[16,1,1024]{2,1,0:T(1,128)S(1)} all-to-all(f32[16,1,1024]{2,1,0:T(1,128)S(1)} %broadcast_in_dim.53), channel_id=1, replica_groups=mesh['src'=16,'tgt'=8] {'src'}, dimensions={0} | all-to-all | bytes 131072 | tf_op jit(solution)/shard_map/all_to_all | solution.py:27
  153.6 10.3 %all_to_all.99 = f32[8,1,1024]{2,1,0:T(1,128)S(1)} all-to-all(f32[8,1,1024]{2,1,0:T(1,128)S(1)} %broadcast_in_dim.54), channel_id=1, replica_groups=mesh['src'=16,'tgt'=8] {'tgt'}, dimensions={0} | all-to-all | bytes 65536 | tf_op jit(solution)/shard_map/all_to_all | solution.py:27
  164.5 8.7 %all_to_all.100 = f32[16,1,1024]{2,1,0:T(1,128)S(1)} all-to-all(f32[16,1,1024]{2,1,0:T(1,128)S(1)} %broadcast_in_dim.55), channel_id=1, replica_groups=mesh['src'=16,'tgt'=8] {'src'}, dimensions={0} | all-to-all | bytes 131072 | tf_op jit(solution)/shard_map/all_to_all | solution.py:27
  173.8 10.4 %all_to_all.101 = f32[8,1,1024]{2,1,0:T(1,128)S(1)} all-to-all(f32[8,1,1024]{2,1,0:T(1,128)S(1)} %broadcast_in_dim.56), channel_id=1, replica_groups=mesh['src'=16,'tgt'=8] {'tgt'}, dimensions={0} | all-to-all | bytes 65536 | tf_op jit(solution)/shard_map/all_to_all | solution.py:27
  184.8 8.7 %all_to_all.102 = f32[16,1,1024]{2,1,0:T(1,128)S(1)} all-to-all(f32[16,1,1024]{2,1,0:T(1,128)S(1)} %broadcast_in_dim.57), channel_id=1, replica_groups=mesh['src'=16,'tgt'=8] {'src'}, dimensions={0} | all-to-all | bytes 131072 | tf_op jit(solution)/shard_map/all_to_all | solution.py:27
  194.7 3.6 %all-to-all-start.14 = ((f32[8,1,1024]{2,1,0:T(1,128)}), f32[8,1,1024]{2,1,0:T(1,128)S(1)}, u32[]{:S(2)}, u32[]{:S(2)}) async-start(f32[8,1,1024]{2,1,0:T(1,128)} %broadcast_in_dim.58), calls=%async_computation.14 | async-start | bytes 65536 | tf_op jit(solution)/shard_map/all_to_all | solution.py:27
  198.4 7.3 %all-to-all-done.14 = f32[8,1,1024]{2,1,0:T(1,128)S(1)} async-done(((f32[8,1,1024]{2,1,0:T(1,128)}), f32[8,1,1024]{2,1,0:T(1,128)S(1)}, u32[]{:S(2)}, u32[]{:S(2)}) %all-to-all-start.14) | async-done | bytes 32800 | tf_op jit(solution)/shard_map/all_to_all | solution.py:27
  206.0 3.5 %fusion.14 = bf16[1024,1024]{1,0:T(8,128)(2,1)S(1)} fusion(bf16[1024,1024]{1,0:T(8,128)(2,1)S(1)} %get-tuple-element.35, f32[1024,1024]{1,0:T(8,128)} %get-tuple-element.36, bf16[1024,72]{0,1:T(8,128)(2,1)S(1)} %get-tuple-element.37, bf16[1024,72]{0,1:T(8,128)(2,1)S(1)} %get-tuple-element.38, f32[1024]{0:T(1024)S(1)} %get-tuple-element.7, f32[1024]{0:T(1024)S(1)} %div.68), kind=kOutput, calls=%fused_computation.31 | convolution fusion | flops 159383552 | bytes 8691712 | tf_op jit(solution)/shard_map/dot_general | solution.py:158
  218.4 16.2 %collective-permute-done.14 = f32[2,2,128,384]{3,2,1,0:T(8,128)S(1)} collective-permute-done((f32[2,2,128,384]{3,2,1,0:T(8,128)S(1)}, f32[2,2,128,384]{3,2,1,0:T(8,128)S(1)}, u32[]{:S(2)}, u32[]{:S(2)}) %collective-permute-start.14) | collective-permute-done | bytes 786464 | tf_op jit(solution)/shard_map/ppermute | solution.py:57
  235.4 2.6 collective-permute-done.17
  240.4 3.7 %collective-permute-done.21 = f32[2,2,64,384]{3,2,1,0:T(8,128)S(1)} collective-permute-done((f32[2,2,64,384]{3,2,1,0:T(8,128)S(1)}, f32[2,2,64,384]{3,2,1,0:T(8,128)S(1)}, u32[]{:S(2)}, u32[]{:S(2)}) %collective-permute-start.21) | collective-permute-done | bytes 393248 | tf_op jit(solution)/shard_map/ppermute | solution.py:57
  244.8 10.1 %collective-permute-done.15 = f32[2,128,384]{2,1,0:T(8,128)S(1)} collective-permute-done((f32[2,128,384]{2,1,0:T(8,128)S(1)}, f32[2,128,384]{2,1,0:T(8,128)S(1)}, u32[]{:S(2)}, u32[]{:S(2)}) %collective-permute-start.15) | collective-permute-done | bytes 393248 | tf_op jit(solution)/shard_map/ppermute | solution.py:57
  255.0 2.1 collective-permute-start.16
  260.1 2.4 collective-permute-start.23
  (213 shorter events, 43.0 us)
Async XLA Ops:
  1.5 8.7 %collective-permute-start.10 = (bf16[64,384]{1,0:T(8,128)(2,1)S(1)}, bf16[64,384]{1,0:T(8,128)(2,1)S(1)}, u32[]{:S(2)}, u32[]{:S(2)}) collective-permute-start(bf16[64,384]{1,0:T(8,128)(2,1)S(1)} %get-tuple-element.31), channel_id=1, source_target_pairs={{0,32},{8,40},{16,48},{24,56},{32,0},{40,8},{48,16},{56,24},{64,96... | collective-permute-start | bytes 147464 | tf_op jit(solution)/shard_map/ppermute | solution.py:34
  5.5 5.6 %collective-permute-start.6 = (bf16[64,384]{1,0:T(8,128)(2,1)S(1)}, bf16[64,384]{1,0:T(8,128)(2,1)S(1)}, u32[]{:S(2)}, u32[]{:S(2)}) collective-permute-start(bf16[64,384]{1,0:T(8,128)(2,1)S(1)} %get-tuple-element.32), channel_id=1, source_target_pairs={{0,32},{8,40},{16,48},{24,56},{32,0},{40,8},{48,16},{56,24},{64,96... | collective-permute-start | bytes 147464 | tf_op jit(solution)/shard_map/ppermute | solution.py:34
  6.6 12.6 %collective-permute-start.3 = (bf16[128,384]{1,0:T(8,128)(2,1)S(1)}, bf16[128,384]{1,0:T(8,128)(2,1)S(1)}, u32[]{:S(2)}, u32[]{:S(2)}) collective-permute-start(bf16[128,384]{1,0:T(8,128)(2,1)S(1)} %get-tuple-element.23), channel_id=1, source_target_pairs={{0,2},{1,3},{2,0},{3,1},{4,6},{5,7},{6,4},{7,5},{8,10},{9,11},{10,... | collective-permute-start | bytes 294920 | tf_op jit(solution)/shard_map/ppermute | solution.py:34
  9.7 6.1 %collective-permute-start = (bf16[128,384]{1,0:T(8,128)(2,1)S(1)}, bf16[128,384]{1,0:T(8,128)(2,1)S(1)}, u32[]{:S(2)}, u32[]{:S(2)}) collective-permute-start(bf16[128,384]{1,0:T(8,128)(2,1)S(1)} %get-tuple-element.24), channel_id=1, source_target_pairs={{0,2},{1,3},{2,0},{3,1},{4,6},{5,7},{6,4},{7,5},{8,10},{9,11},{10,... | collective-permute-start | bytes 294920 | tf_op jit(solution)/shard_map/ppermute | solution.py:34
  11.1 10.5 %collective-permute-start.7 = (bf16[2,64,384]{2,1,0:T(8,128)(2,1)S(1)}, bf16[2,64,384]{2,1,0:T(8,128)(2,1)S(1)}, u32[]{:S(2)}, u32[]{:S(2)}) collective-permute-start(bf16[2,64,384]{2,1,0:T(8,128)(2,1)S(1)} %maximum_select_fusion.19), channel_id=1, source_target_pairs={{0,16},{8,24},{16,0},{24,8},{32,48},{40,56},{48,32},{56,40},{64,80... | collective-permute-start | bytes 294920 | tf_op jit(solution)/shard_map/ppermute | solution.py:34
  12.3 7.8 %collective-permute-start.11 = (bf16[2,64,384]{2,1,0:T(8,128)(2,1)S(1)}, bf16[2,64,384]{2,1,0:T(8,128)(2,1)S(1)}, u32[]{:S(2)}, u32[]{:S(2)}) collective-permute-start(bf16[2,64,384]{2,1,0:T(8,128)(2,1)S(1)} %maximum_select_fusion.20), channel_id=1, source_target_pairs={{0,64},{8,72},{16,80},{24,88},{32,96},{40,104},{48,112},{56,120},{... | collective-permute-start | bytes 294920 | tf_op jit(solution)/shard_map/ppermute | solution.py:34
  15.9 9.6 %collective-permute-start.1 = (bf16[2,128,384]{2,1,0:T(8,128)(2,1)S(1)}, bf16[2,128,384]{2,1,0:T(8,128)(2,1)S(1)}, u32[]{:S(2)}, u32[]{:S(2)}) collective-permute-start(bf16[2,128,384]{2,1,0:T(8,128)(2,1)S(1)} %maximum_select_fusion.12), channel_id=1, source_target_pairs={{0,4},{1,5},{2,6},{3,7},{4,0},{5,1},{6,2},{7,3},{8,12},{9,13},{10,... | collective-permute-start | bytes 589832 | tf_op jit(solution)/shard_map/ppermute | solution.py:34
  19.3 5.8 %collective-permute-start.4 = (bf16[2,128,384]{2,1,0:T(8,128)(2,1)S(1)}, bf16[2,128,384]{2,1,0:T(8,128)(2,1)S(1)}, u32[]{:S(2)}, u32[]{:S(2)}) collective-permute-start(bf16[2,128,384]{2,1,0:T(8,128)(2,1)S(1)} %maximum_select_fusion.14), channel_id=1, source_target_pairs={{0,1},{1,0},{2,3},{3,2},{4,5},{5,4},{6,7},{7,6},{8,9},{9,8},{10,11... | collective-permute-start | bytes 589832 | tf_op jit(solution)/shard_map/ppermute | solution.py:34
  20.1 9.7 %collective-permute-start.12 = (bf16[2,2,64,384]{3,2,1,0:T(8,128)(2,1)S(1)}, bf16[2,2,64,384]{3,2,1,0:T(8,128)(2,1)S(1)}, u32[]{:S(2)}, u32[]{:S(2)}) collective-permute-start(bf16[2,2,64,384]{3,2,1,0:T(8,128)(2,1)S(1)} %maximum_select_fusion.17), channel_id=1, source_target_pairs={{0,16},{8,24},{16,0},{24,8},{32,48},{40,56},{48,32},{56,40},{64,80... | collective-permute-start | bytes 589832 | tf_op jit(solution)/shard_map/ppermute | solution.py:34
  21.7 7.9 %collective-permute-start.8 = (bf16[2,2,64,384]{3,2,0,1:T(8,128)(2,1)S(1)}, bf16[2,2,64,384]{3,2,0,1:T(8,128)(2,1)S(1)}, u32[]{:S(2)}, u32[]{:S(2)}) collective-permute-start(bf16[2,2,64,384]{3,2,0,1:T(8,128)(2,1)S(1)} %maximum_select_fusion.16), channel_id=1, source_target_pairs={{0,64},{8,72},{16,80},{24,88},{32,96},{40,104},{48,112},{56,120},{... | collective-permute-start | bytes 589832 | tf_op jit(solution)/shard_map/ppermute | solution.py:34
  25.1 11.2 %collective-permute-start.5 = (bf16[2,2,128,384]{3,2,1,0:T(8,128)(2,1)S(1)}, bf16[2,2,128,384]{3,2,1,0:T(8,128)(2,1)S(1)}, u32[]{:S(2)}, u32[]{:S(2)}) collective-permute-start(bf16[2,2,128,384]{3,2,1,0:T(8,128)(2,1)S(1)} %maximum_select_fusion.6), channel_id=1, source_target_pairs={{0,4},{1,5},{2,6},{3,7},{4,0},{5,1},{6,2},{7,3},{8,12},{9,13},{10,... | collective-permute-start | bytes 1179656 | tf_op jit(solution)/shard_map/ppermute | solution.py:34
  25.6 11.0 %collective-permute-start.2 = (bf16[2,2,128,384]{3,2,1,0:T(8,128)(2,1)S(1)}, bf16[2,2,128,384]{3,2,1,0:T(8,128)(2,1)S(1)}, u32[]{:S(2)}, u32[]{:S(2)}) collective-permute-start(bf16[2,2,128,384]{3,2,1,0:T(8,128)(2,1)S(1)} %maximum_select_fusion.4), channel_id=1, source_target_pairs={{0,1},{1,0},{2,3},{3,2},{4,5},{5,4},{6,7},{7,6},{8,9},{9,8},{10,11... | collective-permute-start | bytes 1179656 | tf_op jit(solution)/shard_map/ppermute | solution.py:34
  29.6 7.3 %collective-permute-start.9 = (bf16[2,2,2,64,384]{4,3,1,2,0:T(8,128)(2,1)S(1)}, bf16[2,2,2,64,384]{4,3,1,2,0:T(8,128)(2,1)S(1)}, u32[]{:S(2)}, u32[]{:S(2)}) collective-permute-start(bf16[2,2,2,64,384]{4,3,1,2,0:T(8,128)(2,1)S(1)} %maximum_select_fusion.8), channel_id=1, source_target_pairs={{0,8},{8,0},{16,24},{24,16},{32,40},{40,32},{48,56},{56,48},{64,72... | collective-permute-start | bytes 1179656 | tf_op jit(solution)/shard_map/ppermute | solution.py:34
  29.8 6.9 %collective-permute-start.13 = (bf16[2,2,2,64,384]{4,3,2,1,0:T(8,128)(2,1)S(1)}, bf16[2,2,2,64,384]{4,3,2,1,0:T(8,128)(2,1)S(1)}, u32[]{:S(2)}, u32[]{:S(2)}) collective-permute-start(bf16[2,2,2,64,384]{4,3,2,1,0:T(8,128)(2,1)S(1)} %maximum_select_fusion.10), channel_id=1, source_target_pairs={{0,8},{8,0},{16,24},{24,16},{32,40},{40,32},{48,56},{56,48},{64,72... | collective-permute-start | bytes 1179656 | tf_op jit(solution)/shard_map/ppermute | solution.py:34
  36.7 4.6 %copy-start.4 = (bf16[2,2,2,128,384]{4,3,0,2,1:T(8,128)(2,1)}, bf16[2,2,2,128,384]{4,3,0,2,1:T(8,128)(2,1)S(1)}, u32[]{:S(2)}) copy-start(bf16[2,2,2,128,384]{4,3,0,2,1:T(8,128)(2,1)S(1)} %maximum_select_fusion) | copy-start | bytes 2359300
  37.5 16.9 %copy-start.6 = (f32[1024]{0:T(1024)S(1)}, f32[1024]{0:T(1024)}, u32[]{:S(2)}) copy-start(f32[1024]{0:T(1024)} %param.6) | copy-start | bytes 12292
  41.3 24.4 %copy-start.7 = (f32[1024]{0:T(1024)S(1)}, f32[1024]{0:T(1024)}, u32[]{:S(2)}) copy-start(f32[1024]{0:T(1024)} %param.7) | copy-start | bytes 12292
  194.7 11.0 %all-to-all-start.14 = ((f32[8,1,1024]{2,1,0:T(1,128)}), f32[8,1,1024]{2,1,0:T(1,128)S(1)}, u32[]{:S(2)}, u32[]{:S(2)}) async-start(f32[8,1,1024]{2,1,0:T(1,128)} %broadcast_in_dim.58), calls=%async_computation.14 | async-start | bytes 65536 | tf_op jit(solution)/shard_map/all_to_all | solution.py:27
  212.1 4.5 %collective-permute-start.24 = (f32[2,2,2,64,384]{4,3,1,0,2:T(8,128)S(1)}, f32[2,2,2,64,384]{4,3,1,0,2:T(8,128)S(1)}, u32[]{:S(2)}, u32[]{:S(2)}) collective-permute-start(f32[2,2,2,64,384]{4,3,1,0,2:T(8,128)S(1)} %select_bitcast_fusion), channel_id=1, source_target_pairs={{0,8},{8,0},{16,24},{24,16},{32,40},{40,32},{48,56},{56,48},{64,72... | collective-permute-start | bytes 2359304 | tf_op jit(solution)/shard_map/ppermute | solution.py:57
  212.3 5.1 %collective-permute-start.20 = (f32[2,2,2,64,384]{4,3,1,0,2:T(8,128)S(1)}, f32[2,2,2,64,384]{4,3,1,0,2:T(8,128)S(1)}, u32[]{:S(2)}, u32[]{:S(2)}) collective-permute-start(f32[2,2,2,64,384]{4,3,1,0,2:T(8,128)S(1)} %select_bitcast_fusion.1), channel_id=1, source_target_pairs={{0,8},{8,0},{16,24},{24,16},{32,40},{40,32},{48,56},{56,48},{64,72... | collective-permute-start | bytes 2359304 | tf_op jit(solution)/shard_map/ppermute | solution.py:57
  215.3 19.3 %collective-permute-start.14 = (f32[2,2,128,384]{3,2,1,0:T(8,128)S(1)}, f32[2,2,128,384]{3,2,1,0:T(8,128)S(1)}, u32[]{:S(2)}, u32[]{:S(2)}) collective-permute-start(f32[2,2,128,384]{3,2,1,0:T(8,128)S(1)} %select_bitcast_fusion.2), channel_id=1, source_target_pairs={{0,1},{1,0},{2,3},{3,2},{4,5},{5,4},{6,7},{7,6},{8,9},{9,8},{10,11... | collective-permute-start | bytes 2359304 | tf_op jit(solution)/shard_map/ppermute | solution.py:57
  216.0 22.0 %collective-permute-start.17 = (f32[2,2,128,384]{3,2,0,1:T(8,128)S(1)}, f32[2,2,128,384]{3,2,0,1:T(8,128)S(1)}, u32[]{:S(2)}, u32[]{:S(2)}) collective-permute-start(f32[2,2,128,384]{3,2,0,1:T(8,128)S(1)} %copy.97), channel_id=1, source_target_pairs={{0,4},{1,5},{2,6},{3,7},{4,0},{5,1},{6,2},{7,3},{8,12},{9,13},{10,... | collective-permute-start | bytes 2359304 | tf_op jit(solution)/shard_map/ppermute | solution.py:57
  216.7 22.9 %collective-permute-start.25 = (f32[2,2,64,384]{3,2,1,0:T(8,128)S(1)}, f32[2,2,64,384]{3,2,1,0:T(8,128)S(1)}, u32[]{:S(2)}, u32[]{:S(2)}) collective-permute-start(f32[2,2,64,384]{3,2,1,0:T(8,128)S(1)} %select_bitcast_fusion.3), channel_id=1, source_target_pairs={{0,16},{8,24},{16,0},{24,8},{32,48},{40,56},{48,32},{56,40},{64,80... | collective-permute-start | bytes 1179656 | tf_op jit(solution)/shard_map/ppermute | solution.py:57
  217.7 26.4 %collective-permute-start.21 = (f32[2,2,64,384]{3,2,1,0:T(8,128)S(1)}, f32[2,2,64,384]{3,2,1,0:T(8,128)S(1)}, u32[]{:S(2)}, u32[]{:S(2)}) collective-permute-start(f32[2,2,64,384]{3,2,1,0:T(8,128)S(1)} %fusion.18), channel_id=1, source_target_pairs={{0,64},{8,72},{16,80},{24,88},{32,96},{40,104},{48,112},{56,120},{... | collective-permute-start | bytes 1179656 | tf_op jit(solution)/shard_map/ppermute | solution.py:57
  234.8 20.1 %collective-permute-start.15 = (f32[2,128,384]{2,1,0:T(8,128)S(1)}, f32[2,128,384]{2,1,0:T(8,128)S(1)}, u32[]{:S(2)}, u32[]{:S(2)}) collective-permute-start(f32[2,128,384]{2,1,0:T(8,128)S(1)} %select_bitcast_fusion.6), channel_id=1, source_target_pairs={{0,4},{1,5},{2,6},{3,7},{4,0},{5,1},{6,2},{7,3},{8,12},{9,13},{10,... | collective-permute-start | bytes 1179656 | tf_op jit(solution)/shard_map/ppermute | solution.py:57
  238.2 18.9 %collective-permute-start.18 = (f32[2,128,384]{2,1,0:T(8,128)S(1)}, f32[2,128,384]{2,1,0:T(8,128)S(1)}, u32[]{:S(2)}, u32[]{:S(2)}) collective-permute-start(f32[2,128,384]{2,1,0:T(8,128)S(1)} %select_bitcast_fusion.5), channel_id=1, source_target_pairs={{0,1},{1,0},{2,3},{3,2},{4,5},{5,4},{6,7},{7,6},{8,9},{9,8},{10,11... | collective-permute-start | bytes 1179656 | tf_op jit(solution)/shard_map/ppermute | solution.py:57
  239.7 19.0 %collective-permute-start.26 = (f32[2,64,384]{2,1,0:T(8,128)S(1)}, f32[2,64,384]{2,1,0:T(8,128)S(1)}, u32[]{:S(2)}, u32[]{:S(2)}) collective-permute-start(f32[2,64,384]{2,1,0:T(8,128)S(1)} %select_bitcast_fusion.7), channel_id=1, source_target_pairs={{0,64},{8,72},{16,80},{24,88},{32,96},{40,104},{48,112},{56,120},{... | collective-permute-start | bytes 589832 | tf_op jit(solution)/shard_map/ppermute | solution.py:57
  244.1 16.0 %collective-permute-start.22 = (f32[2,64,384]{2,1,0:T(8,128)S(1)}, f32[2,64,384]{2,1,0:T(8,128)S(1)}, u32[]{:S(2)}, u32[]{:S(2)}) collective-permute-start(f32[2,64,384]{2,1,0:T(8,128)S(1)} %select_bitcast_fusion.8), channel_id=1, source_target_pairs={{0,16},{8,24},{16,0},{24,8},{32,48},{40,56},{48,32},{56,40},{64,80... | collective-permute-start | bytes 589832 | tf_op jit(solution)/shard_map/ppermute | solution.py:57
  255.0 7.6 %collective-permute-start.16 = (f32[128,384]{1,0:T(8,128)S(1)}, f32[128,384]{1,0:T(8,128)S(1)}, u32[]{:S(2)}, u32[]{:S(2)}) collective-permute-start(f32[128,384]{1,0:T(8,128)S(1)} %select_bitcast_fusion.10), channel_id=1, source_target_pairs={{0,2},{1,3},{2,0},{3,1},{4,6},{5,7},{6,4},{7,5},{8,10},{9,11},{10,... | collective-permute-start | bytes 589832 | tf_op jit(solution)/shard_map/ppermute | solution.py:57
  257.2 7.4 %collective-permute-start.19 = (f32[128,384]{1,0:T(8,128)S(1)}, f32[128,384]{1,0:T(8,128)S(1)}, u32[]{:S(2)}, u32[]{:S(2)}) collective-permute-start(f32[128,384]{1,0:T(8,128)S(1)} %select_bitcast_fusion.9), channel_id=1, source_target_pairs={{0,2},{1,3},{2,0},{3,1},{4,6},{5,7},{6,4},{7,5},{8,10},{9,11},{10,... | collective-permute-start | bytes 589832 | tf_op jit(solution)/shard_map/ppermute | solution.py:57
  258.8 6.5 %collective-permute-start.27 = (f32[64,384]{1,0:T(8,128)S(1)}, f32[64,384]{1,0:T(8,128)S(1)}, u32[]{:S(2)}, u32[]{:S(2)}) collective-permute-start(f32[64,384]{1,0:T(8,128)S(1)} %select_bitcast_fusion.11), channel_id=1, source_target_pairs={{0,32},{8,40},{16,48},{24,56},{32,0},{40,8},{48,16},{56,24},{64,96... | collective-permute-start | bytes 294920 | tf_op jit(solution)/shard_map/ppermute | solution.py:57
  260.1 6.2 %collective-permute-start.23 = (f32[64,384]{1,0:T(8,128)S(1)}, f32[64,384]{1,0:T(8,128)S(1)}, u32[]{:S(2)}, u32[]{:S(2)}) collective-permute-start(f32[64,384]{1,0:T(8,128)S(1)} %select_bitcast_fusion.12), channel_id=1, source_target_pairs={{0,32},{8,40},{16,48},{24,56},{32,0},{40,8},{48,16},{56,24},{64,96... | collective-permute-start | bytes 294920 | tf_op jit(solution)/shard_map/ppermute | solution.py:57
  (5 other events, 13.3 us)

commit v3 on v1

--- a/solution.py
+++ b/solution.py
@@ -1,7 +1,7 @@
 import jax
 import jax.numpy as jnp
 from jax import lax
-from jax.sharding import PartitionSpec as P
+from jax.sharding import Mesh, PartitionSpec as P
 
 ITERS = 4
 
@@ -9,8 +9,12 @@
 regularizer_epsilon = 0.05
 highest = lax.Precision.HIGHEST
 
-GATHER_BITS = {"tgt": ((1, 2, 0), (1, 0, 2)), "src": ((2, 1, 3, 0), (2, 3, 1, 0))}
-SCATTER_BITS = {"tgt": ((0, 2, 1), (2, 0, 1)), "src": ((0, 3, 1, 2), (0, 1, 3, 2))}
+PHYSICAL = ("y_lo", "z", "core", "y_hi", "x")
+ROWS = ("y_lo", "core", "y_hi")
+COLS = ("z", "x")
+
+GATHER_BITS = {ROWS: ((0, 2, 1), (2, 0, 1)), COLS: ((1, 3, 2, 0), (3, 1, 0, 2))}
+SCATTER_BITS = {ROWS: ((1, 2, 0), (1, 0, 2)), COLS: ((0, 2, 1, 3), (2, 0, 3, 1))}
 
 
 def partner(axis, n, bit):
@@ -76,11 +80,11 @@
 
 
 def row_total(part):
-    return tree_sum(part, "tgt")
+    return tree_sum(part, ROWS)
 
 
 def col_total(part):
-    return tree_sum(part, "src")
+    return tree_sum(part, COLS)
 
 
 def times_vector(kernel, vector):
@@ -92,8 +96,16 @@
 
 
 def per_device(src_emb, right_sentence_vectors, src_mass, tgt_mass):
-    src_rows = split_gather(src_emb, "tgt")
-    target_rows = split_gather(right_sentence_vectors, "src")
+    src_rows = split_gather(src_emb, ROWS)
+    target_rows = split_gather(right_sentence_vectors, COLS)
+    src_count = src_emb.shape[0]
+    tgt_count = right_sentence_vectors.shape[0]
+    own_src = lax.dynamic_slice_in_dim(src_mass, lax.axis_index(("y_hi", "x")) * src_count, src_count)
+    own_tgt = lax.dynamic_slice_in_dim(
+        tgt_mass, lax.axis_index(("y_lo", "z", "core")) * tgt_count, tgt_count
+    )
+    src_mass = tree_gather(own_src, ROWS, GATHER_BITS[ROWS][0])
+    tgt_mass = tree_gather(own_tgt, COLS, GATHER_BITS[COLS][0])
 
     kernel_grid = (
         lax.dot_general(
@@ -156,17 +168,25 @@
         )
         / regularizer_epsilon
     )
-    grad_src = split_scatter(left_share_piece, "tgt")
-    grad_tgt = split_scatter(right_share_piece, "src")
+    grad_src = split_scatter(left_share_piece, ROWS)
+    grad_tgt = split_scatter(right_share_piece, COLS)
     return (grad_src, grad_tgt)
 
 
 def solution(mesh):
-    placed = (P(("src", "tgt"), None), P(("tgt", "src"), None), P("src"), P("tgt"))
+    physical = Mesh(mesh.devices.reshape(2, 4, 2, 2, 4), PHYSICAL)
+    src_axes = ("y_lo", "z", "core")
+    tgt_axes = ("y_hi", "x")
+    placed = (
+        P(src_axes + tgt_axes, None),
+        P(tgt_axes + src_axes, None),
+        P(src_axes),
+        P(tgt_axes),
+    )
     return jax.shard_map(
         per_device,
-        mesh=mesh,
+        mesh=physical,
         in_specs=placed,
-        out_specs=(P(("src", "tgt"), None), P(("tgt", "src"), None)),
+        out_specs=(P(src_axes + tgt_axes, None), P(tgt_axes + src_axes, None)),
         check_vma=False,
     )

time: 268 us -> 285 us (1.063)
  blocking collectives: 149 us -> 108 us
  waiting for transfers between devices: 50 us -> 79.7 us
  starting transfers between devices: 32.3 us -> 53.6 us
  local copies, waits for them, and re-layouts: 3.09 us -> 9.9 us
    all_to_all x15 -> x12, blocking collectives: 149 us -> 108 us  [tree_sum(): return lax.all_to_all(spread, axis, 0, 0, tiled=False).sum(0)]
    all_to_all x0 -> x3, waiting for transfers between devices: none -> 20.6 us  [tree_sum(): return lax.all_to_all(spread, axis, 0, 0, tiled=False).sum(0)]
    ppermute x14 -> x21, waiting for transfers between devices: 14.2 us -> 31.9 us  [tree_gather(): other = lax.ppermute(x, axis, partner(axis, n, bit))]
    all_to_all x0 -> x3, starting transfers between devices: none -> 12.2 us  [tree_sum(): return lax.all_to_all(spread, axis, 0, 0, tiled=False).sum(0)]
    ppermute x14, waiting for transfers between devices: 35.8 us -> 27.2 us  [tree_scatter(): x = keep + lax.ppermute(send, axis, partner(axis, n, bit))]
    ppermute x14 -> x21, starting transfers between devices: 18.5 us -> 25 us  [tree_gather(): other = lax.ppermute(x, axis, partner(axis, n, bit))]
    another operation x2 -> x6, local copies, waits for them, and re-layouts: 1.84 us -> 4.87 us  [tree_gather(): x = jnp.where(up, jnp.stack([other, x]), jnp.stack([x, other]))]
  transfers between devices with their start and end apart: 28 -> 38, of which waited for: 12 -> 17; matrix products, arithmetic and copies ran while one was open for 3% -> 6% of each run, Pallas kernels for 0% -> 0%
where the time goes in v3:
time: 285 us; the launch traced here: 284 us
  blocking collectives  108 us (38%)
  waiting for transfers between devices  79.7 us (28%)
  starting transfers between devices  53.6 us (19%)
  other arithmetic  23.5 us (8%)
  local copies, waits for them, and re-layouts  9.9 us (3%)
  matrix products  7.5 us (3%)
    all_to_all x12, blocking collectives, tree_sum(): return lax.all_to_all(spread, axis, 0, 0, tiled=False).sum(0)  108 us
    ppermute x21, waiting for transfers between devices, tree_gather(): other = lax.ppermute(x, axis, partner(axis, n, bit))  31.9 us
    ppermute x14, waiting for transfers between devices, tree_scatter(): x = keep + lax.ppermute(send, axis, partner(axis, n, bit))  27.2 us
    ppermute x21, starting transfers between devices, tree_gather(): other = lax.ppermute(x, axis, partner(axis, n, bit))  25 us
    all_to_all x3, waiting for transfers between devices, tree_sum(): return lax.all_to_all(spread, axis, 0, 0, tiled=False).sum(0)  20.6 us
    ppermute x14, starting transfers between devices, tree_scatter(): x = keep + lax.ppermute(send, axis, partner(axis, n, bit))  16.4 us
    all_to_all x3, starting transfers between devices, tree_sum(): return lax.all_to_all(spread, axis, 0, 0, tiled=False).sum(0)  12.2 us
    reduce_sum x8, other arithmetic, times_vector(): return jnp.sum(kernel.astype(jnp.float32) * vector[None, :], axis=1)  6.73 us
  transfers between devices with their start and end apart: 38, of which 17 were waited for; matrix products, arithmetic and copies ran while one was open for 6% of the time, Pallas kernels for 0%

profile of v3, /device:TPU:0, one launch (start us, length us, event | category | flops | bytes accessed | tf_op | source)
XLA Modules:
  0.0 283.7 jit_solution(5054772068206684936)
XLA Ops:
  9.3 4.0 %collective-permute-start.10 = (bf16[64,384]{1,0:T(8,128)(2,1)S(1)}, bf16[64,384]{1,0:T(8,128)(2,1)S(1)}, u32[]{:S(2)}, u32[]{:S(2)}) collective-permute-start(bf16[64,384]{1,0:T(8,128)(2,1)S(1)} %get-tuple-element.32), channel_id=1, source_target_pairs={{0,32},{1,33},{2,34},{3,35},{16,48},{17,49},{18,50},{19,51},{32,0}... | collective-permute-start | bytes 147464 | tf_op jit(solution)/shard_map/ppermute | solution.py:38
  20.7 4.9 %collective-permute-done.18 = f32[2,64]{1,0:T(2,128)S(1)} collective-permute-done((f32[2,64]{1,0:T(2,128)S(1)}, f32[2,64]{1,0:T(2,128)S(1)}, u32[]{:S(2)}, u32[]{:S(2)}) %collective-permute-start.18) | collective-permute-done | bytes 544 | tf_op jit(solution)/shard_map/ppermute | solution.py:38
  25.7 3.5 %collective-permute-done.15 = f32[2,128]{1,0:T(2,128)S(1)} collective-permute-done((f32[2,128]{1,0:T(2,128)S(1)}, f32[2,128]{1,0:T(2,128)S(1)}, u32[]{:S(2)}, u32[]{:S(2)}) %collective-permute-start.15) | collective-permute-done | bytes 1056 | tf_op jit(solution)/shard_map/ppermute | solution.py:38
  37.9 3.2 %collective-permute-done.11 = bf16[2,64,384]{2,1,0:T(8,128)(2,1)S(1)} collective-permute-done((bf16[2,64,384]{2,1,0:T(8,128)(2,1)S(1)}, bf16[2,64,384]{2,1,0:T(8,128)(2,1)S(1)}, u32[]{:S(2)}, u32[]{:S(2)}) %collective-permute-start.11) | collective-permute-done | bytes 98336 | tf_op jit(solution)/shard_map/ppermute | solution.py:38
  43.7 6.6 %collective-permute-done.4 = bf16[2,128,384]{2,1,0:T(8,128)(2,1)S(1)} collective-permute-done((bf16[2,128,384]{2,1,0:T(8,128)(2,1)S(1)}, bf16[2,128,384]{2,1,0:T(8,128)(2,1)S(1)}, u32[]{:S(2)}, u32[]{:S(2)}) %collective-permute-start.4) | collective-permute-done | bytes 196640 | tf_op jit(solution)/shard_map/ppermute | solution.py:38
  52.6 3.4 %collective-permute-done.8 = bf16[2,2,64,384]{3,2,1,0:T(8,128)(2,1)S(1)} collective-permute-done((bf16[2,2,64,384]{3,2,1,0:T(8,128)(2,1)S(1)}, bf16[2,2,64,384]{3,2,1,0:T(8,128)(2,1)S(1)}, u32[]{:S(2)}, u32[]{:S(2)}) %collective-permute-start.8) | collective-permute-done | bytes 196640 | tf_op jit(solution)/shard_map/ppermute | solution.py:38
  58.2 6.6 %collective-permute-done.13 = bf16[2,2,2,64,384]{4,3,1,2,0:T(8,128)(2,1)S(1)} collective-permute-done((bf16[2,2,2,64,384]{4,3,1,2,0:T(8,128)(2,1)S(1)}, bf16[2,2,2,64,384]{4,3,1,2,0:T(8,128)(2,1)S(1)}, u32[]{:S(2)}, u32[]{:S(2)}) %collective-permute-start.13) | collective-permute-done | bytes 393248 | tf_op jit(solution)/shard_map/ppermute | solution.py:38
  66.1 3.8 %exponential_convert_fusion = (bf16[1024,1024]{1,0:T(8,128)(2,1)S(1)}, f32[1024,1024]{1,0:T(8,128)}) fusion(bf16[1024,384]{1,0:T(8,128)(2,1)S(1)} %bitcast.212, bf16[1024,384]{1,0:T(8,128)(2,1)S(1)} %bitcast.214, bf16[1024,384]{1,0:T(8,128)(2,1)S(1)} %bitcast.208, bf16[1024,384]{1,0:T(8,128)(2,1)S(1)} %bitcast.210), kind=kOutput, calls=%fused_computation.34 | convolution fusion | flops 1619001344 | bytes 9437184 | tf_op jit(solution)/shard_map/dot_general | solution.py:111
  70.8 3.3 %all-to-all-start = ((f32[8,1,1024]{2,1,0:T(1,128)}), f32[8,1,1024]{2,1,0:T(1,128)S(1)}, u32[]{:S(2)}, u32[]{:S(2)}) async-start(f32[8,1,1024]{2,1,0:T(1,128)} %broadcast_in_dim.30), calls=%async_computation | async-start | bytes 65536 | tf_op jit(solution)/shard_map/all_to_all | solution.py:31
  74.2 5.2 %all-to-all-done = f32[8,1,1024]{2,1,0:T(1,128)S(1)} async-done(((f32[8,1,1024]{2,1,0:T(1,128)}), f32[8,1,1024]{2,1,0:T(1,128)S(1)}, u32[]{:S(2)}, u32[]{:S(2)}) %all-to-all-start) | async-done | bytes 32800 | tf_op jit(solution)/shard_map/all_to_all | solution.py:31
  80.6 5.3 %all-to-all-start.1 = ((f32[16,1,1024]{2,1,0:T(1,128)}), f32[16,1,1024]{2,1,0:T(1,128)S(1)}, u32[]{:S(2)}, u32[]{:S(2)}) async-start(f32[16,1,1024]{2,1,0:T(1,128)} %broadcast_in_dim.31), calls=%async_computation.1 | async-start | bytes 131072 | tf_op jit(solution)/shard_map/all_to_all | solution.py:31
  86.0 7.5 %all-to-all-done.1 = f32[16,1,1024]{2,1,0:T(1,128)S(1)} async-done(((f32[16,1,1024]{2,1,0:T(1,128)}), f32[16,1,1024]{2,1,0:T(1,128)S(1)}, u32[]{:S(2)}, u32[]{:S(2)}) %all-to-all-start.1) | async-done | bytes 65568 | tf_op jit(solution)/shard_map/all_to_all | solution.py:31
  94.2 7.7 %all_to_all.89 = f32[8,1,1024]{2,1,0:T(1,128)S(1)} all-to-all(f32[8,1,1024]{2,1,0:T(1,128)S(1)} %broadcast_in_dim.32), channel_id=1, replica_groups=mesh['y_lo'=2,'z'=4,'core'=2,'y_hi'=2,'x'=4] {'y_lo','core','y_hi'}, dimensions={0} | all-to-all | bytes 65536 | tf_op jit(solution)/shard_map/all_to_all | solution.py:31
  102.4 10.8 %all_to_all.90 = f32[16,1,1024]{2,1,0:T(1,128)S(1)} all-to-all(f32[16,1,1024]{2,1,0:T(1,128)S(1)} %broadcast_in_dim.33), channel_id=1, replica_groups=mesh['y_lo'=2,'z'=4,'core'=2,'y_hi'=2,'x'=4] {'z','x'}, dimensions={0} | all-to-all | bytes 131072 | tf_op jit(solution)/shard_map/all_to_all | solution.py:31
  113.8 7.7 %all_to_all.91 = f32[8,1,1024]{2,1,0:T(1,128)S(1)} all-to-all(f32[8,1,1024]{2,1,0:T(1,128)S(1)} %broadcast_in_dim.34), channel_id=1, replica_groups=mesh['y_lo'=2,'z'=4,'core'=2,'y_hi'=2,'x'=4] {'y_lo','core','y_hi'}, dimensions={0} | all-to-all | bytes 65536 | tf_op jit(solution)/shard_map/all_to_all | solution.py:31
  122.1 10.8 %all_to_all.92 = f32[16,1,1024]{2,1,0:T(1,128)S(1)} all-to-all(f32[16,1,1024]{2,1,0:T(1,128)S(1)} %broadcast_in_dim.35), channel_id=1, replica_groups=mesh['y_lo'=2,'z'=4,'core'=2,'y_hi'=2,'x'=4] {'z','x'}, dimensions={0} | all-to-all | bytes 131072 | tf_op jit(solution)/shard_map/all_to_all | solution.py:31
  133.5 7.7 %all_to_all.93 = f32[8,1,1024]{2,1,0:T(1,128)S(1)} all-to-all(f32[8,1,1024]{2,1,0:T(1,128)S(1)} %broadcast_in_dim.36), channel_id=1, replica_groups=mesh['y_lo'=2,'z'=4,'core'=2,'y_hi'=2,'x'=4] {'y_lo','core','y_hi'}, dimensions={0} | all-to-all | bytes 65536 | tf_op jit(solution)/shard_map/all_to_all | solution.py:31
  145.1 3.5 %all-to-all-start.7 = ((f32[16,2,1024]{2,1,0:T(2,128)}), f32[16,2,1024]{2,1,0:T(2,128)S(1)}, u32[]{:S(2)}, u32[]{:S(2)}) async-start(f32[16,2,1024]{2,1,0:T(2,128)} %broadcast_in_dim.37), calls=%async_computation.7 | async-start | bytes 262144 | tf_op jit(solution)/shard_map/all_to_all | solution.py:31
  148.7 7.9 %all-to-all-done.7 = f32[16,2,1024]{2,1,0:T(2,128)S(1)} async-done(((f32[16,2,1024]{2,1,0:T(2,128)}), f32[16,2,1024]{2,1,0:T(2,128)S(1)}, u32[]{:S(2)}, u32[]{:S(2)}) %all-to-all-start.7) | async-done | bytes 131104 | tf_op jit(solution)/shard_map/all_to_all | solution.py:31
  156.7 3.5 %multiply_reduce_fusion = (f32[1024]{0:T(1024)S(1)}, f32[1024]{0:T(1024)S(1)}) fusion(f32[1024,1024]{1,0:T(8,128)} %get-tuple-element.35, bf16[1024,1024]{1,0:T(8,128)(2,1)S(1)} %get-tuple-element.34, f32[1024]{0:T(1024)S(1)} %bitcast.240, f32[1024]{0:T(1024)S(1)} %bitcast.238), kind=kLoop, calls=%fused_computation.32 | loop fusion | flops 7337984 | bytes 6307840 | tf_op jit(solution)/shard_map/reduce_sum | solution.py:91
  160.2 7.7 %all_to_all.94 = f32[8,1,1024]{2,1,0:T(1,128)S(1)} all-to-all(f32[8,1,1024]{2,1,0:T(1,128)S(1)} %broadcast_in_dim.38), channel_id=1, replica_groups=mesh['y_lo'=2,'z'=4,'core'=2,'y_hi'=2,'x'=4] {'y_lo','core','y_hi'}, dimensions={0} | all-to-all | bytes 65536 | tf_op jit(solution)/shard_map/all_to_all | solution.py:31
  168.5 10.7 %all_to_all.95 = f32[16,1,1024]{2,1,0:T(1,128)S(1)} all-to-all(f32[16,1,1024]{2,1,0:T(1,128)S(1)} %broadcast_in_dim.39), channel_id=1, replica_groups=mesh['y_lo'=2,'z'=4,'core'=2,'y_hi'=2,'x'=4] {'z','x'}, dimensions={0} | all-to-all | bytes 131072 | tf_op jit(solution)/shard_map/all_to_all | solution.py:31
  179.8 7.7 %all_to_all.96 = f32[8,1,1024]{2,1,0:T(1,128)S(1)} all-to-all(f32[8,1,1024]{2,1,0:T(1,128)S(1)} %broadcast_in_dim.40), channel_id=1, replica_groups=mesh['y_lo'=2,'z'=4,'core'=2,'y_hi'=2,'x'=4] {'y_lo','core','y_hi'}, dimensions={0} | all-to-all | bytes 65536 | tf_op jit(solution)/shard_map/all_to_all | solution.py:31
  188.1 10.8 %all_to_all.97 = f32[16,1,1024]{2,1,0:T(1,128)S(1)} all-to-all(f32[16,1,1024]{2,1,0:T(1,128)S(1)} %broadcast_in_dim.41), channel_id=1, replica_groups=mesh['y_lo'=2,'z'=4,'core'=2,'y_hi'=2,'x'=4] {'z','x'}, dimensions={0} | all-to-all | bytes 131072 | tf_op jit(solution)/shard_map/all_to_all | solution.py:31
  199.5 7.7 %all_to_all.98 = f32[8,1,1024]{2,1,0:T(1,128)S(1)} all-to-all(f32[8,1,1024]{2,1,0:T(1,128)S(1)} %broadcast_in_dim.42), channel_id=1, replica_groups=mesh['y_lo'=2,'z'=4,'core'=2,'y_hi'=2,'x'=4] {'y_lo','core','y_hi'}, dimensions={0} | all-to-all | bytes 65536 | tf_op jit(solution)/shard_map/all_to_all | solution.py:31
  207.7 10.8 %all_to_all.99 = f32[16,1,1024]{2,1,0:T(1,128)S(1)} all-to-all(f32[16,1,1024]{2,1,0:T(1,128)S(1)} %broadcast_in_dim.43), channel_id=1, replica_groups=mesh['y_lo'=2,'z'=4,'core'=2,'y_hi'=2,'x'=4] {'z','x'}, dimensions={0} | all-to-all | bytes 131072 | tf_op jit(solution)/shard_map/all_to_all | solution.py:31
  219.1 7.7 %all_to_all.100 = f32[8,1,1024]{2,1,0:T(1,128)S(1)} all-to-all(f32[8,1,1024]{2,1,0:T(1,128)S(1)} %broadcast_in_dim.44), channel_id=1, replica_groups=mesh['y_lo'=2,'z'=4,'core'=2,'y_hi'=2,'x'=4] {'y_lo','core','y_hi'}, dimensions={0} | all-to-all | bytes 65536 | tf_op jit(solution)/shard_map/all_to_all | solution.py:31
  226.9 5.4 %fusion.14 = bf16[1024,1024]{1,0:T(8,128)(2,1)S(1)} fusion(bf16[1024,1024]{1,0:T(8,128)(2,1)S(1)} %get-tuple-element.34, f32[1024,1024]{1,0:T(8,128)} %get-tuple-element.35, f32[1024]{0:T(1024)S(1)} %multiply_divide_fusion, f32[1024]{0:T(1024)S(1)} %multiply_divide_fusion.1, f32[1024]{0:T(1024)S(1)} %multiply_divide_fusion.2, ...), kind=kLoop, calls=%fused_computation.31 | loop fusion | flops 23068672 | bytes 8454144 | tf_op jit(solution)/shard_map/convert_element_type | solution.py:160
  241.9 15.5 %collective-permute-done.31 = f32[2,2,2,64,384]{4,3,1,0,2:T(8,128)S(1)} collective-permute-done((f32[2,2,2,64,384]{4,3,1,0,2:T(8,128)S(1)}, f32[2,2,2,64,384]{4,3,1,0,2:T(8,128)S(1)}, u32[]{:S(2)}, u32[]{:S(2)}) %collective-permute-start.31) | collective-permute-done | bytes 786464 | tf_op jit(solution)/shard_map/ppermute | solution.py:61
  262.6 5.3 %collective-permute-done.32 = f32[2,2,64,384]{3,2,1,0:T(8,128)S(1)} collective-permute-done((f32[2,2,64,384]{3,2,1,0:T(8,128)S(1)}, f32[2,2,64,384]{3,2,1,0:T(8,128)S(1)}, u32[]{:S(2)}, u32[]{:S(2)}) %collective-permute-start.32) | collective-permute-done | bytes 393248 | tf_op jit(solution)/shard_map/ppermute | solution.py:61
  270.9 4.4 %collective-permute-done.33 = f32[2,64,384]{2,1,0:T(8,128)S(1)} collective-permute-done((f32[2,64,384]{2,1,0:T(8,128)S(1)}, f32[2,64,384]{2,1,0:T(8,128)S(1)}, u32[]{:S(2)}, u32[]{:S(2)}) %collective-permute-start.33) | collective-permute-done | bytes 196640 | tf_op jit(solution)/shard_map/ppermute | solution.py:61
  276.8 3.4 %collective-permute-start.30 = (f32[64,384]{1,0:T(8,128)S(1)}, f32[64,384]{1,0:T(8,128)S(1)}, u32[]{:S(2)}, u32[]{:S(2)}) collective-permute-start(f32[64,384]{1,0:T(8,128)S(1)} %select_bitcast_fusion.11), channel_id=1, source_target_pairs={{0,32},{1,33},{2,34},{3,35},{16,48},{17,49},{18,50},{19,51},{32,0}... | collective-permute-start | bytes 294920 | tf_op jit(solution)/shard_map/ppermute | solution.py:61
  (230 shorter events, 67.8 us)
Async XLA Ops:
  1.4 17.2 %collective-permute-start.17 = (f32[64]{0:T(128)S(1)}, f32[64]{0:T(128)S(1)}, u32[]{:S(2)}, u32[]{:S(2)}) collective-permute-start(f32[64]{0:T(128)S(1)} %dynamic_slice.7), channel_id=1, source_target_pairs={{0,2},{1,3},{2,0},{3,1},{16,18},{17,19},{18,16},{19,17},{32,34},{3... | collective-permute-start | bytes 776 | tf_op jit(solution)/shard_map/ppermute | solution.py:38
  5.3 15.2 %collective-permute-start.14 = (f32[128]{0:T(128)S(1)}, f32[128]{0:T(128)S(1)}, u32[]{:S(2)}, u32[]{:S(2)}) collective-permute-start(f32[128]{0:T(128)S(1)} %dynamic_slice.6), channel_id=1, source_target_pairs={{0,4},{4,0},{8,12},{12,8},{64,68},{68,64},{72,76},{76,72},{1,5},{5... | collective-permute-start | bytes 1544 | tf_op jit(solution)/shard_map/ppermute | solution.py:38
  9.3 25.1 %collective-permute-start.10 = (bf16[64,384]{1,0:T(8,128)(2,1)S(1)}, bf16[64,384]{1,0:T(8,128)(2,1)S(1)}, u32[]{:S(2)}, u32[]{:S(2)}) collective-permute-start(bf16[64,384]{1,0:T(8,128)(2,1)S(1)} %get-tuple-element.32), channel_id=1, source_target_pairs={{0,32},{1,33},{2,34},{3,35},{16,48},{17,49},{18,50},{19,51},{32,0}... | collective-permute-start | bytes 147464 | tf_op jit(solution)/shard_map/ppermute | solution.py:38
  13.3 19.5 %collective-permute-start.6 = (bf16[64,384]{1,0:T(8,128)(2,1)S(1)}, bf16[64,384]{1,0:T(8,128)(2,1)S(1)}, u32[]{:S(2)}, u32[]{:S(2)}) collective-permute-start(bf16[64,384]{1,0:T(8,128)(2,1)S(1)} %get-tuple-element.33), channel_id=1, source_target_pairs={{0,2},{1,3},{2,0},{3,1},{16,18},{17,19},{18,16},{19,17},{32,34},{3... | collective-permute-start | bytes 147464 | tf_op jit(solution)/shard_map/ppermute | solution.py:38
  14.8 22.9 %collective-permute-start.3 = (bf16[128,384]{1,0:T(8,128)(2,1)S(1)}, bf16[128,384]{1,0:T(8,128)(2,1)S(1)}, u32[]{:S(2)}, u32[]{:S(2)}) collective-permute-start(bf16[128,384]{1,0:T(8,128)(2,1)S(1)} %get-tuple-element.24), channel_id=1, source_target_pairs={{0,64},{4,68},{8,72},{12,76},{64,0},{68,4},{72,8},{76,12},{1,65},{... | collective-permute-start | bytes 294920 | tf_op jit(solution)/shard_map/ppermute | solution.py:38
  18.6 16.2 %collective-permute-start = (bf16[128,384]{1,0:T(8,128)(2,1)S(1)}, bf16[128,384]{1,0:T(8,128)(2,1)S(1)}, u32[]{:S(2)}, u32[]{:S(2)}) collective-permute-start(bf16[128,384]{1,0:T(8,128)(2,1)S(1)} %get-tuple-element.25), channel_id=1, source_target_pairs={{0,4},{4,0},{8,12},{12,8},{64,68},{68,64},{72,76},{76,72},{1,5},{5... | collective-permute-start | bytes 294920 | tf_op jit(solution)/shard_map/ppermute | solution.py:38
  32.8 41.4 %collective-permute-start.16 = (f32[2,2,128]{2,1,0:T(2,128)S(1)}, f32[2,2,128]{2,1,0:T(2,128)S(1)}, u32[]{:S(2)}, u32[]{:S(2)}) collective-permute-start(f32[2,2,128]{2,1,0:T(2,128)S(1)} %maximum_select_fusion.26), channel_id=1, source_target_pairs={{0,8},{4,12},{8,0},{12,4},{64,72},{68,76},{72,64},{76,68},{1,9},{5... | collective-permute-start | bytes 6152 | tf_op jit(solution)/shard_map/ppermute | solution.py:38
  32.8 53.1 %collective-permute-start.20 = (f32[2,2,2,64]{3,2,1,0:T(2,128)S(1)}, f32[2,2,2,64]{3,2,1,0:T(2,128)S(1)}, u32[]{:S(2)}, u32[]{:S(2)}) collective-permute-start(f32[2,2,2,64]{3,2,1,0:T(2,128)S(1)} %maximum_select_fusion.24), channel_id=1, source_target_pairs={{0,1},{1,0},{2,3},{3,2},{16,17},{17,16},{18,19},{19,18},{32,33},{3... | collective-permute-start | bytes 6152 | tf_op jit(solution)/shard_map/ppermute | solution.py:38
  34.5 8.4 %collective-permute-start.7 = (bf16[2,64,384]{2,1,0:T(8,128)(2,1)S(1)}, bf16[2,64,384]{2,1,0:T(8,128)(2,1)S(1)}, u32[]{:S(2)}, u32[]{:S(2)}) collective-permute-start(bf16[2,64,384]{2,1,0:T(8,128)(2,1)S(1)} %maximum_select_fusion.19), channel_id=1, source_target_pairs={{0,32},{1,33},{2,34},{3,35},{16,48},{17,49},{18,50},{19,51},{32,0}... | collective-permute-start | bytes 294920 | tf_op jit(solution)/shard_map/ppermute | solution.py:38
  34.8 6.4 %collective-permute-start.11 = (bf16[2,64,384]{2,1,0:T(8,128)(2,1)S(1)}, bf16[2,64,384]{2,1,0:T(8,128)(2,1)S(1)}, u32[]{:S(2)}, u32[]{:S(2)}) collective-permute-start(bf16[2,64,384]{2,1,0:T(8,128)(2,1)S(1)} %maximum_select_fusion.21), channel_id=1, source_target_pairs={{0,2},{1,3},{2,0},{3,1},{16,18},{17,19},{18,16},{19,17},{32,34},{3... | collective-permute-start | bytes 294920 | tf_op jit(solution)/shard_map/ppermute | solution.py:38
  37.8 13.9 %collective-permute-start.1 = (bf16[2,128,384]{2,1,0:T(8,128)(2,1)S(1)}, bf16[2,128,384]{2,1,0:T(8,128)(2,1)S(1)}, u32[]{:S(2)}, u32[]{:S(2)}) collective-permute-start(bf16[2,128,384]{2,1,0:T(8,128)(2,1)S(1)} %maximum_select_fusion.12), channel_id=1, source_target_pairs={{0,64},{4,68},{8,72},{12,76},{64,0},{68,4},{72,8},{76,12},{1,65},{... | collective-permute-start | bytes 589832 | tf_op jit(solution)/shard_map/ppermute | solution.py:38
  41.2 9.2 %collective-permute-start.4 = (bf16[2,128,384]{2,1,0:T(8,128)(2,1)S(1)}, bf16[2,128,384]{2,1,0:T(8,128)(2,1)S(1)}, u32[]{:S(2)}, u32[]{:S(2)}) collective-permute-start(bf16[2,128,384]{2,1,0:T(8,128)(2,1)S(1)} %maximum_select_fusion.14), channel_id=1, source_target_pairs={{0,4},{4,0},{8,12},{12,8},{64,68},{68,64},{72,76},{76,72},{1,5},{5... | collective-permute-start | bytes 589832 | tf_op jit(solution)/shard_map/ppermute | solution.py:38
  42.9 9.1 %collective-permute-start.12 = (bf16[2,2,64,384]{3,2,0,1:T(8,128)(2,1)S(1)}, bf16[2,2,64,384]{3,2,0,1:T(8,128)(2,1)S(1)}, u32[]{:S(2)}, u32[]{:S(2)}) collective-permute-start(bf16[2,2,64,384]{3,2,0,1:T(8,128)(2,1)S(1)} %maximum_select_fusion.18), channel_id=1, source_target_pairs={{0,1},{1,0},{2,3},{3,2},{16,17},{17,16},{18,19},{19,18},{32,33},{3... | collective-permute-start | bytes 589832 | tf_op jit(solution)/shard_map/ppermute | solution.py:38
  51.7 5.8 %collective-permute-start.5 = (bf16[2,2,128,384]{3,2,1,0:T(8,128)(2,1)S(1)}, bf16[2,2,128,384]{3,2,1,0:T(8,128)(2,1)S(1)}, u32[]{:S(2)}, u32[]{:S(2)}) collective-permute-start(bf16[2,2,128,384]{3,2,1,0:T(8,128)(2,1)S(1)} %maximum_select_fusion.6), channel_id=1, source_target_pairs={{0,8},{4,12},{8,0},{12,4},{64,72},{68,76},{72,64},{76,68},{1,9},{5... | collective-permute-start | bytes 1179656 | tf_op jit(solution)/shard_map/ppermute | solution.py:38
  52.0 6.0 %collective-permute-start.2 = (bf16[2,2,128,384]{3,2,1,0:T(8,128)(2,1)S(1)}, bf16[2,2,128,384]{3,2,1,0:T(8,128)(2,1)S(1)}, u32[]{:S(2)}, u32[]{:S(2)}) collective-permute-start(bf16[2,2,128,384]{3,2,1,0:T(8,128)(2,1)S(1)} %maximum_select_fusion.4), channel_id=1, source_target_pairs={{0,8},{4,12},{8,0},{12,4},{64,72},{68,76},{72,64},{76,68},{1,9},{5... | collective-permute-start | bytes 1179656 | tf_op jit(solution)/shard_map/ppermute | solution.py:38
  56.1 8.7 %collective-permute-start.13 = (bf16[2,2,2,64,384]{4,3,1,2,0:T(8,128)(2,1)S(1)}, bf16[2,2,2,64,384]{4,3,1,2,0:T(8,128)(2,1)S(1)}, u32[]{:S(2)}, u32[]{:S(2)}) collective-permute-start(bf16[2,2,2,64,384]{4,3,1,2,0:T(8,128)(2,1)S(1)} %maximum_select_fusion.10), channel_id=1, source_target_pairs={{0,16},{1,17},{2,18},{3,19},{16,0},{17,1},{18,2},{19,3},{32,48},{3... | collective-permute-start | bytes 1179656 | tf_op jit(solution)/shard_map/ppermute | solution.py:38
  57.5 8.4 %collective-permute-start.9 = (bf16[2,2,2,64,384]{4,3,2,1,0:T(8,128)(2,1)S(1)}, bf16[2,2,2,64,384]{4,3,2,1,0:T(8,128)(2,1)S(1)}, u32[]{:S(2)}, u32[]{:S(2)}) collective-permute-start(bf16[2,2,2,64,384]{4,3,2,1,0:T(8,128)(2,1)S(1)} %maximum_select_fusion.8), channel_id=1, source_target_pairs={{0,1},{1,0},{2,3},{3,2},{16,17},{17,16},{18,19},{19,18},{32,33},{3... | collective-permute-start | bytes 1179656 | tf_op jit(solution)/shard_map/ppermute | solution.py:38
  70.8 8.6 %all-to-all-start = ((f32[8,1,1024]{2,1,0:T(1,128)}), f32[8,1,1024]{2,1,0:T(1,128)S(1)}, u32[]{:S(2)}, u32[]{:S(2)}) async-start(f32[8,1,1024]{2,1,0:T(1,128)} %broadcast_in_dim.30), calls=%async_computation | async-start | bytes 65536 | tf_op jit(solution)/shard_map/all_to_all | solution.py:31
  80.6 13.0 %all-to-all-start.1 = ((f32[16,1,1024]{2,1,0:T(1,128)}), f32[16,1,1024]{2,1,0:T(1,128)S(1)}, u32[]{:S(2)}, u32[]{:S(2)}) async-start(f32[16,1,1024]{2,1,0:T(1,128)} %broadcast_in_dim.31), calls=%async_computation.1 | async-start | bytes 131072 | tf_op jit(solution)/shard_map/all_to_all | solution.py:31
  145.1 11.5 %all-to-all-start.7 = ((f32[16,2,1024]{2,1,0:T(2,128)}), f32[16,2,1024]{2,1,0:T(2,128)S(1)}, u32[]{:S(2)}, u32[]{:S(2)}) async-start(f32[16,2,1024]{2,1,0:T(2,128)} %broadcast_in_dim.37), calls=%async_computation.7 | async-start | bytes 262144 | tf_op jit(solution)/shard_map/all_to_all | solution.py:31
  237.7 19.6 %collective-permute-start.31 = (f32[2,2,2,64,384]{4,3,1,0,2:T(8,128)S(1)}, f32[2,2,2,64,384]{4,3,1,0,2:T(8,128)S(1)}, u32[]{:S(2)}, u32[]{:S(2)}) collective-permute-start(f32[2,2,2,64,384]{4,3,1,0,2:T(8,128)S(1)} %select_bitcast_fusion), channel_id=1, source_target_pairs={{0,16},{1,17},{2,18},{3,19},{16,0},{17,1},{18,2},{19,3},{32,48},{3... | collective-permute-start | bytes 2359304 | tf_op jit(solution)/shard_map/ppermute | solution.py:61
  238.5 19.7 %collective-permute-start.27 = (f32[2,2,2,64,384]{4,3,0,2,1:T(8,128)S(1)}, f32[2,2,2,64,384]{4,3,0,2,1:T(8,128)S(1)}, u32[]{:S(2)}, u32[]{:S(2)}) collective-permute-start(f32[2,2,2,64,384]{4,3,0,2,1:T(8,128)S(1)} %select_bitcast_fusion.1), channel_id=1, source_target_pairs={{0,1},{1,0},{2,3},{3,2},{16,17},{17,16},{18,19},{19,18},{32,33},{3... | collective-permute-start | bytes 2359304 | tf_op jit(solution)/shard_map/ppermute | solution.py:61
  239.4 20.3 %collective-permute-start.25 = (f32[2,128,384]{2,1,0:T(8,128)S(1)}, f32[2,128,384]{2,1,0:T(8,128)S(1)}, u32[]{:S(2)}, u32[]{:S(2)}) collective-permute-start(f32[2,128,384]{2,1,0:T(8,128)S(1)} %select_bitcast_fusion.6), channel_id=1, source_target_pairs={{0,4},{4,0},{8,12},{12,8},{64,68},{68,64},{72,76},{76,72},{1,5},{5... | collective-permute-start | bytes 1179656 | tf_op jit(solution)/shard_map/ppermute | solution.py:61
  241.0 19.4 %collective-permute-start.22 = (f32[2,128,384]{2,1,0:T(8,128)S(1)}, f32[2,128,384]{2,1,0:T(8,128)S(1)}, u32[]{:S(2)}, u32[]{:S(2)}) collective-permute-start(f32[2,128,384]{2,1,0:T(8,128)S(1)} %fusion.17), channel_id=1, source_target_pairs={{0,64},{4,68},{8,72},{12,76},{64,0},{68,4},{72,8},{76,12},{1,65},{... | collective-permute-start | bytes 1179656 | tf_op jit(solution)/shard_map/ppermute | solution.py:61
  257.6 10.4 %collective-permute-start.32 = (f32[2,2,64,384]{3,2,1,0:T(8,128)S(1)}, f32[2,2,64,384]{3,2,1,0:T(8,128)S(1)}, u32[]{:S(2)}, u32[]{:S(2)}) collective-permute-start(f32[2,2,64,384]{3,2,1,0:T(8,128)S(1)} %select_bitcast_fusion.4), channel_id=1, source_target_pairs={{0,1},{1,0},{2,3},{3,2},{16,17},{17,16},{18,19},{19,18},{32,33},{3... | collective-permute-start | bytes 1179656 | tf_op jit(solution)/shard_map/ppermute | solution.py:61
  258.4 10.9 %collective-permute-start.28 = (f32[2,2,64,384]{3,2,0,1:T(8,128)S(1)}, f32[2,2,64,384]{3,2,0,1:T(8,128)S(1)}, u32[]{:S(2)}, u32[]{:S(2)}) collective-permute-start(f32[2,2,64,384]{3,2,0,1:T(8,128)S(1)} %select_bitcast_fusion.5), channel_id=1, source_target_pairs={{0,16},{1,17},{2,18},{3,19},{16,0},{17,1},{18,2},{19,3},{32,48},{3... | collective-permute-start | bytes 1179656 | tf_op jit(solution)/shard_map/ppermute | solution.py:61
  259.8 20.4 %collective-permute-start.26 = (f32[128,384]{1,0:T(8,128)S(1)}, f32[128,384]{1,0:T(8,128)S(1)}, u32[]{:S(2)}, u32[]{:S(2)}) collective-permute-start(f32[128,384]{1,0:T(8,128)S(1)} %select_bitcast_fusion.8), channel_id=1, source_target_pairs={{0,64},{4,68},{8,72},{12,76},{64,0},{68,4},{72,8},{76,12},{1,65},{... | collective-permute-start | bytes 589832 | tf_op jit(solution)/shard_map/ppermute | solution.py:61
  260.5 19.7 %collective-permute-start.23 = (f32[128,384]{1,0:T(8,128)S(1)}, f32[128,384]{1,0:T(8,128)S(1)}, u32[]{:S(2)}, u32[]{:S(2)}) collective-permute-start(f32[128,384]{1,0:T(8,128)S(1)} %select_bitcast_fusion.9), channel_id=1, source_target_pairs={{0,4},{4,0},{8,12},{12,8},{64,68},{68,64},{72,76},{76,72},{1,5},{5... | collective-permute-start | bytes 589832 | tf_op jit(solution)/shard_map/ppermute | solution.py:61
  268.0 7.3 %collective-permute-start.33 = (f32[2,64,384]{2,1,0:T(8,128)S(1)}, f32[2,64,384]{2,1,0:T(8,128)S(1)}, u32[]{:S(2)}, u32[]{:S(2)}) collective-permute-start(f32[2,64,384]{2,1,0:T(8,128)S(1)} %fusion.18), channel_id=1, source_target_pairs={{0,32},{1,33},{2,34},{3,35},{16,48},{17,49},{18,50},{19,51},{32,0}... | collective-permute-start | bytes 589832 | tf_op jit(solution)/shard_map/ppermute | solution.py:61
  269.4 7.3 %collective-permute-start.29 = (f32[2,64,384]{2,1,0:T(8,128)S(1)}, f32[2,64,384]{2,1,0:T(8,128)S(1)}, u32[]{:S(2)}, u32[]{:S(2)}) collective-permute-start(f32[2,64,384]{2,1,0:T(8,128)S(1)} %select_bitcast_fusion.7), channel_id=1, source_target_pairs={{0,2},{1,3},{2,0},{3,1},{16,18},{17,19},{18,16},{19,17},{32,34},{3... | collective-permute-start | bytes 589832 | tf_op jit(solution)/shard_map/ppermute | solution.py:61
  275.4 6.2 %collective-permute-start.34 = (f32[64,384]{1,0:T(8,128)S(1)}, f32[64,384]{1,0:T(8,128)S(1)}, u32[]{:S(2)}, u32[]{:S(2)}) collective-permute-start(f32[64,384]{1,0:T(8,128)S(1)} %select_bitcast_fusion.10), channel_id=1, source_target_pairs={{0,2},{1,3},{2,0},{3,1},{16,18},{17,19},{18,16},{19,17},{32,34},{3... | collective-permute-start | bytes 294920 | tf_op jit(solution)/shard_map/ppermute | solution.py:61
  276.8 6.2 %collective-permute-start.30 = (f32[64,384]{1,0:T(8,128)S(1)}, f32[64,384]{1,0:T(8,128)S(1)}, u32[]{:S(2)}, u32[]{:S(2)}) collective-permute-start(f32[64,384]{1,0:T(8,128)S(1)} %select_bitcast_fusion.11), channel_id=1, source_target_pairs={{0,32},{1,33},{2,34},{3,35},{16,48},{17,49},{18,50},{19,51},{32,0}... | collective-permute-start | bytes 294920 | tf_op jit(solution)/shard_map/ppermute | solution.py:61
  (12 other events, 53.7 us)

commit v4 on v3

--- a/solution.py
+++ b/solution.py
@@ -79,6 +79,33 @@
     )
 
 
+def to_bf16_grid(x):
+    return lax.reduce_precision(x, exponent_bits=8, mantissa_bits=7)
+
+
+def split3(x):
+    high = to_bf16_grid(x)
+    rest = x - high
+    mid = to_bf16_grid(rest)
+    low = rest - mid
+    return [p.astype(jnp.bfloat16) for p in (high, mid, low)]
+
+
+EXTRA = 16
+
+
+def gather_with_mass(rows, mass, axis):
+    count, width = rows.shape
+    pieces = jnp.concatenate(split3(mass))
+    extra = jnp.zeros((EXTRA, width), rows.dtype)
+    extra = lax.dynamic_update_slice(extra, pieces[None, :], (0, 0))
+    both = split_gather(jnp.concatenate([rows, extra]), axis)
+    n = both.shape[0] // (count + EXTRA)
+    both = both.reshape(n, count + EXTRA, width)
+    got = both[:, count, : 3 * count].astype(jnp.float32).reshape(n, 3, count)
+    return both[:, :count].reshape(n * count, width), (got[:, 0] + got[:, 1] + got[:, 2]).reshape(n * count)
+
+
 def row_total(part):
     return tree_sum(part, ROWS)
 
@@ -96,16 +123,14 @@
 
 
 def per_device(src_emb, right_sentence_vectors, src_mass, tgt_mass):
-    src_rows = split_gather(src_emb, ROWS)
-    target_rows = split_gather(right_sentence_vectors, COLS)
     src_count = src_emb.shape[0]
     tgt_count = right_sentence_vectors.shape[0]
     own_src = lax.dynamic_slice_in_dim(src_mass, lax.axis_index(("y_hi", "x")) * src_count, src_count)
     own_tgt = lax.dynamic_slice_in_dim(
         tgt_mass, lax.axis_index(("y_lo", "z", "core")) * tgt_count, tgt_count
     )
-    src_mass = tree_gather(own_src, ROWS, GATHER_BITS[ROWS][0])
-    tgt_mass = tree_gather(own_tgt, COLS, GATHER_BITS[COLS][0])
+    src_rows, src_mass = gather_with_mass(src_emb, own_src, ROWS)
+    target_rows, tgt_mass = gather_with_mass(right_sentence_vectors, own_tgt, COLS)
 
     kernel_grid = (
         lax.dot_general(

time: 285 us -> 265 us (0.930)
  waiting for transfers between devices: 79.7 us -> 67.4 us
  starting transfers between devices: 53.6 us -> 46.9 us
  local copies, waits for them, and re-layouts: 9.9 us -> 4.24 us
  other arithmetic: 23.5 us -> 28.4 us
    ppermute x21 -> x14, waiting for transfers between devices: 31.9 us -> 20.9 us  [tree_gather(): other = lax.ppermute(x, axis, partner(axis, n, bit))]
    ppermute x21 -> x14, starting transfers between devices: 25 us -> 19.1 us  [tree_gather(): other = lax.ppermute(x, axis, partner(axis, n, bit))]
    another operation x6 -> x2, local copies, waits for them, and re-layouts: 4.87 us -> 0.09 us  [tree_gather(): x = jnp.where(up, jnp.stack([other, x]), jnp.stack([x, other]))]
  transfers between devices with their start and end apart: 38 -> 31, of which waited for: 17 -> 12; matrix products, arithmetic and copies ran while one was open for 6% -> 3% of each run, Pallas kernels for 0% -> 0%
where the time goes in v4:
time: 265 us; the launch traced here: 264 us
  blocking collectives  108 us (41%)
  waiting for transfers between devices  67.4 us (25%)
  starting transfers between devices  46.9 us (18%)
  other arithmetic  28.4 us (11%)
  matrix products  7.48 us (3%)
  local copies, waits for them, and re-layouts  4.24 us (2%)
    all_to_all x12, blocking collectives, tree_sum(): return lax.all_to_all(spread, axis, 0, 0, tiled=False).sum(0)  108 us
    ppermute x14, waiting for transfers between devices, tree_scatter(): x = keep + lax.ppermute(send, axis, partner(axis, n, bit))  27.2 us
    ppermute x14, waiting for transfers between devices, tree_gather(): other = lax.ppermute(x, axis, partner(axis, n, bit))  20.9 us
    all_to_all x3, waiting for transfers between devices, tree_sum(): return lax.all_to_all(spread, axis, 0, 0, tiled=False).sum(0)  19.3 us
    ppermute x14, starting transfers between devices, tree_gather(): other = lax.ppermute(x, axis, partner(axis, n, bit))  19.1 us
    ppermute x14, starting transfers between devices, tree_scatter(): x = keep + lax.ppermute(send, axis, partner(axis, n, bit))  16.4 us
    all_to_all x3, starting transfers between devices, tree_sum(): return lax.all_to_all(spread, axis, 0, 0, tiled=False).sum(0)  11.3 us
    reduce_sum x8, other arithmetic, times_vector(): return jnp.sum(kernel.astype(jnp.float32) * vector[None, :], axis=1)  6.72 us
  transfers between devices with their start and end apart: 31, of which 12 were waited for; matrix products, arithmetic and copies ran while one was open for 3% of the time, Pallas kernels for 0%

profile of v4, /device:TPU:0, one launch (start us, length us, event | category | flops | bytes accessed | tf_op | source)
XLA Modules:
  0.0 263.7 jit_solution(8535862227716593446)
XLA Ops:
  2.4 4.0 %collective-permute-start.10 = (bf16[80,384]{1,0:T(8,128)(2,1)S(1)}, bf16[80,384]{1,0:T(8,128)(2,1)S(1)}, u32[]{:S(2)}, u32[]{:S(2)}) collective-permute-start(bf16[80,384]{1,0:T(8,128)(2,1)S(1)} %get-tuple-element.34), channel_id=1, source_target_pairs={{0,32},{1,33},{2,34},{3,35},{16,48},{17,49},{18,50},{19,51},{32,0}... | collective-permute-start | bytes 184328 | tf_op jit(solution)/shard_map/ppermute | solution.py:38
  6.5 3.0 %collective-permute-start.6 = (bf16[80,384]{1,0:T(8,128)(2,1)S(1)}, bf16[80,384]{1,0:T(8,128)(2,1)S(1)}, u32[]{:S(2)}, u32[]{:S(2)}) collective-permute-start(bf16[80,384]{1,0:T(8,128)(2,1)S(1)} %get-tuple-element.35), channel_id=1, source_target_pairs={{0,2},{1,3},{2,0},{3,1},{16,18},{17,19},{18,16},{19,17},{32,34},{3... | collective-permute-start | bytes 184328 | tf_op jit(solution)/shard_map/ppermute | solution.py:38
  13.0 2.9 %collective-permute-start = (bf16[144,384]{1,0:T(8,128)(2,1)S(1)}, bf16[144,384]{1,0:T(8,128)(2,1)S(1)}, u32[]{:S(2)}, u32[]{:S(2)}) collective-permute-start(bf16[144,384]{1,0:T(8,128)(2,1)S(1)} %get-tuple-element.29), channel_id=1, source_target_pairs={{0,4},{4,0},{8,12},{12,8},{64,68},{68,64},{72,76},{76,72},{1,5},{5... | collective-permute-start | bytes 331784 | tf_op jit(solution)/shard_map/ppermute | solution.py:38
  16.8 3.6 %collective-permute-done = bf16[144,384]{1,0:T(8,128)(2,1)S(1)} collective-permute-done((bf16[144,384]{1,0:T(8,128)(2,1)S(1)}, bf16[144,384]{1,0:T(8,128)(2,1)S(1)}, u32[]{:S(2)}, u32[]{:S(2)}) %collective-permute-start) | collective-permute-done | bytes 110624 | tf_op jit(solution)/shard_map/ppermute | solution.py:38
  25.3 6.1 %collective-permute-done.4 = bf16[2,144,384]{2,1,0:T(8,128)(2,1)S(1)} collective-permute-done((bf16[2,144,384]{2,1,0:T(8,128)(2,1)S(1)}, bf16[2,144,384]{2,1,0:T(8,128)(2,1)S(1)}, u32[]{:S(2)}, u32[]{:S(2)}) %collective-permute-start.4) | collective-permute-done | bytes 221216 | tf_op jit(solution)/shard_map/ppermute | solution.py:38
  35.2 11.1 %collective-permute-done.13 = bf16[2,2,2,80,384]{4,3,2,1,0:T(8,128)(2,1)S(1)} collective-permute-done((bf16[2,2,2,80,384]{4,3,2,1,0:T(8,128)(2,1)S(1)}, bf16[2,2,2,80,384]{4,3,2,1,0:T(8,128)(2,1)S(1)}, u32[]{:S(2)}, u32[]{:S(2)}) %collective-permute-start.13) | collective-permute-done | bytes 491552 | tf_op jit(solution)/shard_map/ppermute | solution.py:38
  47.0 3.8 %exponential_convert_fusion = (bf16[1024,1024]{1,0:T(8,128)(2,1)S(1)}, f32[1024,1024]{1,0:T(8,128)}) fusion(bf16[1024,768]{1,0:T(8,128)(2,1)S(1)} %bitcast.174, bf16[1024,768]{1,0:T(8,128)(2,1)S(1)} %bitcast.172), kind=kOutput, calls=%fused_computation.34 | convolution fusion | flops 1612709888 | bytes 9437184 | tf_op jit(solution)/shard_map/dot_general | solution.py:136
  51.7 3.3 %all-to-all-start = ((f32[8,1,1024]{2,1,0:T(1,128)}), f32[8,1,1024]{2,1,0:T(1,128)S(1)}, u32[]{:S(2)}, u32[]{:S(2)}) async-start(f32[8,1,1024]{2,1,0:T(1,128)} %broadcast_in_dim.36), calls=%async_computation | async-start | bytes 65536 | tf_op jit(solution)/shard_map/all_to_all | solution.py:31
  55.2 5.1 %all-to-all-done = f32[8,1,1024]{2,1,0:T(1,128)S(1)} async-done(((f32[8,1,1024]{2,1,0:T(1,128)}), f32[8,1,1024]{2,1,0:T(1,128)S(1)}, u32[]{:S(2)}, u32[]{:S(2)}) %all-to-all-start) | async-done | bytes 32800 | tf_op jit(solution)/shard_map/all_to_all | solution.py:31
  61.5 4.5 %all-to-all-start.1 = ((f32[16,1,1024]{2,1,0:T(1,128)}), f32[16,1,1024]{2,1,0:T(1,128)S(1)}, u32[]{:S(2)}, u32[]{:S(2)}) async-start(f32[16,1,1024]{2,1,0:T(1,128)} %broadcast_in_dim.37), calls=%async_computation.1 | async-start | bytes 131072 | tf_op jit(solution)/shard_map/all_to_all | solution.py:31
  67.2 6.4 %all-to-all-done.1 = f32[16,1,1024]{2,1,0:T(1,128)S(1)} async-done(((f32[16,1,1024]{2,1,0:T(1,128)}), f32[16,1,1024]{2,1,0:T(1,128)S(1)}, u32[]{:S(2)}, u32[]{:S(2)}) %all-to-all-start.1) | async-done | bytes 65568 | tf_op jit(solution)/shard_map/all_to_all | solution.py:31
  74.2 7.7 %all_to_all.89 = f32[8,1,1024]{2,1,0:T(1,128)S(1)} all-to-all(f32[8,1,1024]{2,1,0:T(1,128)S(1)} %broadcast_in_dim.38), channel_id=1, replica_groups=mesh['y_lo'=2,'z'=4,'core'=2,'y_hi'=2,'x'=4] {'y_lo','core','y_hi'}, dimensions={0} | all-to-all | bytes 65536 | tf_op jit(solution)/shard_map/all_to_all | solution.py:31
  82.5 10.8 %all_to_all.90 = f32[16,1,1024]{2,1,0:T(1,128)S(1)} all-to-all(f32[16,1,1024]{2,1,0:T(1,128)S(1)} %broadcast_in_dim.39), channel_id=1, replica_groups=mesh['y_lo'=2,'z'=4,'core'=2,'y_hi'=2,'x'=4] {'z','x'}, dimensions={0} | all-to-all | bytes 131072 | tf_op jit(solution)/shard_map/all_to_all | solution.py:31
  93.8 7.7 %all_to_all.91 = f32[8,1,1024]{2,1,0:T(1,128)S(1)} all-to-all(f32[8,1,1024]{2,1,0:T(1,128)S(1)} %broadcast_in_dim.40), channel_id=1, replica_groups=mesh['y_lo'=2,'z'=4,'core'=2,'y_hi'=2,'x'=4] {'y_lo','core','y_hi'}, dimensions={0} | all-to-all | bytes 65536 | tf_op jit(solution)/shard_map/all_to_all | solution.py:31
  102.1 10.8 %all_to_all.92 = f32[16,1,1024]{2,1,0:T(1,128)S(1)} all-to-all(f32[16,1,1024]{2,1,0:T(1,128)S(1)} %broadcast_in_dim.41), channel_id=1, replica_groups=mesh['y_lo'=2,'z'=4,'core'=2,'y_hi'=2,'x'=4] {'z','x'}, dimensions={0} | all-to-all | bytes 131072 | tf_op jit(solution)/shard_map/all_to_all | solution.py:31
  113.5 7.7 %all_to_all.93 = f32[8,1,1024]{2,1,0:T(1,128)S(1)} all-to-all(f32[8,1,1024]{2,1,0:T(1,128)S(1)} %broadcast_in_dim.42), channel_id=1, replica_groups=mesh['y_lo'=2,'z'=4,'core'=2,'y_hi'=2,'x'=4] {'y_lo','core','y_hi'}, dimensions={0} | all-to-all | bytes 65536 | tf_op jit(solution)/shard_map/all_to_all | solution.py:31
  121.2 3.2 %fusion.6 = (f32[1024]{0:T(1024)S(1)}, f32[1024]{0:T(1024)S(1)}) fusion(bf16[1024,1024]{1,0:T(8,128)(2,1)S(1)} %get-tuple-element.42, f32[1024]{0:T(1024)S(1)} %div.148, f32[1024,1024]{1,0:T(8,128)} %get-tuple-element.43), kind=kLoop, calls=%fused_computation.23 | loop fusion | flops 7337984 | bytes 6303744 | tf_op jit(solution)/shard_map/reduce_sum | solution.py:122
  125.1 3.5 %all-to-all-start.7 = ((f32[16,2,1024]{2,1,0:T(2,128)}), f32[16,2,1024]{2,1,0:T(2,128)S(1)}, u32[]{:S(2)}, u32[]{:S(2)}) async-start(f32[16,2,1024]{2,1,0:T(2,128)} %broadcast_in_dim.43), calls=%async_computation.7 | async-start | bytes 262144 | tf_op jit(solution)/shard_map/all_to_all | solution.py:31
  128.7 7.9 %all-to-all-done.7 = f32[16,2,1024]{2,1,0:T(2,128)S(1)} async-done(((f32[16,2,1024]{2,1,0:T(2,128)}), f32[16,2,1024]{2,1,0:T(2,128)S(1)}, u32[]{:S(2)}, u32[]{:S(2)}) %all-to-all-start.7) | async-done | bytes 131104 | tf_op jit(solution)/shard_map/all_to_all | solution.py:31
  136.7 3.5 %multiply_reduce_fusion = (f32[1024]{0:T(1024)S(1)}, f32[1024]{0:T(1024)S(1)}) fusion(f32[1024,1024]{1,0:T(8,128)} %get-tuple-element.43, bf16[1024,1024]{1,0:T(8,128)(2,1)S(1)} %get-tuple-element.42, f32[1024]{0:T(1024)S(1)} %bitcast.207, f32[1024]{0:T(1024)S(1)} %bitcast.205), kind=kLoop, calls=%fused_computation.32 | loop fusion | flops 7337984 | bytes 6307840 | tf_op jit(solution)/shard_map/reduce_sum | solution.py:118
  140.2 7.7 %all_to_all.94 = f32[8,1,1024]{2,1,0:T(1,128)S(1)} all-to-all(f32[8,1,1024]{2,1,0:T(1,128)S(1)} %broadcast_in_dim.44), channel_id=1, replica_groups=mesh['y_lo'=2,'z'=4,'core'=2,'y_hi'=2,'x'=4] {'y_lo','core','y_hi'}, dimensions={0} | all-to-all | bytes 65536 | tf_op jit(solution)/shard_map/all_to_all | solution.py:31
  148.5 10.7 %all_to_all.95 = f32[16,1,1024]{2,1,0:T(1,128)S(1)} all-to-all(f32[16,1,1024]{2,1,0:T(1,128)S(1)} %broadcast_in_dim.45), channel_id=1, replica_groups=mesh['y_lo'=2,'z'=4,'core'=2,'y_hi'=2,'x'=4] {'z','x'}, dimensions={0} | all-to-all | bytes 131072 | tf_op jit(solution)/shard_map/all_to_all | solution.py:31
  159.8 7.7 %all_to_all.96 = f32[8,1,1024]{2,1,0:T(1,128)S(1)} all-to-all(f32[8,1,1024]{2,1,0:T(1,128)S(1)} %broadcast_in_dim.46), channel_id=1, replica_groups=mesh['y_lo'=2,'z'=4,'core'=2,'y_hi'=2,'x'=4] {'y_lo','core','y_hi'}, dimensions={0} | all-to-all | bytes 65536 | tf_op jit(solution)/shard_map/all_to_all | solution.py:31
  168.1 10.8 %all_to_all.97 = f32[16,1,1024]{2,1,0:T(1,128)S(1)} all-to-all(f32[16,1,1024]{2,1,0:T(1,128)S(1)} %broadcast_in_dim.47), channel_id=1, replica_groups=mesh['y_lo'=2,'z'=4,'core'=2,'y_hi'=2,'x'=4] {'z','x'}, dimensions={0} | all-to-all | bytes 131072 | tf_op jit(solution)/shard_map/all_to_all | solution.py:31
  179.5 7.7 %all_to_all.98 = f32[8,1,1024]{2,1,0:T(1,128)S(1)} all-to-all(f32[8,1,1024]{2,1,0:T(1,128)S(1)} %broadcast_in_dim.48), channel_id=1, replica_groups=mesh['y_lo'=2,'z'=4,'core'=2,'y_hi'=2,'x'=4] {'y_lo','core','y_hi'}, dimensions={0} | all-to-all | bytes 65536 | tf_op jit(solution)/shard_map/all_to_all | solution.py:31
  187.7 10.8 %all_to_all.99 = f32[16,1,1024]{2,1,0:T(1,128)S(1)} all-to-all(f32[16,1,1024]{2,1,0:T(1,128)S(1)} %broadcast_in_dim.49), channel_id=1, replica_groups=mesh['y_lo'=2,'z'=4,'core'=2,'y_hi'=2,'x'=4] {'z','x'}, dimensions={0} | all-to-all | bytes 131072 | tf_op jit(solution)/shard_map/all_to_all | solution.py:31
  199.1 7.7 %all_to_all.100 = f32[8,1,1024]{2,1,0:T(1,128)S(1)} all-to-all(f32[8,1,1024]{2,1,0:T(1,128)S(1)} %broadcast_in_dim.50), channel_id=1, replica_groups=mesh['y_lo'=2,'z'=4,'core'=2,'y_hi'=2,'x'=4] {'y_lo','core','y_hi'}, dimensions={0} | all-to-all | bytes 65536 | tf_op jit(solution)/shard_map/all_to_all | solution.py:31
  206.9 5.4 %fusion.14 = bf16[1024,1024]{1,0:T(8,128)(2,1)S(1)} fusion(bf16[1024,1024]{1,0:T(8,128)(2,1)S(1)} %get-tuple-element.42, f32[1024,1024]{1,0:T(8,128)} %get-tuple-element.43, f32[1024]{0:T(1024)S(1)} %multiply_divide_fusion, f32[1024]{0:T(1024)S(1)} %multiply_divide_fusion.1, f32[1024]{0:T(1024)S(1)} %multiply_divide_fusion.2, ...), kind=kLoop, calls=%fused_computation.31 | loop fusion | flops 23068672 | bytes 8454144 | tf_op jit(solution)/shard_map/convert_element_type | solution.py:185
  221.9 15.5 %collective-permute-done.24 = f32[2,2,2,64,384]{4,3,1,0,2:T(8,128)S(1)} collective-permute-done((f32[2,2,2,64,384]{4,3,1,0,2:T(8,128)S(1)}, f32[2,2,2,64,384]{4,3,1,0,2:T(8,128)S(1)}, u32[]{:S(2)}, u32[]{:S(2)}) %collective-permute-start.24) | collective-permute-done | bytes 786464 | tf_op jit(solution)/shard_map/ppermute | solution.py:61
  242.7 5.3 %collective-permute-done.25 = f32[2,2,64,384]{3,2,1,0:T(8,128)S(1)} collective-permute-done((f32[2,2,64,384]{3,2,1,0:T(8,128)S(1)}, f32[2,2,64,384]{3,2,1,0:T(8,128)S(1)}, u32[]{:S(2)}, u32[]{:S(2)}) %collective-permute-start.25) | collective-permute-done | bytes 393248 | tf_op jit(solution)/shard_map/ppermute | solution.py:61
  250.9 4.4 %collective-permute-done.26 = f32[2,64,384]{2,1,0:T(8,128)S(1)} collective-permute-done((f32[2,64,384]{2,1,0:T(8,128)S(1)}, f32[2,64,384]{2,1,0:T(8,128)S(1)}, u32[]{:S(2)}, u32[]{:S(2)}) %collective-permute-start.26) | collective-permute-done | bytes 196640 | tf_op jit(solution)/shard_map/ppermute | solution.py:61
  256.8 3.4 %collective-permute-start.23 = (f32[64,384]{1,0:T(8,128)S(1)}, f32[64,384]{1,0:T(8,128)S(1)}, u32[]{:S(2)}, u32[]{:S(2)}) collective-permute-start(f32[64,384]{1,0:T(8,128)S(1)} %select_bitcast_fusion.13), channel_id=1, source_target_pairs={{0,32},{1,33},{2,34},{3,35},{16,48},{17,49},{18,50},{19,51},{32,0}... | collective-permute-start | bytes 294920 | tf_op jit(solution)/shard_map/ppermute | solution.py:61
  (205 shorter events, 48.4 us)
Async XLA Ops:
  2.4 13.7 %collective-permute-start.10 = (bf16[80,384]{1,0:T(8,128)(2,1)S(1)}, bf16[80,384]{1,0:T(8,128)(2,1)S(1)}, u32[]{:S(2)}, u32[]{:S(2)}) collective-permute-start(bf16[80,384]{1,0:T(8,128)(2,1)S(1)} %get-tuple-element.34), channel_id=1, source_target_pairs={{0,32},{1,33},{2,34},{3,35},{16,48},{17,49},{18,50},{19,51},{32,0}... | collective-permute-start | bytes 184328 | tf_op jit(solution)/shard_map/ppermute | solution.py:38
  6.5 9.4 %collective-permute-start.6 = (bf16[80,384]{1,0:T(8,128)(2,1)S(1)}, bf16[80,384]{1,0:T(8,128)(2,1)S(1)}, u32[]{:S(2)}, u32[]{:S(2)}) collective-permute-start(bf16[80,384]{1,0:T(8,128)(2,1)S(1)} %get-tuple-element.35), channel_id=1, source_target_pairs={{0,2},{1,3},{2,0},{3,1},{16,18},{17,19},{18,16},{19,17},{32,34},{3... | collective-permute-start | bytes 184328 | tf_op jit(solution)/shard_map/ppermute | solution.py:38
  11.3 9.5 %collective-permute-start.3 = (bf16[144,384]{1,0:T(8,128)(2,1)S(1)}, bf16[144,384]{1,0:T(8,128)(2,1)S(1)}, u32[]{:S(2)}, u32[]{:S(2)}) collective-permute-start(bf16[144,384]{1,0:T(8,128)(2,1)S(1)} %get-tuple-element.28), channel_id=1, source_target_pairs={{0,64},{4,68},{8,72},{12,76},{64,0},{68,4},{72,8},{76,12},{1,65},{... | collective-permute-start | bytes 331784 | tf_op jit(solution)/shard_map/ppermute | solution.py:38
  13.0 7.5 %collective-permute-start = (bf16[144,384]{1,0:T(8,128)(2,1)S(1)}, bf16[144,384]{1,0:T(8,128)(2,1)S(1)}, u32[]{:S(2)}, u32[]{:S(2)}) collective-permute-start(bf16[144,384]{1,0:T(8,128)(2,1)S(1)} %get-tuple-element.29), channel_id=1, source_target_pairs={{0,4},{4,0},{8,12},{12,8},{64,68},{68,64},{72,76},{76,72},{1,5},{5... | collective-permute-start | bytes 331784 | tf_op jit(solution)/shard_map/ppermute | solution.py:38
  15.9 8.2 %collective-permute-start.7 = (bf16[2,80,384]{2,1,0:T(8,128)(2,1)S(1)}, bf16[2,80,384]{2,1,0:T(8,128)(2,1)S(1)}, u32[]{:S(2)}, u32[]{:S(2)}) collective-permute-start(bf16[2,80,384]{2,1,0:T(8,128)(2,1)S(1)} %maximum_select_fusion.20), channel_id=1, source_target_pairs={{0,32},{1,33},{2,34},{3,35},{16,48},{17,49},{18,50},{19,51},{32,0}... | collective-permute-start | bytes 368648 | tf_op jit(solution)/shard_map/ppermute | solution.py:38
  16.2 7.1 %collective-permute-start.11 = (bf16[2,80,384]{2,1,0:T(8,128)(2,1)S(1)}, bf16[2,80,384]{2,1,0:T(8,128)(2,1)S(1)}, u32[]{:S(2)}, u32[]{:S(2)}) collective-permute-start(bf16[2,80,384]{2,1,0:T(8,128)(2,1)S(1)} %maximum_select_fusion.22), channel_id=1, source_target_pairs={{0,2},{1,3},{2,0},{3,1},{16,18},{17,19},{18,16},{19,17},{32,34},{3... | collective-permute-start | bytes 368648 | tf_op jit(solution)/shard_map/ppermute | solution.py:38
  20.5 11.1 %collective-permute-start.1 = (bf16[2,144,384]{2,1,0:T(8,128)(2,1)S(1)}, bf16[2,144,384]{2,1,0:T(8,128)(2,1)S(1)}, u32[]{:S(2)}, u32[]{:S(2)}) collective-permute-start(bf16[2,144,384]{2,1,0:T(8,128)(2,1)S(1)} %maximum_select_fusion.16), channel_id=1, source_target_pairs={{0,64},{4,68},{8,72},{12,76},{64,0},{68,4},{72,8},{76,12},{1,65},{... | collective-permute-start | bytes 663560 | tf_op jit(solution)/shard_map/ppermute | solution.py:38
  20.8 10.6 %collective-permute-start.4 = (bf16[2,144,384]{2,1,0:T(8,128)(2,1)S(1)}, bf16[2,144,384]{2,1,0:T(8,128)(2,1)S(1)}, u32[]{:S(2)}, u32[]{:S(2)}) collective-permute-start(bf16[2,144,384]{2,1,0:T(8,128)(2,1)S(1)} %maximum_select_fusion.18), channel_id=1, source_target_pairs={{0,4},{4,0},{8,12},{12,8},{64,68},{68,64},{72,76},{76,72},{1,5},{5... | collective-permute-start | bytes 663560 | tf_op jit(solution)/shard_map/ppermute | solution.py:38
  23.3 9.9 %collective-permute-start.12 = (bf16[2,2,80,384]{3,2,1,0:T(8,128)(2,1)S(1)}, bf16[2,2,80,384]{3,2,1,0:T(8,128)(2,1)S(1)}, u32[]{:S(2)}, u32[]{:S(2)}) collective-permute-start(bf16[2,2,80,384]{3,2,1,0:T(8,128)(2,1)S(1)} %maximum_select_fusion.14), channel_id=1, source_target_pairs={{0,1},{1,0},{2,3},{3,2},{16,17},{17,16},{18,19},{19,18},{32,33},{3... | collective-permute-start | bytes 737288 | tf_op jit(solution)/shard_map/ppermute | solution.py:38
  24.1 8.3 %collective-permute-start.8 = (bf16[2,2,80,384]{3,2,1,0:T(8,128)(2,1)S(1)}, bf16[2,2,80,384]{3,2,1,0:T(8,128)(2,1)S(1)}, u32[]{:S(2)}, u32[]{:S(2)}) collective-permute-start(bf16[2,2,80,384]{3,2,1,0:T(8,128)(2,1)S(1)} %maximum_select_fusion.12), channel_id=1, source_target_pairs={{0,16},{1,17},{2,18},{3,19},{16,0},{17,1},{18,2},{19,3},{32,48},{3... | collective-permute-start | bytes 737288 | tf_op jit(solution)/shard_map/ppermute | solution.py:38
  31.5 3.1 %collective-permute-start.5 = (bf16[2,2,144,384]{3,2,1,0:T(8,128)(2,1)S(1)}, bf16[2,2,144,384]{3,2,1,0:T(8,128)(2,1)S(1)}, u32[]{:S(2)}, u32[]{:S(2)}) collective-permute-start(bf16[2,2,144,384]{3,2,1,0:T(8,128)(2,1)S(1)} %maximum_select_fusion.10), channel_id=1, source_target_pairs={{0,8},{4,12},{8,0},{12,4},{64,72},{68,76},{72,64},{76,68},{1,9},{5... | collective-permute-start | bytes 1327112 | tf_op jit(solution)/shard_map/ppermute | solution.py:38
  31.7 3.2 %collective-permute-start.2 = (bf16[2,2,144,384]{3,2,1,0:T(8,128)(2,1)S(1)}, bf16[2,2,144,384]{3,2,1,0:T(8,128)(2,1)S(1)}, u32[]{:S(2)}, u32[]{:S(2)}) collective-permute-start(bf16[2,2,144,384]{3,2,1,0:T(8,128)(2,1)S(1)} %maximum_select_fusion.8), channel_id=1, source_target_pairs={{0,8},{4,12},{8,0},{12,4},{64,72},{68,76},{72,64},{76,68},{1,9},{5... | collective-permute-start | bytes 1327112 | tf_op jit(solution)/shard_map/ppermute | solution.py:38
  32.6 14.0 %collective-permute-start.9 = (bf16[2,2,2,80,384]{4,3,2,1,0:T(8,128)(2,1)S(1)}, bf16[2,2,2,80,384]{4,3,2,1,0:T(8,128)(2,1)S(1)}, u32[]{:S(2)}, u32[]{:S(2)}) collective-permute-start(bf16[2,2,2,80,384]{4,3,2,1,0:T(8,128)(2,1)S(1)} %maximum_select_fusion.4), channel_id=1, source_target_pairs={{0,1},{1,0},{2,3},{3,2},{16,17},{17,16},{18,19},{19,18},{32,33},{3... | collective-permute-start | bytes 1474568 | tf_op jit(solution)/shard_map/ppermute | solution.py:38
  33.3 12.9 %collective-permute-start.13 = (bf16[2,2,2,80,384]{4,3,2,1,0:T(8,128)(2,1)S(1)}, bf16[2,2,2,80,384]{4,3,2,1,0:T(8,128)(2,1)S(1)}, u32[]{:S(2)}, u32[]{:S(2)}) collective-permute-start(bf16[2,2,2,80,384]{4,3,2,1,0:T(8,128)(2,1)S(1)} %maximum_select_fusion.6), channel_id=1, source_target_pairs={{0,16},{1,17},{2,18},{3,19},{16,0},{17,1},{18,2},{19,3},{32,48},{3... | collective-permute-start | bytes 1474568 | tf_op jit(solution)/shard_map/ppermute | solution.py:38
  35.2 11.8 %copy-start.2 = (bf16[8,128,768]{2,1,0:T(8,128)(2,1)}, bf16[8,128,768]{2,1,0:T(8,128)(2,1)S(1)}, u32[]{:S(2)}) copy-start(bf16[8,128,768]{2,1,0:T(8,128)(2,1)S(1)} %pad_maximum_fusion.1) | copy-start | bytes 4718596
  51.7 8.6 %all-to-all-start = ((f32[8,1,1024]{2,1,0:T(1,128)}), f32[8,1,1024]{2,1,0:T(1,128)S(1)}, u32[]{:S(2)}, u32[]{:S(2)}) async-start(f32[8,1,1024]{2,1,0:T(1,128)} %broadcast_in_dim.36), calls=%async_computation | async-start | bytes 65536 | tf_op jit(solution)/shard_map/all_to_all | solution.py:31
  61.5 12.1 %all-to-all-start.1 = ((f32[16,1,1024]{2,1,0:T(1,128)}), f32[16,1,1024]{2,1,0:T(1,128)S(1)}, u32[]{:S(2)}, u32[]{:S(2)}) async-start(f32[16,1,1024]{2,1,0:T(1,128)} %broadcast_in_dim.37), calls=%async_computation.1 | async-start | bytes 131072 | tf_op jit(solution)/shard_map/all_to_all | solution.py:31
  125.1 11.5 %all-to-all-start.7 = ((f32[16,2,1024]{2,1,0:T(2,128)}), f32[16,2,1024]{2,1,0:T(2,128)S(1)}, u32[]{:S(2)}, u32[]{:S(2)}) async-start(f32[16,2,1024]{2,1,0:T(2,128)} %broadcast_in_dim.43), calls=%async_computation.7 | async-start | bytes 262144 | tf_op jit(solution)/shard_map/all_to_all | solution.py:31
  216.9 2.4 collective-permute-start.17
  217.2 3.6 %collective-permute-start.14 = (f32[2,2,128,384]{3,2,0,1:T(8,128)S(1)}, f32[2,2,128,384]{3,2,0,1:T(8,128)S(1)}, u32[]{:S(2)}, u32[]{:S(2)}) collective-permute-start(f32[2,2,128,384]{3,2,0,1:T(8,128)S(1)} %select_bitcast_fusion.3), channel_id=1, source_target_pairs={{0,8},{4,12},{8,0},{12,4},{64,72},{68,76},{72,64},{76,68},{1,9},{5... | collective-permute-start | bytes 2359304 | tf_op jit(solution)/shard_map/ppermute | solution.py:61
  217.7 19.6 %collective-permute-start.24 = (f32[2,2,2,64,384]{4,3,1,0,2:T(8,128)S(1)}, f32[2,2,2,64,384]{4,3,1,0,2:T(8,128)S(1)}, u32[]{:S(2)}, u32[]{:S(2)}) collective-permute-start(f32[2,2,2,64,384]{4,3,1,0,2:T(8,128)S(1)} %select_bitcast_fusion), channel_id=1, source_target_pairs={{0,16},{1,17},{2,18},{3,19},{16,0},{17,1},{18,2},{19,3},{32,48},{3... | collective-permute-start | bytes 2359304 | tf_op jit(solution)/shard_map/ppermute | solution.py:61
  218.5 19.7 %collective-permute-start.20 = (f32[2,2,2,64,384]{4,3,0,2,1:T(8,128)S(1)}, f32[2,2,2,64,384]{4,3,0,2,1:T(8,128)S(1)}, u32[]{:S(2)}, u32[]{:S(2)}) collective-permute-start(f32[2,2,2,64,384]{4,3,0,2,1:T(8,128)S(1)} %select_bitcast_fusion.1), channel_id=1, source_target_pairs={{0,1},{1,0},{2,3},{3,2},{16,17},{17,16},{18,19},{19,18},{32,33},{3... | collective-permute-start | bytes 2359304 | tf_op jit(solution)/shard_map/ppermute | solution.py:61
  219.4 20.3 %collective-permute-start.18 = (f32[2,128,384]{2,1,0:T(8,128)S(1)}, f32[2,128,384]{2,1,0:T(8,128)S(1)}, u32[]{:S(2)}, u32[]{:S(2)}) collective-permute-start(f32[2,128,384]{2,1,0:T(8,128)S(1)} %select_bitcast_fusion.6), channel_id=1, source_target_pairs={{0,4},{4,0},{8,12},{12,8},{64,68},{68,64},{72,76},{76,72},{1,5},{5... | collective-permute-start | bytes 1179656 | tf_op jit(solution)/shard_map/ppermute | solution.py:61
  221.0 19.5 %collective-permute-start.15 = (f32[2,128,384]{2,1,0:T(8,128)S(1)}, f32[2,128,384]{2,1,0:T(8,128)S(1)}, u32[]{:S(2)}, u32[]{:S(2)}) collective-permute-start(f32[2,128,384]{2,1,0:T(8,128)S(1)} %select_bitcast_fusion.7), channel_id=1, source_target_pairs={{0,64},{4,68},{8,72},{12,76},{64,0},{68,4},{72,8},{76,12},{1,65},{... | collective-permute-start | bytes 1179656 | tf_op jit(solution)/shard_map/ppermute | solution.py:61
  237.6 10.4 %collective-permute-start.25 = (f32[2,2,64,384]{3,2,1,0:T(8,128)S(1)}, f32[2,2,64,384]{3,2,1,0:T(8,128)S(1)}, u32[]{:S(2)}, u32[]{:S(2)}) collective-permute-start(f32[2,2,64,384]{3,2,1,0:T(8,128)S(1)} %select_bitcast_fusion.4), channel_id=1, source_target_pairs={{0,1},{1,0},{2,3},{3,2},{16,17},{17,16},{18,19},{19,18},{32,33},{3... | collective-permute-start | bytes 1179656 | tf_op jit(solution)/shard_map/ppermute | solution.py:61
  238.4 10.9 %collective-permute-start.21 = (f32[2,2,64,384]{3,2,0,1:T(8,128)S(1)}, f32[2,2,64,384]{3,2,0,1:T(8,128)S(1)}, u32[]{:S(2)}, u32[]{:S(2)}) collective-permute-start(f32[2,2,64,384]{3,2,0,1:T(8,128)S(1)} %select_bitcast_fusion.5), channel_id=1, source_target_pairs={{0,16},{1,17},{2,18},{3,19},{16,0},{17,1},{18,2},{19,3},{32,48},{3... | collective-permute-start | bytes 1179656 | tf_op jit(solution)/shard_map/ppermute | solution.py:61
  239.8 20.4 %collective-permute-start.19 = (f32[128,384]{1,0:T(8,128)S(1)}, f32[128,384]{1,0:T(8,128)S(1)}, u32[]{:S(2)}, u32[]{:S(2)}) collective-permute-start(f32[128,384]{1,0:T(8,128)S(1)} %select_bitcast_fusion.10), channel_id=1, source_target_pairs={{0,64},{4,68},{8,72},{12,76},{64,0},{68,4},{72,8},{76,12},{1,65},{... | collective-permute-start | bytes 589832 | tf_op jit(solution)/shard_map/ppermute | solution.py:61
  240.5 19.7 %collective-permute-start.16 = (f32[128,384]{1,0:T(8,128)S(1)}, f32[128,384]{1,0:T(8,128)S(1)}, u32[]{:S(2)}, u32[]{:S(2)}) collective-permute-start(f32[128,384]{1,0:T(8,128)S(1)} %select_bitcast_fusion.11), channel_id=1, source_target_pairs={{0,4},{4,0},{8,12},{12,8},{64,68},{68,64},{72,76},{76,72},{1,5},{5... | collective-permute-start | bytes 589832 | tf_op jit(solution)/shard_map/ppermute | solution.py:61
  248.1 7.3 %collective-permute-start.26 = (f32[2,64,384]{2,1,0:T(8,128)S(1)}, f32[2,64,384]{2,1,0:T(8,128)S(1)}, u32[]{:S(2)}, u32[]{:S(2)}) collective-permute-start(f32[2,64,384]{2,1,0:T(8,128)S(1)} %select_bitcast_fusion.8), channel_id=1, source_target_pairs={{0,32},{1,33},{2,34},{3,35},{16,48},{17,49},{18,50},{19,51},{32,0}... | collective-permute-start | bytes 589832 | tf_op jit(solution)/shard_map/ppermute | solution.py:61
  249.4 7.4 %collective-permute-start.22 = (f32[2,64,384]{2,1,0:T(8,128)S(1)}, f32[2,64,384]{2,1,0:T(8,128)S(1)}, u32[]{:S(2)}, u32[]{:S(2)}) collective-permute-start(f32[2,64,384]{2,1,0:T(8,128)S(1)} %select_bitcast_fusion.9), channel_id=1, source_target_pairs={{0,2},{1,3},{2,0},{3,1},{16,18},{17,19},{18,16},{19,17},{32,34},{3... | collective-permute-start | bytes 589832 | tf_op jit(solution)/shard_map/ppermute | solution.py:61
  255.4 6.2 %collective-permute-start.27 = (f32[64,384]{1,0:T(8,128)S(1)}, f32[64,384]{1,0:T(8,128)S(1)}, u32[]{:S(2)}, u32[]{:S(2)}) collective-permute-start(f32[64,384]{1,0:T(8,128)S(1)} %select_bitcast_fusion.12), channel_id=1, source_target_pairs={{0,2},{1,3},{2,0},{3,1},{16,18},{17,19},{18,16},{19,17},{32,34},{3... | collective-permute-start | bytes 294920 | tf_op jit(solution)/shard_map/ppermute | solution.py:61
  256.8 6.2 %collective-permute-start.23 = (f32[64,384]{1,0:T(8,128)S(1)}, f32[64,384]{1,0:T(8,128)S(1)}, u32[]{:S(2)}, u32[]{:S(2)}) collective-permute-start(f32[64,384]{1,0:T(8,128)S(1)} %select_bitcast_fusion.13), channel_id=1, source_target_pairs={{0,32},{1,33},{2,34},{3,35},{16,48},{17,49},{18,50},{19,51},{32,0}... | collective-permute-start | bytes 294920 | tf_op jit(solution)/shard_map/ppermute | solution.py:61
  (3 other events, 11.2 us)

commit v5 on v4

--- a/solution.py
+++ b/solution.py
@@ -63,19 +63,23 @@
     return x
 
 
+def column_parts(width, axis):
+    if axis == COLS:
+        return ((0, 2 * width // 3), (2 * width // 3, width))
+    return ((0, width // 2), (width // 2, width))
+
+
 def split_gather(x, axis):
-    orders = GATHER_BITS[axis]
-    w = x.shape[1] // len(orders)
+    parts = column_parts(x.shape[1], axis)
     return jnp.concatenate(
-        [tree_gather(x[:, i * w:(i + 1) * w], axis, o) for i, o in enumerate(orders)], 1
+        [tree_gather(x[:, a:b], axis, o) for (a, b), o in zip(parts, GATHER_BITS[axis])], 1
     )
 
 
 def split_scatter(x, axis):
-    orders = SCATTER_BITS[axis]
-    w = x.shape[1] // len(orders)
+    parts = column_parts(x.shape[1], axis)
     return jnp.concatenate(
-        [tree_scatter(x[:, i * w:(i + 1) * w], axis, o) for i, o in enumerate(orders)], 1
+        [tree_scatter(x[:, a:b], axis, o) for (a, b), o in zip(parts, SCATTER_BITS[axis])], 1
     )
 
 

time: 265 us -> 292 us (1.10)
  waiting for transfers between devices: 67.4 us -> 97.3 us
    ppermute x14, waiting for transfers between devices: 27.2 us -> 55.2 us  [tree_scatter(): x = keep + lax.ppermute(send, axis, partner(axis, n, bit))]
    ppermute x14, starting transfers between devices: 16.4 us -> 13.1 us  [tree_scatter(): x = keep + lax.ppermute(send, axis, partner(axis, n, bit))]
  transfers between devices with their start and end apart: 31 -> 31, of which waited for: 12 -> 17; matrix products, arithmetic and copies ran while one was open for 3% -> 3% of each run, Pallas kernels for 0% -> 0%
where the time goes in v5:
time: 292 us; the launch traced here: 291 us
  blocking collectives  108 us (37%)
  waiting for transfers between devices  97.3 us (33%)
  starting transfers between devices  44.3 us (15%)
  other arithmetic  28.4 us (10%)
  matrix products  7.5 us (3%)
  local copies, waits for them, and re-layouts  4.34 us (1%)
    all_to_all x12, blocking collectives, tree_sum(): return lax.all_to_all(spread, axis, 0, 0, tiled=False).sum(0)  108 us
    ppermute x14, waiting for transfers between devices, tree_scatter(): x = keep + lax.ppermute(send, axis, partner(axis, n, bit))  55.2 us
    ppermute x14, waiting for transfers between devices, tree_gather(): other = lax.ppermute(x, axis, partner(axis, n, bit))  22.7 us
    ppermute x14, starting transfers between devices, tree_gather(): other = lax.ppermute(x, axis, partner(axis, n, bit))  20.5 us
    all_to_all x3, waiting for transfers between devices, tree_sum(): return lax.all_to_all(spread, axis, 0, 0, tiled=False).sum(0)  19.3 us
    ppermute x14, starting transfers between devices, tree_scatter(): x = keep + lax.ppermute(send, axis, partner(axis, n, bit))  13.1 us
    all_to_all x3, starting transfers between devices, tree_sum(): return lax.all_to_all(spread, axis, 0, 0, tiled=False).sum(0)  10.7 us
    reduce_sum x8, other arithmetic, times_vector(): return jnp.sum(kernel.astype(jnp.float32) * vector[None, :], axis=1)  6.72 us
  transfers between devices with their start and end apart: 31, of which 17 were waited for; matrix products, arithmetic and copies ran while one was open for 3% of the time, Pallas kernels for 0%

profile of v5, /device:TPU:0, one launch (start us, length us, event | category | flops | bytes accessed | tf_op | source)
XLA Modules:
  0.0 291.1 jit_solution(16224891092305544189)
XLA Ops:
  2.4 4.0 %collective-permute-start.10 = (bf16[80,256]{1,0:T(8,128)(2,1)S(1)}, bf16[80,256]{1,0:T(8,128)(2,1)S(1)}, u32[]{:S(2)}, u32[]{:S(2)}) collective-permute-start(bf16[80,256]{1,0:T(8,128)(2,1)S(1)} %get-tuple-element.33), channel_id=1, source_target_pairs={{0,32},{1,33},{2,34},{3,35},{16,48},{17,49},{18,50},{19,51},{32,0}... | collective-permute-start | bytes 122888 | tf_op jit(solution)/shard_map/ppermute | solution.py:38
  16.8 3.8 %collective-permute-done = bf16[144,384]{1,0:T(8,128)(2,1)S(1)} collective-permute-done((bf16[144,384]{1,0:T(8,128)(2,1)S(1)}, bf16[144,384]{1,0:T(8,128)(2,1)S(1)}, u32[]{:S(2)}, u32[]{:S(2)}) %collective-permute-start) | collective-permute-done | bytes 110624 | tf_op jit(solution)/shard_map/ppermute | solution.py:38
  25.3 3.4 %collective-permute-done.12 = bf16[2,2,80,256]{3,2,1,0:T(8,128)(2,1)S(1)} collective-permute-done((bf16[2,2,80,256]{3,2,1,0:T(8,128)(2,1)S(1)}, bf16[2,2,80,256]{3,2,1,0:T(8,128)(2,1)S(1)}, u32[]{:S(2)}, u32[]{:S(2)}) %collective-permute-start.12) | collective-permute-done | bytes 163872 | tf_op jit(solution)/shard_map/ppermute | solution.py:38
  39.2 10.1 %collective-permute-done.9 = bf16[2,2,2,80,512]{4,3,2,1,0:T(8,128)(2,1)S(1)} collective-permute-done((bf16[2,2,2,80,512]{4,3,2,1,0:T(8,128)(2,1)S(1)}, bf16[2,2,2,80,512]{4,3,2,1,0:T(8,128)(2,1)S(1)}, u32[]{:S(2)}, u32[]{:S(2)}) %collective-permute-start.9) | collective-permute-done | bytes 655392 | tf_op jit(solution)/shard_map/ppermute | solution.py:38
  49.7 3.8 %exponential_convert_fusion = (bf16[1024,1024]{1,0:T(8,128)(2,1)S(1)}, f32[1024,1024]{1,0:T(8,128)}) fusion(bf16[1024,768]{1,0:T(8,128)(2,1)S(1)} %bitcast.174, bf16[1024,768]{1,0:T(8,128)(2,1)S(1)} %bitcast.172), kind=kOutput, calls=%fused_computation.34 | convolution fusion | flops 1612709888 | bytes 9437184 | tf_op jit(solution)/shard_map/dot_general | solution.py:140
  57.9 5.1 %all-to-all-done = f32[8,1,1024]{2,1,0:T(1,128)S(1)} async-done(((f32[8,1,1024]{2,1,0:T(1,128)}), f32[8,1,1024]{2,1,0:T(1,128)S(1)}, u32[]{:S(2)}, u32[]{:S(2)}) %all-to-all-start) | async-done | bytes 32800 | tf_op jit(solution)/shard_map/all_to_all | solution.py:31
  64.2 3.8 %all-to-all-start.1 = ((f32[16,1,1024]{2,1,0:T(1,128)}), f32[16,1,1024]{2,1,0:T(1,128)S(1)}, u32[]{:S(2)}, u32[]{:S(2)}) async-start(f32[16,1,1024]{2,1,0:T(1,128)} %broadcast_in_dim.37), calls=%async_computation.1 | async-start | bytes 131072 | tf_op jit(solution)/shard_map/all_to_all | solution.py:31
  69.3 6.4 %all-to-all-done.1 = f32[16,1,1024]{2,1,0:T(1,128)S(1)} async-done(((f32[16,1,1024]{2,1,0:T(1,128)}), f32[16,1,1024]{2,1,0:T(1,128)S(1)}, u32[]{:S(2)}, u32[]{:S(2)}) %all-to-all-start.1) | async-done | bytes 65568 | tf_op jit(solution)/shard_map/all_to_all | solution.py:31
  76.3 7.7 %all_to_all.89 = f32[8,1,1024]{2,1,0:T(1,128)S(1)} all-to-all(f32[8,1,1024]{2,1,0:T(1,128)S(1)} %broadcast_in_dim.38), channel_id=1, replica_groups=mesh['y_lo'=2,'z'=4,'core'=2,'y_hi'=2,'x'=4] {'y_lo','core','y_hi'}, dimensions={0} | all-to-all | bytes 65536 | tf_op jit(solution)/shard_map/all_to_all | solution.py:31
  84.5 10.8 %all_to_all.90 = f32[16,1,1024]{2,1,0:T(1,128)S(1)} all-to-all(f32[16,1,1024]{2,1,0:T(1,128)S(1)} %broadcast_in_dim.39), channel_id=1, replica_groups=mesh['y_lo'=2,'z'=4,'core'=2,'y_hi'=2,'x'=4] {'z','x'}, dimensions={0} | all-to-all | bytes 131072 | tf_op jit(solution)/shard_map/all_to_all | solution.py:31
  95.9 7.7 %all_to_all.91 = f32[8,1,1024]{2,1,0:T(1,128)S(1)} all-to-all(f32[8,1,1024]{2,1,0:T(1,128)S(1)} %broadcast_in_dim.40), channel_id=1, replica_groups=mesh['y_lo'=2,'z'=4,'core'=2,'y_hi'=2,'x'=4] {'y_lo','core','y_hi'}, dimensions={0} | all-to-all | bytes 65536 | tf_op jit(solution)/shard_map/all_to_all | solution.py:31
  104.2 10.8 %all_to_all.92 = f32[16,1,1024]{2,1,0:T(1,128)S(1)} all-to-all(f32[16,1,1024]{2,1,0:T(1,128)S(1)} %broadcast_in_dim.41), channel_id=1, replica_groups=mesh['y_lo'=2,'z'=4,'core'=2,'y_hi'=2,'x'=4] {'z','x'}, dimensions={0} | all-to-all | bytes 131072 | tf_op jit(solution)/shard_map/all_to_all | solution.py:31
  115.6 7.7 %all_to_all.93 = f32[8,1,1024]{2,1,0:T(1,128)S(1)} all-to-all(f32[8,1,1024]{2,1,0:T(1,128)S(1)} %broadcast_in_dim.42), channel_id=1, replica_groups=mesh['y_lo'=2,'z'=4,'core'=2,'y_hi'=2,'x'=4] {'y_lo','core','y_hi'}, dimensions={0} | all-to-all | bytes 65536 | tf_op jit(solution)/shard_map/all_to_all | solution.py:31
  127.2 3.5 %all-to-all-start.7 = ((f32[16,2,1024]{2,1,0:T(2,128)}), f32[16,2,1024]{2,1,0:T(2,128)S(1)}, u32[]{:S(2)}, u32[]{:S(2)}) async-start(f32[16,2,1024]{2,1,0:T(2,128)} %broadcast_in_dim.43), calls=%async_computation.7 | async-start | bytes 262144 | tf_op jit(solution)/shard_map/all_to_all | solution.py:31
  130.8 7.9 %all-to-all-done.7 = f32[16,2,1024]{2,1,0:T(2,128)S(1)} async-done(((f32[16,2,1024]{2,1,0:T(2,128)}), f32[16,2,1024]{2,1,0:T(2,128)S(1)}, u32[]{:S(2)}, u32[]{:S(2)}) %all-to-all-start.7) | async-done | bytes 131104 | tf_op jit(solution)/shard_map/all_to_all | solution.py:31
  138.8 3.5 %multiply_reduce_fusion = (f32[1024]{0:T(1024)S(1)}, f32[1024]{0:T(1024)S(1)}) fusion(f32[1024,1024]{1,0:T(8,128)} %get-tuple-element.41, bf16[1024,1024]{1,0:T(8,128)(2,1)S(1)} %get-tuple-element.40, f32[1024]{0:T(1024)S(1)} %bitcast.207, f32[1024]{0:T(1024)S(1)} %bitcast.205), kind=kLoop, calls=%fused_computation.32 | loop fusion | flops 7337984 | bytes 6307840 | tf_op jit(solution)/shard_map/reduce_sum | solution.py:122
  142.3 7.7 %all_to_all.94 = f32[8,1,1024]{2,1,0:T(1,128)S(1)} all-to-all(f32[8,1,1024]{2,1,0:T(1,128)S(1)} %broadcast_in_dim.44), channel_id=1, replica_groups=mesh['y_lo'=2,'z'=4,'core'=2,'y_hi'=2,'x'=4] {'y_lo','core','y_hi'}, dimensions={0} | all-to-all | bytes 65536 | tf_op jit(solution)/shard_map/all_to_all | solution.py:31
  150.6 10.7 %all_to_all.95 = f32[16,1,1024]{2,1,0:T(1,128)S(1)} all-to-all(f32[16,1,1024]{2,1,0:T(1,128)S(1)} %broadcast_in_dim.45), channel_id=1, replica_groups=mesh['y_lo'=2,'z'=4,'core'=2,'y_hi'=2,'x'=4] {'z','x'}, dimensions={0} | all-to-all | bytes 131072 | tf_op jit(solution)/shard_map/all_to_all | solution.py:31
  161.9 7.7 %all_to_all.96 = f32[8,1,1024]{2,1,0:T(1,128)S(1)} all-to-all(f32[8,1,1024]{2,1,0:T(1,128)S(1)} %broadcast_in_dim.46), channel_id=1, replica_groups=mesh['y_lo'=2,'z'=4,'core'=2,'y_hi'=2,'x'=4] {'y_lo','core','y_hi'}, dimensions={0} | all-to-all | bytes 65536 | tf_op jit(solution)/shard_map/all_to_all | solution.py:31
  170.2 10.8 %all_to_all.97 = f32[16,1,1024]{2,1,0:T(1,128)S(1)} all-to-all(f32[16,1,1024]{2,1,0:T(1,128)S(1)} %broadcast_in_dim.47), channel_id=1, replica_groups=mesh['y_lo'=2,'z'=4,'core'=2,'y_hi'=2,'x'=4] {'z','x'}, dimensions={0} | all-to-all | bytes 131072 | tf_op jit(solution)/shard_map/all_to_all | solution.py:31
  181.6 7.7 %all_to_all.98 = f32[8,1,1024]{2,1,0:T(1,128)S(1)} all-to-all(f32[8,1,1024]{2,1,0:T(1,128)S(1)} %broadcast_in_dim.48), channel_id=1, replica_groups=mesh['y_lo'=2,'z'=4,'core'=2,'y_hi'=2,'x'=4] {'y_lo','core','y_hi'}, dimensions={0} | all-to-all | bytes 65536 | tf_op jit(solution)/shard_map/all_to_all | solution.py:31
  189.8 10.8 %all_to_all.99 = f32[16,1,1024]{2,1,0:T(1,128)S(1)} all-to-all(f32[16,1,1024]{2,1,0:T(1,128)S(1)} %broadcast_in_dim.49), channel_id=1, replica_groups=mesh['y_lo'=2,'z'=4,'core'=2,'y_hi'=2,'x'=4] {'z','x'}, dimensions={0} | all-to-all | bytes 131072 | tf_op jit(solution)/shard_map/all_to_all | solution.py:31
  201.2 7.7 %all_to_all.100 = f32[8,1,1024]{2,1,0:T(1,128)S(1)} all-to-all(f32[8,1,1024]{2,1,0:T(1,128)S(1)} %broadcast_in_dim.50), channel_id=1, replica_groups=mesh['y_lo'=2,'z'=4,'core'=2,'y_hi'=2,'x'=4] {'y_lo','core','y_hi'}, dimensions={0} | all-to-all | bytes 65536 | tf_op jit(solution)/shard_map/all_to_all | solution.py:31
  209.0 5.4 %fusion.14 = bf16[1024,1024]{1,0:T(8,128)(2,1)S(1)} fusion(bf16[1024,1024]{1,0:T(8,128)(2,1)S(1)} %get-tuple-element.40, f32[1024,1024]{1,0:T(8,128)} %get-tuple-element.41, f32[1024]{0:T(1024)S(1)} %multiply_divide_fusion, f32[1024]{0:T(1024)S(1)} %multiply_divide_fusion.1, f32[1024]{0:T(1024)S(1)} %multiply_divide_fusion.2, ...), kind=kLoop, calls=%fused_computation.31 | loop fusion | flops 23068672 | bytes 8454144 | tf_op jit(solution)/shard_map/convert_element_type | solution.py:189
  221.6 12.3 %collective-permute-done.24 = f32[2,2,2,64,256]{4,3,1,0,2:T(8,128)S(1)} collective-permute-done((f32[2,2,2,64,256]{4,3,1,0,2:T(8,128)S(1)}, f32[2,2,2,64,256]{4,3,1,0,2:T(8,128)S(1)}, u32[]{:S(2)}, u32[]{:S(2)}) %collective-permute-start.24) | collective-permute-done | bytes 524320 | tf_op jit(solution)/shard_map/ppermute | solution.py:61
  235.9 15.9 %collective-permute-done.25 = f32[2,2,64,256]{3,2,1,0:T(8,128)S(1)} collective-permute-done((f32[2,2,64,256]{3,2,1,0:T(8,128)S(1)}, f32[2,2,64,256]{3,2,1,0:T(8,128)S(1)}, u32[]{:S(2)}, u32[]{:S(2)}) %collective-permute-start.25) | collective-permute-done | bytes 262176 | tf_op jit(solution)/shard_map/ppermute | solution.py:61
  253.9 4.5 %collective-permute-done.26 = f32[2,64,256]{2,1,0:T(8,128)S(1)} collective-permute-done((f32[2,64,256]{2,1,0:T(8,128)S(1)}, f32[2,64,256]{2,1,0:T(8,128)S(1)}, u32[]{:S(2)}, u32[]{:S(2)}) %collective-permute-start.26) | collective-permute-done | bytes 131104 | tf_op jit(solution)/shard_map/ppermute | solution.py:61
  260.5 3.8 %collective-permute-done.27 = f32[64,256]{1,0:T(8,128)S(1)} collective-permute-done((f32[64,256]{1,0:T(8,128)S(1)}, f32[64,256]{1,0:T(8,128)S(1)}, u32[]{:S(2)}, u32[]{:S(2)}) %collective-permute-start.27) | collective-permute-done | bytes 65568 | tf_op jit(solution)/shard_map/ppermute | solution.py:61
  266.9 4.0 %collective-permute-done.15 = f32[2,128,384]{2,1,0:T(8,128)S(1)} collective-permute-done((f32[2,128,384]{2,1,0:T(8,128)S(1)}, f32[2,128,384]{2,1,0:T(8,128)S(1)}, u32[]{:S(2)}, u32[]{:S(2)}) %collective-permute-start.15) | collective-permute-done | bytes 393248 | tf_op jit(solution)/shard_map/ppermute | solution.py:61
  270.9 4.7 %collective-permute-done.21 = f32[2,2,64,512]{3,2,0,1:T(8,128)S(1)} collective-permute-done((f32[2,2,64,512]{3,2,0,1:T(8,128)S(1)}, f32[2,2,64,512]{3,2,0,1:T(8,128)S(1)}, u32[]{:S(2)}, u32[]{:S(2)}) %collective-permute-start.21) | collective-permute-done | bytes 524320 | tf_op jit(solution)/shard_map/ppermute | solution.py:61
  277.8 6.0 %collective-permute-done.22 = f32[2,64,512]{2,1,0:T(8,128)S(1)} collective-permute-done((f32[2,64,512]{2,1,0:T(8,128)S(1)}, f32[2,64,512]{2,1,0:T(8,128)S(1)}, u32[]{:S(2)}, u32[]{:S(2)}) %collective-permute-start.22) | collective-permute-done | bytes 262176 | tf_op jit(solution)/shard_map/ppermute | solution.py:61
  286.3 4.1 %collective-permute-done.23 = f32[64,512]{1,0:T(8,128)S(1)} collective-permute-done((f32[64,512]{1,0:T(8,128)S(1)}, f32[64,512]{1,0:T(8,128)S(1)}, u32[]{:S(2)}, u32[]{:S(2)}) %collective-permute-start.23) | collective-permute-done | bytes 131104 | tf_op jit(solution)/shard_map/ppermute | solution.py:61
  (211 shorter events, 65.8 us)
Async XLA Ops:
  2.4 13.5 %collective-permute-start.10 = (bf16[80,256]{1,0:T(8,128)(2,1)S(1)}, bf16[80,256]{1,0:T(8,128)(2,1)S(1)}, u32[]{:S(2)}, u32[]{:S(2)}) collective-permute-start(bf16[80,256]{1,0:T(8,128)(2,1)S(1)} %get-tuple-element.33), channel_id=1, source_target_pairs={{0,32},{1,33},{2,34},{3,35},{16,48},{17,49},{18,50},{19,51},{32,0}... | collective-permute-start | bytes 122888 | tf_op jit(solution)/shard_map/ppermute | solution.py:38
  6.5 10.1 %collective-permute-start.6 = (bf16[80,512]{1,0:T(8,128)(2,1)S(1)}, bf16[80,512]{1,0:T(8,128)(2,1)S(1)}, u32[]{:S(2)}, u32[]{:S(2)}) collective-permute-start(bf16[80,512]{1,0:T(8,128)(2,1)S(1)} %get-tuple-element.30), channel_id=1, source_target_pairs={{0,2},{1,3},{2,0},{3,1},{16,18},{17,19},{18,16},{19,17},{32,34},{3... | collective-permute-start | bytes 245768 | tf_op jit(solution)/shard_map/ppermute | solution.py:38
  11.4 9.5 %collective-permute-start.3 = (bf16[144,384]{1,0:T(8,128)(2,1)S(1)}, bf16[144,384]{1,0:T(8,128)(2,1)S(1)}, u32[]{:S(2)}, u32[]{:S(2)}) collective-permute-start(bf16[144,384]{1,0:T(8,128)(2,1)S(1)} %get-tuple-element.26), channel_id=1, source_target_pairs={{0,64},{4,68},{8,72},{12,76},{64,0},{68,4},{72,8},{76,12},{1,65},{... | collective-permute-start | bytes 331784 | tf_op jit(solution)/shard_map/ppermute | solution.py:38
  13.0 7.5 %collective-permute-start = (bf16[144,384]{1,0:T(8,128)(2,1)S(1)}, bf16[144,384]{1,0:T(8,128)(2,1)S(1)}, u32[]{:S(2)}, u32[]{:S(2)}) collective-permute-start(bf16[144,384]{1,0:T(8,128)(2,1)S(1)} %get-tuple-element.27), channel_id=1, source_target_pairs={{0,4},{4,0},{8,12},{12,8},{64,68},{68,64},{72,76},{76,72},{1,5},{5... | collective-permute-start | bytes 331784 | tf_op jit(solution)/shard_map/ppermute | solution.py:38
  16.0 7.4 %collective-permute-start.11 = (bf16[2,80,256]{2,1,0:T(8,128)(2,1)S(1)}, bf16[2,80,256]{2,1,0:T(8,128)(2,1)S(1)}, u32[]{:S(2)}, u32[]{:S(2)}) collective-permute-start(bf16[2,80,256]{2,1,0:T(8,128)(2,1)S(1)} %maximum_select_fusion.22), channel_id=1, source_target_pairs={{0,2},{1,3},{2,0},{3,1},{16,18},{17,19},{18,16},{19,17},{32,34},{3... | collective-permute-start | bytes 245768 | tf_op jit(solution)/shard_map/ppermute | solution.py:38
  16.6 7.5 %collective-permute-start.7 = (bf16[2,80,512]{2,1,0:T(8,128)(2,1)S(1)}, bf16[2,80,512]{2,1,0:T(8,128)(2,1)S(1)}, u32[]{:S(2)}, u32[]{:S(2)}) collective-permute-start(bf16[2,80,512]{2,1,0:T(8,128)(2,1)S(1)} %maximum_select_fusion.18), channel_id=1, source_target_pairs={{0,32},{1,33},{2,34},{3,35},{16,48},{17,49},{18,50},{19,51},{32,0}... | collective-permute-start | bytes 491528 | tf_op jit(solution)/shard_map/ppermute | solution.py:38
  20.6 11.1 %collective-permute-start.1 = (bf16[2,144,384]{2,1,0:T(8,128)(2,1)S(1)}, bf16[2,144,384]{2,1,0:T(8,128)(2,1)S(1)}, u32[]{:S(2)}, u32[]{:S(2)}) collective-permute-start(bf16[2,144,384]{2,1,0:T(8,128)(2,1)S(1)} %maximum_select_fusion.14), channel_id=1, source_target_pairs={{0,64},{4,68},{8,72},{12,76},{64,0},{68,4},{72,8},{76,12},{1,65},{... | collective-permute-start | bytes 663560 | tf_op jit(solution)/shard_map/ppermute | solution.py:38
  20.9 10.6 %collective-permute-start.4 = (bf16[2,144,384]{2,1,0:T(8,128)(2,1)S(1)}, bf16[2,144,384]{2,1,0:T(8,128)(2,1)S(1)}, u32[]{:S(2)}, u32[]{:S(2)}) collective-permute-start(bf16[2,144,384]{2,1,0:T(8,128)(2,1)S(1)} %maximum_select_fusion.16), channel_id=1, source_target_pairs={{0,4},{4,0},{8,12},{12,8},{64,68},{68,64},{72,76},{76,72},{1,5},{5... | collective-permute-start | bytes 663560 | tf_op jit(solution)/shard_map/ppermute | solution.py:38
  23.4 5.4 %collective-permute-start.12 = (bf16[2,2,80,256]{3,2,1,0:T(8,128)(2,1)S(1)}, bf16[2,2,80,256]{3,2,1,0:T(8,128)(2,1)S(1)}, u32[]{:S(2)}, u32[]{:S(2)}) collective-permute-start(bf16[2,2,80,256]{3,2,1,0:T(8,128)(2,1)S(1)} %maximum_select_fusion.20), channel_id=1, source_target_pairs={{0,1},{1,0},{2,3},{3,2},{16,17},{17,16},{18,19},{19,18},{32,33},{3... | collective-permute-start | bytes 491528 | tf_op jit(solution)/shard_map/ppermute | solution.py:38
  24.2 10.2 %collective-permute-start.8 = (bf16[2,2,80,512]{3,2,1,0:T(8,128)(2,1)S(1)}, bf16[2,2,80,512]{3,2,1,0:T(8,128)(2,1)S(1)}, u32[]{:S(2)}, u32[]{:S(2)}) collective-permute-start(bf16[2,2,80,512]{3,2,1,0:T(8,128)(2,1)S(1)} %maximum_select_fusion.10), channel_id=1, source_target_pairs={{0,16},{1,17},{2,18},{3,19},{16,0},{17,1},{18,2},{19,3},{32,48},{3... | collective-permute-start | bytes 983048 | tf_op jit(solution)/shard_map/ppermute | solution.py:38
  28.8 9.6 %collective-permute-start.13 = (bf16[2,2,2,80,256]{4,3,2,1,0:T(8,128)(2,1)S(1)}, bf16[2,2,2,80,256]{4,3,2,1,0:T(8,128)(2,1)S(1)}, u32[]{:S(2)}, u32[]{:S(2)}) collective-permute-start(bf16[2,2,2,80,256]{4,3,2,1,0:T(8,128)(2,1)S(1)} %maximum_select_fusion.12), channel_id=1, source_target_pairs={{0,16},{1,17},{2,18},{3,19},{16,0},{17,1},{18,2},{19,3},{32,48},{3... | collective-permute-start | bytes 983048 | tf_op jit(solution)/shard_map/ppermute | solution.py:38
  31.6 7.0 %collective-permute-start.5 = (bf16[2,2,144,384]{3,2,1,0:T(8,128)(2,1)S(1)}, bf16[2,2,144,384]{3,2,1,0:T(8,128)(2,1)S(1)}, u32[]{:S(2)}, u32[]{:S(2)}) collective-permute-start(bf16[2,2,144,384]{3,2,1,0:T(8,128)(2,1)S(1)} %maximum_select_fusion.8), channel_id=1, source_target_pairs={{0,8},{4,12},{8,0},{12,4},{64,72},{68,76},{72,64},{76,68},{1,9},{5... | collective-permute-start | bytes 1327112 | tf_op jit(solution)/shard_map/ppermute | solution.py:38
  31.8 7.1 %collective-permute-start.2 = (bf16[2,2,144,384]{3,2,1,0:T(8,128)(2,1)S(1)}, bf16[2,2,144,384]{3,2,1,0:T(8,128)(2,1)S(1)}, u32[]{:S(2)}, u32[]{:S(2)}) collective-permute-start(bf16[2,2,144,384]{3,2,1,0:T(8,128)(2,1)S(1)} %maximum_select_fusion.6), channel_id=1, source_target_pairs={{0,8},{4,12},{8,0},{12,4},{64,72},{68,76},{72,64},{76,68},{1,9},{5... | collective-permute-start | bytes 1327112 | tf_op jit(solution)/shard_map/ppermute | solution.py:38
  34.5 14.9 %collective-permute-start.9 = (bf16[2,2,2,80,512]{4,3,2,1,0:T(8,128)(2,1)S(1)}, bf16[2,2,2,80,512]{4,3,2,1,0:T(8,128)(2,1)S(1)}, u32[]{:S(2)}, u32[]{:S(2)}) collective-permute-start(bf16[2,2,2,80,512]{4,3,2,1,0:T(8,128)(2,1)S(1)} %maximum_select_fusion.3), channel_id=1, source_target_pairs={{0,1},{1,0},{2,3},{3,2},{16,17},{17,16},{18,19},{19,18},{32,33},{3... | collective-permute-start | bytes 1966088 | tf_op jit(solution)/shard_map/ppermute | solution.py:38
  39.2 14.3 %copy-start.3 = (bf16[8,128,768]{2,1,0:T(8,128)(2,1)}, bf16[8,128,768]{2,1,0:T(8,128)(2,1)S(1)}, u32[]{:S(2)}) copy-start(bf16[8,128,768]{2,1,0:T(8,128)(2,1)S(1)} %pad_maximum_fusion.1) | copy-start | bytes 4718596
  54.4 8.6 %all-to-all-start = ((f32[8,1,1024]{2,1,0:T(1,128)}), f32[8,1,1024]{2,1,0:T(1,128)S(1)}, u32[]{:S(2)}, u32[]{:S(2)}) async-start(f32[8,1,1024]{2,1,0:T(1,128)} %broadcast_in_dim.36), calls=%async_computation | async-start | bytes 65536 | tf_op jit(solution)/shard_map/all_to_all | solution.py:31
  64.2 11.5 %all-to-all-start.1 = ((f32[16,1,1024]{2,1,0:T(1,128)}), f32[16,1,1024]{2,1,0:T(1,128)S(1)}, u32[]{:S(2)}, u32[]{:S(2)}) async-start(f32[16,1,1024]{2,1,0:T(1,128)} %broadcast_in_dim.37), calls=%async_computation.1 | async-start | bytes 131072 | tf_op jit(solution)/shard_map/all_to_all | solution.py:31
  127.2 11.5 %all-to-all-start.7 = ((f32[16,2,1024]{2,1,0:T(2,128)}), f32[16,2,1024]{2,1,0:T(2,128)S(1)}, u32[]{:S(2)}, u32[]{:S(2)}) async-start(f32[16,2,1024]{2,1,0:T(2,128)} %broadcast_in_dim.43), calls=%async_computation.7 | async-start | bytes 262144 | tf_op jit(solution)/shard_map/all_to_all | solution.py:31
  218.7 16.0 %collective-permute-start.17 = (f32[2,2,128,384]{3,2,0,1:T(8,128)S(1)}, f32[2,2,128,384]{3,2,0,1:T(8,128)S(1)}, u32[]{:S(2)}, u32[]{:S(2)}) collective-permute-start(f32[2,2,128,384]{3,2,0,1:T(8,128)S(1)} %select_bitcast_fusion.1), channel_id=1, source_target_pairs={{0,8},{4,12},{8,0},{12,4},{64,72},{68,76},{72,64},{76,68},{1,9},{5... | collective-permute-start | bytes 2359304 | tf_op jit(solution)/shard_map/ppermute | solution.py:61
  219.0 34.8 %collective-permute-start.14 = (f32[2,2,128,384]{3,2,0,1:T(8,128)S(1)}, f32[2,2,128,384]{3,2,0,1:T(8,128)S(1)}, u32[]{:S(2)}, u32[]{:S(2)}) collective-permute-start(f32[2,2,128,384]{3,2,0,1:T(8,128)S(1)} %select_bitcast_fusion.2), channel_id=1, source_target_pairs={{0,8},{4,12},{8,0},{12,4},{64,72},{68,76},{72,64},{76,68},{1,9},{5... | collective-permute-start | bytes 2359304 | tf_op jit(solution)/shard_map/ppermute | solution.py:61
  219.9 14.0 %collective-permute-start.24 = (f32[2,2,2,64,256]{4,3,1,0,2:T(8,128)S(1)}, f32[2,2,2,64,256]{4,3,1,0,2:T(8,128)S(1)}, u32[]{:S(2)}, u32[]{:S(2)}) collective-permute-start(f32[2,2,2,64,256]{4,3,1,0,2:T(8,128)S(1)} %select_bitcast_fusion.3), channel_id=1, source_target_pairs={{0,16},{1,17},{2,18},{3,19},{16,0},{17,1},{18,2},{19,3},{32,48},{3... | collective-permute-start | bytes 1572872 | tf_op jit(solution)/shard_map/ppermute | solution.py:61
  221.0 43.4 %collective-permute-start.20 = (f32[2,2,2,64,512]{4,3,0,2,1:T(8,128)S(1)}, f32[2,2,2,64,512]{4,3,0,2,1:T(8,128)S(1)}, u32[]{:S(2)}, u32[]{:S(2)}) collective-permute-start(f32[2,2,2,64,512]{4,3,0,2,1:T(8,128)S(1)} %select_bitcast_fusion), channel_id=1, source_target_pairs={{0,1},{1,0},{2,3},{3,2},{16,17},{17,16},{18,19},{19,18},{32,33},{3... | collective-permute-start | bytes 3145736 | tf_op jit(solution)/shard_map/ppermute | solution.py:61
  234.1 17.7 %collective-permute-start.25 = (f32[2,2,64,256]{3,2,1,0:T(8,128)S(1)}, f32[2,2,64,256]{3,2,1,0:T(8,128)S(1)}, u32[]{:S(2)}, u32[]{:S(2)}) collective-permute-start(f32[2,2,64,256]{3,2,1,0:T(8,128)S(1)} %select_bitcast_fusion.7), channel_id=1, source_target_pairs={{0,1},{1,0},{2,3},{3,2},{16,17},{17,16},{18,19},{19,18},{32,33},{3... | collective-permute-start | bytes 786440 | tf_op jit(solution)/shard_map/ppermute | solution.py:61
  234.9 31.3 %collective-permute-start.18 = (f32[2,128,384]{2,1,0:T(8,128)S(1)}, f32[2,128,384]{2,1,0:T(8,128)S(1)}, u32[]{:S(2)}, u32[]{:S(2)}) collective-permute-start(f32[2,128,384]{2,1,0:T(8,128)S(1)} %select_bitcast_fusion.5), channel_id=1, source_target_pairs={{0,4},{4,0},{8,12},{12,8},{64,68},{68,64},{72,76},{76,72},{1,5},{5... | collective-permute-start | bytes 1179656 | tf_op jit(solution)/shard_map/ppermute | solution.py:61
  251.9 6.6 %collective-permute-start.26 = (f32[2,64,256]{2,1,0:T(8,128)S(1)}, f32[2,64,256]{2,1,0:T(8,128)S(1)}, u32[]{:S(2)}, u32[]{:S(2)}) collective-permute-start(f32[2,64,256]{2,1,0:T(8,128)S(1)} %select_bitcast_fusion.11), channel_id=1, source_target_pairs={{0,32},{1,33},{2,34},{3,35},{16,48},{17,49},{18,50},{19,51},{32,0}... | collective-permute-start | bytes 393224 | tf_op jit(solution)/shard_map/ppermute | solution.py:61
  258.5 5.8 %collective-permute-start.27 = (f32[64,256]{1,0:T(8,128)S(1)}, f32[64,256]{1,0:T(8,128)S(1)}, u32[]{:S(2)}, u32[]{:S(2)}) collective-permute-start(f32[64,256]{1,0:T(8,128)S(1)} %select_bitcast_fusion.13), channel_id=1, source_target_pairs={{0,2},{1,3},{2,0},{3,1},{16,18},{17,19},{18,16},{19,17},{32,34},{3... | collective-permute-start | bytes 196616 | tf_op jit(solution)/shard_map/ppermute | solution.py:61
  259.9 11.0 %collective-permute-start.15 = (f32[2,128,384]{2,1,0:T(8,128)S(1)}, f32[2,128,384]{2,1,0:T(8,128)S(1)}, u32[]{:S(2)}, u32[]{:S(2)}) collective-permute-start(f32[2,128,384]{2,1,0:T(8,128)S(1)} %select_bitcast_fusion.6), channel_id=1, source_target_pairs={{0,64},{4,68},{8,72},{12,76},{64,0},{68,4},{72,8},{76,12},{1,65},{... | collective-permute-start | bytes 1179656 | tf_op jit(solution)/shard_map/ppermute | solution.py:61
  264.8 10.8 %collective-permute-start.21 = (f32[2,2,64,512]{3,2,0,1:T(8,128)S(1)}, f32[2,2,64,512]{3,2,0,1:T(8,128)S(1)}, u32[]{:S(2)}, u32[]{:S(2)}) collective-permute-start(f32[2,2,64,512]{3,2,0,1:T(8,128)S(1)} %select_bitcast_fusion.4), channel_id=1, source_target_pairs={{0,16},{1,17},{2,18},{3,19},{16,0},{17,1},{18,2},{19,3},{32,48},{3... | collective-permute-start | bytes 1572872 | tf_op jit(solution)/shard_map/ppermute | solution.py:61
  266.2 11.5 %collective-permute-start.19 = (f32[128,384]{1,0:T(8,128)S(1)}, f32[128,384]{1,0:T(8,128)S(1)}, u32[]{:S(2)}, u32[]{:S(2)}) collective-permute-start(f32[128,384]{1,0:T(8,128)S(1)} %select_bitcast_fusion.9), channel_id=1, source_target_pairs={{0,64},{4,68},{8,72},{12,76},{64,0},{68,4},{72,8},{76,12},{1,65},{... | collective-permute-start | bytes 589832 | tf_op jit(solution)/shard_map/ppermute | solution.py:61
  275.8 8.0 %collective-permute-start.22 = (f32[2,64,512]{2,1,0:T(8,128)S(1)}, f32[2,64,512]{2,1,0:T(8,128)S(1)}, u32[]{:S(2)}, u32[]{:S(2)}) collective-permute-start(f32[2,64,512]{2,1,0:T(8,128)S(1)} %select_bitcast_fusion.8), channel_id=1, source_target_pairs={{0,2},{1,3},{2,0},{3,1},{16,18},{17,19},{18,16},{19,17},{32,34},{3... | collective-permute-start | bytes 786440 | tf_op jit(solution)/shard_map/ppermute | solution.py:61
  277.2 8.3 %collective-permute-start.16 = (f32[128,384]{1,0:T(8,128)S(1)}, f32[128,384]{1,0:T(8,128)S(1)}, u32[]{:S(2)}, u32[]{:S(2)}) collective-permute-start(f32[128,384]{1,0:T(8,128)S(1)} %select_bitcast_fusion.10), channel_id=1, source_target_pairs={{0,4},{4,0},{8,12},{12,8},{64,68},{68,64},{72,76},{76,72},{1,5},{5... | collective-permute-start | bytes 589832 | tf_op jit(solution)/shard_map/ppermute | solution.py:61
  283.9 6.6 %collective-permute-start.23 = (f32[64,512]{1,0:T(8,128)S(1)}, f32[64,512]{1,0:T(8,128)S(1)}, u32[]{:S(2)}, u32[]{:S(2)}) collective-permute-start(f32[64,512]{1,0:T(8,128)S(1)} %select_bitcast_fusion.12), channel_id=1, source_target_pairs={{0,32},{1,33},{2,34},{3,35},{16,48},{17,49},{18,50},{19,51},{32,0}... | collective-permute-start | bytes 393224 | tf_op jit(solution)/shard_map/ppermute | solution.py:61
  (6 other events, 16.1 us)

commit v6 on v4

--- a/solution.py
+++ b/solution.py
@@ -177,9 +177,12 @@
         col_bars[iteration] = col_bar
     left = jnp.stack(row_bars + src_saved, axis=1)
     right = jnp.stack(old_saved + col_bars, axis=1)
-    lowrank = left[:, 0, None] * right[None, :, 0]
-    for k in range(1, left.shape[1]):
-        lowrank = lowrank + left[:, k, None] * right[None, :, k]
+    left_pieces, right_pieces = split3(left), split3(right)
+    left_all = jnp.concatenate([a for a in left_pieces for b in right_pieces], axis=1)
+    right_all = jnp.concatenate([b for a in left_pieces for b in right_pieces], axis=1)
+    lowrank = lax.dot_general(
+        left_all, right_all, (((1,), (1,)), ((), ())), preferred_element_type=jnp.float32
+    )
     cross_term_grid = (
         kernel * (last_src[:, None] * last_tgt[None, :] * (1.0 + kernel_grid) + lowrank)
     ).astype(jnp.bfloat16)

time: 265 us -> 266 us (level)
  blocking collectives: 108 us -> 89.3 us
  waiting for transfers between devices: 67.4 us -> 79.7 us
  starting transfers between devices: 46.9 us -> 53.9 us
  other arithmetic: 28.4 us -> 23.1 us
  matrix products: 7.48 us -> 11 us
    all_to_all x12 -> x10, blocking collectives: 108 us -> 89.3 us  [tree_sum(): return lax.all_to_all(spread, axis, 0, 0, tiled=False).sum(0)]
    all_to_all x3 -> x5, waiting for transfers between devices: 19.3 us -> 31.6 us  [tree_sum(): return lax.all_to_all(spread, axis, 0, 0, tiled=False).sum(0)]
    all_to_all x3 -> x5, starting transfers between devices: 11.3 us -> 18.4 us  [tree_sum(): return lax.all_to_all(spread, axis, 0, 0, tiled=False).sum(0)]
    convert_element_type x1 -> x0, other arithmetic: 5.41 us -> none  [per_device(): cross_term_grid = (kernel * (last_src[:, None] * last_tgt[None, :] * (1.0...]
    dot_general x0 -> x1, matrix products: none -> 3.54 us  [per_device(): lax.dot_general(left_all, right_all, (((1,), (1,)), ((), ())), preferred_...]
  transfers between devices with their start and end apart: 31 -> 33, of which waited for: 12 -> 14; matrix products, arithmetic and copies ran while one was open for 3% -> 3% of each run, Pallas kernels for 0% -> 0%
where the time goes in v6:
time: 266 us; the launch traced here: 265 us
  blocking collectives  89.3 us (34%)
  waiting for transfers between devices  79.7 us (30%)
  starting transfers between devices  53.9 us (20%)
  other arithmetic  23.1 us (9%)
  matrix products  11 us (4%)
  local copies, waits for them, and re-layouts  5.7 us (2%)
    all_to_all x10, blocking collectives, tree_sum(): return lax.all_to_all(spread, axis, 0, 0, tiled=False).sum(0)  89.3 us
    all_to_all x5, waiting for transfers between devices, tree_sum(): return lax.all_to_all(spread, axis, 0, 0, tiled=False).sum(0)  31.6 us
    ppermute x14, waiting for transfers between devices, tree_scatter(): x = keep + lax.ppermute(send, axis, partner(axis, n, bit))  27.3 us
    ppermute x14, waiting for transfers between devices, tree_gather(): other = lax.ppermute(x, axis, partner(axis, n, bit))  20.9 us
    ppermute x14, starting transfers between devices, tree_gather(): other = lax.ppermute(x, axis, partner(axis, n, bit))  19.1 us
    all_to_all x5, starting transfers between devices, tree_sum(): return lax.all_to_all(spread, axis, 0, 0, tiled=False).sum(0)  18.4 us
    ppermute x14, starting transfers between devices, tree_scatter(): x = keep + lax.ppermute(send, axis, partner(axis, n, bit))  16.4 us
    reduce_sum x8, other arithmetic, times_vector(): return jnp.sum(kernel.astype(jnp.float32) * vector[None, :], axis=1)  6.72 us
  transfers between devices with their start and end apart: 33, of which 14 were waited for; matrix products, arithmetic and copies ran while one was open for 3% of the time, Pallas kernels for 0%

profile of v6, /device:TPU:0, one launch (start us, length us, event | category | flops | bytes accessed | tf_op | source)
XLA Modules:
  0.0 264.6 jit_solution(15368752010079287487)
XLA Ops:
  2.4 4.0 %collective-permute-start.10 = (bf16[80,384]{1,0:T(8,128)(2,1)S(1)}, bf16[80,384]{1,0:T(8,128)(2,1)S(1)}, u32[]{:S(2)}, u32[]{:S(2)}) collective-permute-start(bf16[80,384]{1,0:T(8,128)(2,1)S(1)} %get-tuple-element.48), channel_id=1, source_target_pairs={{0,32},{1,33},{2,34},{3,35},{16,48},{17,49},{18,50},{19,51},{32,0}... | collective-permute-start | bytes 184328 | tf_op jit(solution)/shard_map/ppermute | solution.py:38
  16.8 3.6 %collective-permute-done = bf16[144,384]{1,0:T(8,128)(2,1)S(1)} collective-permute-done((bf16[144,384]{1,0:T(8,128)(2,1)S(1)}, bf16[144,384]{1,0:T(8,128)(2,1)S(1)}, u32[]{:S(2)}, u32[]{:S(2)}) %collective-permute-start) | collective-permute-done | bytes 110624 | tf_op jit(solution)/shard_map/ppermute | solution.py:38
  25.3 6.1 %collective-permute-done.4 = bf16[2,144,384]{2,1,0:T(8,128)(2,1)S(1)} collective-permute-done((bf16[2,144,384]{2,1,0:T(8,128)(2,1)S(1)}, bf16[2,144,384]{2,1,0:T(8,128)(2,1)S(1)}, u32[]{:S(2)}, u32[]{:S(2)}) %collective-permute-start.4) | collective-permute-done | bytes 221216 | tf_op jit(solution)/shard_map/ppermute | solution.py:38
  35.2 11.1 %collective-permute-done.13 = bf16[2,2,2,80,384]{4,3,2,1,0:T(8,128)(2,1)S(1)} collective-permute-done((bf16[2,2,2,80,384]{4,3,2,1,0:T(8,128)(2,1)S(1)}, bf16[2,2,2,80,384]{4,3,2,1,0:T(8,128)(2,1)S(1)}, u32[]{:S(2)}, u32[]{:S(2)}) %collective-permute-start.13) | collective-permute-done | bytes 491552 | tf_op jit(solution)/shard_map/ppermute | solution.py:38
  47.0 3.8 %exponential_convert_fusion = (bf16[1024,1024]{1,0:T(8,128)(2,1)S(1)}, f32[1024,1024]{1,0:T(8,128)}) fusion(bf16[1024,768]{1,0:T(8,128)(2,1)S(1)} %bitcast.202, bf16[1024,768]{1,0:T(8,128)(2,1)S(1)} %bitcast.200), kind=kOutput, calls=%fused_computation.34 | convolution fusion | flops 1612709888 | bytes 9437184 | tf_op jit(solution)/shard_map/dot_general | solution.py:136
  51.7 3.3 %all-to-all-start = ((f32[8,1,1024]{2,1,0:T(1,128)}), f32[8,1,1024]{2,1,0:T(1,128)S(1)}, u32[]{:S(2)}, u32[]{:S(2)}) async-start(f32[8,1,1024]{2,1,0:T(1,128)} %broadcast_in_dim.36), calls=%async_computation | async-start | bytes 65536 | tf_op jit(solution)/shard_map/all_to_all | solution.py:31
  55.2 5.1 %all-to-all-done = f32[8,1,1024]{2,1,0:T(1,128)S(1)} async-done(((f32[8,1,1024]{2,1,0:T(1,128)}), f32[8,1,1024]{2,1,0:T(1,128)S(1)}, u32[]{:S(2)}, u32[]{:S(2)}) %all-to-all-start) | async-done | bytes 32800 | tf_op jit(solution)/shard_map/all_to_all | solution.py:31
  61.5 4.5 %all-to-all-start.1 = ((f32[16,1,1024]{2,1,0:T(1,128)}), f32[16,1,1024]{2,1,0:T(1,128)S(1)}, u32[]{:S(2)}, u32[]{:S(2)}) async-start(f32[16,1,1024]{2,1,0:T(1,128)} %broadcast_in_dim.37), calls=%async_computation.1 | async-start | bytes 131072 | tf_op jit(solution)/shard_map/all_to_all | solution.py:31
  67.2 6.4 %all-to-all-done.1 = f32[16,1,1024]{2,1,0:T(1,128)S(1)} async-done(((f32[16,1,1024]{2,1,0:T(1,128)}), f32[16,1,1024]{2,1,0:T(1,128)S(1)}, u32[]{:S(2)}, u32[]{:S(2)}) %all-to-all-start.1) | async-done | bytes 65568 | tf_op jit(solution)/shard_map/all_to_all | solution.py:31
  74.2 7.7 %all_to_all.89 = f32[8,1,1024]{2,1,0:T(1,128)S(1)} all-to-all(f32[8,1,1024]{2,1,0:T(1,128)S(1)} %broadcast_in_dim.38), channel_id=1, replica_groups=mesh['y_lo'=2,'z'=4,'core'=2,'y_hi'=2,'x'=4] {'y_lo','core','y_hi'}, dimensions={0} | all-to-all | bytes 65536 | tf_op jit(solution)/shard_map/all_to_all | solution.py:31
  82.5 10.8 %all_to_all.90 = f32[16,1,1024]{2,1,0:T(1,128)S(1)} all-to-all(f32[16,1,1024]{2,1,0:T(1,128)S(1)} %broadcast_in_dim.39), channel_id=1, replica_groups=mesh['y_lo'=2,'z'=4,'core'=2,'y_hi'=2,'x'=4] {'z','x'}, dimensions={0} | all-to-all | bytes 131072 | tf_op jit(solution)/shard_map/all_to_all | solution.py:31
  93.8 7.7 %all_to_all.91 = f32[8,1,1024]{2,1,0:T(1,128)S(1)} all-to-all(f32[8,1,1024]{2,1,0:T(1,128)S(1)} %broadcast_in_dim.40), channel_id=1, replica_groups=mesh['y_lo'=2,'z'=4,'core'=2,'y_hi'=2,'x'=4] {'y_lo','core','y_hi'}, dimensions={0} | all-to-all | bytes 65536 | tf_op jit(solution)/shard_map/all_to_all | solution.py:31
  102.1 10.8 %all_to_all.92 = f32[16,1,1024]{2,1,0:T(1,128)S(1)} all-to-all(f32[16,1,1024]{2,1,0:T(1,128)S(1)} %broadcast_in_dim.41), channel_id=1, replica_groups=mesh['y_lo'=2,'z'=4,'core'=2,'y_hi'=2,'x'=4] {'z','x'}, dimensions={0} | all-to-all | bytes 131072 | tf_op jit(solution)/shard_map/all_to_all | solution.py:31
  113.5 7.7 %all_to_all.93 = f32[8,1,1024]{2,1,0:T(1,128)S(1)} all-to-all(f32[8,1,1024]{2,1,0:T(1,128)S(1)} %broadcast_in_dim.42), channel_id=1, replica_groups=mesh['y_lo'=2,'z'=4,'core'=2,'y_hi'=2,'x'=4] {'y_lo','core','y_hi'}, dimensions={0} | all-to-all | bytes 65536 | tf_op jit(solution)/shard_map/all_to_all | solution.py:31
  121.2 3.2 %fusion.6 = (f32[1024]{0:T(1024)S(1)}, f32[1024]{0:T(1024)S(1)}) fusion(bf16[1024,1024]{1,0:T(8,128)(2,1)S(1)} %get-tuple-element.79, f32[1024]{0:T(1024)S(1)} %bitcast_divide_fusion.2, f32[1024,1024]{1,0:T(8,128)} %get-tuple-element.80), kind=kLoop, calls=%fused_computation.23 | loop fusion | flops 7337984 | bytes 6303744 | tf_op jit(solution)/shard_map/reduce_sum | solution.py:122
  125.1 3.5 %all-to-all-start.7 = ((f32[16,2,1024]{2,1,0:T(2,128)}), f32[16,2,1024]{2,1,0:T(2,128)S(1)}, u32[]{:S(2)}, u32[]{:S(2)}) async-start(f32[16,2,1024]{2,1,0:T(2,128)} %broadcast_in_dim.43), calls=%async_computation.7 | async-start | bytes 262144 | tf_op jit(solution)/shard_map/all_to_all | solution.py:31
  128.7 7.9 %all-to-all-done.7 = f32[16,2,1024]{2,1,0:T(2,128)S(1)} async-done(((f32[16,2,1024]{2,1,0:T(2,128)}), f32[16,2,1024]{2,1,0:T(2,128)S(1)}, u32[]{:S(2)}, u32[]{:S(2)}) %all-to-all-start.7) | async-done | bytes 131104 | tf_op jit(solution)/shard_map/all_to_all | solution.py:31
  136.7 3.5 %multiply_reduce_fusion = (f32[1024]{0:T(1024)S(1)}, f32[1024]{0:T(1024)S(1)}) fusion(f32[1024,1024]{1,0:T(8,128)} %get-tuple-element.80, bf16[1024,1024]{1,0:T(8,128)(2,1)S(1)} %get-tuple-element.79, f32[1024]{0:T(1024)S(1)} %bitcast.242, f32[1024]{0:T(1024)S(1)} %bitcast.245), kind=kLoop, calls=%fused_computation.32 | loop fusion | flops 7337984 | bytes 6307840 | tf_op jit(solution)/shard_map/reduce_sum | solution.py:118
  140.2 7.7 %all_to_all.94 = f32[8,1,1024]{2,1,0:T(1,128)S(1)} all-to-all(f32[8,1,1024]{2,1,0:T(1,128)S(1)} %broadcast_in_dim.44), channel_id=1, replica_groups=mesh['y_lo'=2,'z'=4,'core'=2,'y_hi'=2,'x'=4] {'y_lo','core','y_hi'}, dimensions={0} | all-to-all | bytes 65536 | tf_op jit(solution)/shard_map/all_to_all | solution.py:31
  148.5 10.7 %all_to_all.95 = f32[16,1,1024]{2,1,0:T(1,128)S(1)} all-to-all(f32[16,1,1024]{2,1,0:T(1,128)S(1)} %broadcast_in_dim.45), channel_id=1, replica_groups=mesh['y_lo'=2,'z'=4,'core'=2,'y_hi'=2,'x'=4] {'z','x'}, dimensions={0} | all-to-all | bytes 131072 | tf_op jit(solution)/shard_map/all_to_all | solution.py:31
  159.8 7.7 %all_to_all.96 = f32[8,1,1024]{2,1,0:T(1,128)S(1)} all-to-all(f32[8,1,1024]{2,1,0:T(1,128)S(1)} %broadcast_in_dim.46), channel_id=1, replica_groups=mesh['y_lo'=2,'z'=4,'core'=2,'y_hi'=2,'x'=4] {'y_lo','core','y_hi'}, dimensions={0} | all-to-all | bytes 65536 | tf_op jit(solution)/shard_map/all_to_all | solution.py:31
  168.1 10.8 %all_to_all.97 = f32[16,1,1024]{2,1,0:T(1,128)S(1)} all-to-all(f32[16,1,1024]{2,1,0:T(1,128)S(1)} %broadcast_in_dim.47), channel_id=1, replica_groups=mesh['y_lo'=2,'z'=4,'core'=2,'y_hi'=2,'x'=4] {'z','x'}, dimensions={0} | all-to-all | bytes 131072 | tf_op jit(solution)/shard_map/all_to_all | solution.py:31
  179.5 7.7 %all_to_all.98 = f32[8,1,1024]{2,1,0:T(1,128)S(1)} all-to-all(f32[8,1,1024]{2,1,0:T(1,128)S(1)} %broadcast_in_dim.48), channel_id=1, replica_groups=mesh['y_lo'=2,'z'=4,'core'=2,'y_hi'=2,'x'=4] {'y_lo','core','y_hi'}, dimensions={0} | all-to-all | bytes 65536 | tf_op jit(solution)/shard_map/all_to_all | solution.py:31
  188.4 3.5 %all-to-all-start.13 = ((f32[16,1,1024]{2,1,0:T(1,128)}), f32[16,1,1024]{2,1,0:T(1,128)S(1)}, u32[]{:S(2)}, u32[]{:S(2)}) async-start(f32[16,1,1024]{2,1,0:T(1,128)} %broadcast_in_dim.49), calls=%async_computation.13 | async-start | bytes 131072 | tf_op jit(solution)/shard_map/all_to_all | solution.py:31
  191.9 7.5 %all-to-all-done.13 = f32[16,1,1024]{2,1,0:T(1,128)S(1)} async-done(((f32[16,1,1024]{2,1,0:T(1,128)}), f32[16,1,1024]{2,1,0:T(1,128)S(1)}, u32[]{:S(2)}, u32[]{:S(2)}) %all-to-all-start.13) | async-done | bytes 65568 | tf_op jit(solution)/shard_map/all_to_all | solution.py:31
  200.7 3.6 %all-to-all-start.14 = ((f32[8,1,1024]{2,1,0:T(1,128)}), f32[8,1,1024]{2,1,0:T(1,128)S(1)}, u32[]{:S(2)}, u32[]{:S(2)}) async-start(f32[8,1,1024]{2,1,0:T(1,128)} %broadcast_in_dim.50), calls=%async_computation.14 | async-start | bytes 65536 | tf_op jit(solution)/shard_map/all_to_all | solution.py:31
  204.5 4.8 %all-to-all-done.14 = f32[8,1,1024]{2,1,0:T(1,128)S(1)} async-done(((f32[8,1,1024]{2,1,0:T(1,128)}), f32[8,1,1024]{2,1,0:T(1,128)S(1)}, u32[]{:S(2)}, u32[]{:S(2)}) %all-to-all-start.14) | async-done | bytes 32800 | tf_op jit(solution)/shard_map/all_to_all | solution.py:31
  209.5 3.5 %fusion.14 = bf16[1024,1024]{1,0:T(8,128)(2,1)S(1)} fusion(bf16[1024,1024]{1,0:T(8,128)(2,1)S(1)} %get-tuple-element.79, f32[1024,1024]{1,0:T(8,128)} %get-tuple-element.80, bf16[1024,72]{0,1:T(8,128)(2,1)S(1)} %get-tuple-element.81, bf16[1024,72]{0,1:T(8,128)(2,1)S(1)} %get-tuple-element.82, f32[1024]{0:T(1024)S(1)} %bitcast.243, ...), kind=kOutput, calls=%fused_computation.31 | convolution fusion | flops 159383552 | bytes 8691712 | tf_op jit(solution)/shard_map/dot_general | solution.py:183
  222.6 15.5 %collective-permute-done.24 = f32[2,2,2,64,384]{4,3,1,0,2:T(8,128)S(1)} collective-permute-done((f32[2,2,2,64,384]{4,3,1,0,2:T(8,128)S(1)}, f32[2,2,2,64,384]{4,3,1,0,2:T(8,128)S(1)}, u32[]{:S(2)}, u32[]{:S(2)}) %collective-permute-start.24) | collective-permute-done | bytes 786464 | tf_op jit(solution)/shard_map/ppermute | solution.py:61
  243.5 5.3 %collective-permute-done.25 = f32[2,2,64,384]{3,2,1,0:T(8,128)S(1)} collective-permute-done((f32[2,2,64,384]{3,2,1,0:T(8,128)S(1)}, f32[2,2,64,384]{3,2,1,0:T(8,128)S(1)}, u32[]{:S(2)}, u32[]{:S(2)}) %collective-permute-start.25) | collective-permute-done | bytes 393248 | tf_op jit(solution)/shard_map/ppermute | solution.py:61
  251.7 4.4 %collective-permute-done.26 = f32[2,64,384]{2,1,0:T(8,128)S(1)} collective-permute-done((f32[2,64,384]{2,1,0:T(8,128)S(1)}, f32[2,64,384]{2,1,0:T(8,128)S(1)}, u32[]{:S(2)}, u32[]{:S(2)}) %collective-permute-start.26) | collective-permute-done | bytes 196640 | tf_op jit(solution)/shard_map/ppermute | solution.py:61
  257.6 3.3 %collective-permute-start.23 = (f32[64,384]{1,0:T(8,128)S(1)}, f32[64,384]{1,0:T(8,128)S(1)}, u32[]{:S(2)}, u32[]{:S(2)}) collective-permute-start(f32[64,384]{1,0:T(8,128)S(1)} %select_bitcast_fusion.13), channel_id=1, source_target_pairs={{0,32},{1,33},{2,34},{3,35},{16,48},{17,49},{18,50},{19,51},{32,0}... | collective-permute-start | bytes 294920 | tf_op jit(solution)/shard_map/ppermute | solution.py:61
  (230 shorter events, 56.2 us)
Async XLA Ops:
  2.4 13.7 %collective-permute-start.10 = (bf16[80,384]{1,0:T(8,128)(2,1)S(1)}, bf16[80,384]{1,0:T(8,128)(2,1)S(1)}, u32[]{:S(2)}, u32[]{:S(2)}) collective-permute-start(bf16[80,384]{1,0:T(8,128)(2,1)S(1)} %get-tuple-element.48), channel_id=1, source_target_pairs={{0,32},{1,33},{2,34},{3,35},{16,48},{17,49},{18,50},{19,51},{32,0}... | collective-permute-start | bytes 184328 | tf_op jit(solution)/shard_map/ppermute | solution.py:38
  6.5 9.4 %collective-permute-start.6 = (bf16[80,384]{1,0:T(8,128)(2,1)S(1)}, bf16[80,384]{1,0:T(8,128)(2,1)S(1)}, u32[]{:S(2)}, u32[]{:S(2)}) collective-permute-start(bf16[80,384]{1,0:T(8,128)(2,1)S(1)} %get-tuple-element.49), channel_id=1, source_target_pairs={{0,2},{1,3},{2,0},{3,1},{16,18},{17,19},{18,16},{19,17},{32,34},{3... | collective-permute-start | bytes 184328 | tf_op jit(solution)/shard_map/ppermute | solution.py:38
  11.3 9.5 %collective-permute-start.3 = (bf16[144,384]{1,0:T(8,128)(2,1)S(1)}, bf16[144,384]{1,0:T(8,128)(2,1)S(1)}, u32[]{:S(2)}, u32[]{:S(2)}) collective-permute-start(bf16[144,384]{1,0:T(8,128)(2,1)S(1)} %get-tuple-element.42), channel_id=1, source_target_pairs={{0,64},{4,68},{8,72},{12,76},{64,0},{68,4},{72,8},{76,12},{1,65},{... | collective-permute-start | bytes 331784 | tf_op jit(solution)/shard_map/ppermute | solution.py:38
  13.0 7.5 %collective-permute-start = (bf16[144,384]{1,0:T(8,128)(2,1)S(1)}, bf16[144,384]{1,0:T(8,128)(2,1)S(1)}, u32[]{:S(2)}, u32[]{:S(2)}) collective-permute-start(bf16[144,384]{1,0:T(8,128)(2,1)S(1)} %get-tuple-element.43), channel_id=1, source_target_pairs={{0,4},{4,0},{8,12},{12,8},{64,68},{68,64},{72,76},{76,72},{1,5},{5... | collective-permute-start | bytes 331784 | tf_op jit(solution)/shard_map/ppermute | solution.py:38
  15.9 8.2 %collective-permute-start.7 = (bf16[2,80,384]{2,1,0:T(8,128)(2,1)S(1)}, bf16[2,80,384]{2,1,0:T(8,128)(2,1)S(1)}, u32[]{:S(2)}, u32[]{:S(2)}) collective-permute-start(bf16[2,80,384]{2,1,0:T(8,128)(2,1)S(1)} %maximum_select_fusion.20), channel_id=1, source_target_pairs={{0,32},{1,33},{2,34},{3,35},{16,48},{17,49},{18,50},{19,51},{32,0}... | collective-permute-start | bytes 368648 | tf_op jit(solution)/shard_map/ppermute | solution.py:38
  16.2 7.1 %collective-permute-start.11 = (bf16[2,80,384]{2,1,0:T(8,128)(2,1)S(1)}, bf16[2,80,384]{2,1,0:T(8,128)(2,1)S(1)}, u32[]{:S(2)}, u32[]{:S(2)}) collective-permute-start(bf16[2,80,384]{2,1,0:T(8,128)(2,1)S(1)} %maximum_select_fusion.22), channel_id=1, source_target_pairs={{0,2},{1,3},{2,0},{3,1},{16,18},{17,19},{18,16},{19,17},{32,34},{3... | collective-permute-start | bytes 368648 | tf_op jit(solution)/shard_map/ppermute | solution.py:38
  20.5 11.1 %collective-permute-start.1 = (bf16[2,144,384]{2,1,0:T(8,128)(2,1)S(1)}, bf16[2,144,384]{2,1,0:T(8,128)(2,1)S(1)}, u32[]{:S(2)}, u32[]{:S(2)}) collective-permute-start(bf16[2,144,384]{2,1,0:T(8,128)(2,1)S(1)} %maximum_select_fusion.16), channel_id=1, source_target_pairs={{0,64},{4,68},{8,72},{12,76},{64,0},{68,4},{72,8},{76,12},{1,65},{... | collective-permute-start | bytes 663560 | tf_op jit(solution)/shard_map/ppermute | solution.py:38
  20.8 10.6 %collective-permute-start.4 = (bf16[2,144,384]{2,1,0:T(8,128)(2,1)S(1)}, bf16[2,144,384]{2,1,0:T(8,128)(2,1)S(1)}, u32[]{:S(2)}, u32[]{:S(2)}) collective-permute-start(bf16[2,144,384]{2,1,0:T(8,128)(2,1)S(1)} %maximum_select_fusion.18), channel_id=1, source_target_pairs={{0,4},{4,0},{8,12},{12,8},{64,68},{68,64},{72,76},{76,72},{1,5},{5... | collective-permute-start | bytes 663560 | tf_op jit(solution)/shard_map/ppermute | solution.py:38
  23.3 9.9 %collective-permute-start.12 = (bf16[2,2,80,384]{3,2,1,0:T(8,128)(2,1)S(1)}, bf16[2,2,80,384]{3,2,1,0:T(8,128)(2,1)S(1)}, u32[]{:S(2)}, u32[]{:S(2)}) collective-permute-start(bf16[2,2,80,384]{3,2,1,0:T(8,128)(2,1)S(1)} %maximum_select_fusion.14), channel_id=1, source_target_pairs={{0,1},{1,0},{2,3},{3,2},{16,17},{17,16},{18,19},{19,18},{32,33},{3... | collective-permute-start | bytes 737288 | tf_op jit(solution)/shard_map/ppermute | solution.py:38
  24.1 8.3 %collective-permute-start.8 = (bf16[2,2,80,384]{3,2,1,0:T(8,128)(2,1)S(1)}, bf16[2,2,80,384]{3,2,1,0:T(8,128)(2,1)S(1)}, u32[]{:S(2)}, u32[]{:S(2)}) collective-permute-start(bf16[2,2,80,384]{3,2,1,0:T(8,128)(2,1)S(1)} %maximum_select_fusion.12), channel_id=1, source_target_pairs={{0,16},{1,17},{2,18},{3,19},{16,0},{17,1},{18,2},{19,3},{32,48},{3... | collective-permute-start | bytes 737288 | tf_op jit(solution)/shard_map/ppermute | solution.py:38
  31.5 3.1 %collective-permute-start.5 = (bf16[2,2,144,384]{3,2,1,0:T(8,128)(2,1)S(1)}, bf16[2,2,144,384]{3,2,1,0:T(8,128)(2,1)S(1)}, u32[]{:S(2)}, u32[]{:S(2)}) collective-permute-start(bf16[2,2,144,384]{3,2,1,0:T(8,128)(2,1)S(1)} %maximum_select_fusion.10), channel_id=1, source_target_pairs={{0,8},{4,12},{8,0},{12,4},{64,72},{68,76},{72,64},{76,68},{1,9},{5... | collective-permute-start | bytes 1327112 | tf_op jit(solution)/shard_map/ppermute | solution.py:38
  31.7 3.2 %collective-permute-start.2 = (bf16[2,2,144,384]{3,2,1,0:T(8,128)(2,1)S(1)}, bf16[2,2,144,384]{3,2,1,0:T(8,128)(2,1)S(1)}, u32[]{:S(2)}, u32[]{:S(2)}) collective-permute-start(bf16[2,2,144,384]{3,2,1,0:T(8,128)(2,1)S(1)} %maximum_select_fusion.8), channel_id=1, source_target_pairs={{0,8},{4,12},{8,0},{12,4},{64,72},{68,76},{72,64},{76,68},{1,9},{5... | collective-permute-start | bytes 1327112 | tf_op jit(solution)/shard_map/ppermute | solution.py:38
  32.6 14.0 %collective-permute-start.9 = (bf16[2,2,2,80,384]{4,3,2,1,0:T(8,128)(2,1)S(1)}, bf16[2,2,2,80,384]{4,3,2,1,0:T(8,128)(2,1)S(1)}, u32[]{:S(2)}, u32[]{:S(2)}) collective-permute-start(bf16[2,2,2,80,384]{4,3,2,1,0:T(8,128)(2,1)S(1)} %maximum_select_fusion.4), channel_id=1, source_target_pairs={{0,1},{1,0},{2,3},{3,2},{16,17},{17,16},{18,19},{19,18},{32,33},{3... | collective-permute-start | bytes 1474568 | tf_op jit(solution)/shard_map/ppermute | solution.py:38
  33.3 12.9 %collective-permute-start.13 = (bf16[2,2,2,80,384]{4,3,2,1,0:T(8,128)(2,1)S(1)}, bf16[2,2,2,80,384]{4,3,2,1,0:T(8,128)(2,1)S(1)}, u32[]{:S(2)}, u32[]{:S(2)}) collective-permute-start(bf16[2,2,2,80,384]{4,3,2,1,0:T(8,128)(2,1)S(1)} %maximum_select_fusion.6), channel_id=1, source_target_pairs={{0,16},{1,17},{2,18},{3,19},{16,0},{17,1},{18,2},{19,3},{32,48},{3... | collective-permute-start | bytes 1474568 | tf_op jit(solution)/shard_map/ppermute | solution.py:38
  51.7 8.6 %all-to-all-start = ((f32[8,1,1024]{2,1,0:T(1,128)}), f32[8,1,1024]{2,1,0:T(1,128)S(1)}, u32[]{:S(2)}, u32[]{:S(2)}) async-start(f32[8,1,1024]{2,1,0:T(1,128)} %broadcast_in_dim.36), calls=%async_computation | async-start | bytes 65536 | tf_op jit(solution)/shard_map/all_to_all | solution.py:31
  61.5 12.1 %all-to-all-start.1 = ((f32[16,1,1024]{2,1,0:T(1,128)}), f32[16,1,1024]{2,1,0:T(1,128)S(1)}, u32[]{:S(2)}, u32[]{:S(2)}) async-start(f32[16,1,1024]{2,1,0:T(1,128)} %broadcast_in_dim.37), calls=%async_computation.1 | async-start | bytes 131072 | tf_op jit(solution)/shard_map/all_to_all | solution.py:31
  125.1 11.5 %all-to-all-start.7 = ((f32[16,2,1024]{2,1,0:T(2,128)}), f32[16,2,1024]{2,1,0:T(2,128)S(1)}, u32[]{:S(2)}, u32[]{:S(2)}) async-start(f32[16,2,1024]{2,1,0:T(2,128)} %broadcast_in_dim.43), calls=%async_computation.7 | async-start | bytes 262144 | tf_op jit(solution)/shard_map/all_to_all | solution.py:31
  188.4 11.1 %all-to-all-start.13 = ((f32[16,1,1024]{2,1,0:T(1,128)}), f32[16,1,1024]{2,1,0:T(1,128)S(1)}, u32[]{:S(2)}, u32[]{:S(2)}) async-start(f32[16,1,1024]{2,1,0:T(1,128)} %broadcast_in_dim.49), calls=%async_computation.13 | async-start | bytes 131072 | tf_op jit(solution)/shard_map/all_to_all | solution.py:31
  200.7 8.6 %all-to-all-start.14 = ((f32[8,1,1024]{2,1,0:T(1,128)}), f32[8,1,1024]{2,1,0:T(1,128)S(1)}, u32[]{:S(2)}, u32[]{:S(2)}) async-start(f32[8,1,1024]{2,1,0:T(1,128)} %broadcast_in_dim.50), calls=%async_computation.14 | async-start | bytes 65536 | tf_op jit(solution)/shard_map/all_to_all | solution.py:31
  218.0 3.7 %collective-permute-start.14 = (f32[2,2,128,384]{3,2,0,1:T(8,128)S(1)}, f32[2,2,128,384]{3,2,0,1:T(8,128)S(1)}, u32[]{:S(2)}, u32[]{:S(2)}) collective-permute-start(f32[2,2,128,384]{3,2,0,1:T(8,128)S(1)} %select_bitcast_fusion.3), channel_id=1, source_target_pairs={{0,8},{4,12},{8,0},{12,4},{64,72},{68,76},{72,64},{76,68},{1,9},{5... | collective-permute-start | bytes 2359304 | tf_op jit(solution)/shard_map/ppermute | solution.py:61
  218.5 19.6 %collective-permute-start.24 = (f32[2,2,2,64,384]{4,3,1,0,2:T(8,128)S(1)}, f32[2,2,2,64,384]{4,3,1,0,2:T(8,128)S(1)}, u32[]{:S(2)}, u32[]{:S(2)}) collective-permute-start(f32[2,2,2,64,384]{4,3,1,0,2:T(8,128)S(1)} %select_bitcast_fusion), channel_id=1, source_target_pairs={{0,16},{1,17},{2,18},{3,19},{16,0},{17,1},{18,2},{19,3},{32,48},{3... | collective-permute-start | bytes 2359304 | tf_op jit(solution)/shard_map/ppermute | solution.py:61
  219.3 19.7 %collective-permute-start.20 = (f32[2,2,2,64,384]{4,3,0,2,1:T(8,128)S(1)}, f32[2,2,2,64,384]{4,3,0,2,1:T(8,128)S(1)}, u32[]{:S(2)}, u32[]{:S(2)}) collective-permute-start(f32[2,2,2,64,384]{4,3,0,2,1:T(8,128)S(1)} %select_bitcast_fusion.1), channel_id=1, source_target_pairs={{0,1},{1,0},{2,3},{3,2},{16,17},{17,16},{18,19},{19,18},{32,33},{3... | collective-permute-start | bytes 2359304 | tf_op jit(solution)/shard_map/ppermute | solution.py:61
  220.2 20.3 %collective-permute-start.18 = (f32[2,128,384]{2,1,0:T(8,128)S(1)}, f32[2,128,384]{2,1,0:T(8,128)S(1)}, u32[]{:S(2)}, u32[]{:S(2)}) collective-permute-start(f32[2,128,384]{2,1,0:T(8,128)S(1)} %select_bitcast_fusion.6), channel_id=1, source_target_pairs={{0,4},{4,0},{8,12},{12,8},{64,68},{68,64},{72,76},{76,72},{1,5},{5... | collective-permute-start | bytes 1179656 | tf_op jit(solution)/shard_map/ppermute | solution.py:61
  221.8 19.5 %collective-permute-start.15 = (f32[2,128,384]{2,1,0:T(8,128)S(1)}, f32[2,128,384]{2,1,0:T(8,128)S(1)}, u32[]{:S(2)}, u32[]{:S(2)}) collective-permute-start(f32[2,128,384]{2,1,0:T(8,128)S(1)} %select_bitcast_fusion.7), channel_id=1, source_target_pairs={{0,64},{4,68},{8,72},{12,76},{64,0},{68,4},{72,8},{76,12},{1,65},{... | collective-permute-start | bytes 1179656 | tf_op jit(solution)/shard_map/ppermute | solution.py:61
  238.4 10.4 %collective-permute-start.25 = (f32[2,2,64,384]{3,2,1,0:T(8,128)S(1)}, f32[2,2,64,384]{3,2,1,0:T(8,128)S(1)}, u32[]{:S(2)}, u32[]{:S(2)}) collective-permute-start(f32[2,2,64,384]{3,2,1,0:T(8,128)S(1)} %select_bitcast_fusion.4), channel_id=1, source_target_pairs={{0,1},{1,0},{2,3},{3,2},{16,17},{17,16},{18,19},{19,18},{32,33},{3... | collective-permute-start | bytes 1179656 | tf_op jit(solution)/shard_map/ppermute | solution.py:61
  239.2 10.9 %collective-permute-start.21 = (f32[2,2,64,384]{3,2,0,1:T(8,128)S(1)}, f32[2,2,64,384]{3,2,0,1:T(8,128)S(1)}, u32[]{:S(2)}, u32[]{:S(2)}) collective-permute-start(f32[2,2,64,384]{3,2,0,1:T(8,128)S(1)} %select_bitcast_fusion.5), channel_id=1, source_target_pairs={{0,16},{1,17},{2,18},{3,19},{16,0},{17,1},{18,2},{19,3},{32,48},{3... | collective-permute-start | bytes 1179656 | tf_op jit(solution)/shard_map/ppermute | solution.py:61
  240.6 20.4 %collective-permute-start.19 = (f32[128,384]{1,0:T(8,128)S(1)}, f32[128,384]{1,0:T(8,128)S(1)}, u32[]{:S(2)}, u32[]{:S(2)}) collective-permute-start(f32[128,384]{1,0:T(8,128)S(1)} %select_bitcast_fusion.10), channel_id=1, source_target_pairs={{0,64},{4,68},{8,72},{12,76},{64,0},{68,4},{72,8},{76,12},{1,65},{... | collective-permute-start | bytes 589832 | tf_op jit(solution)/shard_map/ppermute | solution.py:61
  241.4 19.7 %collective-permute-start.16 = (f32[128,384]{1,0:T(8,128)S(1)}, f32[128,384]{1,0:T(8,128)S(1)}, u32[]{:S(2)}, u32[]{:S(2)}) collective-permute-start(f32[128,384]{1,0:T(8,128)S(1)} %select_bitcast_fusion.11), channel_id=1, source_target_pairs={{0,4},{4,0},{8,12},{12,8},{64,68},{68,64},{72,76},{76,72},{1,5},{5... | collective-permute-start | bytes 589832 | tf_op jit(solution)/shard_map/ppermute | solution.py:61
  248.8 7.3 %collective-permute-start.26 = (f32[2,64,384]{2,1,0:T(8,128)S(1)}, f32[2,64,384]{2,1,0:T(8,128)S(1)}, u32[]{:S(2)}, u32[]{:S(2)}) collective-permute-start(f32[2,64,384]{2,1,0:T(8,128)S(1)} %select_bitcast_fusion.8), channel_id=1, source_target_pairs={{0,32},{1,33},{2,34},{3,35},{16,48},{17,49},{18,50},{19,51},{32,0}... | collective-permute-start | bytes 589832 | tf_op jit(solution)/shard_map/ppermute | solution.py:61
  250.2 7.4 %collective-permute-start.22 = (f32[2,64,384]{2,1,0:T(8,128)S(1)}, f32[2,64,384]{2,1,0:T(8,128)S(1)}, u32[]{:S(2)}, u32[]{:S(2)}) collective-permute-start(f32[2,64,384]{2,1,0:T(8,128)S(1)} %select_bitcast_fusion.9), channel_id=1, source_target_pairs={{0,2},{1,3},{2,0},{3,1},{16,18},{17,19},{18,16},{19,17},{32,34},{3... | collective-permute-start | bytes 589832 | tf_op jit(solution)/shard_map/ppermute | solution.py:61
  256.1 6.2 %collective-permute-start.27 = (f32[64,384]{1,0:T(8,128)S(1)}, f32[64,384]{1,0:T(8,128)S(1)}, u32[]{:S(2)}, u32[]{:S(2)}) collective-permute-start(f32[64,384]{1,0:T(8,128)S(1)} %select_bitcast_fusion.12), channel_id=1, source_target_pairs={{0,2},{1,3},{2,0},{3,1},{16,18},{17,19},{18,16},{19,17},{32,34},{3... | collective-permute-start | bytes 294920 | tf_op jit(solution)/shard_map/ppermute | solution.py:61
  257.6 6.2 %collective-permute-start.23 = (f32[64,384]{1,0:T(8,128)S(1)}, f32[64,384]{1,0:T(8,128)S(1)}, u32[]{:S(2)}, u32[]{:S(2)}) collective-permute-start(f32[64,384]{1,0:T(8,128)S(1)} %select_bitcast_fusion.13), channel_id=1, source_target_pairs={{0,32},{1,33},{2,34},{3,35},{16,48},{17,49},{18,50},{19,51},{32,0}... | collective-permute-start | bytes 294920 | tf_op jit(solution)/shard_map/ppermute | solution.py:61
  (5 other events, 23.4 us)

commit v7 on v5

--- a/solution.py
+++ b/solution.py
@@ -65,7 +65,7 @@
 
 def column_parts(width, axis):
     if axis == COLS:
-        return ((0, 2 * width // 3), (2 * width // 3, width))
+        return ((0, width // 3), (width // 3, width))
     return ((0, width // 2), (width // 2, width))
 
 

time: 292 us -> 294 us (level)
  other arithmetic: 28.4 us -> 32.4 us
  transfers between devices with their start and end apart: 31 -> 31, of which waited for: 17 -> 17; matrix products, arithmetic and copies ran while one was open for 3% -> 4% of each run, Pallas kernels for 0% -> 0%
where the time goes in v7:
time: 294 us; the launch traced here: 293 us
  blocking collectives  108 us (37%)
  waiting for transfers between devices  96.4 us (33%)
  starting transfers between devices  42.6 us (14%)
  other arithmetic  32.4 us (11%)
  matrix products  7.5 us (3%)
  local copies, waits for them, and re-layouts  4.38 us (1%)
    all_to_all x12, blocking collectives, tree_sum(): return lax.all_to_all(spread, axis, 0, 0, tiled=False).sum(0)  108 us
    ppermute x14, waiting for transfers between devices, tree_scatter(): x = keep + lax.ppermute(send, axis, partner(axis, n, bit))  55.3 us
    ppermute x14, waiting for transfers between devices, tree_gather(): other = lax.ppermute(x, axis, partner(axis, n, bit))  21.6 us
    all_to_all x3, waiting for transfers between devices, tree_sum(): return lax.all_to_all(spread, axis, 0, 0, tiled=False).sum(0)  19.5 us
    ppermute x14, starting transfers between devices, tree_gather(): other = lax.ppermute(x, axis, partner(axis, n, bit))  19 us
    ppermute x14, starting transfers between devices, tree_scatter(): x = keep + lax.ppermute(send, axis, partner(axis, n, bit))  13 us
    all_to_all x3, starting transfers between devices, tree_sum(): return lax.all_to_all(spread, axis, 0, 0, tiled=False).sum(0)  10.7 us
    reduce_sum x8, other arithmetic, times_vector(): return jnp.sum(kernel.astype(jnp.float32) * vector[None, :], axis=1)  6.72 us
  transfers between devices with their start and end apart: 31, of which 17 were waited for; matrix products, arithmetic and copies ran while one was open for 4% of the time, Pallas kernels for 0%

profile of v7, /device:TPU:0, one launch (start us, length us, event | category | flops | bytes accessed | tf_op | source)
XLA Modules:
  0.0 292.6 jit_solution(7961679323914463929)
XLA Ops:
  5.6 4.0 %collective-permute-start.10 = (bf16[80,512]{1,0:T(8,128)(2,1)S(1)}, bf16[80,512]{1,0:T(8,128)(2,1)S(1)}, u32[]{:S(2)}, u32[]{:S(2)}) collective-permute-start(bf16[80,512]{1,0:T(8,128)(2,1)S(1)} %get-tuple-element.33), channel_id=1, source_target_pairs={{0,32},{1,33},{2,34},{3,35},{16,48},{17,49},{18,50},{19,51},{32,0}... | collective-permute-start | bytes 245768 | tf_op jit(solution)/shard_map/ppermute | solution.py:38
  16.8 3.8 %collective-permute-done = bf16[144,384]{1,0:T(8,128)(2,1)S(1)} collective-permute-done((bf16[144,384]{1,0:T(8,128)(2,1)S(1)}, bf16[144,384]{1,0:T(8,128)(2,1)S(1)}, u32[]{:S(2)}, u32[]{:S(2)}) %collective-permute-start) | collective-permute-done | bytes 110624 | tf_op jit(solution)/shard_map/ppermute | solution.py:38
  25.3 3.4 %collective-permute-done.8 = bf16[2,2,80,256]{3,2,1,0:T(8,128)(2,1)S(1)} collective-permute-done((bf16[2,2,80,256]{3,2,1,0:T(8,128)(2,1)S(1)}, bf16[2,2,80,256]{3,2,1,0:T(8,128)(2,1)S(1)}, u32[]{:S(2)}, u32[]{:S(2)}) %collective-permute-start.8) | collective-permute-done | bytes 163872 | tf_op jit(solution)/shard_map/ppermute | solution.py:38
  42.0 8.7 %collective-permute-done.13 = bf16[2,2,2,80,512]{4,3,2,1,0:T(8,128)(2,1)S(1)} collective-permute-done((bf16[2,2,2,80,512]{4,3,2,1,0:T(8,128)(2,1)S(1)}, bf16[2,2,2,80,512]{4,3,2,1,0:T(8,128)(2,1)S(1)}, u32[]{:S(2)}, u32[]{:S(2)}) %collective-permute-start.13) | collective-permute-done | bytes 655392 | tf_op jit(solution)/shard_map/ppermute | solution.py:38
  51.2 3.8 %exponential_convert_fusion = (bf16[1024,1024]{1,0:T(8,128)(2,1)S(1)}, f32[1024,1024]{1,0:T(8,128)}) fusion(bf16[1024,768]{1,0:T(8,128)(2,1)S(1)} %bitcast.173, bf16[1024,768]{1,0:T(8,128)(2,1)S(1)} %bitcast.171), kind=kOutput, calls=%fused_computation.34 | convolution fusion | flops 1612709888 | bytes 9437184 | tf_op jit(solution)/shard_map/dot_general | solution.py:140
  59.4 5.2 %all-to-all-done = f32[8,1,1024]{2,1,0:T(1,128)S(1)} async-done(((f32[8,1,1024]{2,1,0:T(1,128)}), f32[8,1,1024]{2,1,0:T(1,128)S(1)}, u32[]{:S(2)}, u32[]{:S(2)}) %all-to-all-start) | async-done | bytes 32800 | tf_op jit(solution)/shard_map/all_to_all | solution.py:31
  65.8 3.8 %all-to-all-start.1 = ((f32[16,1,1024]{2,1,0:T(1,128)}), f32[16,1,1024]{2,1,0:T(1,128)S(1)}, u32[]{:S(2)}, u32[]{:S(2)}) async-start(f32[16,1,1024]{2,1,0:T(1,128)} %broadcast_in_dim.37), calls=%async_computation.1 | async-start | bytes 131072 | tf_op jit(solution)/shard_map/all_to_all | solution.py:31
  70.8 6.4 %all-to-all-done.1 = f32[16,1,1024]{2,1,0:T(1,128)S(1)} async-done(((f32[16,1,1024]{2,1,0:T(1,128)}), f32[16,1,1024]{2,1,0:T(1,128)S(1)}, u32[]{:S(2)}, u32[]{:S(2)}) %all-to-all-start.1) | async-done | bytes 65568 | tf_op jit(solution)/shard_map/all_to_all | solution.py:31
  77.8 7.7 %all_to_all.89 = f32[8,1,1024]{2,1,0:T(1,128)S(1)} all-to-all(f32[8,1,1024]{2,1,0:T(1,128)S(1)} %broadcast_in_dim.38), channel_id=1, replica_groups=mesh['y_lo'=2,'z'=4,'core'=2,'y_hi'=2,'x'=4] {'y_lo','core','y_hi'}, dimensions={0} | all-to-all | bytes 65536 | tf_op jit(solution)/shard_map/all_to_all | solution.py:31
  86.1 10.8 %all_to_all.90 = f32[16,1,1024]{2,1,0:T(1,128)S(1)} all-to-all(f32[16,1,1024]{2,1,0:T(1,128)S(1)} %broadcast_in_dim.39), channel_id=1, replica_groups=mesh['y_lo'=2,'z'=4,'core'=2,'y_hi'=2,'x'=4] {'z','x'}, dimensions={0} | all-to-all | bytes 131072 | tf_op jit(solution)/shard_map/all_to_all | solution.py:31
  97.5 7.7 %all_to_all.91 = f32[8,1,1024]{2,1,0:T(1,128)S(1)} all-to-all(f32[8,1,1024]{2,1,0:T(1,128)S(1)} %broadcast_in_dim.40), channel_id=1, replica_groups=mesh['y_lo'=2,'z'=4,'core'=2,'y_hi'=2,'x'=4] {'y_lo','core','y_hi'}, dimensions={0} | all-to-all | bytes 65536 | tf_op jit(solution)/shard_map/all_to_all | solution.py:31
  105.7 10.8 %all_to_all.92 = f32[16,1,1024]{2,1,0:T(1,128)S(1)} all-to-all(f32[16,1,1024]{2,1,0:T(1,128)S(1)} %broadcast_in_dim.41), channel_id=1, replica_groups=mesh['y_lo'=2,'z'=4,'core'=2,'y_hi'=2,'x'=4] {'z','x'}, dimensions={0} | all-to-all | bytes 131072 | tf_op jit(solution)/shard_map/all_to_all | solution.py:31
  117.1 7.7 %all_to_all.93 = f32[8,1,1024]{2,1,0:T(1,128)S(1)} all-to-all(f32[8,1,1024]{2,1,0:T(1,128)S(1)} %broadcast_in_dim.42), channel_id=1, replica_groups=mesh['y_lo'=2,'z'=4,'core'=2,'y_hi'=2,'x'=4] {'y_lo','core','y_hi'}, dimensions={0} | all-to-all | bytes 65536 | tf_op jit(solution)/shard_map/all_to_all | solution.py:31
  128.8 3.5 %all-to-all-start.7 = ((f32[16,2,1024]{2,1,0:T(2,128)}), f32[16,2,1024]{2,1,0:T(2,128)S(1)}, u32[]{:S(2)}, u32[]{:S(2)}) async-start(f32[16,2,1024]{2,1,0:T(2,128)} %broadcast_in_dim.43), calls=%async_computation.7 | async-start | bytes 262144 | tf_op jit(solution)/shard_map/all_to_all | solution.py:31
  132.4 7.9 %all-to-all-done.7 = f32[16,2,1024]{2,1,0:T(2,128)S(1)} async-done(((f32[16,2,1024]{2,1,0:T(2,128)}), f32[16,2,1024]{2,1,0:T(2,128)S(1)}, u32[]{:S(2)}, u32[]{:S(2)}) %all-to-all-start.7) | async-done | bytes 131104 | tf_op jit(solution)/shard_map/all_to_all | solution.py:31
  140.3 3.5 %multiply_reduce_fusion = (f32[1024]{0:T(1024)S(1)}, f32[1024]{0:T(1024)S(1)}) fusion(f32[1024,1024]{1,0:T(8,128)} %get-tuple-element.41, bf16[1024,1024]{1,0:T(8,128)(2,1)S(1)} %get-tuple-element.40, f32[1024]{0:T(1024)S(1)} %bitcast.205, f32[1024]{0:T(1024)S(1)} %bitcast.203), kind=kLoop, calls=%fused_computation.32 | loop fusion | flops 7337984 | bytes 6307840 | tf_op jit(solution)/shard_map/reduce_sum | solution.py:122
  143.8 7.7 %all_to_all.94 = f32[8,1,1024]{2,1,0:T(1,128)S(1)} all-to-all(f32[8,1,1024]{2,1,0:T(1,128)S(1)} %broadcast_in_dim.44), channel_id=1, replica_groups=mesh['y_lo'=2,'z'=4,'core'=2,'y_hi'=2,'x'=4] {'y_lo','core','y_hi'}, dimensions={0} | all-to-all | bytes 65536 | tf_op jit(solution)/shard_map/all_to_all | solution.py:31
  152.1 10.7 %all_to_all.95 = f32[16,1,1024]{2,1,0:T(1,128)S(1)} all-to-all(f32[16,1,1024]{2,1,0:T(1,128)S(1)} %broadcast_in_dim.45), channel_id=1, replica_groups=mesh['y_lo'=2,'z'=4,'core'=2,'y_hi'=2,'x'=4] {'z','x'}, dimensions={0} | all-to-all | bytes 131072 | tf_op jit(solution)/shard_map/all_to_all | solution.py:31
  163.4 7.7 %all_to_all.96 = f32[8,1,1024]{2,1,0:T(1,128)S(1)} all-to-all(f32[8,1,1024]{2,1,0:T(1,128)S(1)} %broadcast_in_dim.46), channel_id=1, replica_groups=mesh['y_lo'=2,'z'=4,'core'=2,'y_hi'=2,'x'=4] {'y_lo','core','y_hi'}, dimensions={0} | all-to-all | bytes 65536 | tf_op jit(solution)/shard_map/all_to_all | solution.py:31
  171.7 10.8 %all_to_all.97 = f32[16,1,1024]{2,1,0:T(1,128)S(1)} all-to-all(f32[16,1,1024]{2,1,0:T(1,128)S(1)} %broadcast_in_dim.47), channel_id=1, replica_groups=mesh['y_lo'=2,'z'=4,'core'=2,'y_hi'=2,'x'=4] {'z','x'}, dimensions={0} | all-to-all | bytes 131072 | tf_op jit(solution)/shard_map/all_to_all | solution.py:31
  183.1 7.7 %all_to_all.98 = f32[8,1,1024]{2,1,0:T(1,128)S(1)} all-to-all(f32[8,1,1024]{2,1,0:T(1,128)S(1)} %broadcast_in_dim.48), channel_id=1, replica_groups=mesh['y_lo'=2,'z'=4,'core'=2,'y_hi'=2,'x'=4] {'y_lo','core','y_hi'}, dimensions={0} | all-to-all | bytes 65536 | tf_op jit(solution)/shard_map/all_to_all | solution.py:31
  191.4 10.8 %all_to_all.99 = f32[16,1,1024]{2,1,0:T(1,128)S(1)} all-to-all(f32[16,1,1024]{2,1,0:T(1,128)S(1)} %broadcast_in_dim.49), channel_id=1, replica_groups=mesh['y_lo'=2,'z'=4,'core'=2,'y_hi'=2,'x'=4] {'z','x'}, dimensions={0} | all-to-all | bytes 131072 | tf_op jit(solution)/shard_map/all_to_all | solution.py:31
  202.7 7.7 %all_to_all.100 = f32[8,1,1024]{2,1,0:T(1,128)S(1)} all-to-all(f32[8,1,1024]{2,1,0:T(1,128)S(1)} %broadcast_in_dim.50), channel_id=1, replica_groups=mesh['y_lo'=2,'z'=4,'core'=2,'y_hi'=2,'x'=4] {'y_lo','core','y_hi'}, dimensions={0} | all-to-all | bytes 65536 | tf_op jit(solution)/shard_map/all_to_all | solution.py:31
  210.5 5.4 %fusion.14 = bf16[1024,1024]{1,0:T(8,128)(2,1)S(1)} fusion(bf16[1024,1024]{1,0:T(8,128)(2,1)S(1)} %get-tuple-element.40, f32[1024,1024]{1,0:T(8,128)} %get-tuple-element.41, f32[1024]{0:T(1024)S(1)} %multiply_divide_fusion, f32[1024]{0:T(1024)S(1)} %multiply_divide_fusion.1, f32[1024]{0:T(1024)S(1)} %multiply_divide_fusion.2, ...), kind=kLoop, calls=%fused_computation.31 | loop fusion | flops 23068672 | bytes 8454144 | tf_op jit(solution)/shard_map/convert_element_type | solution.py:189
  223.1 12.3 %collective-permute-done.20 = f32[2,2,2,64,256]{4,3,0,2,1:T(8,128)S(1)} collective-permute-done((f32[2,2,2,64,256]{4,3,0,2,1:T(8,128)S(1)}, f32[2,2,2,64,256]{4,3,0,2,1:T(8,128)S(1)}, u32[]{:S(2)}, u32[]{:S(2)}) %collective-permute-start.20) | collective-permute-done | bytes 524320 | tf_op jit(solution)/shard_map/ppermute | solution.py:61
  237.4 15.9 %collective-permute-done.21 = f32[2,2,64,256]{3,2,0,1:T(8,128)S(1)} collective-permute-done((f32[2,2,64,256]{3,2,0,1:T(8,128)S(1)}, f32[2,2,64,256]{3,2,0,1:T(8,128)S(1)}, u32[]{:S(2)}, u32[]{:S(2)}) %collective-permute-start.21) | collective-permute-done | bytes 262176 | tf_op jit(solution)/shard_map/ppermute | solution.py:61
  255.5 4.5 %collective-permute-done.22 = f32[2,64,256]{2,1,0:T(8,128)S(1)} collective-permute-done((f32[2,64,256]{2,1,0:T(8,128)S(1)}, f32[2,64,256]{2,1,0:T(8,128)S(1)}, u32[]{:S(2)}, u32[]{:S(2)}) %collective-permute-start.22) | collective-permute-done | bytes 131104 | tf_op jit(solution)/shard_map/ppermute | solution.py:61
  262.0 3.9 %collective-permute-done.23 = f32[64,256]{1,0:T(8,128)S(1)} collective-permute-done((f32[64,256]{1,0:T(8,128)S(1)}, f32[64,256]{1,0:T(8,128)S(1)}, u32[]{:S(2)}, u32[]{:S(2)}) %collective-permute-start.23) | collective-permute-done | bytes 65568 | tf_op jit(solution)/shard_map/ppermute | solution.py:61
  268.4 3.8 %collective-permute-done.15 = f32[2,128,384]{2,1,0:T(8,128)S(1)} collective-permute-done((f32[2,128,384]{2,1,0:T(8,128)S(1)}, f32[2,128,384]{2,1,0:T(8,128)S(1)}, u32[]{:S(2)}, u32[]{:S(2)}) %collective-permute-start.15) | collective-permute-done | bytes 393248 | tf_op jit(solution)/shard_map/ppermute | solution.py:61
  272.3 4.8 %collective-permute-done.25 = f32[2,2,64,512]{3,2,1,0:T(8,128)S(1)} collective-permute-done((f32[2,2,64,512]{3,2,1,0:T(8,128)S(1)}, f32[2,2,64,512]{3,2,1,0:T(8,128)S(1)}, u32[]{:S(2)}, u32[]{:S(2)}) %collective-permute-start.25) | collective-permute-done | bytes 524320 | tf_op jit(solution)/shard_map/ppermute | solution.py:61
  279.2 6.1 %collective-permute-done.26 = f32[2,64,512]{2,1,0:T(8,128)S(1)} collective-permute-done((f32[2,64,512]{2,1,0:T(8,128)S(1)}, f32[2,64,512]{2,1,0:T(8,128)S(1)}, u32[]{:S(2)}, u32[]{:S(2)}) %collective-permute-start.26) | collective-permute-done | bytes 262176 | tf_op jit(solution)/shard_map/ppermute | solution.py:61
  287.9 4.0 %collective-permute-done.27 = f32[64,512]{1,0:T(8,128)S(1)} collective-permute-done((f32[64,512]{1,0:T(8,128)S(1)}, f32[64,512]{1,0:T(8,128)S(1)}, u32[]{:S(2)}, u32[]{:S(2)}) %collective-permute-start.27) | collective-permute-done | bytes 131104 | tf_op jit(solution)/shard_map/ppermute | solution.py:61
  (211 shorter events, 68.7 us)
Async XLA Ops:
  2.4 13.5 %collective-permute-start.6 = (bf16[80,256]{1,0:T(8,128)(2,1)S(1)}, bf16[80,256]{1,0:T(8,128)(2,1)S(1)}, u32[]{:S(2)}, u32[]{:S(2)}) collective-permute-start(bf16[80,256]{1,0:T(8,128)(2,1)S(1)} %get-tuple-element.30), channel_id=1, source_target_pairs={{0,2},{1,3},{2,0},{3,1},{16,18},{17,19},{18,16},{19,17},{32,34},{3... | collective-permute-start | bytes 122888 | tf_op jit(solution)/shard_map/ppermute | solution.py:38
  5.6 10.5 %collective-permute-start.10 = (bf16[80,512]{1,0:T(8,128)(2,1)S(1)}, bf16[80,512]{1,0:T(8,128)(2,1)S(1)}, u32[]{:S(2)}, u32[]{:S(2)}) collective-permute-start(bf16[80,512]{1,0:T(8,128)(2,1)S(1)} %get-tuple-element.33), channel_id=1, source_target_pairs={{0,32},{1,33},{2,34},{3,35},{16,48},{17,49},{18,50},{19,51},{32,0}... | collective-permute-start | bytes 245768 | tf_op jit(solution)/shard_map/ppermute | solution.py:38
  11.4 9.5 %collective-permute-start.3 = (bf16[144,384]{1,0:T(8,128)(2,1)S(1)}, bf16[144,384]{1,0:T(8,128)(2,1)S(1)}, u32[]{:S(2)}, u32[]{:S(2)}) collective-permute-start(bf16[144,384]{1,0:T(8,128)(2,1)S(1)} %get-tuple-element.26), channel_id=1, source_target_pairs={{0,64},{4,68},{8,72},{12,76},{64,0},{68,4},{72,8},{76,12},{1,65},{... | collective-permute-start | bytes 331784 | tf_op jit(solution)/shard_map/ppermute | solution.py:38
  13.0 7.5 %collective-permute-start = (bf16[144,384]{1,0:T(8,128)(2,1)S(1)}, bf16[144,384]{1,0:T(8,128)(2,1)S(1)}, u32[]{:S(2)}, u32[]{:S(2)}) collective-permute-start(bf16[144,384]{1,0:T(8,128)(2,1)S(1)} %get-tuple-element.27), channel_id=1, source_target_pairs={{0,4},{4,0},{8,12},{12,8},{64,68},{68,64},{72,76},{76,72},{1,5},{5... | collective-permute-start | bytes 331784 | tf_op jit(solution)/shard_map/ppermute | solution.py:38
  16.0 7.4 %collective-permute-start.7 = (bf16[2,80,256]{2,1,0:T(8,128)(2,1)S(1)}, bf16[2,80,256]{2,1,0:T(8,128)(2,1)S(1)}, u32[]{:S(2)}, u32[]{:S(2)}) collective-permute-start(bf16[2,80,256]{2,1,0:T(8,128)(2,1)S(1)} %maximum_select_fusion.22), channel_id=1, source_target_pairs={{0,32},{1,33},{2,34},{3,35},{16,48},{17,49},{18,50},{19,51},{32,0}... | collective-permute-start | bytes 245768 | tf_op jit(solution)/shard_map/ppermute | solution.py:38
  16.1 8.4 %collective-permute-start.11 = (bf16[2,80,512]{2,1,0:T(8,128)(2,1)S(1)}, bf16[2,80,512]{2,1,0:T(8,128)(2,1)S(1)}, u32[]{:S(2)}, u32[]{:S(2)}) collective-permute-start(bf16[2,80,512]{2,1,0:T(8,128)(2,1)S(1)} %maximum_select_fusion.20), channel_id=1, source_target_pairs={{0,2},{1,3},{2,0},{3,1},{16,18},{17,19},{18,16},{19,17},{32,34},{3... | collective-permute-start | bytes 491528 | tf_op jit(solution)/shard_map/ppermute | solution.py:38
  20.6 11.8 %collective-permute-start.1 = (bf16[2,144,384]{2,1,0:T(8,128)(2,1)S(1)}, bf16[2,144,384]{2,1,0:T(8,128)(2,1)S(1)}, u32[]{:S(2)}, u32[]{:S(2)}) collective-permute-start(bf16[2,144,384]{2,1,0:T(8,128)(2,1)S(1)} %maximum_select_fusion.14), channel_id=1, source_target_pairs={{0,64},{4,68},{8,72},{12,76},{64,0},{68,4},{72,8},{76,12},{1,65},{... | collective-permute-start | bytes 663560 | tf_op jit(solution)/shard_map/ppermute | solution.py:38
  20.9 10.6 %collective-permute-start.4 = (bf16[2,144,384]{2,1,0:T(8,128)(2,1)S(1)}, bf16[2,144,384]{2,1,0:T(8,128)(2,1)S(1)}, u32[]{:S(2)}, u32[]{:S(2)}) collective-permute-start(bf16[2,144,384]{2,1,0:T(8,128)(2,1)S(1)} %maximum_select_fusion.16), channel_id=1, source_target_pairs={{0,4},{4,0},{8,12},{12,8},{64,68},{68,64},{72,76},{76,72},{1,5},{5... | collective-permute-start | bytes 663560 | tf_op jit(solution)/shard_map/ppermute | solution.py:38
  23.4 5.4 %collective-permute-start.8 = (bf16[2,2,80,256]{3,2,1,0:T(8,128)(2,1)S(1)}, bf16[2,2,80,256]{3,2,1,0:T(8,128)(2,1)S(1)}, u32[]{:S(2)}, u32[]{:S(2)}) collective-permute-start(bf16[2,2,80,256]{3,2,1,0:T(8,128)(2,1)S(1)} %maximum_select_fusion.18), channel_id=1, source_target_pairs={{0,16},{1,17},{2,18},{3,19},{16,0},{17,1},{18,2},{19,3},{32,48},{3... | collective-permute-start | bytes 491528 | tf_op jit(solution)/shard_map/ppermute | solution.py:38
  24.6 10.6 %collective-permute-start.12 = (bf16[2,2,80,512]{3,2,1,0:T(8,128)(2,1)S(1)}, bf16[2,2,80,512]{3,2,1,0:T(8,128)(2,1)S(1)}, u32[]{:S(2)}, u32[]{:S(2)}) collective-permute-start(bf16[2,2,80,512]{3,2,1,0:T(8,128)(2,1)S(1)} %maximum_select_fusion.12), channel_id=1, source_target_pairs={{0,1},{1,0},{2,3},{3,2},{16,17},{17,16},{18,19},{19,18},{32,33},{3... | collective-permute-start | bytes 983048 | tf_op jit(solution)/shard_map/ppermute | solution.py:38
  28.8 10.1 %collective-permute-start.9 = (bf16[2,2,2,80,256]{4,3,2,1,0:T(8,128)(2,1)S(1)}, bf16[2,2,2,80,256]{4,3,2,1,0:T(8,128)(2,1)S(1)}, u32[]{:S(2)}, u32[]{:S(2)}) collective-permute-start(bf16[2,2,2,80,256]{4,3,2,1,0:T(8,128)(2,1)S(1)} %maximum_select_fusion.10), channel_id=1, source_target_pairs={{0,1},{1,0},{2,3},{3,2},{16,17},{17,16},{18,19},{19,18},{32,33},{3... | collective-permute-start | bytes 983048 | tf_op jit(solution)/shard_map/ppermute | solution.py:38
  32.4 6.7 %collective-permute-start.5 = (bf16[2,2,144,384]{3,2,1,0:T(8,128)(2,1)}, bf16[2,2,144,384]{3,2,1,0:T(8,128)(2,1)}, u32[]{:S(2)}, u32[]{:S(2)}) collective-permute-start(bf16[2,2,144,384]{3,2,1,0:T(8,128)(2,1)} %maximum_select_fusion.8), channel_id=1, source_target_pairs={{0,8},{4,12},{8,0},{12,4},{64,72},{68,76},{72,64},{76,68},{1,9},{5... | collective-permute-start | bytes 1327112 | tf_op jit(solution)/shard_map/ppermute | solution.py:38
  33.2 7.3 %collective-permute-start.2 = (bf16[2,2,144,384]{3,2,1,0:T(8,128)(2,1)}, bf16[2,2,144,384]{3,2,1,0:T(8,128)(2,1)}, u32[]{:S(2)}, u32[]{:S(2)}) collective-permute-start(bf16[2,2,144,384]{3,2,1,0:T(8,128)(2,1)} %maximum_select_fusion.6), channel_id=1, source_target_pairs={{0,8},{4,12},{8,0},{12,4},{64,72},{68,76},{72,64},{76,68},{1,9},{5... | collective-permute-start | bytes 1327112 | tf_op jit(solution)/shard_map/ppermute | solution.py:38
  35.3 15.4 %collective-permute-start.13 = (bf16[2,2,2,80,512]{4,3,2,1,0:T(8,128)(2,1)S(1)}, bf16[2,2,2,80,512]{4,3,2,1,0:T(8,128)(2,1)S(1)}, u32[]{:S(2)}, u32[]{:S(2)}) collective-permute-start(bf16[2,2,2,80,512]{4,3,2,1,0:T(8,128)(2,1)S(1)} %maximum_select_fusion.4), channel_id=1, source_target_pairs={{0,16},{1,17},{2,18},{3,19},{16,0},{17,1},{18,2},{19,3},{32,48},{3... | collective-permute-start | bytes 1966088 | tf_op jit(solution)/shard_map/ppermute | solution.py:38
  42.0 9.2 %copy-start.3 = (bf16[8,128,768]{2,1,0:T(8,128)(2,1)}, bf16[8,128,768]{2,1,0:T(8,128)(2,1)S(1)}, u32[]{:S(2)}) copy-start(bf16[8,128,768]{2,1,0:T(8,128)(2,1)S(1)} %pad_maximum_fusion.1) | copy-start | bytes 4718596
  56.0 8.6 %all-to-all-start = ((f32[8,1,1024]{2,1,0:T(1,128)}), f32[8,1,1024]{2,1,0:T(1,128)S(1)}, u32[]{:S(2)}, u32[]{:S(2)}) async-start(f32[8,1,1024]{2,1,0:T(1,128)} %broadcast_in_dim.36), calls=%async_computation | async-start | bytes 65536 | tf_op jit(solution)/shard_map/all_to_all | solution.py:31
  65.8 11.5 %all-to-all-start.1 = ((f32[16,1,1024]{2,1,0:T(1,128)}), f32[16,1,1024]{2,1,0:T(1,128)S(1)}, u32[]{:S(2)}, u32[]{:S(2)}) async-start(f32[16,1,1024]{2,1,0:T(1,128)} %broadcast_in_dim.37), calls=%async_computation.1 | async-start | bytes 131072 | tf_op jit(solution)/shard_map/all_to_all | solution.py:31
  128.8 11.5 %all-to-all-start.7 = ((f32[16,2,1024]{2,1,0:T(2,128)}), f32[16,2,1024]{2,1,0:T(2,128)S(1)}, u32[]{:S(2)}, u32[]{:S(2)}) async-start(f32[16,2,1024]{2,1,0:T(2,128)} %broadcast_in_dim.43), calls=%async_computation.7 | async-start | bytes 262144 | tf_op jit(solution)/shard_map/all_to_all | solution.py:31
  220.3 16.0 %collective-permute-start.17 = (f32[2,2,128,384]{3,2,0,1:T(8,128)S(1)}, f32[2,2,128,384]{3,2,0,1:T(8,128)S(1)}, u32[]{:S(2)}, u32[]{:S(2)}) collective-permute-start(f32[2,2,128,384]{3,2,0,1:T(8,128)S(1)} %select_bitcast_fusion.1), channel_id=1, source_target_pairs={{0,8},{4,12},{8,0},{12,4},{64,72},{68,76},{72,64},{76,68},{1,9},{5... | collective-permute-start | bytes 2359304 | tf_op jit(solution)/shard_map/ppermute | solution.py:61
  220.5 34.8 %collective-permute-start.14 = (f32[2,2,128,384]{3,2,0,1:T(8,128)S(1)}, f32[2,2,128,384]{3,2,0,1:T(8,128)S(1)}, u32[]{:S(2)}, u32[]{:S(2)}) collective-permute-start(f32[2,2,128,384]{3,2,0,1:T(8,128)S(1)} %select_bitcast_fusion.2), channel_id=1, source_target_pairs={{0,8},{4,12},{8,0},{12,4},{64,72},{68,76},{72,64},{76,68},{1,9},{5... | collective-permute-start | bytes 2359304 | tf_op jit(solution)/shard_map/ppermute | solution.py:61
  221.4 14.0 %collective-permute-start.20 = (f32[2,2,2,64,256]{4,3,0,2,1:T(8,128)S(1)}, f32[2,2,2,64,256]{4,3,0,2,1:T(8,128)S(1)}, u32[]{:S(2)}, u32[]{:S(2)}) collective-permute-start(f32[2,2,2,64,256]{4,3,0,2,1:T(8,128)S(1)} %select_bitcast_fusion.4), channel_id=1, source_target_pairs={{0,1},{1,0},{2,3},{3,2},{16,17},{17,16},{18,19},{19,18},{32,33},{3... | collective-permute-start | bytes 1572872 | tf_op jit(solution)/shard_map/ppermute | solution.py:61
  222.5 43.3 %collective-permute-start.24 = (f32[2,2,2,64,512]{4,3,1,0,2:T(8,128)S(1)}, f32[2,2,2,64,512]{4,3,1,0,2:T(8,128)S(1)}, u32[]{:S(2)}, u32[]{:S(2)}) collective-permute-start(f32[2,2,2,64,512]{4,3,1,0,2:T(8,128)S(1)} %select_bitcast_fusion), channel_id=1, source_target_pairs={{0,16},{1,17},{2,18},{3,19},{16,0},{17,1},{18,2},{19,3},{32,48},{3... | collective-permute-start | bytes 3145736 | tf_op jit(solution)/shard_map/ppermute | solution.py:61
  235.6 17.7 %collective-permute-start.21 = (f32[2,2,64,256]{3,2,0,1:T(8,128)S(1)}, f32[2,2,64,256]{3,2,0,1:T(8,128)S(1)}, u32[]{:S(2)}, u32[]{:S(2)}) collective-permute-start(f32[2,2,64,256]{3,2,0,1:T(8,128)S(1)} %select_bitcast_fusion.8), channel_id=1, source_target_pairs={{0,16},{1,17},{2,18},{3,19},{16,0},{17,1},{18,2},{19,3},{32,48},{3... | collective-permute-start | bytes 786440 | tf_op jit(solution)/shard_map/ppermute | solution.py:61
  236.4 31.3 %collective-permute-start.18 = (f32[2,128,384]{2,1,0:T(8,128)S(1)}, f32[2,128,384]{2,1,0:T(8,128)S(1)}, u32[]{:S(2)}, u32[]{:S(2)}) collective-permute-start(f32[2,128,384]{2,1,0:T(8,128)S(1)} %select_bitcast_fusion.5), channel_id=1, source_target_pairs={{0,4},{4,0},{8,12},{12,8},{64,68},{68,64},{72,76},{76,72},{1,5},{5... | collective-permute-start | bytes 1179656 | tf_op jit(solution)/shard_map/ppermute | solution.py:61
  253.4 6.6 %collective-permute-start.22 = (f32[2,64,256]{2,1,0:T(8,128)S(1)}, f32[2,64,256]{2,1,0:T(8,128)S(1)}, u32[]{:S(2)}, u32[]{:S(2)}) collective-permute-start(f32[2,64,256]{2,1,0:T(8,128)S(1)} %select_bitcast_fusion.12), channel_id=1, source_target_pairs={{0,2},{1,3},{2,0},{3,1},{16,18},{17,19},{18,16},{19,17},{32,34},{3... | collective-permute-start | bytes 393224 | tf_op jit(solution)/shard_map/ppermute | solution.py:61
  260.0 5.8 %collective-permute-start.23 = (f32[64,256]{1,0:T(8,128)S(1)}, f32[64,256]{1,0:T(8,128)S(1)}, u32[]{:S(2)}, u32[]{:S(2)}) collective-permute-start(f32[64,256]{1,0:T(8,128)S(1)} %select_bitcast_fusion.13), channel_id=1, source_target_pairs={{0,32},{1,33},{2,34},{3,35},{16,48},{17,49},{18,50},{19,51},{32,0}... | collective-permute-start | bytes 196616 | tf_op jit(solution)/shard_map/ppermute | solution.py:61
  261.3 11.0 %collective-permute-start.15 = (f32[2,128,384]{2,1,0:T(8,128)S(1)}, f32[2,128,384]{2,1,0:T(8,128)S(1)}, u32[]{:S(2)}, u32[]{:S(2)}) collective-permute-start(f32[2,128,384]{2,1,0:T(8,128)S(1)} %select_bitcast_fusion.6), channel_id=1, source_target_pairs={{0,64},{4,68},{8,72},{12,76},{64,0},{68,4},{72,8},{76,12},{1,65},{... | collective-permute-start | bytes 1179656 | tf_op jit(solution)/shard_map/ppermute | solution.py:61
  266.3 10.8 %collective-permute-start.25 = (f32[2,2,64,512]{3,2,1,0:T(8,128)S(1)}, f32[2,2,64,512]{3,2,1,0:T(8,128)S(1)}, u32[]{:S(2)}, u32[]{:S(2)}) collective-permute-start(f32[2,2,64,512]{3,2,1,0:T(8,128)S(1)} %select_bitcast_fusion.3), channel_id=1, source_target_pairs={{0,1},{1,0},{2,3},{3,2},{16,17},{17,16},{18,19},{19,18},{32,33},{3... | collective-permute-start | bytes 1572872 | tf_op jit(solution)/shard_map/ppermute | solution.py:61
  267.8 11.4 %collective-permute-start.19 = (f32[128,384]{1,0:T(8,128)S(1)}, f32[128,384]{1,0:T(8,128)S(1)}, u32[]{:S(2)}, u32[]{:S(2)}) collective-permute-start(f32[128,384]{1,0:T(8,128)S(1)} %select_bitcast_fusion.9), channel_id=1, source_target_pairs={{0,64},{4,68},{8,72},{12,76},{64,0},{68,4},{72,8},{76,12},{1,65},{... | collective-permute-start | bytes 589832 | tf_op jit(solution)/shard_map/ppermute | solution.py:61
  277.3 8.0 %collective-permute-start.26 = (f32[2,64,512]{2,1,0:T(8,128)S(1)}, f32[2,64,512]{2,1,0:T(8,128)S(1)}, u32[]{:S(2)}, u32[]{:S(2)}) collective-permute-start(f32[2,64,512]{2,1,0:T(8,128)S(1)} %select_bitcast_fusion.7), channel_id=1, source_target_pairs={{0,32},{1,33},{2,34},{3,35},{16,48},{17,49},{18,50},{19,51},{32,0}... | collective-permute-start | bytes 786440 | tf_op jit(solution)/shard_map/ppermute | solution.py:61
  278.6 8.5 %collective-permute-start.16 = (f32[128,384]{1,0:T(8,128)S(1)}, f32[128,384]{1,0:T(8,128)S(1)}, u32[]{:S(2)}, u32[]{:S(2)}) collective-permute-start(f32[128,384]{1,0:T(8,128)S(1)} %select_bitcast_fusion.10), channel_id=1, source_target_pairs={{0,4},{4,0},{8,12},{12,8},{64,68},{68,64},{72,76},{76,72},{1,5},{5... | collective-permute-start | bytes 589832 | tf_op jit(solution)/shard_map/ppermute | solution.py:61
  285.4 6.6 %collective-permute-start.27 = (f32[64,512]{1,0:T(8,128)S(1)}, f32[64,512]{1,0:T(8,128)S(1)}, u32[]{:S(2)}, u32[]{:S(2)}) collective-permute-start(f32[64,512]{1,0:T(8,128)S(1)} %select_bitcast_fusion.11), channel_id=1, source_target_pairs={{0,2},{1,3},{2,0},{3,1},{16,18},{17,19},{18,16},{19,17},{32,34},{3... | collective-permute-start | bytes 393224 | tf_op jit(solution)/shard_map/ppermute | solution.py:61
  (6 other events, 16.1 us)

commit v8 on v4

--- a/solution.py
+++ b/solution.py
@@ -106,6 +106,15 @@
     return both[:, :count].reshape(n * count, width), (got[:, 0] + got[:, 1] + got[:, 2]).reshape(n * count)
 
 
+def sum_and_gather(x, own, axis):
+    n = axis_size(axis)
+    count = own.shape[0]
+    padded = jnp.concatenate([own, jnp.zeros((x.shape[0] - count,), own.dtype)])
+    spread = jnp.broadcast_to(jnp.stack([x, padded])[None], (n, 2) + x.shape)
+    got = lax.all_to_all(spread, axis, 0, 0, tiled=False)
+    return got[:, 0].sum(0), got[:, 1, :count].reshape(n * count)
+
+
 def row_total(part):
     return tree_sum(part, ROWS)
 
@@ -129,8 +138,8 @@
     own_tgt = lax.dynamic_slice_in_dim(
         tgt_mass, lax.axis_index(("y_lo", "z", "core")) * tgt_count, tgt_count
     )
-    src_rows, src_mass = gather_with_mass(src_emb, own_src, ROWS)
-    target_rows, tgt_mass = gather_with_mass(right_sentence_vectors, own_tgt, COLS)
+    src_rows = split_gather(src_emb, ROWS)
+    target_rows = split_gather(right_sentence_vectors, COLS)
 
     kernel_grid = (
         lax.dot_general(
@@ -141,18 +150,23 @@
     kernel = lax.optimization_barrier(jnp.exp(kernel_grid).astype(jnp.bfloat16))
     weighted = kernel * kernel_grid
 
-    vector = jnp.ones(tgt_mass.shape, jnp.float32)
+    vector = jnp.ones((target_rows.shape[0],), jnp.float32)
     old_saved, row_saved, src_saved, col_saved, tgt_saved = ([], [], [], [], [])
     tgt_adj = None
     for iteration in range(ITERS):
         old_saved.append(vector)
-        row_sum = row_total(times_vector(kernel, vector))
+        if iteration == 0:
+            row_sum, src_mass = sum_and_gather(times_vector(kernel, vector), own_src, ROWS)
+        else:
+            row_sum = row_total(times_vector(kernel, vector))
         src_scale = src_mass / row_sum
         if iteration == ITERS - 1:
             both = col_total(
                 jnp.stack([vector_times(src_scale, kernel), vector_times(src_scale, weighted)])
             )
             col_sum, tgt_adj = both[0], both[1]
+        elif iteration == 0:
+            col_sum, tgt_mass = sum_and_gather(vector_times(src_scale, kernel), own_tgt, COLS)
         else:
             col_sum = col_total(vector_times(src_scale, kernel))
         vector = tgt_mass / col_sum

time: 265 us -> 260 us (0.981)
  blocking collectives: 108 us -> 121 us
  waiting for transfers between devices: 67.4 us -> 55.6 us
  other arithmetic: 28.4 us -> 23.4 us
  starting transfers between devices: 46.9 us -> 43.6 us
    all_to_all x0 -> x1, blocking collectives: none -> 13.1 us  [sum_and_gather(): got = lax.all_to_all(spread, axis, 0, 0, tiled=False)]
    all_to_all x3 -> x1, waiting for transfers between devices: 19.3 us -> 7.87 us  [tree_sum(): return lax.all_to_all(spread, axis, 0, 0, tiled=False).sum(0)]
    all_to_all x3 -> x1, starting transfers between devices: 11.3 us -> 3.51 us  [tree_sum(): return lax.all_to_all(spread, axis, 0, 0, tiled=False).sum(0)]
    ppermute x14, waiting for transfers between devices: 20.9 us -> 16.1 us  [tree_gather(): other = lax.ppermute(x, axis, partner(axis, n, bit))]
    all_to_all x0 -> x1, waiting for transfers between devices: none -> 4.47 us  [sum_and_gather(): got = lax.all_to_all(spread, axis, 0, 0, tiled=False)]
    all_to_all x0 -> x1, starting transfers between devices: none -> 3.35 us  [sum_and_gather(): got = lax.all_to_all(spread, axis, 0, 0, tiled=False)]
  transfers between devices with their start and end apart: 31 -> 30, of which waited for: 12 -> 12; matrix products, arithmetic and copies ran while one was open for 3% -> 2% of each run, Pallas kernels for 0% -> 0%
where the time goes in v8:
time: 260 us; the launch traced here: 259 us
  blocking collectives  121 us (47%)
  waiting for transfers between devices  55.6 us (21%)
  starting transfers between devices  43.6 us (17%)
  other arithmetic  23.4 us (9%)
  matrix products  7.5 us (3%)
  local copies, waits for them, and re-layouts  6.26 us (2%)
    all_to_all x12, blocking collectives, tree_sum(): return lax.all_to_all(spread, axis, 0, 0, tiled=False).sum(0)  108 us
    ppermute x14, waiting for transfers between devices, tree_scatter(): x = keep + lax.ppermute(send, axis, partner(axis, n, bit))  27.2 us
    ppermute x14, starting transfers between devices, tree_gather(): other = lax.ppermute(x, axis, partner(axis, n, bit))  20.3 us
    ppermute x14, starting transfers between devices, tree_scatter(): x = keep + lax.ppermute(send, axis, partner(axis, n, bit))  16.4 us
    ppermute x14, waiting for transfers between devices, tree_gather(): other = lax.ppermute(x, axis, partner(axis, n, bit))  16.1 us
    all_to_all x1, blocking collectives, sum_and_gather(): got = lax.all_to_all(spread, axis, 0, 0, tiled=False)  13.1 us
    all_to_all x1, waiting for transfers between devices, tree_sum(): return lax.all_to_all(spread, axis, 0, 0, tiled=False).sum(0)  7.87 us
    reduce_sum x8, other arithmetic, times_vector(): return jnp.sum(kernel.astype(jnp.float32) * vector[None, :], axis=1)  6.72 us
  transfers between devices with their start and end apart: 30, of which 12 were waited for; matrix products, arithmetic and copies ran while one was open for 2% of the time, Pallas kernels for 0%

profile of v8, /device:TPU:0, one launch (start us, length us, event | category | flops | bytes accessed | tf_op | source)
XLA Modules:
  0.0 258.9 jit_solution(15155348611858833909)
XLA Ops:
  1.5 4.0 %collective-permute-start.10 = (bf16[64,384]{1,0:T(8,128)(2,1)S(1)}, bf16[64,384]{1,0:T(8,128)(2,1)S(1)}, u32[]{:S(2)}, u32[]{:S(2)}) collective-permute-start(bf16[64,384]{1,0:T(8,128)(2,1)S(1)} %get-tuple-element.34), channel_id=1, source_target_pairs={{0,32},{1,33},{2,34},{3,35},{16,48},{17,49},{18,50},{19,51},{32,0}... | collective-permute-start | bytes 147464 | tf_op jit(solution)/shard_map/ppermute | solution.py:38
  5.5 3.0 %collective-permute-start.6 = (bf16[64,384]{1,0:T(8,128)(2,1)S(1)}, bf16[64,384]{1,0:T(8,128)(2,1)S(1)}, u32[]{:S(2)}, u32[]{:S(2)}) collective-permute-start(bf16[64,384]{1,0:T(8,128)(2,1)S(1)} %get-tuple-element.35), channel_id=1, source_target_pairs={{0,2},{1,3},{2,0},{3,1},{16,18},{17,19},{18,16},{19,17},{32,34},{3... | collective-permute-start | bytes 147464 | tf_op jit(solution)/shard_map/ppermute | solution.py:38
  11.2 2.9 %collective-permute-start = (bf16[128,384]{1,0:T(8,128)(2,1)S(1)}, bf16[128,384]{1,0:T(8,128)(2,1)S(1)}, u32[]{:S(2)}, u32[]{:S(2)}) collective-permute-start(bf16[128,384]{1,0:T(8,128)(2,1)S(1)} %get-tuple-element.25), channel_id=1, source_target_pairs={{0,4},{4,0},{8,12},{12,8},{64,68},{68,64},{72,76},{76,72},{1,5},{5... | collective-permute-start | bytes 294920 | tf_op jit(solution)/shard_map/ppermute | solution.py:38
  15.8 2.4 collective-permute-done
  18.5 2.8 %collective-permute-start.4 = (bf16[2,128,384]{2,1,0:T(8,128)(2,1)S(1)}, bf16[2,128,384]{2,1,0:T(8,128)(2,1)S(1)}, u32[]{:S(2)}, u32[]{:S(2)}) collective-permute-start(bf16[2,128,384]{2,1,0:T(8,128)(2,1)S(1)} %maximum_select_fusion.14), channel_id=1, source_target_pairs={{0,4},{4,0},{8,12},{12,8},{64,68},{68,64},{72,76},{76,72},{1,5},{5... | collective-permute-start | bytes 589832 | tf_op jit(solution)/shard_map/ppermute | solution.py:38
  24.2 4.2 %collective-permute-done.4 = bf16[2,128,384]{2,1,0:T(8,128)(2,1)S(1)} collective-permute-done((bf16[2,128,384]{2,1,0:T(8,128)(2,1)S(1)}, bf16[2,128,384]{2,1,0:T(8,128)(2,1)S(1)}, u32[]{:S(2)}, u32[]{:S(2)}) %collective-permute-start.4) | collective-permute-done | bytes 196640 | tf_op jit(solution)/shard_map/ppermute | solution.py:38
  31.8 8.8 %collective-permute-done.13 = bf16[2,2,2,64,384]{4,3,1,2,0:T(8,128)(2,1)S(1)} collective-permute-done((bf16[2,2,2,64,384]{4,3,1,2,0:T(8,128)(2,1)S(1)}, bf16[2,2,2,64,384]{4,3,1,2,0:T(8,128)(2,1)S(1)}, u32[]{:S(2)}, u32[]{:S(2)}) %collective-permute-start.13) | collective-permute-done | bytes 393248 | tf_op jit(solution)/shard_map/ppermute | solution.py:38
  41.6 3.8 %exponential_convert_fusion = (bf16[1024,1024]{1,0:T(8,128)(2,1)S(1)}, f32[1024,1024]{1,0:T(8,128)}) fusion(bf16[1024,384]{1,0:T(8,128)(2,1)S(1)} %bitcast.187, bf16[1024,384]{1,0:T(8,128)(2,1)S(1)} %bitcast.189, bf16[1024,384]{1,0:T(8,128)(2,1)S(1)} %bitcast.183, bf16[1024,384]{1,0:T(8,128)(2,1)S(1)} %bitcast.185), kind=kOutput, calls=%fused_computation.34 | convolution fusion | flops 1619001344 | bytes 9437184 | tf_op jit(solution)/shard_map/dot_general | solution.py:145
  46.4 3.4 %all-to-all-start = ((f32[8,2,1024]{2,1,0:T(2,128)}), f32[8,2,1024]{2,1,0:T(2,128)S(1)}, u32[]{:S(2)}, u32[]{:S(2)}) async-start(f32[8,2,1024]{2,1,0:T(2,128)} %broadcast_in_dim.30), calls=%async_computation | async-start | bytes 131072 | tf_op jit(solution)/shard_map/all_to_all | solution.py:114
  50.5 4.5 %all-to-all-done = f32[8,2,1024]{2,1,0:T(2,128)S(1)} async-done(((f32[8,2,1024]{2,1,0:T(2,128)}), f32[8,2,1024]{2,1,0:T(2,128)S(1)}, u32[]{:S(2)}, u32[]{:S(2)}) %all-to-all-start) | async-done | bytes 65568 | tf_op jit(solution)/shard_map/all_to_all | solution.py:114
  55.6 13.1 %all_to_all.87 = f32[16,2,1024]{2,1,0:T(2,128)S(1)} all-to-all(f32[16,2,1024]{2,1,0:T(2,128)S(1)} %broadcast_in_dim.31), channel_id=1, replica_groups=mesh['y_lo'=2,'z'=4,'core'=2,'y_hi'=2,'x'=4] {'z','x'}, dimensions={0} | all-to-all | bytes 262144 | tf_op jit(solution)/shard_map/all_to_all | solution.py:114
  69.4 7.8 %all_to_all.88 = f32[8,1,1024]{2,1,0:T(1,128)S(1)} all-to-all(f32[8,1,1024]{2,1,0:T(1,128)S(1)} %broadcast_in_dim.32), channel_id=1, replica_groups=mesh['y_lo'=2,'z'=4,'core'=2,'y_hi'=2,'x'=4] {'y_lo','core','y_hi'}, dimensions={0} | all-to-all | bytes 65536 | tf_op jit(solution)/shard_map/all_to_all | solution.py:31
  77.8 10.7 %all_to_all.89 = f32[16,1,1024]{2,1,0:T(1,128)S(1)} all-to-all(f32[16,1,1024]{2,1,0:T(1,128)S(1)} %broadcast_in_dim.33), channel_id=1, replica_groups=mesh['y_lo'=2,'z'=4,'core'=2,'y_hi'=2,'x'=4] {'z','x'}, dimensions={0} | all-to-all | bytes 131072 | tf_op jit(solution)/shard_map/all_to_all | solution.py:31
  89.1 7.7 %all_to_all.90 = f32[8,1,1024]{2,1,0:T(1,128)S(1)} all-to-all(f32[8,1,1024]{2,1,0:T(1,128)S(1)} %broadcast_in_dim.34), channel_id=1, replica_groups=mesh['y_lo'=2,'z'=4,'core'=2,'y_hi'=2,'x'=4] {'y_lo','core','y_hi'}, dimensions={0} | all-to-all | bytes 65536 | tf_op jit(solution)/shard_map/all_to_all | solution.py:31
  97.3 10.8 %all_to_all.91 = f32[16,1,1024]{2,1,0:T(1,128)S(1)} all-to-all(f32[16,1,1024]{2,1,0:T(1,128)S(1)} %broadcast_in_dim.35), channel_id=1, replica_groups=mesh['y_lo'=2,'z'=4,'core'=2,'y_hi'=2,'x'=4] {'z','x'}, dimensions={0} | all-to-all | bytes 131072 | tf_op jit(solution)/shard_map/all_to_all | solution.py:31
  108.7 7.7 %all_to_all.92 = f32[8,1,1024]{2,1,0:T(1,128)S(1)} all-to-all(f32[8,1,1024]{2,1,0:T(1,128)S(1)} %broadcast_in_dim.36), channel_id=1, replica_groups=mesh['y_lo'=2,'z'=4,'core'=2,'y_hi'=2,'x'=4] {'y_lo','core','y_hi'}, dimensions={0} | all-to-all | bytes 65536 | tf_op jit(solution)/shard_map/all_to_all | solution.py:31
  116.5 3.2 %fusion.6 = (f32[1024]{0:T(1024)S(1)}, f32[1024]{0:T(1024)S(1)}) fusion(bf16[1024,1024]{1,0:T(8,128)(2,1)S(1)} %get-tuple-element.36, f32[1024]{0:T(1024)S(1)} %div.148, f32[1024,1024]{1,0:T(8,128)} %get-tuple-element.37), kind=kLoop, calls=%fused_computation.23 | loop fusion | flops 7337984 | bytes 6303744 | tf_op jit(solution)/shard_map/reduce_sum | solution.py:131
  120.4 3.5 %all-to-all-start.7 = ((f32[16,2,1024]{2,1,0:T(2,128)}), f32[16,2,1024]{2,1,0:T(2,128)S(1)}, u32[]{:S(2)}, u32[]{:S(2)}) async-start(f32[16,2,1024]{2,1,0:T(2,128)} %broadcast_in_dim.37), calls=%async_computation.7 | async-start | bytes 262144 | tf_op jit(solution)/shard_map/all_to_all | solution.py:31
  124.0 7.9 %all-to-all-done.7 = f32[16,2,1024]{2,1,0:T(2,128)S(1)} async-done(((f32[16,2,1024]{2,1,0:T(2,128)}), f32[16,2,1024]{2,1,0:T(2,128)S(1)}, u32[]{:S(2)}, u32[]{:S(2)}) %all-to-all-start.7) | async-done | bytes 131104 | tf_op jit(solution)/shard_map/all_to_all | solution.py:31
  131.9 3.5 %multiply_reduce_fusion = (f32[1024]{0:T(1024)S(1)}, f32[1024]{0:T(1024)S(1)}) fusion(f32[1024,1024]{1,0:T(8,128)} %get-tuple-element.37, bf16[1024,1024]{1,0:T(8,128)(2,1)S(1)} %get-tuple-element.36, f32[1024]{0:T(1024)S(1)} %bitcast.215, f32[1024]{0:T(1024)S(1)} %bitcast.213), kind=kLoop, calls=%fused_computation.32 | loop fusion | flops 7337984 | bytes 6307840 | tf_op jit(solution)/shard_map/reduce_sum | solution.py:127
  135.5 7.7 %all_to_all.93 = f32[8,1,1024]{2,1,0:T(1,128)S(1)} all-to-all(f32[8,1,1024]{2,1,0:T(1,128)S(1)} %broadcast_in_dim.38), channel_id=1, replica_groups=mesh['y_lo'=2,'z'=4,'core'=2,'y_hi'=2,'x'=4] {'y_lo','core','y_hi'}, dimensions={0} | all-to-all | bytes 65536 | tf_op jit(solution)/shard_map/all_to_all | solution.py:31
  143.7 10.7 %all_to_all.94 = f32[16,1,1024]{2,1,0:T(1,128)S(1)} all-to-all(f32[16,1,1024]{2,1,0:T(1,128)S(1)} %broadcast_in_dim.39), channel_id=1, replica_groups=mesh['y_lo'=2,'z'=4,'core'=2,'y_hi'=2,'x'=4] {'z','x'}, dimensions={0} | all-to-all | bytes 131072 | tf_op jit(solution)/shard_map/all_to_all | solution.py:31
  155.1 7.7 %all_to_all.95 = f32[8,1,1024]{2,1,0:T(1,128)S(1)} all-to-all(f32[8,1,1024]{2,1,0:T(1,128)S(1)} %broadcast_in_dim.40), channel_id=1, replica_groups=mesh['y_lo'=2,'z'=4,'core'=2,'y_hi'=2,'x'=4] {'y_lo','core','y_hi'}, dimensions={0} | all-to-all | bytes 65536 | tf_op jit(solution)/shard_map/all_to_all | solution.py:31
  163.3 10.8 %all_to_all.96 = f32[16,1,1024]{2,1,0:T(1,128)S(1)} all-to-all(f32[16,1,1024]{2,1,0:T(1,128)S(1)} %broadcast_in_dim.41), channel_id=1, replica_groups=mesh['y_lo'=2,'z'=4,'core'=2,'y_hi'=2,'x'=4] {'z','x'}, dimensions={0} | all-to-all | bytes 131072 | tf_op jit(solution)/shard_map/all_to_all | solution.py:31
  174.7 7.7 %all_to_all.97 = f32[8,1,1024]{2,1,0:T(1,128)S(1)} all-to-all(f32[8,1,1024]{2,1,0:T(1,128)S(1)} %broadcast_in_dim.42), channel_id=1, replica_groups=mesh['y_lo'=2,'z'=4,'core'=2,'y_hi'=2,'x'=4] {'y_lo','core','y_hi'}, dimensions={0} | all-to-all | bytes 65536 | tf_op jit(solution)/shard_map/all_to_all | solution.py:31
  183.0 10.8 %all_to_all.98 = f32[16,1,1024]{2,1,0:T(1,128)S(1)} all-to-all(f32[16,1,1024]{2,1,0:T(1,128)S(1)} %broadcast_in_dim.43), channel_id=1, replica_groups=mesh['y_lo'=2,'z'=4,'core'=2,'y_hi'=2,'x'=4] {'z','x'}, dimensions={0} | all-to-all | bytes 131072 | tf_op jit(solution)/shard_map/all_to_all | solution.py:31
  194.4 7.7 %all_to_all.99 = f32[8,1,1024]{2,1,0:T(1,128)S(1)} all-to-all(f32[8,1,1024]{2,1,0:T(1,128)S(1)} %broadcast_in_dim.44), channel_id=1, replica_groups=mesh['y_lo'=2,'z'=4,'core'=2,'y_hi'=2,'x'=4] {'y_lo','core','y_hi'}, dimensions={0} | all-to-all | bytes 65536 | tf_op jit(solution)/shard_map/all_to_all | solution.py:31
  202.1 5.4 %fusion.14 = bf16[1024,1024]{1,0:T(8,128)(2,1)S(1)} fusion(bf16[1024,1024]{1,0:T(8,128)(2,1)S(1)} %get-tuple-element.36, f32[1024,1024]{1,0:T(8,128)} %get-tuple-element.37, f32[1024]{0:T(1024)S(1)} %multiply_divide_fusion, f32[1024]{0:T(1024)S(1)} %multiply_divide_fusion.1, f32[1024]{0:T(1024)S(1)} %multiply_divide_fusion.2, ...), kind=kLoop, calls=%fused_computation.31 | loop fusion | flops 23068672 | bytes 8454144 | tf_op jit(solution)/shard_map/convert_element_type | solution.py:199
  217.1 15.5 %collective-permute-done.24 = f32[2,2,2,64,384]{4,3,1,0,2:T(8,128)S(1)} collective-permute-done((f32[2,2,2,64,384]{4,3,1,0,2:T(8,128)S(1)}, f32[2,2,2,64,384]{4,3,1,0,2:T(8,128)S(1)}, u32[]{:S(2)}, u32[]{:S(2)}) %collective-permute-start.24) | collective-permute-done | bytes 786464 | tf_op jit(solution)/shard_map/ppermute | solution.py:61
  237.9 5.3 %collective-permute-done.25 = f32[2,2,64,384]{3,2,1,0:T(8,128)S(1)} collective-permute-done((f32[2,2,64,384]{3,2,1,0:T(8,128)S(1)}, f32[2,2,64,384]{3,2,1,0:T(8,128)S(1)}, u32[]{:S(2)}, u32[]{:S(2)}) %collective-permute-start.25) | collective-permute-done | bytes 393248 | tf_op jit(solution)/shard_map/ppermute | solution.py:61
  246.1 4.4 %collective-permute-done.26 = f32[2,64,384]{2,1,0:T(8,128)S(1)} collective-permute-done((f32[2,64,384]{2,1,0:T(8,128)S(1)}, f32[2,64,384]{2,1,0:T(8,128)S(1)}, u32[]{:S(2)}, u32[]{:S(2)}) %collective-permute-start.26) | collective-permute-done | bytes 196640 | tf_op jit(solution)/shard_map/ppermute | solution.py:61
  252.0 3.4 %collective-permute-start.23 = (f32[64,384]{1,0:T(8,128)S(1)}, f32[64,384]{1,0:T(8,128)S(1)}, u32[]{:S(2)}, u32[]{:S(2)}) collective-permute-start(f32[64,384]{1,0:T(8,128)S(1)} %select_bitcast_fusion.11), channel_id=1, source_target_pairs={{0,32},{1,33},{2,34},{3,35},{16,48},{17,49},{18,50},{19,51},{32,0}... | collective-permute-start | bytes 294920 | tf_op jit(solution)/shard_map/ppermute | solution.py:61
  (200 shorter events, 44.8 us)
Async XLA Ops:
  1.5 13.6 %collective-permute-start.10 = (bf16[64,384]{1,0:T(8,128)(2,1)S(1)}, bf16[64,384]{1,0:T(8,128)(2,1)S(1)}, u32[]{:S(2)}, u32[]{:S(2)}) collective-permute-start(bf16[64,384]{1,0:T(8,128)(2,1)S(1)} %get-tuple-element.34), channel_id=1, source_target_pairs={{0,32},{1,33},{2,34},{3,35},{16,48},{17,49},{18,50},{19,51},{32,0}... | collective-permute-start | bytes 147464 | tf_op jit(solution)/shard_map/ppermute | solution.py:38
  5.5 9.3 %collective-permute-start.6 = (bf16[64,384]{1,0:T(8,128)(2,1)S(1)}, bf16[64,384]{1,0:T(8,128)(2,1)S(1)}, u32[]{:S(2)}, u32[]{:S(2)}) collective-permute-start(bf16[64,384]{1,0:T(8,128)(2,1)S(1)} %get-tuple-element.35), channel_id=1, source_target_pairs={{0,2},{1,3},{2,0},{3,1},{16,18},{17,19},{18,16},{19,17},{32,34},{3... | collective-permute-start | bytes 147464 | tf_op jit(solution)/shard_map/ppermute | solution.py:38
  9.5 8.9 %collective-permute-start.3 = (bf16[128,384]{1,0:T(8,128)(2,1)S(1)}, bf16[128,384]{1,0:T(8,128)(2,1)S(1)}, u32[]{:S(2)}, u32[]{:S(2)}) collective-permute-start(bf16[128,384]{1,0:T(8,128)(2,1)S(1)} %get-tuple-element.24), channel_id=1, source_target_pairs={{0,64},{4,68},{8,72},{12,76},{64,0},{68,4},{72,8},{76,12},{1,65},{... | collective-permute-start | bytes 294920 | tf_op jit(solution)/shard_map/ppermute | solution.py:38
  11.2 7.0 %collective-permute-start = (bf16[128,384]{1,0:T(8,128)(2,1)S(1)}, bf16[128,384]{1,0:T(8,128)(2,1)S(1)}, u32[]{:S(2)}, u32[]{:S(2)}) collective-permute-start(bf16[128,384]{1,0:T(8,128)(2,1)S(1)} %get-tuple-element.25), channel_id=1, source_target_pairs={{0,4},{4,0},{8,12},{12,8},{64,68},{68,64},{72,76},{76,72},{1,5},{5... | collective-permute-start | bytes 294920 | tf_op jit(solution)/shard_map/ppermute | solution.py:38
  14.9 7.1 %collective-permute-start.7 = (bf16[2,64,384]{2,1,0:T(8,128)(2,1)S(1)}, bf16[2,64,384]{2,1,0:T(8,128)(2,1)S(1)}, u32[]{:S(2)}, u32[]{:S(2)}) collective-permute-start(bf16[2,64,384]{2,1,0:T(8,128)(2,1)S(1)} %maximum_select_fusion.19), channel_id=1, source_target_pairs={{0,32},{1,33},{2,34},{3,35},{16,48},{17,49},{18,50},{19,51},{32,0}... | collective-permute-start | bytes 294920 | tf_op jit(solution)/shard_map/ppermute | solution.py:38
  15.1 6.2 %collective-permute-start.11 = (bf16[2,64,384]{2,1,0:T(8,128)(2,1)S(1)}, bf16[2,64,384]{2,1,0:T(8,128)(2,1)S(1)}, u32[]{:S(2)}, u32[]{:S(2)}) collective-permute-start(bf16[2,64,384]{2,1,0:T(8,128)(2,1)S(1)} %maximum_select_fusion.21), channel_id=1, source_target_pairs={{0,2},{1,3},{2,0},{3,1},{16,18},{17,19},{18,16},{19,17},{32,34},{3... | collective-permute-start | bytes 294920 | tf_op jit(solution)/shard_map/ppermute | solution.py:38
  18.2 10.3 %collective-permute-start.1 = (bf16[2,128,384]{2,1,0:T(8,128)(2,1)S(1)}, bf16[2,128,384]{2,1,0:T(8,128)(2,1)S(1)}, u32[]{:S(2)}, u32[]{:S(2)}) collective-permute-start(bf16[2,128,384]{2,1,0:T(8,128)(2,1)S(1)} %maximum_select_fusion.12), channel_id=1, source_target_pairs={{0,64},{4,68},{8,72},{12,76},{64,0},{68,4},{72,8},{76,12},{1,65},{... | collective-permute-start | bytes 589832 | tf_op jit(solution)/shard_map/ppermute | solution.py:38
  18.5 9.8 %collective-permute-start.4 = (bf16[2,128,384]{2,1,0:T(8,128)(2,1)S(1)}, bf16[2,128,384]{2,1,0:T(8,128)(2,1)S(1)}, u32[]{:S(2)}, u32[]{:S(2)}) collective-permute-start(bf16[2,128,384]{2,1,0:T(8,128)(2,1)S(1)} %maximum_select_fusion.14), channel_id=1, source_target_pairs={{0,4},{4,0},{8,12},{12,8},{64,68},{68,64},{72,76},{76,72},{1,5},{5... | collective-permute-start | bytes 589832 | tf_op jit(solution)/shard_map/ppermute | solution.py:38
  21.4 7.9 %collective-permute-start.12 = (bf16[2,2,64,384]{3,2,0,1:T(8,128)(2,1)S(1)}, bf16[2,2,64,384]{3,2,0,1:T(8,128)(2,1)S(1)}, u32[]{:S(2)}, u32[]{:S(2)}) collective-permute-start(bf16[2,2,64,384]{3,2,0,1:T(8,128)(2,1)S(1)} %maximum_select_fusion.18), channel_id=1, source_target_pairs={{0,1},{1,0},{2,3},{3,2},{16,17},{17,16},{18,19},{19,18},{32,33},{3... | collective-permute-start | bytes 589832 | tf_op jit(solution)/shard_map/ppermute | solution.py:38
  22.1 8.4 %collective-permute-start.8 = (bf16[2,2,64,384]{3,2,1,0:T(8,128)(2,1)S(1)}, bf16[2,2,64,384]{3,2,1,0:T(8,128)(2,1)S(1)}, u32[]{:S(2)}, u32[]{:S(2)}) collective-permute-start(bf16[2,2,64,384]{3,2,1,0:T(8,128)(2,1)S(1)} %maximum_select_fusion.16), channel_id=1, source_target_pairs={{0,16},{1,17},{2,18},{3,19},{16,0},{17,1},{18,2},{19,3},{32,48},{3... | collective-permute-start | bytes 589832 | tf_op jit(solution)/shard_map/ppermute | solution.py:38
  28.4 2.9 %collective-permute-start.5 = (bf16[2,2,128,384]{3,2,1,0:T(8,128)(2,1)S(1)}, bf16[2,2,128,384]{3,2,1,0:T(8,128)(2,1)S(1)}, u32[]{:S(2)}, u32[]{:S(2)}) collective-permute-start(bf16[2,2,128,384]{3,2,1,0:T(8,128)(2,1)S(1)} %maximum_select_fusion.6), channel_id=1, source_target_pairs={{0,8},{4,12},{8,0},{12,4},{64,72},{68,76},{72,64},{76,68},{1,9},{5... | collective-permute-start | bytes 1179656 | tf_op jit(solution)/shard_map/ppermute | solution.py:38
  28.6 3.0 %collective-permute-start.2 = (bf16[2,2,128,384]{3,2,1,0:T(8,128)(2,1)S(1)}, bf16[2,2,128,384]{3,2,1,0:T(8,128)(2,1)S(1)}, u32[]{:S(2)}, u32[]{:S(2)}) collective-permute-start(bf16[2,2,128,384]{3,2,1,0:T(8,128)(2,1)S(1)} %maximum_select_fusion.4), channel_id=1, source_target_pairs={{0,8},{4,12},{8,0},{12,4},{64,72},{68,76},{72,64},{76,68},{1,9},{5... | collective-permute-start | bytes 1179656 | tf_op jit(solution)/shard_map/ppermute | solution.py:38
  29.4 11.1 %collective-permute-start.13 = (bf16[2,2,2,64,384]{4,3,1,2,0:T(8,128)(2,1)S(1)}, bf16[2,2,2,64,384]{4,3,1,2,0:T(8,128)(2,1)S(1)}, u32[]{:S(2)}, u32[]{:S(2)}) collective-permute-start(bf16[2,2,2,64,384]{4,3,1,2,0:T(8,128)(2,1)S(1)} %maximum_select_fusion.10), channel_id=1, source_target_pairs={{0,16},{1,17},{2,18},{3,19},{16,0},{17,1},{18,2},{19,3},{32,48},{3... | collective-permute-start | bytes 1179656 | tf_op jit(solution)/shard_map/ppermute | solution.py:38
  30.6 10.8 %collective-permute-start.9 = (bf16[2,2,2,64,384]{4,3,2,1,0:T(8,128)(2,1)S(1)}, bf16[2,2,2,64,384]{4,3,2,1,0:T(8,128)(2,1)S(1)}, u32[]{:S(2)}, u32[]{:S(2)}) collective-permute-start(bf16[2,2,2,64,384]{4,3,2,1,0:T(8,128)(2,1)S(1)} %maximum_select_fusion.8), channel_id=1, source_target_pairs={{0,1},{1,0},{2,3},{3,2},{16,17},{17,16},{18,19},{19,18},{32,33},{3... | collective-permute-start | bytes 1179656 | tf_op jit(solution)/shard_map/ppermute | solution.py:38
  31.7 13.6 %copy-start = (bf16[2,2,2,128,384]{4,3,2,0,1:T(8,128)(2,1)}, bf16[2,2,2,128,384]{4,3,2,0,1:T(8,128)(2,1)S(1)}, u32[]{:S(2)}) copy-start(bf16[2,2,2,128,384]{4,3,2,0,1:T(8,128)(2,1)S(1)} %maximum_select_fusion) | copy-start | bytes 2359300
  46.4 8.6 %all-to-all-start = ((f32[8,2,1024]{2,1,0:T(2,128)}), f32[8,2,1024]{2,1,0:T(2,128)S(1)}, u32[]{:S(2)}, u32[]{:S(2)}) async-start(f32[8,2,1024]{2,1,0:T(2,128)} %broadcast_in_dim.30), calls=%async_computation | async-start | bytes 131072 | tf_op jit(solution)/shard_map/all_to_all | solution.py:114
  120.4 11.5 %all-to-all-start.7 = ((f32[16,2,1024]{2,1,0:T(2,128)}), f32[16,2,1024]{2,1,0:T(2,128)S(1)}, u32[]{:S(2)}, u32[]{:S(2)}) async-start(f32[16,2,1024]{2,1,0:T(2,128)} %broadcast_in_dim.37), calls=%async_computation.7 | async-start | bytes 262144 | tf_op jit(solution)/shard_map/all_to_all | solution.py:31
  202.1 5.4 %copy-start.1 = (bf16[2,2,2,128,384]{4,3,2,0,1:T(8,128)(2,1)S(1)}, bf16[2,2,2,128,384]{4,3,2,0,1:T(8,128)(2,1)}, u32[]{:S(2)}) copy-start(bf16[2,2,2,128,384]{4,3,2,0,1:T(8,128)(2,1)} %copy-done) | copy-start | bytes 2359300
  212.1 2.4 collective-permute-start.17
  212.4 3.6 %collective-permute-start.14 = (f32[2,2,128,384]{3,2,0,1:T(8,128)S(1)}, f32[2,2,128,384]{3,2,0,1:T(8,128)S(1)}, u32[]{:S(2)}, u32[]{:S(2)}) collective-permute-start(f32[2,2,128,384]{3,2,0,1:T(8,128)S(1)} %select_bitcast_fusion.3), channel_id=1, source_target_pairs={{0,8},{4,12},{8,0},{12,4},{64,72},{68,76},{72,64},{76,68},{1,9},{5... | collective-permute-start | bytes 2359304 | tf_op jit(solution)/shard_map/ppermute | solution.py:61
  213.0 19.6 %collective-permute-start.24 = (f32[2,2,2,64,384]{4,3,1,0,2:T(8,128)S(1)}, f32[2,2,2,64,384]{4,3,1,0,2:T(8,128)S(1)}, u32[]{:S(2)}, u32[]{:S(2)}) collective-permute-start(f32[2,2,2,64,384]{4,3,1,0,2:T(8,128)S(1)} %select_bitcast_fusion), channel_id=1, source_target_pairs={{0,16},{1,17},{2,18},{3,19},{16,0},{17,1},{18,2},{19,3},{32,48},{3... | collective-permute-start | bytes 2359304 | tf_op jit(solution)/shard_map/ppermute | solution.py:61
  213.8 19.7 %collective-permute-start.20 = (f32[2,2,2,64,384]{4,3,0,2,1:T(8,128)S(1)}, f32[2,2,2,64,384]{4,3,0,2,1:T(8,128)S(1)}, u32[]{:S(2)}, u32[]{:S(2)}) collective-permute-start(f32[2,2,2,64,384]{4,3,0,2,1:T(8,128)S(1)} %select_bitcast_fusion.1), channel_id=1, source_target_pairs={{0,1},{1,0},{2,3},{3,2},{16,17},{17,16},{18,19},{19,18},{32,33},{3... | collective-permute-start | bytes 2359304 | tf_op jit(solution)/shard_map/ppermute | solution.py:61
  214.6 20.3 %collective-permute-start.18 = (f32[2,128,384]{2,1,0:T(8,128)S(1)}, f32[2,128,384]{2,1,0:T(8,128)S(1)}, u32[]{:S(2)}, u32[]{:S(2)}) collective-permute-start(f32[2,128,384]{2,1,0:T(8,128)S(1)} %select_bitcast_fusion.6), channel_id=1, source_target_pairs={{0,4},{4,0},{8,12},{12,8},{64,68},{68,64},{72,76},{76,72},{1,5},{5... | collective-permute-start | bytes 1179656 | tf_op jit(solution)/shard_map/ppermute | solution.py:61
  216.2 19.5 %collective-permute-start.15 = (f32[2,128,384]{2,1,0:T(8,128)S(1)}, f32[2,128,384]{2,1,0:T(8,128)S(1)}, u32[]{:S(2)}, u32[]{:S(2)}) collective-permute-start(f32[2,128,384]{2,1,0:T(8,128)S(1)} %fusion.17), channel_id=1, source_target_pairs={{0,64},{4,68},{8,72},{12,76},{64,0},{68,4},{72,8},{76,12},{1,65},{... | collective-permute-start | bytes 1179656 | tf_op jit(solution)/shard_map/ppermute | solution.py:61
  232.8 10.4 %collective-permute-start.25 = (f32[2,2,64,384]{3,2,1,0:T(8,128)S(1)}, f32[2,2,64,384]{3,2,1,0:T(8,128)S(1)}, u32[]{:S(2)}, u32[]{:S(2)}) collective-permute-start(f32[2,2,64,384]{3,2,1,0:T(8,128)S(1)} %select_bitcast_fusion.4), channel_id=1, source_target_pairs={{0,1},{1,0},{2,3},{3,2},{16,17},{17,16},{18,19},{19,18},{32,33},{3... | collective-permute-start | bytes 1179656 | tf_op jit(solution)/shard_map/ppermute | solution.py:61
  233.7 10.9 %collective-permute-start.21 = (f32[2,2,64,384]{3,2,0,1:T(8,128)S(1)}, f32[2,2,64,384]{3,2,0,1:T(8,128)S(1)}, u32[]{:S(2)}, u32[]{:S(2)}) collective-permute-start(f32[2,2,64,384]{3,2,0,1:T(8,128)S(1)} %select_bitcast_fusion.5), channel_id=1, source_target_pairs={{0,16},{1,17},{2,18},{3,19},{16,0},{17,1},{18,2},{19,3},{32,48},{3... | collective-permute-start | bytes 1179656 | tf_op jit(solution)/shard_map/ppermute | solution.py:61
  235.0 20.4 %collective-permute-start.19 = (f32[128,384]{1,0:T(8,128)S(1)}, f32[128,384]{1,0:T(8,128)S(1)}, u32[]{:S(2)}, u32[]{:S(2)}) collective-permute-start(f32[128,384]{1,0:T(8,128)S(1)} %select_bitcast_fusion.8), channel_id=1, source_target_pairs={{0,64},{4,68},{8,72},{12,76},{64,0},{68,4},{72,8},{76,12},{1,65},{... | collective-permute-start | bytes 589832 | tf_op jit(solution)/shard_map/ppermute | solution.py:61
  235.8 19.7 %collective-permute-start.16 = (f32[128,384]{1,0:T(8,128)S(1)}, f32[128,384]{1,0:T(8,128)S(1)}, u32[]{:S(2)}, u32[]{:S(2)}) collective-permute-start(f32[128,384]{1,0:T(8,128)S(1)} %select_bitcast_fusion.9), channel_id=1, source_target_pairs={{0,4},{4,0},{8,12},{12,8},{64,68},{68,64},{72,76},{76,72},{1,5},{5... | collective-permute-start | bytes 589832 | tf_op jit(solution)/shard_map/ppermute | solution.py:61
  243.3 7.3 %collective-permute-start.26 = (f32[2,64,384]{2,1,0:T(8,128)S(1)}, f32[2,64,384]{2,1,0:T(8,128)S(1)}, u32[]{:S(2)}, u32[]{:S(2)}) collective-permute-start(f32[2,64,384]{2,1,0:T(8,128)S(1)} %fusion.18), channel_id=1, source_target_pairs={{0,32},{1,33},{2,34},{3,35},{16,48},{17,49},{18,50},{19,51},{32,0}... | collective-permute-start | bytes 589832 | tf_op jit(solution)/shard_map/ppermute | solution.py:61
  244.6 7.4 %collective-permute-start.22 = (f32[2,64,384]{2,1,0:T(8,128)S(1)}, f32[2,64,384]{2,1,0:T(8,128)S(1)}, u32[]{:S(2)}, u32[]{:S(2)}) collective-permute-start(f32[2,64,384]{2,1,0:T(8,128)S(1)} %select_bitcast_fusion.7), channel_id=1, source_target_pairs={{0,2},{1,3},{2,0},{3,1},{16,18},{17,19},{18,16},{19,17},{32,34},{3... | collective-permute-start | bytes 589832 | tf_op jit(solution)/shard_map/ppermute | solution.py:61
  250.6 6.2 %collective-permute-start.27 = (f32[64,384]{1,0:T(8,128)S(1)}, f32[64,384]{1,0:T(8,128)S(1)}, u32[]{:S(2)}, u32[]{:S(2)}) collective-permute-start(f32[64,384]{1,0:T(8,128)S(1)} %select_bitcast_fusion.10), channel_id=1, source_target_pairs={{0,2},{1,3},{2,0},{3,1},{16,18},{17,19},{18,16},{19,17},{32,34},{3... | collective-permute-start | bytes 294920 | tf_op jit(solution)/shard_map/ppermute | solution.py:61
  252.0 6.2 %collective-permute-start.23 = (f32[64,384]{1,0:T(8,128)S(1)}, f32[64,384]{1,0:T(8,128)S(1)}, u32[]{:S(2)}, u32[]{:S(2)}) collective-permute-start(f32[64,384]{1,0:T(8,128)S(1)} %select_bitcast_fusion.11), channel_id=1, source_target_pairs={{0,32},{1,33},{2,34},{3,35},{16,48},{17,49},{18,50},{19,51},{32,0}... | collective-permute-start | bytes 294920 | tf_op jit(solution)/shard_map/ppermute | solution.py:61
  (4 other events, 12.4 us)

commit v9 on v8

--- a/solution.py
+++ b/solution.py
@@ -89,21 +89,6 @@
     mid = to_bf16_grid(rest)
     low = rest - mid
     return [p.astype(jnp.bfloat16) for p in (high, mid, low)]
-
-
-EXTRA = 16
-
-
-def gather_with_mass(rows, mass, axis):
-    count, width = rows.shape
-    pieces = jnp.concatenate(split3(mass))
-    extra = jnp.zeros((EXTRA, width), rows.dtype)
-    extra = lax.dynamic_update_slice(extra, pieces[None, :], (0, 0))
-    both = split_gather(jnp.concatenate([rows, extra]), axis)
-    n = both.shape[0] // (count + EXTRA)
-    both = both.reshape(n, count + EXTRA, width)
-    got = both[:, count, : 3 * count].astype(jnp.float32).reshape(n, 3, count)
-    return both[:, :count].reshape(n * count, width), (got[:, 0] + got[:, 1] + got[:, 2]).reshape(n * count)
 
 
 def sum_and_gather(x, own, axis):
@@ -191,9 +176,12 @@
         col_bars[iteration] = col_bar
     left = jnp.stack(row_bars + src_saved, axis=1)
     right = jnp.stack(old_saved + col_bars, axis=1)
-    lowrank = left[:, 0, None] * right[None, :, 0]
-    for k in range(1, left.shape[1]):
-        lowrank = lowrank + left[:, k, None] * right[None, :, k]
+    left_pieces, right_pieces = split3(left), split3(right)
+    left_all = jnp.concatenate([a for a in left_pieces for b in right_pieces], axis=1)
+    right_all = jnp.concatenate([b for a in left_pieces for b in right_pieces], axis=1)
+    lowrank = lax.dot_general(
+        left_all, right_all, (((1,), (1,)), ((), ())), preferred_element_type=jnp.float32
+    )
     cross_term_grid = (
         kernel * (last_src[:, None] * last_tgt[None, :] * (1.0 + kernel_grid) + lowrank)
     ).astype(jnp.bfloat16)

time: 260 us -> 261 us (level)
  blocking collectives: 121 us -> 102 us
  waiting for transfers between devices: 55.6 us -> 67.9 us
  starting transfers between devices: 43.6 us -> 50.6 us
  other arithmetic: 23.4 us -> 18.3 us
  matrix products: 7.5 us -> 11 us
    all_to_all x12 -> x10, blocking collectives: 108 us -> 89.4 us  [tree_sum(): return lax.all_to_all(spread, axis, 0, 0, tiled=False).sum(0)]
    all_to_all x1 -> x3, waiting for transfers between devices: 7.87 us -> 20.2 us  [tree_sum(): return lax.all_to_all(spread, axis, 0, 0, tiled=False).sum(0)]
    all_to_all x1 -> x3, starting transfers between devices: 3.51 us -> 10.6 us  [tree_sum(): return lax.all_to_all(spread, axis, 0, 0, tiled=False).sum(0)]
    convert_element_type x1 -> x0, other arithmetic: 5.37 us -> none  [per_device(): cross_term_grid = (kernel * (last_src[:, None] * last_tgt[None, :] * (1.0...]
    dot_general x0 -> x1, matrix products: none -> 3.48 us  [per_device(): lax.dot_general(left_all, right_all, (((1,), (1,)), ((), ())), preferred_...]
  transfers between devices with their start and end apart: 30 -> 32, of which waited for: 12 -> 13; matrix products, arithmetic and copies ran while one was open for 2% -> 3% of each run, Pallas kernels for 0% -> 0%
where the time goes in v9:
time: 261 us; the launch traced here: 260 us
  blocking collectives  102 us (39%)
  waiting for transfers between devices  67.9 us (26%)
  starting transfers between devices  50.6 us (19%)
  other arithmetic  18.3 us (7%)
  matrix products  11 us (4%)
  local copies, waits for them, and re-layouts  7.71 us (3%)
    all_to_all x10, blocking collectives, tree_sum(): return lax.all_to_all(spread, axis, 0, 0, tiled=False).sum(0)  89.4 us
    ppermute x14, waiting for transfers between devices, tree_scatter(): x = keep + lax.ppermute(send, axis, partner(axis, n, bit))  27.2 us
    ppermute x14, starting transfers between devices, tree_gather(): other = lax.ppermute(x, axis, partner(axis, n, bit))  20.3 us
    all_to_all x3, waiting for transfers between devices, tree_sum(): return lax.all_to_all(spread, axis, 0, 0, tiled=False).sum(0)  20.2 us
    ppermute x14, starting transfers between devices, tree_scatter(): x = keep + lax.ppermute(send, axis, partner(axis, n, bit))  16.4 us
    ppermute x14, waiting for transfers between devices, tree_gather(): other = lax.ppermute(x, axis, partner(axis, n, bit))  16.1 us
    all_to_all x1, blocking collectives, sum_and_gather(): got = lax.all_to_all(spread, axis, 0, 0, tiled=False)  13.1 us
    all_to_all x3, starting transfers between devices, tree_sum(): return lax.all_to_all(spread, axis, 0, 0, tiled=False).sum(0)  10.6 us
  transfers between devices with their start and end apart: 32, of which 13 were waited for; matrix products, arithmetic and copies ran while one was open for 3% of the time, Pallas kernels for 0%

profile of v9, /device:TPU:0, one launch (start us, length us, event | category | flops | bytes accessed | tf_op | source)
XLA Modules:
  0.0 259.7 jit_solution(3452886255818468609)
XLA Ops:
  1.5 4.0 %collective-permute-start.10 = (bf16[64,384]{1,0:T(8,128)(2,1)S(1)}, bf16[64,384]{1,0:T(8,128)(2,1)S(1)}, u32[]{:S(2)}, u32[]{:S(2)}) collective-permute-start(bf16[64,384]{1,0:T(8,128)(2,1)S(1)} %get-tuple-element.48), channel_id=1, source_target_pairs={{0,32},{1,33},{2,34},{3,35},{16,48},{17,49},{18,50},{19,51},{32,0}... | collective-permute-start | bytes 147464 | tf_op jit(solution)/shard_map/ppermute | solution.py:38
  5.5 3.0 %collective-permute-start.6 = (bf16[64,384]{1,0:T(8,128)(2,1)S(1)}, bf16[64,384]{1,0:T(8,128)(2,1)S(1)}, u32[]{:S(2)}, u32[]{:S(2)}) collective-permute-start(bf16[64,384]{1,0:T(8,128)(2,1)S(1)} %get-tuple-element.49), channel_id=1, source_target_pairs={{0,2},{1,3},{2,0},{3,1},{16,18},{17,19},{18,16},{19,17},{32,34},{3... | collective-permute-start | bytes 147464 | tf_op jit(solution)/shard_map/ppermute | solution.py:38
  11.2 2.9 %collective-permute-start = (bf16[128,384]{1,0:T(8,128)(2,1)S(1)}, bf16[128,384]{1,0:T(8,128)(2,1)S(1)}, u32[]{:S(2)}, u32[]{:S(2)}) collective-permute-start(bf16[128,384]{1,0:T(8,128)(2,1)S(1)} %get-tuple-element.39), channel_id=1, source_target_pairs={{0,4},{4,0},{8,12},{12,8},{64,68},{68,64},{72,76},{76,72},{1,5},{5... | collective-permute-start | bytes 294920 | tf_op jit(solution)/shard_map/ppermute | solution.py:38
  24.2 4.2 %collective-permute-done.4 = bf16[2,128,384]{2,1,0:T(8,128)(2,1)S(1)} collective-permute-done((bf16[2,128,384]{2,1,0:T(8,128)(2,1)S(1)}, bf16[2,128,384]{2,1,0:T(8,128)(2,1)S(1)}, u32[]{:S(2)}, u32[]{:S(2)}) %collective-permute-start.4) | collective-permute-done | bytes 196640 | tf_op jit(solution)/shard_map/ppermute | solution.py:38
  31.8 8.8 %collective-permute-done.13 = bf16[2,2,2,64,384]{4,3,1,2,0:T(8,128)(2,1)S(1)} collective-permute-done((bf16[2,2,2,64,384]{4,3,1,2,0:T(8,128)(2,1)S(1)}, bf16[2,2,2,64,384]{4,3,1,2,0:T(8,128)(2,1)S(1)}, u32[]{:S(2)}, u32[]{:S(2)}) %collective-permute-start.13) | collective-permute-done | bytes 393248 | tf_op jit(solution)/shard_map/ppermute | solution.py:38
  41.6 3.8 %exponential_convert_fusion = (bf16[1024,1024]{1,0:T(8,128)(2,1)S(1)}, f32[1024,1024]{1,0:T(8,128)}) fusion(bf16[1024,384]{1,0:T(8,128)(2,1)S(1)} %bitcast.221, bf16[1024,384]{1,0:T(8,128)(2,1)S(1)} %bitcast.223, bf16[1024,384]{1,0:T(8,128)(2,1)S(1)} %bitcast.217, bf16[1024,384]{1,0:T(8,128)(2,1)S(1)} %bitcast.219), kind=kOutput, calls=%fused_computation.34 | convolution fusion | flops 1619001344 | bytes 9437184 | tf_op jit(solution)/shard_map/dot_general | solution.py:130
  46.4 3.4 %all-to-all-start = ((f32[8,2,1024]{2,1,0:T(2,128)}), f32[8,2,1024]{2,1,0:T(2,128)S(1)}, u32[]{:S(2)}, u32[]{:S(2)}) async-start(f32[8,2,1024]{2,1,0:T(2,128)} %broadcast_in_dim.30), calls=%async_computation | async-start | bytes 131072 | tf_op jit(solution)/shard_map/all_to_all | solution.py:99
  50.5 4.5 %all-to-all-done = f32[8,2,1024]{2,1,0:T(2,128)S(1)} async-done(((f32[8,2,1024]{2,1,0:T(2,128)}), f32[8,2,1024]{2,1,0:T(2,128)S(1)}, u32[]{:S(2)}, u32[]{:S(2)}) %all-to-all-start) | async-done | bytes 65568 | tf_op jit(solution)/shard_map/all_to_all | solution.py:99
  55.6 13.1 %all_to_all.87 = f32[16,2,1024]{2,1,0:T(2,128)S(1)} all-to-all(f32[16,2,1024]{2,1,0:T(2,128)S(1)} %broadcast_in_dim.31), channel_id=1, replica_groups=mesh['y_lo'=2,'z'=4,'core'=2,'y_hi'=2,'x'=4] {'z','x'}, dimensions={0} | all-to-all | bytes 262144 | tf_op jit(solution)/shard_map/all_to_all | solution.py:99
  69.4 7.8 %all_to_all.88 = f32[8,1,1024]{2,1,0:T(1,128)S(1)} all-to-all(f32[8,1,1024]{2,1,0:T(1,128)S(1)} %broadcast_in_dim.32), channel_id=1, replica_groups=mesh['y_lo'=2,'z'=4,'core'=2,'y_hi'=2,'x'=4] {'y_lo','core','y_hi'}, dimensions={0} | all-to-all | bytes 65536 | tf_op jit(solution)/shard_map/all_to_all | solution.py:31
  77.8 10.7 %all_to_all.89 = f32[16,1,1024]{2,1,0:T(1,128)S(1)} all-to-all(f32[16,1,1024]{2,1,0:T(1,128)S(1)} %broadcast_in_dim.33), channel_id=1, replica_groups=mesh['y_lo'=2,'z'=4,'core'=2,'y_hi'=2,'x'=4] {'z','x'}, dimensions={0} | all-to-all | bytes 131072 | tf_op jit(solution)/shard_map/all_to_all | solution.py:31
  89.1 7.7 %all_to_all.90 = f32[8,1,1024]{2,1,0:T(1,128)S(1)} all-to-all(f32[8,1,1024]{2,1,0:T(1,128)S(1)} %broadcast_in_dim.34), channel_id=1, replica_groups=mesh['y_lo'=2,'z'=4,'core'=2,'y_hi'=2,'x'=4] {'y_lo','core','y_hi'}, dimensions={0} | all-to-all | bytes 65536 | tf_op jit(solution)/shard_map/all_to_all | solution.py:31
  97.3 10.8 %all_to_all.91 = f32[16,1,1024]{2,1,0:T(1,128)S(1)} all-to-all(f32[16,1,1024]{2,1,0:T(1,128)S(1)} %broadcast_in_dim.35), channel_id=1, replica_groups=mesh['y_lo'=2,'z'=4,'core'=2,'y_hi'=2,'x'=4] {'z','x'}, dimensions={0} | all-to-all | bytes 131072 | tf_op jit(solution)/shard_map/all_to_all | solution.py:31
  108.7 7.7 %all_to_all.92 = f32[8,1,1024]{2,1,0:T(1,128)S(1)} all-to-all(f32[8,1,1024]{2,1,0:T(1,128)S(1)} %broadcast_in_dim.36), channel_id=1, replica_groups=mesh['y_lo'=2,'z'=4,'core'=2,'y_hi'=2,'x'=4] {'y_lo','core','y_hi'}, dimensions={0} | all-to-all | bytes 65536 | tf_op jit(solution)/shard_map/all_to_all | solution.py:31
  116.5 3.2 %fusion.6 = (f32[1024]{0:T(1024)S(1)}, f32[1024]{0:T(1024)S(1)}) fusion(bf16[1024,1024]{1,0:T(8,128)(2,1)S(1)} %get-tuple-element.73, f32[1024]{0:T(1024)S(1)} %div.284, f32[1024,1024]{1,0:T(8,128)} %get-tuple-element.74), kind=kLoop, calls=%fused_computation.23 | loop fusion | flops 7337984 | bytes 6303744 | tf_op jit(solution)/shard_map/reduce_sum | solution.py:116
  120.4 3.5 %all-to-all-start.7 = ((f32[16,2,1024]{2,1,0:T(2,128)}), f32[16,2,1024]{2,1,0:T(2,128)S(1)}, u32[]{:S(2)}, u32[]{:S(2)}) async-start(f32[16,2,1024]{2,1,0:T(2,128)} %broadcast_in_dim.37), calls=%async_computation.7 | async-start | bytes 262144 | tf_op jit(solution)/shard_map/all_to_all | solution.py:31
  124.0 7.9 %all-to-all-done.7 = f32[16,2,1024]{2,1,0:T(2,128)S(1)} async-done(((f32[16,2,1024]{2,1,0:T(2,128)}), f32[16,2,1024]{2,1,0:T(2,128)S(1)}, u32[]{:S(2)}, u32[]{:S(2)}) %all-to-all-start.7) | async-done | bytes 131104 | tf_op jit(solution)/shard_map/all_to_all | solution.py:31
  131.9 3.5 %multiply_reduce_fusion = (f32[1024]{0:T(1024)S(1)}, f32[1024]{0:T(1024)S(1)}) fusion(f32[1024,1024]{1,0:T(8,128)} %get-tuple-element.74, bf16[1024,1024]{1,0:T(8,128)(2,1)S(1)} %get-tuple-element.73, f32[1024]{0:T(1024)S(1)} %bitcast.255, f32[1024]{0:T(1024)S(1)} %bitcast.258), kind=kLoop, calls=%fused_computation.32 | loop fusion | flops 7337984 | bytes 6307840 | tf_op jit(solution)/shard_map/reduce_sum | solution.py:112
  135.5 7.7 %all_to_all.93 = f32[8,1,1024]{2,1,0:T(1,128)S(1)} all-to-all(f32[8,1,1024]{2,1,0:T(1,128)S(1)} %broadcast_in_dim.38), channel_id=1, replica_groups=mesh['y_lo'=2,'z'=4,'core'=2,'y_hi'=2,'x'=4] {'y_lo','core','y_hi'}, dimensions={0} | all-to-all | bytes 65536 | tf_op jit(solution)/shard_map/all_to_all | solution.py:31
  143.7 10.7 %all_to_all.94 = f32[16,1,1024]{2,1,0:T(1,128)S(1)} all-to-all(f32[16,1,1024]{2,1,0:T(1,128)S(1)} %broadcast_in_dim.39), channel_id=1, replica_groups=mesh['y_lo'=2,'z'=4,'core'=2,'y_hi'=2,'x'=4] {'z','x'}, dimensions={0} | all-to-all | bytes 131072 | tf_op jit(solution)/shard_map/all_to_all | solution.py:31
  155.0 7.7 %all_to_all.95 = f32[8,1,1024]{2,1,0:T(1,128)S(1)} all-to-all(f32[8,1,1024]{2,1,0:T(1,128)S(1)} %broadcast_in_dim.40), channel_id=1, replica_groups=mesh['y_lo'=2,'z'=4,'core'=2,'y_hi'=2,'x'=4] {'y_lo','core','y_hi'}, dimensions={0} | all-to-all | bytes 65536 | tf_op jit(solution)/shard_map/all_to_all | solution.py:31
  163.3 10.8 %all_to_all.96 = f32[16,1,1024]{2,1,0:T(1,128)S(1)} all-to-all(f32[16,1,1024]{2,1,0:T(1,128)S(1)} %broadcast_in_dim.41), channel_id=1, replica_groups=mesh['y_lo'=2,'z'=4,'core'=2,'y_hi'=2,'x'=4] {'z','x'}, dimensions={0} | all-to-all | bytes 131072 | tf_op jit(solution)/shard_map/all_to_all | solution.py:31
  174.7 7.7 %all_to_all.97 = f32[8,1,1024]{2,1,0:T(1,128)S(1)} all-to-all(f32[8,1,1024]{2,1,0:T(1,128)S(1)} %broadcast_in_dim.42), channel_id=1, replica_groups=mesh['y_lo'=2,'z'=4,'core'=2,'y_hi'=2,'x'=4] {'y_lo','core','y_hi'}, dimensions={0} | all-to-all | bytes 65536 | tf_op jit(solution)/shard_map/all_to_all | solution.py:31
  183.6 3.5 %all-to-all-start.13 = ((f32[16,1,1024]{2,1,0:T(1,128)}), f32[16,1,1024]{2,1,0:T(1,128)S(1)}, u32[]{:S(2)}, u32[]{:S(2)}) async-start(f32[16,1,1024]{2,1,0:T(1,128)} %broadcast_in_dim.43), calls=%async_computation.13 | async-start | bytes 131072 | tf_op jit(solution)/shard_map/all_to_all | solution.py:31
  187.2 7.5 %all-to-all-done.13 = f32[16,1,1024]{2,1,0:T(1,128)S(1)} async-done(((f32[16,1,1024]{2,1,0:T(1,128)}), f32[16,1,1024]{2,1,0:T(1,128)S(1)}, u32[]{:S(2)}, u32[]{:S(2)}) %all-to-all-start.13) | async-done | bytes 65568 | tf_op jit(solution)/shard_map/all_to_all | solution.py:31
  195.9 3.6 %all-to-all-start.14 = ((f32[8,1,1024]{2,1,0:T(1,128)}), f32[8,1,1024]{2,1,0:T(1,128)S(1)}, u32[]{:S(2)}, u32[]{:S(2)}) async-start(f32[8,1,1024]{2,1,0:T(1,128)} %broadcast_in_dim.44), calls=%async_computation.14 | async-start | bytes 65536 | tf_op jit(solution)/shard_map/all_to_all | solution.py:31
  199.7 4.8 %all-to-all-done.14 = f32[8,1,1024]{2,1,0:T(1,128)S(1)} async-done(((f32[8,1,1024]{2,1,0:T(1,128)}), f32[8,1,1024]{2,1,0:T(1,128)S(1)}, u32[]{:S(2)}, u32[]{:S(2)}) %all-to-all-start.14) | async-done | bytes 32800 | tf_op jit(solution)/shard_map/all_to_all | solution.py:31
  204.8 3.5 %fusion.14 = bf16[1024,1024]{1,0:T(8,128)(2,1)S(1)} fusion(bf16[1024,1024]{1,0:T(8,128)(2,1)S(1)} %get-tuple-element.73, f32[1024,1024]{1,0:T(8,128)} %get-tuple-element.74, bf16[1024,72]{0,1:T(8,128)(2,1)S(1)} %get-tuple-element.75, bf16[1024,72]{0,1:T(8,128)(2,1)S(1)} %get-tuple-element.76, f32[1024]{0:T(1024)S(1)} %bitcast.256, f32[1024]{0:T(1024)S(1)} %div.284), kind=kOutput, calls=%fused_computation.31 | convolution fusion | flops 159383552 | bytes 8691712 | tf_op jit(solution)/shard_map/dot_general | solution.py:182
  217.9 15.5 %collective-permute-done.24 = f32[2,2,2,64,384]{4,3,1,0,2:T(8,128)S(1)} collective-permute-done((f32[2,2,2,64,384]{4,3,1,0,2:T(8,128)S(1)}, f32[2,2,2,64,384]{4,3,1,0,2:T(8,128)S(1)}, u32[]{:S(2)}, u32[]{:S(2)}) %collective-permute-start.24) | collective-permute-done | bytes 786464 | tf_op jit(solution)/shard_map/ppermute | solution.py:61
  238.7 5.3 %collective-permute-done.25 = f32[2,2,64,384]{3,2,1,0:T(8,128)S(1)} collective-permute-done((f32[2,2,64,384]{3,2,1,0:T(8,128)S(1)}, f32[2,2,64,384]{3,2,1,0:T(8,128)S(1)}, u32[]{:S(2)}, u32[]{:S(2)}) %collective-permute-start.25) | collective-permute-done | bytes 393248 | tf_op jit(solution)/shard_map/ppermute | solution.py:61
  246.9 4.4 %collective-permute-done.26 = f32[2,64,384]{2,1,0:T(8,128)S(1)} collective-permute-done((f32[2,64,384]{2,1,0:T(8,128)S(1)}, f32[2,64,384]{2,1,0:T(8,128)S(1)}, u32[]{:S(2)}, u32[]{:S(2)}) %collective-permute-start.26) | collective-permute-done | bytes 196640 | tf_op jit(solution)/shard_map/ppermute | solution.py:61
  252.7 3.4 %collective-permute-start.23 = (f32[64,384]{1,0:T(8,128)S(1)}, f32[64,384]{1,0:T(8,128)S(1)}, u32[]{:S(2)}, u32[]{:S(2)}) collective-permute-start(f32[64,384]{1,0:T(8,128)S(1)} %select_bitcast_fusion.11), channel_id=1, source_target_pairs={{0,32},{1,33},{2,34},{3,35},{16,48},{17,49},{18,50},{19,51},{32,0}... | collective-permute-start | bytes 294920 | tf_op jit(solution)/shard_map/ppermute | solution.py:61
  (225 shorter events, 51.5 us)
Async XLA Ops:
  1.5 13.6 %collective-permute-start.10 = (bf16[64,384]{1,0:T(8,128)(2,1)S(1)}, bf16[64,384]{1,0:T(8,128)(2,1)S(1)}, u32[]{:S(2)}, u32[]{:S(2)}) collective-permute-start(bf16[64,384]{1,0:T(8,128)(2,1)S(1)} %get-tuple-element.48), channel_id=1, source_target_pairs={{0,32},{1,33},{2,34},{3,35},{16,48},{17,49},{18,50},{19,51},{32,0}... | collective-permute-start | bytes 147464 | tf_op jit(solution)/shard_map/ppermute | solution.py:38
  5.5 9.3 %collective-permute-start.6 = (bf16[64,384]{1,0:T(8,128)(2,1)S(1)}, bf16[64,384]{1,0:T(8,128)(2,1)S(1)}, u32[]{:S(2)}, u32[]{:S(2)}) collective-permute-start(bf16[64,384]{1,0:T(8,128)(2,1)S(1)} %get-tuple-element.49), channel_id=1, source_target_pairs={{0,2},{1,3},{2,0},{3,1},{16,18},{17,19},{18,16},{19,17},{32,34},{3... | collective-permute-start | bytes 147464 | tf_op jit(solution)/shard_map/ppermute | solution.py:38
  9.5 8.9 %collective-permute-start.3 = (bf16[128,384]{1,0:T(8,128)(2,1)S(1)}, bf16[128,384]{1,0:T(8,128)(2,1)S(1)}, u32[]{:S(2)}, u32[]{:S(2)}) collective-permute-start(bf16[128,384]{1,0:T(8,128)(2,1)S(1)} %get-tuple-element.38), channel_id=1, source_target_pairs={{0,64},{4,68},{8,72},{12,76},{64,0},{68,4},{72,8},{76,12},{1,65},{... | collective-permute-start | bytes 294920 | tf_op jit(solution)/shard_map/ppermute | solution.py:38
  11.2 7.0 %collective-permute-start = (bf16[128,384]{1,0:T(8,128)(2,1)S(1)}, bf16[128,384]{1,0:T(8,128)(2,1)S(1)}, u32[]{:S(2)}, u32[]{:S(2)}) collective-permute-start(bf16[128,384]{1,0:T(8,128)(2,1)S(1)} %get-tuple-element.39), channel_id=1, source_target_pairs={{0,4},{4,0},{8,12},{12,8},{64,68},{68,64},{72,76},{76,72},{1,5},{5... | collective-permute-start | bytes 294920 | tf_op jit(solution)/shard_map/ppermute | solution.py:38
  14.9 7.1 %collective-permute-start.7 = (bf16[2,64,384]{2,1,0:T(8,128)(2,1)S(1)}, bf16[2,64,384]{2,1,0:T(8,128)(2,1)S(1)}, u32[]{:S(2)}, u32[]{:S(2)}) collective-permute-start(bf16[2,64,384]{2,1,0:T(8,128)(2,1)S(1)} %maximum_select_fusion.19), channel_id=1, source_target_pairs={{0,32},{1,33},{2,34},{3,35},{16,48},{17,49},{18,50},{19,51},{32,0}... | collective-permute-start | bytes 294920 | tf_op jit(solution)/shard_map/ppermute | solution.py:38
  15.1 6.2 %collective-permute-start.11 = (bf16[2,64,384]{2,1,0:T(8,128)(2,1)S(1)}, bf16[2,64,384]{2,1,0:T(8,128)(2,1)S(1)}, u32[]{:S(2)}, u32[]{:S(2)}) collective-permute-start(bf16[2,64,384]{2,1,0:T(8,128)(2,1)S(1)} %maximum_select_fusion.21), channel_id=1, source_target_pairs={{0,2},{1,3},{2,0},{3,1},{16,18},{17,19},{18,16},{19,17},{32,34},{3... | collective-permute-start | bytes 294920 | tf_op jit(solution)/shard_map/ppermute | solution.py:38
  18.2 10.3 %collective-permute-start.1 = (bf16[2,128,384]{2,1,0:T(8,128)(2,1)S(1)}, bf16[2,128,384]{2,1,0:T(8,128)(2,1)S(1)}, u32[]{:S(2)}, u32[]{:S(2)}) collective-permute-start(bf16[2,128,384]{2,1,0:T(8,128)(2,1)S(1)} %maximum_select_fusion.12), channel_id=1, source_target_pairs={{0,64},{4,68},{8,72},{12,76},{64,0},{68,4},{72,8},{76,12},{1,65},{... | collective-permute-start | bytes 589832 | tf_op jit(solution)/shard_map/ppermute | solution.py:38
  18.5 9.8 %collective-permute-start.4 = (bf16[2,128,384]{2,1,0:T(8,128)(2,1)S(1)}, bf16[2,128,384]{2,1,0:T(8,128)(2,1)S(1)}, u32[]{:S(2)}, u32[]{:S(2)}) collective-permute-start(bf16[2,128,384]{2,1,0:T(8,128)(2,1)S(1)} %maximum_select_fusion.14), channel_id=1, source_target_pairs={{0,4},{4,0},{8,12},{12,8},{64,68},{68,64},{72,76},{76,72},{1,5},{5... | collective-permute-start | bytes 589832 | tf_op jit(solution)/shard_map/ppermute | solution.py:38
  21.4 7.9 %collective-permute-start.12 = (bf16[2,2,64,384]{3,2,0,1:T(8,128)(2,1)S(1)}, bf16[2,2,64,384]{3,2,0,1:T(8,128)(2,1)S(1)}, u32[]{:S(2)}, u32[]{:S(2)}) collective-permute-start(bf16[2,2,64,384]{3,2,0,1:T(8,128)(2,1)S(1)} %maximum_select_fusion.18), channel_id=1, source_target_pairs={{0,1},{1,0},{2,3},{3,2},{16,17},{17,16},{18,19},{19,18},{32,33},{3... | collective-permute-start | bytes 589832 | tf_op jit(solution)/shard_map/ppermute | solution.py:38
  22.1 8.4 %collective-permute-start.8 = (bf16[2,2,64,384]{3,2,1,0:T(8,128)(2,1)S(1)}, bf16[2,2,64,384]{3,2,1,0:T(8,128)(2,1)S(1)}, u32[]{:S(2)}, u32[]{:S(2)}) collective-permute-start(bf16[2,2,64,384]{3,2,1,0:T(8,128)(2,1)S(1)} %maximum_select_fusion.16), channel_id=1, source_target_pairs={{0,16},{1,17},{2,18},{3,19},{16,0},{17,1},{18,2},{19,3},{32,48},{3... | collective-permute-start | bytes 589832 | tf_op jit(solution)/shard_map/ppermute | solution.py:38
  28.4 2.9 %collective-permute-start.5 = (bf16[2,2,128,384]{3,2,1,0:T(8,128)(2,1)S(1)}, bf16[2,2,128,384]{3,2,1,0:T(8,128)(2,1)S(1)}, u32[]{:S(2)}, u32[]{:S(2)}) collective-permute-start(bf16[2,2,128,384]{3,2,1,0:T(8,128)(2,1)S(1)} %maximum_select_fusion.6), channel_id=1, source_target_pairs={{0,8},{4,12},{8,0},{12,4},{64,72},{68,76},{72,64},{76,68},{1,9},{5... | collective-permute-start | bytes 1179656 | tf_op jit(solution)/shard_map/ppermute | solution.py:38
  28.6 3.0 %collective-permute-start.2 = (bf16[2,2,128,384]{3,2,1,0:T(8,128)(2,1)S(1)}, bf16[2,2,128,384]{3,2,1,0:T(8,128)(2,1)S(1)}, u32[]{:S(2)}, u32[]{:S(2)}) collective-permute-start(bf16[2,2,128,384]{3,2,1,0:T(8,128)(2,1)S(1)} %maximum_select_fusion.4), channel_id=1, source_target_pairs={{0,8},{4,12},{8,0},{12,4},{64,72},{68,76},{72,64},{76,68},{1,9},{5... | collective-permute-start | bytes 1179656 | tf_op jit(solution)/shard_map/ppermute | solution.py:38
  29.4 11.1 %collective-permute-start.13 = (bf16[2,2,2,64,384]{4,3,1,2,0:T(8,128)(2,1)S(1)}, bf16[2,2,2,64,384]{4,3,1,2,0:T(8,128)(2,1)S(1)}, u32[]{:S(2)}, u32[]{:S(2)}) collective-permute-start(bf16[2,2,2,64,384]{4,3,1,2,0:T(8,128)(2,1)S(1)} %maximum_select_fusion.10), channel_id=1, source_target_pairs={{0,16},{1,17},{2,18},{3,19},{16,0},{17,1},{18,2},{19,3},{32,48},{3... | collective-permute-start | bytes 1179656 | tf_op jit(solution)/shard_map/ppermute | solution.py:38
  30.6 10.8 %collective-permute-start.9 = (bf16[2,2,2,64,384]{4,3,2,1,0:T(8,128)(2,1)S(1)}, bf16[2,2,2,64,384]{4,3,2,1,0:T(8,128)(2,1)S(1)}, u32[]{:S(2)}, u32[]{:S(2)}) collective-permute-start(bf16[2,2,2,64,384]{4,3,2,1,0:T(8,128)(2,1)S(1)} %maximum_select_fusion.8), channel_id=1, source_target_pairs={{0,1},{1,0},{2,3},{3,2},{16,17},{17,16},{18,19},{19,18},{32,33},{3... | collective-permute-start | bytes 1179656 | tf_op jit(solution)/shard_map/ppermute | solution.py:38
  46.4 8.6 %all-to-all-start = ((f32[8,2,1024]{2,1,0:T(2,128)}), f32[8,2,1024]{2,1,0:T(2,128)S(1)}, u32[]{:S(2)}, u32[]{:S(2)}) async-start(f32[8,2,1024]{2,1,0:T(2,128)} %broadcast_in_dim.30), calls=%async_computation | async-start | bytes 131072 | tf_op jit(solution)/shard_map/all_to_all | solution.py:99
  120.4 11.5 %all-to-all-start.7 = ((f32[16,2,1024]{2,1,0:T(2,128)}), f32[16,2,1024]{2,1,0:T(2,128)S(1)}, u32[]{:S(2)}, u32[]{:S(2)}) async-start(f32[16,2,1024]{2,1,0:T(2,128)} %broadcast_in_dim.37), calls=%async_computation.7 | async-start | bytes 262144 | tf_op jit(solution)/shard_map/all_to_all | solution.py:31
  183.6 11.1 %all-to-all-start.13 = ((f32[16,1,1024]{2,1,0:T(1,128)}), f32[16,1,1024]{2,1,0:T(1,128)S(1)}, u32[]{:S(2)}, u32[]{:S(2)}) async-start(f32[16,1,1024]{2,1,0:T(1,128)} %broadcast_in_dim.43), calls=%async_computation.13 | async-start | bytes 131072 | tf_op jit(solution)/shard_map/all_to_all | solution.py:31
  195.9 8.6 %all-to-all-start.14 = ((f32[8,1,1024]{2,1,0:T(1,128)}), f32[8,1,1024]{2,1,0:T(1,128)S(1)}, u32[]{:S(2)}, u32[]{:S(2)}) async-start(f32[8,1,1024]{2,1,0:T(1,128)} %broadcast_in_dim.44), calls=%async_computation.14 | async-start | bytes 65536 | tf_op jit(solution)/shard_map/all_to_all | solution.py:31
  212.9 2.4 collective-permute-start.17
  213.2 3.7 %collective-permute-start.14 = (f32[2,2,128,384]{3,2,0,1:T(8,128)S(1)}, f32[2,2,128,384]{3,2,0,1:T(8,128)S(1)}, u32[]{:S(2)}, u32[]{:S(2)}) collective-permute-start(f32[2,2,128,384]{3,2,0,1:T(8,128)S(1)} %select_bitcast_fusion.3), channel_id=1, source_target_pairs={{0,8},{4,12},{8,0},{12,4},{64,72},{68,76},{72,64},{76,68},{1,9},{5... | collective-permute-start | bytes 2359304 | tf_op jit(solution)/shard_map/ppermute | solution.py:61
  213.7 19.6 %collective-permute-start.24 = (f32[2,2,2,64,384]{4,3,1,0,2:T(8,128)S(1)}, f32[2,2,2,64,384]{4,3,1,0,2:T(8,128)S(1)}, u32[]{:S(2)}, u32[]{:S(2)}) collective-permute-start(f32[2,2,2,64,384]{4,3,1,0,2:T(8,128)S(1)} %select_bitcast_fusion), channel_id=1, source_target_pairs={{0,16},{1,17},{2,18},{3,19},{16,0},{17,1},{18,2},{19,3},{32,48},{3... | collective-permute-start | bytes 2359304 | tf_op jit(solution)/shard_map/ppermute | solution.py:61
  214.5 19.7 %collective-permute-start.20 = (f32[2,2,2,64,384]{4,3,0,2,1:T(8,128)S(1)}, f32[2,2,2,64,384]{4,3,0,2,1:T(8,128)S(1)}, u32[]{:S(2)}, u32[]{:S(2)}) collective-permute-start(f32[2,2,2,64,384]{4,3,0,2,1:T(8,128)S(1)} %select_bitcast_fusion.1), channel_id=1, source_target_pairs={{0,1},{1,0},{2,3},{3,2},{16,17},{17,16},{18,19},{19,18},{32,33},{3... | collective-permute-start | bytes 2359304 | tf_op jit(solution)/shard_map/ppermute | solution.py:61
  215.4 20.3 %collective-permute-start.18 = (f32[2,128,384]{2,1,0:T(8,128)S(1)}, f32[2,128,384]{2,1,0:T(8,128)S(1)}, u32[]{:S(2)}, u32[]{:S(2)}) collective-permute-start(f32[2,128,384]{2,1,0:T(8,128)S(1)} %select_bitcast_fusion.6), channel_id=1, source_target_pairs={{0,4},{4,0},{8,12},{12,8},{64,68},{68,64},{72,76},{76,72},{1,5},{5... | collective-permute-start | bytes 1179656 | tf_op jit(solution)/shard_map/ppermute | solution.py:61
  217.0 19.5 %collective-permute-start.15 = (f32[2,128,384]{2,1,0:T(8,128)S(1)}, f32[2,128,384]{2,1,0:T(8,128)S(1)}, u32[]{:S(2)}, u32[]{:S(2)}) collective-permute-start(f32[2,128,384]{2,1,0:T(8,128)S(1)} %fusion.17), channel_id=1, source_target_pairs={{0,64},{4,68},{8,72},{12,76},{64,0},{68,4},{72,8},{76,12},{1,65},{... | collective-permute-start | bytes 1179656 | tf_op jit(solution)/shard_map/ppermute | solution.py:61
  233.6 10.4 %collective-permute-start.25 = (f32[2,2,64,384]{3,2,1,0:T(8,128)S(1)}, f32[2,2,64,384]{3,2,1,0:T(8,128)S(1)}, u32[]{:S(2)}, u32[]{:S(2)}) collective-permute-start(f32[2,2,64,384]{3,2,1,0:T(8,128)S(1)} %select_bitcast_fusion.4), channel_id=1, source_target_pairs={{0,1},{1,0},{2,3},{3,2},{16,17},{17,16},{18,19},{19,18},{32,33},{3... | collective-permute-start | bytes 1179656 | tf_op jit(solution)/shard_map/ppermute | solution.py:61
  234.4 10.9 %collective-permute-start.21 = (f32[2,2,64,384]{3,2,0,1:T(8,128)S(1)}, f32[2,2,64,384]{3,2,0,1:T(8,128)S(1)}, u32[]{:S(2)}, u32[]{:S(2)}) collective-permute-start(f32[2,2,64,384]{3,2,0,1:T(8,128)S(1)} %select_bitcast_fusion.5), channel_id=1, source_target_pairs={{0,16},{1,17},{2,18},{3,19},{16,0},{17,1},{18,2},{19,3},{32,48},{3... | collective-permute-start | bytes 1179656 | tf_op jit(solution)/shard_map/ppermute | solution.py:61
  235.8 20.3 %collective-permute-start.19 = (f32[128,384]{1,0:T(8,128)S(1)}, f32[128,384]{1,0:T(8,128)S(1)}, u32[]{:S(2)}, u32[]{:S(2)}) collective-permute-start(f32[128,384]{1,0:T(8,128)S(1)} %select_bitcast_fusion.8), channel_id=1, source_target_pairs={{0,64},{4,68},{8,72},{12,76},{64,0},{68,4},{72,8},{76,12},{1,65},{... | collective-permute-start | bytes 589832 | tf_op jit(solution)/shard_map/ppermute | solution.py:61
  236.6 19.6 %collective-permute-start.16 = (f32[128,384]{1,0:T(8,128)S(1)}, f32[128,384]{1,0:T(8,128)S(1)}, u32[]{:S(2)}, u32[]{:S(2)}) collective-permute-start(f32[128,384]{1,0:T(8,128)S(1)} %select_bitcast_fusion.9), channel_id=1, source_target_pairs={{0,4},{4,0},{8,12},{12,8},{64,68},{68,64},{72,76},{76,72},{1,5},{5... | collective-permute-start | bytes 589832 | tf_op jit(solution)/shard_map/ppermute | solution.py:61
  244.0 7.3 %collective-permute-start.26 = (f32[2,64,384]{2,1,0:T(8,128)S(1)}, f32[2,64,384]{2,1,0:T(8,128)S(1)}, u32[]{:S(2)}, u32[]{:S(2)}) collective-permute-start(f32[2,64,384]{2,1,0:T(8,128)S(1)} %fusion.18), channel_id=1, source_target_pairs={{0,32},{1,33},{2,34},{3,35},{16,48},{17,49},{18,50},{19,51},{32,0}... | collective-permute-start | bytes 589832 | tf_op jit(solution)/shard_map/ppermute | solution.py:61
  245.4 7.3 %collective-permute-start.22 = (f32[2,64,384]{2,1,0:T(8,128)S(1)}, f32[2,64,384]{2,1,0:T(8,128)S(1)}, u32[]{:S(2)}, u32[]{:S(2)}) collective-permute-start(f32[2,64,384]{2,1,0:T(8,128)S(1)} %select_bitcast_fusion.7), channel_id=1, source_target_pairs={{0,2},{1,3},{2,0},{3,1},{16,18},{17,19},{18,16},{19,17},{32,34},{3... | collective-permute-start | bytes 589832 | tf_op jit(solution)/shard_map/ppermute | solution.py:61
  251.3 6.2 %collective-permute-start.27 = (f32[64,384]{1,0:T(8,128)S(1)}, f32[64,384]{1,0:T(8,128)S(1)}, u32[]{:S(2)}, u32[]{:S(2)}) collective-permute-start(f32[64,384]{1,0:T(8,128)S(1)} %select_bitcast_fusion.10), channel_id=1, source_target_pairs={{0,2},{1,3},{2,0},{3,1},{16,18},{17,19},{18,16},{19,17},{32,34},{3... | collective-permute-start | bytes 294920 | tf_op jit(solution)/shard_map/ppermute | solution.py:61
  252.7 6.2 %collective-permute-start.23 = (f32[64,384]{1,0:T(8,128)S(1)}, f32[64,384]{1,0:T(8,128)S(1)}, u32[]{:S(2)}, u32[]{:S(2)}) collective-permute-start(f32[64,384]{1,0:T(8,128)S(1)} %select_bitcast_fusion.11), channel_id=1, source_target_pairs={{0,32},{1,33},{2,34},{3,35},{16,48},{17,49},{18,50},{19,51},{32,0}... | collective-permute-start | bytes 294920 | tf_op jit(solution)/shard_map/ppermute | solution.py:61
  (6 other events, 29.5 us)
